TPU v7x, 32 devices: a whole 2x2x4 slice. The times are simulated.
32 devices in a mesh: aux: 4 (over y, x), pair: 8 (over z, core).
Axes of the slice: x: 2, y: 2, z: 4, core: 2. Of those that a mesh axis runs over, the one named last changes fastest.
Arguments:
- three_index: bfloat16 [32, 2048, 256], P('pair', 'aux'), may hold values from -6 to 6
- pno_coef: bfloat16 [128, 2, 256, 192], P('pair'), may hold values from -0.375 to 0.375
- pair_orbitals: int32 [128, 2], P('pair'), may hold values from 0 to 31, as said below
- natural_orbital_class: int32 [128], P('pair'), may hold values from 0 to 3
- pno_energy: float32 [128, 192], P('pair'), may hold values from 0.5 to 4
- margin: bfloat16 [128, 2, 192, 192], P('pair'), may hold values from -0.4375 to 0.4375
- neighbour_pairs: int32 [128, 2], P('pair'), may hold values from 0 to 127, as said below
- fock_coupling: float32 [128, 2], P('pair'), may hold values from -0.9 to 0.9
Outputs:
- amplitudes: float32 [128, 192, 192], P('pair')
- residual: float32 [128, 192, 192], P('pair')
Inputs may be any that keep to these rules, and one draw needn't show every extreme that they name: `pair_orbitals`: column 0 names an orbital of the pair's own block of 4 orbitals (pair p's block is p // 16); column 1 names one of that block or of the block just before or after it. `neighbour_pairs`: each entry names another pair of the pair's own block of 16 pairs or of the block just before or after it.
All inputs are finite; a program needn't handle non-finite values.
Results may differ from a plain program's by a relative error of at most 0.0032.
Values may be sent and summed in bfloat16 or wider, within the bound.
No kernel may reach another device: no remote copies, remote signals or barrier semaphores. Data moves between devices by JAX's collectives and lax.ppermute only.
A program may use at most 128 MiB of HBM per device.

v0:
```python
import jax
import jax.numpy as jnp
from jax import lax
from jax.sharding import PartitionSpec as P

NPNO = 192
ITERS = 2


def with_halo(cells, sides, width):
    for axis, dim in sides:
        count = lax.axis_size(axis)
        ends = count - 1
        head = lax.slice_in_dim(cells, 0, width, axis=dim)
        tail = lax.slice_in_dim(cells, cells.shape[dim] - width, cells.shape[dim], axis=dim)
        cells = jnp.concatenate(
            [
                lax.ppermute(tail, axis, [(i, (i + 1) % count) for i in range(ends)]),
                cells,
                lax.ppermute(head, axis, [((i + 1) % count, i) for i in range(ends)]),
            ],
            axis=dim,
        )
    return cells


def class_mask(natural_orbital_class):
    counts = jnp.where(
        natural_orbital_class == 0,
        NPNO // 6,
        jnp.where(
            natural_orbital_class == 1,
            NPNO // 3,
            jnp.where(natural_orbital_class == 2, 2 * NPNO // 3, NPNO),
        ),
    )
    return jnp.arange(NPNO, dtype=jnp.int32)[None, :] < counts[:, None]


def transformed_product(side_blocks, gathered, weights):
    inner_part = jnp.einsum(
        "pnab,pnbc->pnac", side_blocks, gathered, precision=lax.Precision.HIGHEST
    )
    outer_part = jnp.einsum(
        "pnac,pndc->pnad", inner_part, side_blocks, precision=lax.Precision.HIGHEST
    )
    return jnp.einsum("pn,pnad->pad", weights, outer_part, precision=lax.Precision.HIGHEST)


def iterate(exchange_ints, denominator, coupling):
    amplitudes = jnp.zeros_like(exchange_ints)
    for iteration in range(ITERS):
        current_residual = exchange_ints + denominator * amplitudes
        if iteration > 0:
            current_residual = current_residual - coupling(amplitudes)
        amplitudes = amplitudes - current_residual / denominator
    residual = exchange_ints + denominator * amplitudes - coupling(amplitudes)
    return (amplitudes, residual)


def per_device(
    three_index,
    pno_coef,
    pair_orbitals,
    natural_orbital_class,
    pno_energy,
    margin,
    neighbour_pairs,
    fock_coupling,
):
    occ_dev = three_index.shape[0]
    pair_dev = pno_coef.shape[0]
    position = lax.axis_index("pair")
    natural_orbital_mask = class_mask(natural_orbital_class)
    padded = with_halo(three_index, (("pair", 0),), occ_dev)
    local_orbitals = pair_orbitals - (position - 1) * occ_dev
    leading_block = jnp.take(padded, local_orbitals[:, 0], axis=0)
    trailing_block = jnp.take(padded, local_orbitals[:, 1], axis=0)
    masked_coefficient_rows = jnp.where(
        natural_orbital_mask[:, None, None, :], pno_coef, jnp.zeros((), jnp.bfloat16)
    )
    left_half = jnp.einsum(
        "cyg,cgh->cyh",
        leading_block,
        masked_coefficient_rows[:, 0],
        preferred_element_type=jnp.float32,
    ).astype(jnp.bfloat16)
    right_half = jnp.einsum(
        "cyg,cgh->cyh",
        trailing_block,
        masked_coefficient_rows[:, 1],
        preferred_element_type=jnp.float32,
    ).astype(jnp.bfloat16)
    partial_ints = jnp.einsum(
        "pqa,pqb->pab", left_half, right_half, preferred_element_type=jnp.float32
    )
    mask_float = natural_orbital_mask.astype(jnp.float32)
    exchange_ints = lax.psum(partial_ints, "aux")
    denominator = pno_energy[:, :, None] + pno_energy[:, None, :]
    side_blocks = margin.astype(jnp.float32) * mask_float[:, None, :, None]
    local_rows = neighbour_pairs - (position - 1) * pair_dev

    def coupling(current):
        padded_amps = with_halo(current, (("pair", 0),), pair_dev)
        gathered = jnp.take(padded_amps, local_rows, axis=0)
        return transformed_product(side_blocks, gathered, fock_coupling)

    amplitudes, residual = iterate(exchange_ints, denominator, coupling)
    return (amplitudes, residual)


def solution(mesh):
    return jax.shard_map(
        per_device,
        mesh=mesh,
        in_specs=(
            P("pair", "aux", None),
            P("pair", None, None, None),
            P("pair", None),
            P("pair"),
            P("pair", None),
            P("pair", None, None, None),
            P("pair", None),
            P("pair", None),
        ),
        out_specs=(P("pair", None, None), P("pair", None, None)),
        check_vma=False,
    )
```

profile of v0, /device:TPU:1, one launch (start us, length us, event | category | flops | bytes accessed | tf_op | source)
XLA Modules:
  0.0 342.4 jit_solution(12701743786358412983)
XLA Ops:
  7.2 0.0 all-reduce.2.cloned.1.call-start
  7.2 4.6 %collective-permute-start = (bf16[4,512,256]{2,1,0:T(8,128)(2,1)}, bf16[4,512,256]{2,1,0:T(8,128)(2,1)}, u32[]{:S(2)}, u32[]{:S(2)}) collective-permute-start(bf16[4,512,256]{2,1,0:T(8,128)(2,1)} %param.12), channel_id=1, source_target_pairs={{0,1},{1,2},{2,3},{3,4},{4,5},{5,6},{6,7},{8,9},{9,10},{10,11},{11... | collective-permute-start | bytes 3145736 | tf_op jit(solution)/shard_map/ppermute | solution.py:18
  11.8 1.9 collective-permute-start.1
  13.8 0.7 broadcast_subtract_fusion
  14.4 0.7 compare_select_fusion.5
  15.1 0.1 fusion.45
  15.2 3.4 %broadcast_select_fusion = bf16[16,2,256,192]{2,3,1,0:T(8,128)(2,1)} fusion(bf16[16,2,256,192]{2,3,1,0:T(8,128)(2,1)} %param.13, pred[16,192]{1,0:T(8,128)(4,1)S(1)} %get-tuple-element.13), kind=kLoop, calls=%fused_computation.46 | loop fusion | flops 1572864 | bytes 6294528 | tf_op jit(solution)/shard_map/jit(_where)/select_n | solution.py:79
  18.6 5.2 %collective-permute-done = bf16[4,512,256]{2,1,0:T(8,128)(2,1)} collective-permute-done((bf16[4,512,256]{2,1,0:T(8,128)(2,1)}, bf16[4,512,256]{2,1,0:T(8,128)(2,1)}, u32[]{:S(2)}, u32[]{:S(2)}) %collective-permute-start) | collective-permute-done | bytes 1048608 | tf_op jit(solution)/shard_map/ppermute | solution.py:18
  23.9 1.3 constant_dynamic-update-slice_fusion.2
  25.2 0.1 constant_dynamic-update-slice_fusion.1
  25.2 3.0 collective-permute-done.1
  28.3 1.3 constant_dynamic-update-slice_fusion
  29.6 2.8 gather_fusion.1
  32.3 2.8 gather_fusion
  35.1 6.1 %fusion.10 = bf16[16,512,192]{1,2,0:T(8,128)(2,1)} fusion(bf16[16,512,256]{2,1,0:T(8,128)(2,1)} %gather_fusion.1, pred[16]{0:T(512)(128)(4,1)S(1)} %get-tuple-element.10, bf16[16,2,256,192]{2,3,1,0:T(8,128)(2,1)} %broadcast_select_fusion), kind=kOutput, calls=%fused_computation.22 | convolution fusion | flops 807403520 | bytes 8912912 | tf_op jit(solution)/shard_map/cyg,cgh->cyh/dot_general | solution.py:88
  41.2 7.3 %fusion.29 = f32[16,192,192]{2,1,0:T(8,128)} fusion(bf16[16,512,192]{1,2,0:T(8,128)(2,1)} %fusion.10, bf16[16,512,256]{2,1,0:T(8,128)(2,1)} %gather_fusion, pred[16]{0:T(512)(128)(4,1)S(1)} %get-tuple-element.6, bf16[16,2,256,192]{2,3,1,0:T(8,128)(2,1)S(1)} %copy-done.6), kind=kOutput, calls=%fused_computation.41 | convolution fusion | flops 1412956160 | bytes 11272704 | tf_op jit(solution)/shard_map/pqa,pqb->pab/dot_general | solution.py:94
  48.5 0.0 all-reduce.2.cloned.1.call-update
  48.5 0.0 copy-start.9
  48.5 0.0 copy-start.10
  48.5 87.1 %all-reduce.2.cloned.1.call-done = f32[16,192,192]{2,1,0:T(8,128)} async-done(((f32[16,192,192]{2,1,0:T(8,128)}), f32[16,192,192]{2,1,0:T(8,128)}) %all-reduce.2.cloned.1.call-update) | async-done | bytes 2359312 | tf_op jit(solution)/shard_map/psum | solution.py:98
  135.6 2.3 fusion.17
  137.9 2.6 collective-permute-start.3
  140.5 3.2 collective-permute-start.2
  143.7 0.1 copy.14
  143.8 0.1 copy.19
  143.9 0.1 copy.15
  144.0 0.1 reshape.94
  144.1 32.5 %collective-permute-done.3 = f32[16,192,192]{2,1,0:T(8,128)} collective-permute-done((f32[16,192,192]{2,1,0:T(8,128)S(1)}, f32[16,192,192]{2,1,0:T(8,128)}, u32[]{:S(2)}, u32[]{:S(2)}) %collective-permute-start.3) | collective-permute-done | bytes 2359328 | tf_op jit(solution)/shard_map/ppermute | solution.py:20
  176.6 1.1 collective-permute-done.2
  177.7 7.4 %pad_maximum_fusion = f32[48,192,192]{2,1,0:T(8,128)} fusion(f32[16,192,192]{2,1,0:T(8,128)} %collective-permute-done.3, f32[16,192,192]{2,1,0:T(8,128)S(1)} %fusion.17, f32[16,192,192]{2,1,0:T(8,128)} %collective-permute-done.2), kind=kLoop, calls=%fused_computation.4 | loop fusion | flops 3538944 | bytes 14155776 | tf_op jit(solution)/shard_map/concatenate | solution.py:16
  185.2 7.5 %gather_fusion.2 = f32[32,192,192]{2,1,0:T(8,128)} fusion(f32[48,192,192]{2,1,0:T(8,128)} %pad_maximum_fusion, s32[1024]{0:T(1024)S(1)} %pad_clamp_fusion), kind=kCustom, calls=%fused_computation.1.clone | custom fusion | bytes 9437312 | tf_op jit(solution)/shard_map/jit(_take)/gather | solution.py:105
  192.6 9.5 %fusion.2 = f32[16,2,192,192]{3,2,1,0:T(8,128)S(1)} fusion(f32[16,2,192,192]{3,2,1,0:T(8,128)} %bitcast.26, bf16[16,2,192,192]{3,2,1,0:T(8,128)(2,1)S(1)} %copy-done, f32[16,192]{1,0:T(8,128)S(1)} %get-tuple-element.12, pred[16,2]{1,0:T(8,128)(4,1)S(1)} %copy.14), kind=kOutput, calls=%fused_computation.13 | convolution fusion | flops 2721447936 | bytes 11808800 | tf_op jit(solution)/shard_map/pnab,pnbc->pnac/dot_general | solution.py:41
  202.1 8.0 %fusion.5 = f32[16,2,192,192]{3,2,1,0:T(8,128)S(1)} fusion(f32[16,2,192,192]{3,2,1,0:T(8,128)S(1)} %fusion.2, bf16[16,2,192,192]{3,2,1,0:T(8,128)(2,1)S(1)} %copy-done, f32[16,192]{1,0:T(8,128)S(1)} %get-tuple-element.12), kind=kOutput, calls=%fused_computation.17 | convolution fusion | flops 2720268288 | bytes 11808768 | tf_op jit(solution)/shard_map/pnac,pndc->pnad/dot_general | solution.py:44
  210.2 23.4 %fusion.8 = f32[16,1,192,192]{3,1,2,0:T(1,128)S(1)} fusion(f32[16,2,1,1]{1,2,3,0:T(1,128)S(1)} %copy.19, f32[16,2,192,192]{3,2,1,0:T(8,128)S(1)} %fusion.5), kind=kOutput, calls=%fused_computation.20 | convolution fusion | flops 14155776 | bytes 7078016 | tf_op jit(solution)/shard_map/pn,pnad->pad/dot_general | solution.py:47
  233.6 1.4 fusion.20
  235.0 0.0 copy-start.1
  235.0 1.9 collective-permute-start.5
  236.9 4.5 %collective-permute-start.4 = (f32[16,192,192]{2,1,0:T(8,128)S(1)}, f32[16,192,192]{2,1,0:T(8,128)}, u32[]{:S(2)}, u32[]{:S(2)}) collective-permute-start(f32[16,192,192]{2,1,0:T(8,128)S(1)} %fusion.20), channel_id=1, source_target_pairs={{0,1},{1,2},{2,3},{3,4},{4,5},{5,6},{6,7},{8,9},{9,10},{10,11},{11... | collective-permute-start | bytes 7077896 | tf_op jit(solution)/shard_map/ppermute | solution.py:18
  241.4 33.0 %collective-permute-done.5 = f32[16,192,192]{2,1,0:T(8,128)S(1)} collective-permute-done((f32[16,192,192]{2,1,0:T(8,128)S(1)}, f32[16,192,192]{2,1,0:T(8,128)S(1)}, u32[]{:S(2)}, u32[]{:S(2)}) %collective-permute-start.5) | collective-permute-done | bytes 2359328 | tf_op jit(solution)/shard_map/ppermute | solution.py:20
  274.4 1.7 copy-done.5
  276.1 0.0 collective-permute-done.4
  276.1 8.5 %pad_maximum_fusion.1 = f32[48,192,192]{2,1,0:T(8,128)} fusion(f32[16,192,192]{2,1,0:T(8,128)} %copy-done.5, f32[16,192,192]{2,1,0:T(8,128)} %copy-done.1, f32[16,192,192]{2,1,0:T(8,128)} %collective-permute-done.4), kind=kLoop, calls=%fused_computation.5 | loop fusion | flops 3538944 | bytes 14155776 | tf_op jit(solution)/shard_map/concatenate | solution.py:16
  284.7 7.3 %gather_fusion.3 = f32[32,192,192]{2,1,0:T(8,128)} fusion(f32[48,192,192]{2,1,0:T(8,128)} %pad_maximum_fusion.1, s32[1024]{0:T(1024)S(1)} %pad_clamp_fusion), kind=kCustom, calls=%fused_computation.3.clone | custom fusion | bytes 9437312 | tf_op jit(solution)/shard_map/jit(_take)/gather | solution.py:105
  292.0 9.9 %fusion = f32[16,2,192,192]{3,2,1,0:T(8,128)S(1)} fusion(f32[16,2,192,192]{3,2,1,0:T(8,128)} %bitcast.25, bf16[16,2,192,192]{3,2,1,0:T(8,128)(2,1)S(1)} %copy-done, f32[16,192]{1,0:T(8,128)S(1)} %get-tuple-element.12, pred[16,2]{1,0:T(8,128)(4,1)S(1)} %copy.14), kind=kOutput, calls=%fused_computation.11 | convolution fusion | flops 2721447936 | bytes 11808800 | tf_op jit(solution)/shard_map/pnab,pnbc->pnac/dot_general | solution.py:41
  301.9 8.0 %fusion.4 = f32[16,2,192,192]{3,2,1,0:T(8,128)S(1)} fusion(f32[16,2,192,192]{3,2,1,0:T(8,128)S(1)} %fusion, bf16[16,2,192,192]{3,2,1,0:T(8,128)(2,1)S(1)} %copy-done, f32[16,192]{1,0:T(8,128)S(1)} %get-tuple-element.12), kind=kOutput, calls=%fused_computation.16 | convolution fusion | flops 2720268288 | bytes 11808768 | tf_op jit(solution)/shard_map/pnac,pndc->pnad/dot_general | solution.py:44
  309.9 0.0 copy-start.2
  309.9 23.3 %fusion.6 = f32[16,1,192,192]{3,1,2,0:T(1,128)S(1)} fusion(f32[16,2,1,1]{1,2,3,0:T(1,128)S(1)} %copy.19, f32[16,2,192,192]{3,2,1,0:T(8,128)S(1)} %fusion.4), kind=kOutput, calls=%fused_computation.18 | convolution fusion | flops 14155776 | bytes 7078016 | tf_op jit(solution)/shard_map/pn,pnad->pad/dot_general | solution.py:47
  333.3 2.0 fusion.22
  (21 shorter events, 0.1 us)
Async XLA Ops:
  7.2 128.4 %all-reduce.2.cloned.1.call-start = ((), (), s32[]{:S(2)}) async-start(), calls=%async_computation | async-start | bytes 6291456 | tf_op jit(solution)/shard_map/psum | solution.py:98
  7.2 16.6 %collective-permute-start = (bf16[4,512,256]{2,1,0:T(8,128)(2,1)}, bf16[4,512,256]{2,1,0:T(8,128)(2,1)}, u32[]{:S(2)}, u32[]{:S(2)}) collective-permute-start(bf16[4,512,256]{2,1,0:T(8,128)(2,1)} %param.12), channel_id=1, source_target_pairs={{0,1},{1,2},{2,3},{3,4},{4,5},{5,6},{6,7},{8,9},{9,10},{10,11},{11... | collective-permute-start | bytes 3145736 | tf_op jit(solution)/shard_map/ppermute | solution.py:18
  11.8 16.4 %collective-permute-start.1 = (bf16[4,512,256]{2,1,0:T(8,128)(2,1)}, bf16[4,512,256]{2,1,0:T(8,128)(2,1)}, u32[]{:S(2)}, u32[]{:S(2)}) collective-permute-start(bf16[4,512,256]{2,1,0:T(8,128)(2,1)} %param.12), channel_id=1, source_target_pairs={{1,0},{2,1},{3,2},{4,3},{5,4},{6,5},{7,6},{9,8},{10,9},{11,10},{12... | collective-permute-start | bytes 3145736 | tf_op jit(solution)/shard_map/ppermute | solution.py:20
  15.2 10.0 %copy-start.7 = (bf16[4,512,256]{2,1,0:T(8,128)(2,1)S(1)}, bf16[4,512,256]{2,1,0:T(8,128)(2,1)}, u32[]{:S(2)}) copy-start(bf16[4,512,256]{2,1,0:T(8,128)(2,1)} %param.12) | copy-start | bytes 3145732
  35.1 6.1 %copy-start.6 = (bf16[16,2,256,192]{2,3,1,0:T(8,128)(2,1)S(1)}, bf16[16,2,256,192]{2,3,1,0:T(8,128)(2,1)}, u32[]{:S(2)}) copy-start(bf16[16,2,256,192]{2,3,1,0:T(8,128)(2,1)} %broadcast_select_fusion) | copy-start | bytes 9437188
  48.5 87.1 %copy-start.8 = (f32[16,192]{1,0:T(8,128)S(1)}, f32[16,192]{1,0:T(8,128)}, u32[]{:S(2)}) copy-start(f32[16,192]{1,0:T(8,128)} %param.16) | copy-start | bytes 36868
  48.5 95.2 %copy-start.9 = (s32[16,2]{0,1:T(2,128)S(1)}, s32[16,2]{0,1:T(2,128)}, u32[]{:S(2)}) copy-start(s32[16,2]{0,1:T(2,128)} %param.18) | copy-start | bytes 388
  48.5 95.3 %copy-start.10 = (f32[16,2]{0,1:T(2,128)S(1)}, f32[16,2]{0,1:T(2,128)}, u32[]{:S(2)}) copy-start(f32[16,2]{0,1:T(2,128)} %param.19) | copy-start | bytes 388
  137.9 38.7 %collective-permute-start.3 = (f32[16,192,192]{2,1,0:T(8,128)S(1)}, f32[16,192,192]{2,1,0:T(8,128)}, u32[]{:S(2)}, u32[]{:S(2)}) collective-permute-start(f32[16,192,192]{2,1,0:T(8,128)S(1)} %fusion.17), channel_id=1, source_target_pairs={{1,0},{2,1},{3,2},{4,3},{5,4},{6,5},{7,6},{9,8},{10,9},{11,10},{12... | collective-permute-start | bytes 7077896 | tf_op jit(solution)/shard_map/ppermute | solution.py:20
  140.5 37.2 %collective-permute-start.2 = (f32[16,192,192]{2,1,0:T(8,128)S(1)}, f32[16,192,192]{2,1,0:T(8,128)}, u32[]{:S(2)}, u32[]{:S(2)}) collective-permute-start(f32[16,192,192]{2,1,0:T(8,128)S(1)} %fusion.17), channel_id=1, source_target_pairs={{0,1},{1,2},{2,3},{3,4},{4,5},{5,6},{6,7},{8,9},{9,10},{10,11},{11... | collective-permute-start | bytes 7077896 | tf_op jit(solution)/shard_map/ppermute | solution.py:18
  185.2 7.5 %copy-start = (bf16[16,2,192,192]{3,2,1,0:T(8,128)(2,1)S(1)}, bf16[16,2,192,192]{3,2,1,0:T(8,128)(2,1)}, u32[]{:S(2)}) copy-start(bf16[16,2,192,192]{3,2,1,0:T(8,128)(2,1)} %param.17) | copy-start | bytes 7077892
  210.2 23.4 %copy-start.3 = (f32[16,192,192]{2,1,0:T(8,128)S(1)}, f32[16,192,192]{2,1,0:T(8,128)}, u32[]{:S(2)}) copy-start(f32[16,192,192]{2,1,0:T(8,128)} %all-reduce.2.cloned.1.call-done) | copy-start | bytes 7077892
  235.0 1.9 copy-start.1
  235.0 39.4 %collective-permute-start.5 = (f32[16,192,192]{2,1,0:T(8,128)S(1)}, f32[16,192,192]{2,1,0:T(8,128)S(1)}, u32[]{:S(2)}, u32[]{:S(2)}) collective-permute-start(f32[16,192,192]{2,1,0:T(8,128)S(1)} %fusion.20), channel_id=1, source_target_pairs={{1,0},{2,1},{3,2},{4,3},{5,4},{6,5},{7,6},{9,8},{10,9},{11,10},{12... | collective-permute-start | bytes 7077896 | tf_op jit(solution)/shard_map/ppermute | solution.py:20
  236.9 39.2 %collective-permute-start.4 = (f32[16,192,192]{2,1,0:T(8,128)S(1)}, f32[16,192,192]{2,1,0:T(8,128)}, u32[]{:S(2)}, u32[]{:S(2)}) collective-permute-start(f32[16,192,192]{2,1,0:T(8,128)S(1)} %fusion.20), channel_id=1, source_target_pairs={{0,1},{1,2},{2,3},{3,4},{4,5},{5,6},{6,7},{8,9},{9,10},{10,11},{11... | collective-permute-start | bytes 7077896 | tf_op jit(solution)/shard_map/ppermute | solution.py:18
  274.4 1.7 copy-start.5
  309.9 23.4 %copy-start.2 = (f32[16,192,192]{2,1,0:T(8,128)S(1)}, f32[16,192,192]{2,1,0:T(8,128)}, u32[]{:S(2)}) copy-start(f32[16,192,192]{2,1,0:T(8,128)} %copy-done.1) | copy-start | bytes 7077892
  309.9 23.4 %copy-start.4 = (f32[16,192,192]{2,1,0:T(8,128)S(1)}, f32[16,192,192]{2,1,0:T(8,128)}, u32[]{:S(2)}) copy-start(f32[16,192,192]{2,1,0:T(8,128)} %all-reduce.2.cloned.1.call-done) | copy-start | bytes 7077892
Sparse Core Ops, SparseCore 0:
  48.6 86.9 all-reduce.1
where the time goes:
time: 347 us; the launch traced here: 342 us
  waiting for transfers between devices  162 us (47%)
  matrix products  95.6 us (28%)
  other arithmetic  26.6 us (8%)
  local copies, waits for them, and re-layouts  25 us (7%)
  starting transfers between devices  18.7 us (5%)
  between operations  14.5 us (4%)
    psum x1, waiting for transfers between devices, per_device(): exchange_ints = lax.psum(partial_ints, 'aux')  87.1 us
    ppermute x3, waiting for transfers between devices, with_halo(): lax.ppermute(head, axis, [((i + 1) % count, i) for i in range(ends)])  68.6 us
    dot_general x2, matrix products, transformed_product(): jnp.einsum('pn,pnad->pad', weights, outer_part, precision=lax.Precision.H...  46.7 us
    dot_general x2, matrix products, transformed_product(): jnp.einsum('pnab,pnbc->pnac', side_blocks, gathered, precision=lax.Precis...  19.4 us
    dot_general x2, matrix products, transformed_product(): jnp.einsum('pnac,pndc->pnad', inner_part, side_blocks, precision=lax.Prec...  16.1 us
    concatenate x2, other arithmetic, with_halo(): jnp.concatenate([lax.ppermute(tail, axis, [(i, (i + 1) % count) for i in...  16 us
    gather x2, local copies, waits for them, and re-layouts, coupling(): gathered = jnp.take(padded_amps, local_rows, axis=0)  14.8 us
    ppermute x3, starting transfers between devices, with_halo(): lax.ppermute(tail, axis, [(i, (i + 1) % count) for i in range(ends)])  12.3 us
  transfers between devices with their start and end apart: 7, of which 6 were waited for; matrix products, arithmetic and copies ran while one was open for 2% of the time, Pallas kernels for 0%

commit v1 on v0

v1 whole, which is shorter than its diff:
```python
import functools

import jax
import jax.numpy as jnp
from jax import lax
from jax.experimental import pallas as pl
from jax.experimental.pallas import tpu as pltpu
from jax.sharding import PartitionSpec as P

NPNO = 192
ITERS = 2


def with_halo(cells, axis):
    count = lax.axis_size(axis)
    ends = count - 1
    from_left = lax.ppermute(cells, axis, [(i, i + 1) for i in range(ends)])
    from_right = lax.ppermute(cells, axis, [(i + 1, i) for i in range(ends)])
    return jnp.concatenate([from_left, cells, from_right], axis=0)


def class_size(natural_orbital_class):
    return jnp.where(
        natural_orbital_class == 0,
        NPNO // 6,
        jnp.where(
            natural_orbital_class == 1,
            NPNO // 3,
            jnp.where(natural_orbital_class == 2, 2 * NPNO // 3, NPNO),
        ),
    ).astype(jnp.int32)


def exchange_kernel(lead_ref, trail_ref, size_ref, x_lead, x_trail, coef_ref, out_ref):
    p = pl.program_id(0)
    keep = lax.broadcasted_iota(jnp.int32, (1, NPNO), 1) < size_ref[p]
    zero = jnp.zeros((), jnp.bfloat16)
    first = jnp.where(keep, coef_ref[0, 0], zero)
    second = jnp.where(keep, coef_ref[0, 1], zero)
    left = jnp.dot(x_lead[0], first, preferred_element_type=jnp.float32).astype(jnp.bfloat16)
    right = jnp.dot(x_trail[0], second, preferred_element_type=jnp.float32).astype(jnp.bfloat16)
    out_ref[0] = lax.dot_general(
        left, right, (((0,), (0,)), ((), ())), preferred_element_type=jnp.float32
    )


def partial_exchange(lead, trail, sizes, blocks, coef):
    pairs = coef.shape[0]
    nfit, npao = blocks.shape[1], blocks.shape[2]
    grid_spec = pltpu.PrefetchScalarGridSpec(
        num_scalar_prefetch=3,
        grid=(pairs,),
        in_specs=[
            pl.BlockSpec((1, nfit, npao), lambda i, a, b, s: (a[i], 0, 0)),
            pl.BlockSpec((1, nfit, npao), lambda i, a, b, s: (b[i], 0, 0)),
            pl.BlockSpec((1, 2, npao, NPNO), lambda i, a, b, s: (i, 0, 0, 0)),
        ],
        out_specs=pl.BlockSpec((1, NPNO, NPNO), lambda i, a, b, s: (i, 0, 0)),
    )
    flops = pairs * (2 * 2 * nfit * npao * NPNO + 2 * nfit * NPNO * NPNO)
    return pl.pallas_call(
        exchange_kernel,
        grid_spec=grid_spec,
        out_shape=jax.ShapeDtypeStruct((pairs, NPNO, NPNO), jnp.float32),
        cost_estimate=pl.CostEstimate(
            flops=flops,
            bytes_accessed=pairs * (2 * nfit * npao * 2 + 2 * npao * NPNO * 2 + NPNO * NPNO * 4),
            transcendentals=0,
        ),
    )(lead, trail, sizes, blocks, blocks, coef)


def split_bf16(value):
    hi = value.astype(jnp.bfloat16)
    lo = (value - hi.astype(jnp.float32)).astype(jnp.bfloat16)
    return hi, lo


def mm(lhs, rhs, dims=(((1,), (0,)), ((), ()))):
    return lax.dot_general(lhs, rhs, dims, preferred_element_type=jnp.float32)


def coupling_kernel(
    nb_ref, size_ref, fock_ref, t_first, t_second, margin_ref, ex_ref, col_ref, row_ref, own_ref, out_ref, *, final
):
    p = pl.program_id(0)
    keep = lax.broadcasted_iota(jnp.int32, (NPNO, 1), 0) < size_ref[p]
    zero = jnp.zeros((), jnp.bfloat16)
    transposed = (((1,), (1,)), ((), ()))
    total = None
    for n, t_ref in enumerate((t_first, t_second)):
        side = jnp.where(keep, margin_ref[0, n], zero)
        t_hi, t_lo = split_bf16(t_ref[0])
        inner = mm(side, t_hi) + mm(side, t_lo)
        w_hi, w_lo = split_bf16(fock_ref[2 * p + n] * inner)
        outer = mm(w_hi, side, transposed) + mm(w_lo, side, transposed)
        total = outer if total is None else total + outer
    denominator = col_ref[0] + row_ref[0]
    amplitudes = own_ref[0]
    residual = ex_ref[0] + denominator * amplitudes - total
    if final:
        out_ref[0] = residual
    else:
        out_ref[0] = amplitudes - residual / denominator


def coupling_step(nb, sizes, fock, padded, margin, exchange, energy, own, final):
    column = energy.reshape(energy.shape[0], NPNO, 1)
    row = energy.reshape(energy.shape[0], 1, NPNO)
    pairs = own.shape[0]
    grid_spec = pltpu.PrefetchScalarGridSpec(
        num_scalar_prefetch=3,
        grid=(pairs,),
        in_specs=[
            pl.BlockSpec((1, NPNO, NPNO), lambda i, q, s, f: (q[2 * i], 0, 0)),
            pl.BlockSpec((1, NPNO, NPNO), lambda i, q, s, f: (q[2 * i + 1], 0, 0)),
            pl.BlockSpec((1, 2, NPNO, NPNO), lambda i, q, s, f: (i, 0, 0, 0)),
            pl.BlockSpec((1, NPNO, NPNO), lambda i, q, s, f: (i, 0, 0)),
            pl.BlockSpec((1, NPNO, 1), lambda i, q, s, f: (i, 0, 0)),
            pl.BlockSpec((1, 1, NPNO), lambda i, q, s, f: (i, 0, 0)),
            pl.BlockSpec((1, NPNO, NPNO), lambda i, q, s, f: (i, 0, 0)),
        ],
        out_specs=pl.BlockSpec((1, NPNO, NPNO), lambda i, q, s, f: (i, 0, 0)),
    )
    flops = pairs * 2 * 4 * 2 * NPNO * NPNO * NPNO
    return pl.pallas_call(
        functools.partial(coupling_kernel, final=final),
        grid_spec=grid_spec,
        out_shape=jax.ShapeDtypeStruct((pairs, NPNO, NPNO), jnp.float32),
        cost_estimate=pl.CostEstimate(
            flops=flops,
            bytes_accessed=pairs * NPNO * NPNO * (2 * 4 + 2 * 2 + 3 * 4),
            transcendentals=0,
        ),
    )(nb, sizes, fock, padded, padded, margin, exchange, column, row, own)


def per_device(
    three_index,
    pno_coef,
    pair_orbitals,
    natural_orbital_class,
    pno_energy,
    margin,
    neighbour_pairs,
    fock_coupling,
):
    occ_dev = three_index.shape[0]
    pair_dev = pno_coef.shape[0]
    position = lax.axis_index("pair")
    sizes = class_size(natural_orbital_class)
    padded = with_halo(three_index, "pair")
    local_orbitals = (pair_orbitals - (position - 1) * occ_dev).astype(jnp.int32)
    partial_ints = partial_exchange(
        local_orbitals[:, 0], local_orbitals[:, 1], sizes, padded, pno_coef
    )
    exchange_ints = lax.psum(partial_ints, "aux")
    denominator = pno_energy[:, :, None] + pno_energy[:, None, :]
    local_rows = (neighbour_pairs - (position - 1) * pair_dev).astype(jnp.int32).reshape(-1)
    fock = fock_coupling.reshape(-1)

    amplitudes = -(exchange_ints / denominator)
    for iteration in range(1, ITERS):
        padded_amps = with_halo(amplitudes, "pair")
        amplitudes = coupling_step(
            local_rows, sizes, fock, padded_amps, margin, exchange_ints, pno_energy, amplitudes, False
        )
    padded_amps = with_halo(amplitudes, "pair")
    residual = coupling_step(
        local_rows, sizes, fock, padded_amps, margin, exchange_ints, pno_energy, amplitudes, True
    )
    return (amplitudes, residual)


def solution(mesh):
    return jax.shard_map(
        per_device,
        mesh=mesh,
        in_specs=(
            P("pair", "aux", None),
            P("pair", None, None, None),
            P("pair", None),
            P("pair"),
            P("pair", None),
            P("pair", None, None, None),
            P("pair", None),
            P("pair", None),
        ),
        out_specs=(P("pair", None, None), P("pair", None, None)),
        check_vma=False,
    )
```

time: 347 us -> 273 us (0.79); the launches traced: 342 us -> 272 us
  matrix products: 95.6 us -> 0 us
  Pallas kernels: 0 us -> 49.9 us
  local copies, waits for them, and re-layouts: 25 us -> 10.3 us
  other arithmetic: 26.6 us -> 19.6 us
    dot_general x8 -> x0, matrix products: 95.6 us -> none  [the longest x2 46.7 us: transformed_product(): jnp.einsum('pn,pnad->pad', weights, outer_part, precision=lax.Precision.H...]
    pallas_call x0 -> x3, Pallas kernels: none -> 49.9 us  [the longest x2 34 us: coupling_step(): pl.pallas_call(functools.partial(coupling_kernel, final=final), grid_spec...]
    gather x4 -> x0, local copies, waits for them, and re-layouts: 20.3 us -> none  [the longest x2 14.8 us: coupling(): gathered = jnp.take(padded_amps, local_rows, axis=0)]
    sub x4 -> x2, other arithmetic: 6.39 us -> 0.01 us  [the longest x1 0.01 us: per_device(): pair_orbitals - (position - 1) * occ_dev]
    select_n x2 -> x1, other arithmetic: 4.09 us -> 0.54 us  [class_size(): jnp.where(natural_orbital_class == 0, NPNO // 6, jnp.where(natural_orbita...]
    concatenate x2 -> x3, other arithmetic: 16 us -> 16.7 us  [with_halo(): return jnp.concatenate([from_left, cells, from_right], axis=0)]
  transfers between devices with their start and end apart: 7 -> 7, of which waited for: 6 -> 7; matrix products, arithmetic and copies ran while one was open for 2% -> 4% of each run, Pallas kernels for 0% -> 0%
where the time goes in v1:
time: 273 us; the launch traced here: 272 us
  waiting for transfers between devices  159 us (58%)
  Pallas kernels  49.9 us (18%)
  other arithmetic  19.6 us (7%)
  starting transfers between devices  18.6 us (7%)
  between operations  14.1 us (5%)
  local copies, waits for them, and re-layouts  10.3 us (4%)
    psum x1, waiting for transfers between devices, per_device(): exchange_ints = lax.psum(partial_ints, 'aux')  87 us
    ppermute x3, waiting for transfers between devices, with_halo(): from_right = lax.ppermute(cells, axis, [(i + 1, i) for i in range(ends)])  66.9 us
    pallas_call x2, Pallas kernels, coupling_step(): pl.pallas_call(functools.partial(coupling_kernel, final=final), grid_spec...  34 us
    concatenate x3, other arithmetic, with_halo(): return jnp.concatenate([from_left, cells, from_right], axis=0)  16.7 us
    pallas_call x1, Pallas kernels, partial_exchange(): pl.pallas_call(exchange_kernel, grid_spec=grid_spec, out_shape=jax.ShapeD...  15.9 us
    ppermute x3, starting transfers between devices, with_halo(): from_left = lax.ppermute(cells, axis, [(i, i + 1) for i in range(ends)])  12.1 us
    ppermute x3, starting transfers between devices, with_halo(): from_right = lax.ppermute(cells, axis, [(i + 1, i) for i in range(ends)])  6.41 us
    unnamed x16, local copies, waits for them, and re-layouts  6.14 us
  transfers between devices with their start and end apart: 7, of which 7 were waited for; matrix products, arithmetic and copies ran while one was open for 4% of the time, Pallas kernels for 0%

profile of v1, /device:TPU:1, one launch (start us, length us, event | category | flops | bytes accessed | tf_op | source)
XLA Modules:
  0.0 271.9 jit_solution(9586956301765804550)
XLA Ops:
  7.2 0.0 all-reduce.2.cloned.1.call-start
  7.2 4.6 %collective-permute-start = (bf16[4,512,256]{2,1,0:T(8,128)(2,1)}, bf16[4,512,256]{2,1,0:T(8,128)(2,1)S(1)}, u32[]{:S(2)}, u32[]{:S(2)}) collective-permute-start(bf16[4,512,256]{2,1,0:T(8,128)(2,1)} %param.8), channel_id=1, source_target_pairs={{0,1},{1,2},{2,3},{3,4},{4,5},{5,6},{6,7},{8,9},{9,10},{10,11},{11... | collective-permute-start | bytes 3145736 | tf_op jit(solution)/shard_map/ppermute | solution.py:17
  11.8 1.9 collective-permute-start.1
  13.7 0.0 copy-start.6
  13.8 0.0 copy-start.4
  13.8 0.0 copy-start.1
  13.8 6.0 %copy.15.coef_ref = bf16[16,2,256,192]{3,2,1,0:T(8,128)(2,1)} copy(bf16[16,2,256,192]{2,3,1,0:T(8,128)(2,1)} %param.9) | data formatting | bytes 6291456 | tf_op args[1]
  19.8 0.0 copy-done.6
  19.8 0.5 compare_select_fusion.2.size_ref
  20.3 0.0 copy-done.4
  20.4 0.5 slice_bitcast_fusion
  20.9 3.0 %collective-permute-done = bf16[4,512,256]{2,1,0:T(8,128)(2,1)S(1)} collective-permute-done((bf16[4,512,256]{2,1,0:T(8,128)(2,1)}, bf16[4,512,256]{2,1,0:T(8,128)(2,1)S(1)}, u32[]{:S(2)}, u32[]{:S(2)}) %collective-permute-start) | collective-permute-done | bytes 1048608 | tf_op jit(solution)/shard_map/ppermute | solution.py:17
  23.8 4.3 %collective-permute-done.1 = bf16[4,512,256]{2,1,0:T(8,128)(2,1)S(1)} collective-permute-done((bf16[4,512,256]{2,1,0:T(8,128)(2,1)}, bf16[4,512,256]{2,1,0:T(8,128)(2,1)S(1)}, u32[]{:S(2)}, u32[]{:S(2)}) %collective-permute-start.1) | collective-permute-done | bytes 1048608 | tf_op jit(solution)/shard_map/ppermute | solution.py:18
  28.1 0.0 copy-done.1
  28.1 1.8 pad_maximum_fusion.2.x_lead.x_trail
  30.0 15.9 %shard_map.95 = f32[16,192,192]{2,1,0:T(8,128)} custom-call(s32[16]{0:T(128)} %get-tuple-element.3.lead_ref, s32[16]{0:T(128)} %get-tuple-element.2.trail_ref, s32[16]{0:T(128)} %compare_select_fusion.2.size_ref, bf16[12,512,256]{2,1,0:T(8,128)(2,1)} %pad_maximum_fusion.2.x_lead.x_trail, bf16[12,512,256]{2,1,0:T(8,128)(2,1)} %pad_maximum_fusion.2.x_lead.x_trail, ...), custom_call_target="tpu_custom_call" | custom-call | flops 2214592512 | bytes 13893632 | tf_op jit(solution)/shard_map/pallas_call | solution.py:61
  45.9 0.0 copy-start.2
  45.9 0.0 all-reduce.2.cloned.1.call-update
  45.9 0.0 copy-start.5
  45.9 0.0 copy-start.3
  45.9 87.0 %all-reduce.2.cloned.1.call-done.ex_ref = f32[16,192,192]{2,1,0:T(8,128)} async-done(((f32[16,192,192]{2,1,0:T(8,128)}), f32[16,192,192]{2,1,0:T(8,128)}) %all-reduce.2.cloned.1.call-update) | async-done | bytes 2359312 | tf_op jit(solution)/shard_map/psum | solution.py:157
  133.0 0.0 copy-done.2
  133.0 2.4 divide_negate_fusion.own_ref
  135.3 0.0 copy-start
  135.3 2.6 collective-permute-start.3
  137.9 3.0 %collective-permute-start.2 = (f32[16,192,192]{2,1,0:T(8,128)S(1)}, f32[16,192,192]{2,1,0:T(8,128)}, u32[]{:S(2)}, u32[]{:S(2)}) collective-permute-start(f32[16,192,192]{2,1,0:T(8,128)S(1)} %divide_negate_fusion.own_ref), channel_id=1, source_target_pairs={{0,1},{1,2},{2,3},{3,4},{4,5},{5,6},{6,7},{8,9},{9,10},{10,11},{11... | collective-permute-start | bytes 7077896 | tf_op jit(solution)/shard_map/ppermute | solution.py:17
  141.0 0.6 broadcast_in_dim.26.row_ref
  141.6 0.0 copy-done.5
  141.6 0.1 copy.13
  141.7 0.6 reshape.16.nb_ref
  142.3 0.0 copy-done.3
  142.3 0.1 copy.14
  142.4 0.6 reshape.17.fock_ref
  143.0 1.7 copy.16.col_ref
  144.7 29.3 %collective-permute-done.3 = f32[16,192,192]{2,1,0:T(8,128)} collective-permute-done((f32[16,192,192]{2,1,0:T(8,128)S(1)}, f32[16,192,192]{2,1,0:T(8,128)}, u32[]{:S(2)}, u32[]{:S(2)}) %collective-permute-start.3) | collective-permute-done | bytes 2359328 | tf_op jit(solution)/shard_map/ppermute | solution.py:18
  174.1 1.1 collective-permute-done.2
  175.1 7.4 %pad_maximum_fusion.t_first.t_second = f32[48,192,192]{2,1,0:T(8,128)} fusion(f32[16,192,192]{2,1,0:T(8,128)} %collective-permute-done.3, f32[16,192,192]{2,1,0:T(8,128)S(1)} %divide_negate_fusion.own_ref, f32[16,192,192]{2,1,0:T(8,128)} %collective-permute-done.2), kind=kLoop, calls=%fused_computation | loop fusion | flops 3538944 | bytes 14155776 | tf_op jit(solution)/shard_map/concatenate | solution.py:19
  182.6 0.0 copy-done
  182.6 17.0 %shard_map.96.own_ref = f32[16,192,192]{2,1,0:T(8,128)} custom-call(s32[32]{0:T(128)} %reshape.16.nb_ref, s32[16]{0:T(128)} %compare_select_fusion.2.size_ref, f32[32]{0:T(128)} %reshape.17.fock_ref, f32[48,192,192]{2,1,0:T(8,128)} %pad_maximum_fusion.t_first.t_second, f32[48,192,192]{2,1,0:T(8,128)} %pad_maximum_fusion.t_first.t_second, ...), custom_call_target="tpu_custom_call" | custom-call | flops 1811939328 | bytes 14155776 | tf_op jit(solution)/shard_map/pallas_call | solution.py:126
  199.6 1.9 collective-permute-start.5
  201.5 4.5 %collective-permute-start.4 = (f32[16,192,192]{2,1,0:T(8,128)}, f32[16,192,192]{2,1,0:T(8,128)}, u32[]{:S(2)}, u32[]{:S(2)}) collective-permute-start(f32[16,192,192]{2,1,0:T(8,128)} %shard_map.96.own_ref), channel_id=1, source_target_pairs={{0,1},{1,2},{2,3},{3,4},{4,5},{5,6},{6,7},{8,9},{9,10},{10,11},{11... | collective-permute-start | bytes 7077896 | tf_op jit(solution)/shard_map/ppermute | solution.py:17
  206.0 33.2 %collective-permute-done.5 = f32[16,192,192]{2,1,0:T(8,128)S(1)} collective-permute-done((f32[16,192,192]{2,1,0:T(8,128)}, f32[16,192,192]{2,1,0:T(8,128)S(1)}, u32[]{:S(2)}, u32[]{:S(2)}) %collective-permute-start.5) | collective-permute-done | bytes 2359328 | tf_op jit(solution)/shard_map/ppermute | solution.py:18
  239.3 1.3 collective-permute-done.4
  240.6 7.5 %pad_maximum_fusion.1.t_first.t_second = f32[48,192,192]{2,1,0:T(8,128)} fusion(f32[16,192,192]{2,1,0:T(8,128)S(1)} %collective-permute-done.5, f32[16,192,192]{2,1,0:T(8,128)} %shard_map.96.own_ref, f32[16,192,192]{2,1,0:T(8,128)} %collective-permute-done.4), kind=kLoop, calls=%fused_computation.1 | loop fusion | flops 3538944 | bytes 14155776 | tf_op jit(solution)/shard_map/concatenate | solution.py:19
  248.0 17.0 %shard_map.97 = f32[16,192,192]{2,1,0:T(8,128)} custom-call(s32[32]{0:T(128)} %reshape.16.nb_ref, s32[16]{0:T(128)} %compare_select_fusion.2.size_ref, f32[32]{0:T(128)} %reshape.17.fock_ref, f32[48,192,192]{2,1,0:T(8,128)} %pad_maximum_fusion.1.t_first.t_second, f32[48,192,192]{2,1,0:T(8,128)} %pad_maximum_fusion.1.t_first.t_second, ...), custom_call_target="tpu_custom_call" | custom-call | flops 1811939328 | bytes 14155776 | tf_op jit(solution)/shard_map/pallas_call | solution.py:126
  (2 shorter events, 0.0 us)
Async XLA Ops:
  7.2 125.8 %all-reduce.2.cloned.1.call-start = ((), (), s32[]{:S(2)}) async-start(), calls=%async_computation | async-start | bytes 6291456 | tf_op jit(solution)/shard_map/psum | solution.py:157
  7.2 16.6 %collective-permute-start = (bf16[4,512,256]{2,1,0:T(8,128)(2,1)}, bf16[4,512,256]{2,1,0:T(8,128)(2,1)S(1)}, u32[]{:S(2)}, u32[]{:S(2)}) collective-permute-start(bf16[4,512,256]{2,1,0:T(8,128)(2,1)} %param.8), channel_id=1, source_target_pairs={{0,1},{1,2},{2,3},{3,4},{4,5},{5,6},{6,7},{8,9},{9,10},{10,11},{11... | collective-permute-start | bytes 3145736 | tf_op jit(solution)/shard_map/ppermute | solution.py:17
  11.8 16.3 %collective-permute-start.1 = (bf16[4,512,256]{2,1,0:T(8,128)(2,1)}, bf16[4,512,256]{2,1,0:T(8,128)(2,1)S(1)}, u32[]{:S(2)}, u32[]{:S(2)}) collective-permute-start(bf16[4,512,256]{2,1,0:T(8,128)(2,1)} %param.8), channel_id=1, source_target_pairs={{1,0},{2,1},{3,2},{4,3},{5,4},{6,5},{7,6},{9,8},{10,9},{11,10},{12... | collective-permute-start | bytes 3145736 | tf_op jit(solution)/shard_map/ppermute | solution.py:18
  13.7 6.1 %copy-start.6 = (s32[16]{0:T(128)S(1)}, s32[16]{0:T(128)}, u32[]{:S(2)}) copy-start(s32[16]{0:T(128)} %param.11) | copy-start | bytes 196
  13.8 6.6 %copy-start.4 = (s32[16,2]{0,1:T(2,128)S(1)}, s32[16,2]{0,1:T(2,128)}, u32[]{:S(2)}) copy-start(s32[16,2]{0,1:T(2,128)} %param.10) | copy-start | bytes 388
  13.8 14.4 %copy-start.1 = (bf16[4,512,256]{2,1,0:T(8,128)(2,1)S(1)}, bf16[4,512,256]{2,1,0:T(8,128)(2,1)}, u32[]{:S(2)}) copy-start(bf16[4,512,256]{2,1,0:T(8,128)(2,1)} %param.8) | copy-start | bytes 3145732
  45.9 87.1 %copy-start.2 = (f32[16,192]{1,0:T(8,128)S(1)}, f32[16,192]{1,0:T(8,128)}, u32[]{:S(2)}) copy-start(f32[16,192]{1,0:T(8,128)} %param.12) | copy-start | bytes 36868
  45.9 95.7 %copy-start.5 = (s32[16,2]{0,1:T(2,128)S(1)}, s32[16,2]{0,1:T(2,128)}, u32[]{:S(2)}) copy-start(s32[16,2]{0,1:T(2,128)} %param.14) | copy-start | bytes 388
  45.9 96.4 %copy-start.3 = (f32[16,2]{0,1:T(2,128)S(1)}, f32[16,2]{0,1:T(2,128)}, u32[]{:S(2)}) copy-start(f32[16,2]{0,1:T(2,128)} %param.15) | copy-start | bytes 388
  135.3 47.2 %copy-start = (f32[16,192,192]{2,1,0:T(8,128)}, f32[16,192,192]{2,1,0:T(8,128)S(1)}, u32[]{:S(2)}) copy-start(f32[16,192,192]{2,1,0:T(8,128)S(1)} %divide_negate_fusion.own_ref) | copy-start | bytes 7077892
  135.3 38.7 %collective-permute-start.3 = (f32[16,192,192]{2,1,0:T(8,128)S(1)}, f32[16,192,192]{2,1,0:T(8,128)}, u32[]{:S(2)}, u32[]{:S(2)}) collective-permute-start(f32[16,192,192]{2,1,0:T(8,128)S(1)} %divide_negate_fusion.own_ref), channel_id=1, source_target_pairs={{1,0},{2,1},{3,2},{4,3},{5,4},{6,5},{7,6},{9,8},{10,9},{11,10},{12... | collective-permute-start | bytes 7077896 | tf_op jit(solution)/shard_map/ppermute | solution.py:18
  137.9 37.2 %collective-permute-start.2 = (f32[16,192,192]{2,1,0:T(8,128)S(1)}, f32[16,192,192]{2,1,0:T(8,128)}, u32[]{:S(2)}, u32[]{:S(2)}) collective-permute-start(f32[16,192,192]{2,1,0:T(8,128)S(1)} %divide_negate_fusion.own_ref), channel_id=1, source_target_pairs={{0,1},{1,2},{2,3},{3,4},{4,5},{5,6},{6,7},{8,9},{9,10},{10,11},{11... | collective-permute-start | bytes 7077896 | tf_op jit(solution)/shard_map/ppermute | solution.py:17
  199.6 39.7 %collective-permute-start.5 = (f32[16,192,192]{2,1,0:T(8,128)}, f32[16,192,192]{2,1,0:T(8,128)S(1)}, u32[]{:S(2)}, u32[]{:S(2)}) collective-permute-start(f32[16,192,192]{2,1,0:T(8,128)} %shard_map.96.own_ref), channel_id=1, source_target_pairs={{1,0},{2,1},{3,2},{4,3},{5,4},{6,5},{7,6},{9,8},{10,9},{11,10},{12... | collective-permute-start | bytes 7077896 | tf_op jit(solution)/shard_map/ppermute | solution.py:18
  201.5 39.0 %collective-permute-start.4 = (f32[16,192,192]{2,1,0:T(8,128)}, f32[16,192,192]{2,1,0:T(8,128)}, u32[]{:S(2)}, u32[]{:S(2)}) collective-permute-start(f32[16,192,192]{2,1,0:T(8,128)} %shard_map.96.own_ref), channel_id=1, source_target_pairs={{0,1},{1,2},{2,3},{3,4},{4,5},{5,6},{6,7},{8,9},{9,10},{10,11},{11... | collective-permute-start | bytes 7077896 | tf_op jit(solution)/shard_map/ppermute | solution.py:17
Sparse Core Ops, SparseCore 0:
  46.0 86.9 all-reduce.1

commit v2 on v1

v2 whole, which is shorter than its diff:
```python
import functools

import jax
import jax.numpy as jnp
from jax import lax
from jax.experimental import pallas as pl
from jax.experimental.pallas import tpu as pltpu
from jax.sharding import PartitionSpec as P

NPNO = 192
ITERS = 2


def halo_sources(cells, axis):
    count = lax.axis_size(axis)
    ends = count - 1
    from_left = lax.ppermute(cells, axis, [(i, i + 1) for i in range(ends)])
    from_right = lax.ppermute(cells, axis, [(i + 1, i) for i in range(ends)])
    return (from_left, cells, from_right)


def source_index(local, width, source):
    return jnp.where(local // width == source, local % width, 0)


def halving_stream(piece, index, count, bits):
    for bit in bits:
        side = (index // bit) % 2
        half = piece.shape[0] // 2
        keep = lax.dynamic_slice_in_dim(piece, side * half, half, axis=0)
        send = lax.dynamic_slice_in_dim(piece, (1 - side) * half, half, axis=0)
        piece = keep + lax.ppermute(send, "aux", [(i, i ^ bit) for i in range(count)])
    for bit in reversed(bits):
        side = (index // bit) % 2
        other = lax.ppermute(piece, "aux", [(i, i ^ bit) for i in range(count)])
        length = piece.shape[0]
        full = jnp.zeros((2 * length,) + piece.shape[1:], piece.dtype)
        full = lax.dynamic_update_slice_in_dim(full, piece, side * length, axis=0)
        piece = lax.dynamic_update_slice_in_dim(full, other, (1 - side) * length, axis=0)
    return piece


def sum_over_aux(partial):
    count = lax.axis_size("aux")
    if count != 4 or partial.shape[0] % 8:
        return lax.psum(partial, "aux")
    index = lax.axis_index("aux")
    half = partial.shape[0] // 2
    first = halving_stream(partial[:half], index, count, (1, 2))
    second = halving_stream(partial[half:], index, count, (2, 1))
    return jnp.concatenate([first, second], axis=0)


def class_size(natural_orbital_class):
    return jnp.where(
        natural_orbital_class == 0,
        NPNO // 6,
        jnp.where(
            natural_orbital_class == 1,
            NPNO // 3,
            jnp.where(natural_orbital_class == 2, 2 * NPNO // 3, NPNO),
        ),
    ).astype(jnp.int32)


def exchange_kernel(lead_ref, trail_ref, size_ref, x_lead, t_left, t_own, t_right, coef_ref, out_ref, *, occ):
    p = pl.program_id(0)
    keep = lax.broadcasted_iota(jnp.int32, (NPNO, 1), 0) < size_ref[p]
    zero = jnp.zeros((), jnp.bfloat16)
    first = jnp.where(keep, coef_ref[0, 0], zero)
    second = jnp.where(keep, coef_ref[0, 1], zero)
    source = trail_ref[p] // occ
    x_trail = jnp.where(source == 0, t_left[0], jnp.where(source == 1, t_own[0], t_right[0]))
    transposed = (((1,), (1,)), ((), ()))
    left_t = lax.dot_general(first, x_lead[0], transposed, preferred_element_type=jnp.float32)
    right = lax.dot_general(x_trail, second, transposed, preferred_element_type=jnp.float32)
    out_ref[0] = jnp.dot(
        left_t.astype(jnp.bfloat16), right.astype(jnp.bfloat16), preferred_element_type=jnp.float32
    )


def partial_exchange(lead, trail, sizes, sources, coef_t):
    pairs = coef_t.shape[0]
    occ, nfit, npao = sources[1].shape
    block = (1, nfit, npao)

    def trail_spec(source):
        return pl.BlockSpec(block, lambda i, a, b, s: (source_index(b[i], occ, source), 0, 0))

    grid_spec = pltpu.PrefetchScalarGridSpec(
        num_scalar_prefetch=3,
        grid=(pairs,),
        in_specs=[
            pl.BlockSpec(block, lambda i, a, b, s: (a[i], 0, 0)),
            trail_spec(0),
            trail_spec(1),
            trail_spec(2),
            pl.BlockSpec((1, 2, NPNO, npao), lambda i, a, b, s: (i, 0, 0, 0)),
        ],
        out_specs=pl.BlockSpec((1, NPNO, NPNO), lambda i, a, b, s: (i, 0, 0)),
    )
    flops = pairs * (2 * 2 * nfit * npao * NPNO + 2 * nfit * NPNO * NPNO)
    return pl.pallas_call(
        functools.partial(exchange_kernel, occ=occ),
        grid_spec=grid_spec,
        out_shape=jax.ShapeDtypeStruct((pairs, NPNO, NPNO), jnp.float32),
        cost_estimate=pl.CostEstimate(
            flops=flops,
            bytes_accessed=pairs * (2 * nfit * npao * 2 + 2 * npao * NPNO * 2 + NPNO * NPNO * 4),
            transcendentals=0,
        ),
    )(lead, trail, sizes, sources[1], *sources, coef_t)


def split_bf16(value):
    hi = value.astype(jnp.bfloat16)
    lo = (value - hi.astype(jnp.float32)).astype(jnp.bfloat16)
    return hi, lo


def mm(lhs, rhs, dims=(((1,), (0,)), ((), ()))):
    return lax.dot_general(lhs, rhs, dims, preferred_element_type=jnp.float32)


def coupling_kernel(nb_ref, size_ref, fock_ref, *refs, final, width):
    t_refs = refs[:6]
    margin_ref, ex_ref, col_ref, row_ref, own_ref, out_ref = refs[6:]
    p = pl.program_id(0)
    keep = lax.broadcasted_iota(jnp.int32, (NPNO, 1), 0) < size_ref[p]
    zero = jnp.zeros((), jnp.bfloat16)
    transposed = (((1,), (1,)), ((), ()))
    total = None
    for n in range(2):
        source = nb_ref[2 * p + n] // width
        left, own, right = (t_refs[3 * n + k][0] for k in range(3))
        t = jnp.where(source == 0, left, jnp.where(source == 1, own, right))
        side = jnp.where(keep, margin_ref[0, n], zero)
        t_hi, t_lo = split_bf16(t)
        inner = mm(side, t_hi) + mm(side, t_lo)
        w_hi, w_lo = split_bf16(fock_ref[2 * p + n] * inner)
        outer = mm(w_hi, side, transposed) + mm(w_lo, side, transposed)
        total = outer if total is None else total + outer
    denominator = col_ref[0] + row_ref[0]
    amplitudes = own_ref[0]
    residual = ex_ref[0] + denominator * amplitudes - total
    if final:
        out_ref[0] = residual
    else:
        out_ref[0] = amplitudes - residual / denominator


def coupling_step(nb, sizes, fock, sources, margin, exchange, energy, own, final):
    column = energy.reshape(energy.shape[0], NPNO, 1)
    row = energy.reshape(energy.shape[0], 1, NPNO)
    pairs = own.shape[0]
    block = (1, NPNO, NPNO)

    def t_spec(n, source):
        return pl.BlockSpec(
            block, lambda i, q, s, f: (source_index(q[2 * i + n], pairs, source), 0, 0)
        )

    own_spec = pl.BlockSpec(block, lambda i, q, s, f: (i, 0, 0))
    grid_spec = pltpu.PrefetchScalarGridSpec(
        num_scalar_prefetch=3,
        grid=(pairs,),
        in_specs=[t_spec(n, k) for n in range(2) for k in range(3)]
        + [
            pl.BlockSpec((1, 2, NPNO, NPNO), lambda i, q, s, f: (i, 0, 0, 0)),
            own_spec,
            pl.BlockSpec((1, NPNO, 1), lambda i, q, s, f: (i, 0, 0)),
            pl.BlockSpec((1, 1, NPNO), lambda i, q, s, f: (i, 0, 0)),
            own_spec,
        ],
        out_specs=own_spec,
    )
    flops = pairs * 2 * 4 * 2 * NPNO * NPNO * NPNO
    return pl.pallas_call(
        functools.partial(coupling_kernel, final=final, width=pairs),
        grid_spec=grid_spec,
        out_shape=jax.ShapeDtypeStruct((pairs, NPNO, NPNO), jnp.float32),
        cost_estimate=pl.CostEstimate(
            flops=flops,
            bytes_accessed=pairs * NPNO * NPNO * (2 * 4 + 2 * 2 + 3 * 4),
            transcendentals=0,
        ),
    )(nb, sizes, fock, *sources, *sources, margin, exchange, column, row, own)


def per_device(
    three_index,
    pno_coef,
    pair_orbitals,
    natural_orbital_class,
    pno_energy,
    margin,
    neighbour_pairs,
    fock_coupling,
):
    occ_dev = three_index.shape[0]
    pair_dev = pno_coef.shape[0]
    position = lax.axis_index("pair")
    sizes = class_size(natural_orbital_class)
    blocks = halo_sources(three_index, "pair")
    local_orbitals = (pair_orbitals - (position - 1) * occ_dev).astype(jnp.int32)
    partial_ints = partial_exchange(
        local_orbitals[:, 0] - occ_dev,
        local_orbitals[:, 1],
        sizes,
        blocks,
        jnp.swapaxes(pno_coef, 2, 3),
    )
    exchange_ints = sum_over_aux(partial_ints)
    denominator = pno_energy[:, :, None] + pno_energy[:, None, :]
    local_rows = (neighbour_pairs - (position - 1) * pair_dev).astype(jnp.int32).reshape(-1)
    fock = fock_coupling.reshape(-1)

    amplitudes = -(exchange_ints / denominator)
    for iteration in range(1, ITERS):
        amplitudes = coupling_step(
            local_rows, sizes, fock, halo_sources(amplitudes, "pair"), margin, exchange_ints,
            pno_energy, amplitudes, False,
        )
    residual = coupling_step(
        local_rows, sizes, fock, halo_sources(amplitudes, "pair"), margin, exchange_ints,
        pno_energy, amplitudes, True,
    )
    return (amplitudes, residual)


def solution(mesh):
    return jax.shard_map(
        per_device,
        mesh=mesh,
        in_specs=(
            P("pair", "aux", None),
            P("pair", None, None, None),
            P("pair", None),
            P("pair"),
            P("pair", None),
            P("pair", None, None, None),
            P("pair", None),
            P("pair", None),
        ),
        out_specs=(P("pair", None, None), P("pair", None, None)),
        check_vma=False,
    )
```

time: 273 us -> 228 us (0.84)
  waiting for transfers between devices: 159 us -> 112 us
  starting transfers between devices: 18.6 us -> 42.9 us
  between operations: 14.1 us -> 0.91 us
  other arithmetic: 19.6 us -> 8.12 us
  Pallas kernels: 49.9 us -> 53.5 us
    psum x1 -> x0, waiting for transfers between devices: 87 us -> none  [per_device(): exchange_ints = lax.psum(partial_ints, 'aux')]
    ppermute x6 -> x14, waiting for transfers between devices: 72.2 us -> 112 us  [the longest x3 66.8 us: halo_sources(): from_right = lax.ppermute(cells, axis, [(i + 1, i) for i in range(ends)])]
    ppermute x6 -> x14, starting transfers between devices: 18.5 us -> 42.9 us  [the longest x3 26 us: halo_sources(): from_left = lax.ppermute(cells, axis, [(i, i + 1) for i in range(ends)])]
    concatenate x3 -> x1, other arithmetic: 16.7 us -> 2.02 us  [sum_over_aux(): return jnp.concatenate([first, second], axis=0)]
    unnamed x16 -> x17, local copies, waits for them, and re-layouts: 6.14 us -> 1.57 us
    pallas_call x3, Pallas kernels: 49.9 us -> 53.5 us  [the longest x2 37.4 us: coupling_step(): pl.pallas_call(functools.partial(coupling_kernel, final=final, width=pair...]
  transfers between devices with their start and end apart: 7 -> 14, of which waited for: 7 -> 12; matrix products, arithmetic and copies ran while one was open for 4% -> 5% of each run, Pallas kernels for 0% -> 0%
where the time goes in v2:
time: 228 us; the launch traced here: 227 us
  waiting for transfers between devices  112 us (49%)
  Pallas kernels  53.5 us (23%)
  starting transfers between devices  42.9 us (19%)
  local copies, waits for them, and re-layouts  10 us (4%)
  other arithmetic  8.12 us (4%)
    ppermute x3, waiting for transfers between devices, halo_sources(): from_right = lax.ppermute(cells, axis, [(i + 1, i) for i in range(ends)])  66.8 us
    pallas_call x2, Pallas kernels, coupling_step(): pl.pallas_call(functools.partial(coupling_kernel, final=final, width=pair...  37.4 us
    ppermute x3, starting transfers between devices, halo_sources(): from_left = lax.ppermute(cells, axis, [(i, i + 1) for i in range(ends)])  26 us
    ppermute x4, waiting for transfers between devices, halving_stream(): other = lax.ppermute(piece, 'aux', [(i, i ^ bit) for i in range(count)])  17.7 us
    ppermute x4, waiting for transfers between devices, halving_stream(): lax.ppermute(send, 'aux', [(i, i ^ bit) for i in range(count)])  17.1 us
    pallas_call x1, Pallas kernels, partial_exchange(): pl.pallas_call(functools.partial(exchange_kernel, occ=occ), grid_spec=gri...  16.1 us
    ppermute x3, waiting for transfers between devices, halo_sources(): from_left = lax.ppermute(cells, axis, [(i, i + 1) for i in range(ends)])  9.93 us
    ppermute x4, starting transfers between devices, halving_stream(): lax.ppermute(send, 'aux', [(i, i ^ bit) for i in range(count)])  5.99 us
  transfers between devices with their start and end apart: 14, of which 12 were waited for; matrix products, arithmetic and copies ran while one was open for 5% of the time, Pallas kernels for 0%

profile of v2, /device:TPU:1, one launch (start us, length us, event | category | flops | bytes accessed | tf_op | source)
XLA Modules:
  0.0 227.0 jit_solution(1216474123794270663)
XLA Ops:
  0.6 4.6 %collective-permute-start = (bf16[4,512,256]{2,1,0:T(8,128)(2,1)}, bf16[4,512,256]{2,1,0:T(8,128)(2,1)S(1)}, u32[]{:S(2)}, u32[]{:S(2)}) collective-permute-start(bf16[4,512,256]{2,1,0:T(8,128)(2,1)} %t_own.1), channel_id=1, source_target_pairs={{0,1},{1,2},{2,3},{3,4},{4,5},{5,6},{6,7},{8,9},{9,10},{10,11},{11... | collective-permute-start | bytes 3145736 | tf_op jit(solution)/shard_map/ppermute | solution.py:17
  5.2 1.9 collective-permute-start.1
  7.2 1.2 compare_select_fusion.2.size_ref
  8.4 0.7 broadcast_subtract_fusion
  9.1 0.6 slice_bitcast_fusion
  9.7 7.6 %collective-permute-done.t_left = bf16[4,512,256]{2,1,0:T(8,128)(2,1)S(1)} collective-permute-done((bf16[4,512,256]{2,1,0:T(8,128)(2,1)}, bf16[4,512,256]{2,1,0:T(8,128)(2,1)S(1)}, u32[]{:S(2)}, u32[]{:S(2)}) %collective-permute-start) | collective-permute-done | bytes 1048608 | tf_op jit(solution)/shard_map/ppermute | solution.py:17
  17.3 4.3 %collective-permute-done.1.t_right = bf16[4,512,256]{2,1,0:T(8,128)(2,1)S(1)} collective-permute-done((bf16[4,512,256]{2,1,0:T(8,128)(2,1)}, bf16[4,512,256]{2,1,0:T(8,128)(2,1)S(1)}, u32[]{:S(2)}, u32[]{:S(2)}) %collective-permute-start.1) | collective-permute-done | bytes 1048608 | tf_op jit(solution)/shard_map/ppermute | solution.py:18
  21.6 1.0 copy-done.4
  22.6 16.1 %shard_map.95 = f32[16,192,192]{2,1,0:T(8,128)} custom-call(s32[16]{0:T(128)} %get-tuple-element.11.lead_ref, s32[16]{0:T(128)} %get-tuple-element.10.trail_ref, s32[16]{0:T(128)} %compare_select_fusion.2.size_ref, bf16[4,512,256]{2,1,0:T(8,128)(2,1)} %t_own.1, bf16[4,512,256]{2,1,0:T(8,128)(2,1)} %copy-done.3, bf16[4,512,256]{2,1,0:T(8,128)(2,1)} %t_own.1, ...), custom_call_target="tpu_custom_call" | custom-call | flops 2214592512 | bytes 13893632 | tf_op jit(solution)/shard_map/pallas_call | solution.py:103
  38.7 2.2 fusion
  40.9 0.9 constant_dynamic-slice_fusion.1
  41.8 1.2 collective-permute-start.6
  43.1 0.9 constant_dynamic-slice_fusion.3
  44.0 1.2 collective-permute-start.2
  45.2 11.2 %collective-permute-done.6 = f32[4,192,192]{2,1,0:T(8,128)} collective-permute-done((f32[4,192,192]{2,1,0:T(8,128)}, f32[4,192,192]{2,1,0:T(8,128)}, u32[]{:S(2)}, u32[]{:S(2)}) %collective-permute-start.6) | collective-permute-done | bytes 589856 | tf_op jit(solution)/shard_map/ppermute | solution.py:32
  56.4 1.2 dynamic-slice_add_fusion
  57.7 1.7 collective-permute-start.7
  59.4 1.2 dynamic-slice_add_fusion.1
  60.7 1.9 collective-permute-start.3
  62.5 5.9 %collective-permute-done.7 = f32[2,192,192]{2,1,0:T(8,128)S(1)} collective-permute-done((f32[2,192,192]{2,1,0:T(8,128)S(1)}, f32[2,192,192]{2,1,0:T(8,128)S(1)}, u32[]{:S(2)}, u32[]{:S(2)}) %collective-permute-start.7) | collective-permute-done | bytes 294944 | tf_op jit(solution)/shard_map/ppermute | solution.py:32
  68.5 1.1 constant_dynamic-update-slice_fusion.3
  69.6 1.2 collective-permute-start.8
  70.9 1.3 collective-permute-start.4
  72.2 7.9 %collective-permute-done.8 = f32[2,192,192]{2,1,0:T(8,128)S(1)} collective-permute-done((f32[2,192,192]{2,1,0:T(8,128)S(1)}, f32[2,192,192]{2,1,0:T(8,128)S(1)}, u32[]{:S(2)}, u32[]{:S(2)}) %collective-permute-start.8) | collective-permute-done | bytes 294944 | tf_op jit(solution)/shard_map/ppermute | solution.py:35
  80.1 1.6 collective-permute-start.9
  81.7 0.4 collective-permute-done.4
  82.2 1.1 collective-permute-start.5
  83.3 0.1 broadcast.30.clone
  83.5 0.1 broadcast.30.clone.1
  83.7 9.1 %collective-permute-done.9 = f32[4,192,192]{2,1,0:T(8,128)S(1)} collective-permute-done((f32[4,192,192]{2,1,0:T(8,128)S(1)}, f32[4,192,192]{2,1,0:T(8,128)S(1)}, u32[]{:S(2)}, u32[]{:S(2)}) %collective-permute-start.9) | collective-permute-done | bytes 589856 | tf_op jit(solution)/shard_map/ppermute | solution.py:35
  92.9 0.3 collective-permute-done.5
  93.2 2.0 pad_maximum_fusion
  95.2 1.9 collective-permute-start.11
  97.2 16.8 %collective-permute-start.10 = (f32[16,192,192]{2,1,0:T(8,128)S(1)}, f32[16,192,192]{2,1,0:T(8,128)}, u32[]{:S(2)}, u32[]{:S(2)}) collective-permute-start(f32[16,192,192]{2,1,0:T(8,128)S(1)} %get-tuple-element.7.refs_1_.refs_4_.refs_10_), channel_id=1, source_target_pairs={{0,1},{1,2},{2,3},{3,4},{4,5},{5,6},{6,7},{8,9},{9,10},{10,11},{11... | collective-permute-start | bytes 7077896 | tf_op jit(solution)/shard_map/ppermute | solution.py:17
  113.9 0.6 broadcast_in_dim.26.refs_9_
  114.5 0.1 copy.12
  114.6 0.7 reshape.18.nb_ref
  115.4 0.6 reshape.19.fock_ref
  116.0 1.7 copy.14.refs_8_
  117.7 29.3 %collective-permute-done.11.refs_2_.refs_5_ = f32[16,192,192]{2,1,0:T(8,128)} collective-permute-done((f32[16,192,192]{2,1,0:T(8,128)S(1)}, f32[16,192,192]{2,1,0:T(8,128)}, u32[]{:S(2)}, u32[]{:S(2)}) %collective-permute-start.11) | collective-permute-done | bytes 2359328 | tf_op jit(solution)/shard_map/ppermute | solution.py:18
  147.0 1.1 collective-permute-done.10.refs_0_.refs_3_
  148.1 18.7 %shard_map.96.refs_1_.refs_4_.refs_10_ = f32[16,192,192]{2,1,0:T(8,128)} custom-call(s32[32]{0:T(128)} %reshape.18.nb_ref, s32[16]{0:T(128)} %compare_select_fusion.2.size_ref, f32[32]{0:T(128)} %reshape.19.fock_ref, f32[16,192,192]{2,1,0:T(8,128)} %collective-permute-done.10.refs_0_.refs_3_, f32[16,192,192]{2,1,0:T(8,128)} %copy-done, ...), custom_call_target="tpu_custom_call" | custom-call | flops 1811939328 | bytes 14155776 | tf_op jit(solution)/shard_map/pallas_call | solution.py:178
  166.8 1.9 collective-permute-start.13
  168.7 4.6 %collective-permute-start.12 = (f32[16,192,192]{2,1,0:T(8,128)}, f32[16,192,192]{2,1,0:T(8,128)}, u32[]{:S(2)}, u32[]{:S(2)}) collective-permute-start(f32[16,192,192]{2,1,0:T(8,128)} %shard_map.96.refs_1_.refs_4_.refs_10_), channel_id=1, source_target_pairs={{0,1},{1,2},{2,3},{3,4},{4,5},{5,6},{6,7},{8,9},{9,10},{10,11},{11... | collective-permute-start | bytes 7077896 | tf_op jit(solution)/shard_map/ppermute | solution.py:17
  173.3 33.2 %collective-permute-done.13.refs_2_.refs_5_ = f32[16,192,192]{2,1,0:T(8,128)S(1)} collective-permute-done((f32[16,192,192]{2,1,0:T(8,128)}, f32[16,192,192]{2,1,0:T(8,128)S(1)}, u32[]{:S(2)}, u32[]{:S(2)}) %collective-permute-start.13) | collective-permute-done | bytes 2359328 | tf_op jit(solution)/shard_map/ppermute | solution.py:18
  206.5 1.3 collective-permute-done.12.refs_0_.refs_3_
  207.8 0.4 copy-done.1
  208.3 18.8 %shard_map.97 = f32[16,192,192]{2,1,0:T(8,128)} custom-call(s32[32]{0:T(128)} %reshape.18.nb_ref, s32[16]{0:T(128)} %compare_select_fusion.2.size_ref, f32[32]{0:T(128)} %reshape.19.fock_ref, f32[16,192,192]{2,1,0:T(8,128)} %collective-permute-done.12.refs_0_.refs_3_, f32[16,192,192]{2,1,0:T(8,128)} %shard_map.96.refs_1_.refs_4_.refs_10_, ...), custom_call_target="tpu_custom_call" | custom-call | flops 1811939328 | bytes 14155776 | tf_op jit(solution)/shard_map/pallas_call | solution.py:178
  (29 shorter events, 0.7 us)
Async XLA Ops:
  0.6 16.6 %collective-permute-start = (bf16[4,512,256]{2,1,0:T(8,128)(2,1)}, bf16[4,512,256]{2,1,0:T(8,128)(2,1)S(1)}, u32[]{:S(2)}, u32[]{:S(2)}) collective-permute-start(bf16[4,512,256]{2,1,0:T(8,128)(2,1)} %t_own.1), channel_id=1, source_target_pairs={{0,1},{1,2},{2,3},{3,4},{4,5},{5,6},{6,7},{8,9},{9,10},{10,11},{11... | collective-permute-start | bytes 3145736 | tf_op jit(solution)/shard_map/ppermute | solution.py:17
  5.2 16.3 %collective-permute-start.1 = (bf16[4,512,256]{2,1,0:T(8,128)(2,1)}, bf16[4,512,256]{2,1,0:T(8,128)(2,1)S(1)}, u32[]{:S(2)}, u32[]{:S(2)}) collective-permute-start(bf16[4,512,256]{2,1,0:T(8,128)(2,1)} %t_own.1), channel_id=1, source_target_pairs={{1,0},{2,1},{3,2},{4,3},{5,4},{6,5},{7,6},{9,8},{10,9},{11,10},{12... | collective-permute-start | bytes 3145736 | tf_op jit(solution)/shard_map/ppermute | solution.py:18
  17.3 4.3 %copy-start.3 = (bf16[4,512,256]{2,1,0:T(8,128)(2,1)}, bf16[4,512,256]{2,1,0:T(8,128)(2,1)S(1)}, u32[]{:S(2)}) copy-start(bf16[4,512,256]{2,1,0:T(8,128)(2,1)S(1)} %collective-permute-done.t_left) | copy-start | bytes 3145732
  21.6 1.0 copy-start.4
  41.8 14.5 %collective-permute-start.6 = (f32[4,192,192]{2,1,0:T(8,128)}, f32[4,192,192]{2,1,0:T(8,128)}, u32[]{:S(2)}, u32[]{:S(2)}) collective-permute-start(f32[4,192,192]{2,1,0:T(8,128)} %constant_dynamic-slice_fusion.1), channel_id=1, source_target_pairs={{0,16},{8,24},{16,0},{24,8},{1,17},{9,25},{17,1},{25,9},{2,18},{10... | collective-permute-start | bytes 1769480 | tf_op jit(solution)/shard_map/ppermute | solution.py:32
  44.0 15.4 %collective-permute-start.2 = (f32[4,192,192]{2,1,0:T(8,128)}, f32[4,192,192]{2,1,0:T(8,128)}, u32[]{:S(2)}, u32[]{:S(2)}) collective-permute-start(f32[4,192,192]{2,1,0:T(8,128)} %constant_dynamic-slice_fusion.3), channel_id=1, source_target_pairs={{0,8},{8,0},{16,24},{24,16},{1,9},{9,1},{17,25},{25,17},{2,10},{10... | collective-permute-start | bytes 1769480 | tf_op jit(solution)/shard_map/ppermute | solution.py:32
  57.6 3.0 %copy-start.2 = (f32[4,192,192]{2,1,0:T(8,128)}, f32[4,192,192]{2,1,0:T(8,128)S(1)}, u32[]{:S(2)}) copy-start(f32[4,192,192]{2,1,0:T(8,128)S(1)} %dynamic-slice_add_fusion) | copy-start | bytes 1769476
  57.7 10.8 %collective-permute-start.7 = (f32[2,192,192]{2,1,0:T(8,128)S(1)}, f32[2,192,192]{2,1,0:T(8,128)S(1)}, u32[]{:S(2)}, u32[]{:S(2)}) collective-permute-start(f32[2,192,192]{2,1,0:T(8,128)S(1)} %constant_dynamic-slice_fusion), channel_id=1, source_target_pairs={{0,8},{8,0},{16,24},{24,16},{1,9},{9,1},{17,25},{25,17},{2,10},{10... | collective-permute-start | bytes 884744 | tf_op jit(solution)/shard_map/ppermute | solution.py:32
  60.7 10.1 %collective-permute-start.3 = (f32[2,192,192]{2,1,0:T(8,128)S(1)}, f32[2,192,192]{2,1,0:T(8,128)S(1)}, u32[]{:S(2)}, u32[]{:S(2)}) collective-permute-start(f32[2,192,192]{2,1,0:T(8,128)S(1)} %constant_dynamic-slice_fusion.2), channel_id=1, source_target_pairs={{0,16},{8,24},{16,0},{24,8},{1,17},{9,25},{17,1},{25,9},{2,18},{10... | collective-permute-start | bytes 884744 | tf_op jit(solution)/shard_map/ppermute | solution.py:32
  69.6 10.5 %collective-permute-start.8 = (f32[2,192,192]{2,1,0:T(8,128)S(1)}, f32[2,192,192]{2,1,0:T(8,128)S(1)}, u32[]{:S(2)}, u32[]{:S(2)}) collective-permute-start(f32[2,192,192]{2,1,0:T(8,128)S(1)} %get-tuple-element.5), channel_id=1, source_target_pairs={{0,8},{8,0},{16,24},{24,16},{1,9},{9,1},{17,25},{25,17},{2,10},{10... | collective-permute-start | bytes 884744 | tf_op jit(solution)/shard_map/ppermute | solution.py:35
  70.9 11.3 %collective-permute-start.4 = (f32[2,192,192]{2,1,0:T(8,128)S(1)}, f32[2,192,192]{2,1,0:T(8,128)S(1)}, u32[]{:S(2)}, u32[]{:S(2)}) collective-permute-start(f32[2,192,192]{2,1,0:T(8,128)S(1)} %get-tuple-element.3), channel_id=1, source_target_pairs={{0,16},{8,24},{16,0},{24,8},{1,17},{9,25},{17,1},{25,9},{2,18},{10... | collective-permute-start | bytes 884744 | tf_op jit(solution)/shard_map/ppermute | solution.py:35
  80.1 12.7 %collective-permute-start.9 = (f32[4,192,192]{2,1,0:T(8,128)S(1)}, f32[4,192,192]{2,1,0:T(8,128)S(1)}, u32[]{:S(2)}, u32[]{:S(2)}) collective-permute-start(f32[4,192,192]{2,1,0:T(8,128)S(1)} %constant_dynamic-update-slice_fusion.2), channel_id=1, source_target_pairs={{0,16},{8,24},{16,0},{24,8},{1,17},{9,25},{17,1},{25,9},{2,18},{10... | collective-permute-start | bytes 1769480 | tf_op jit(solution)/shard_map/ppermute | solution.py:35
  82.2 10.9 %collective-permute-start.5 = (f32[4,192,192]{2,1,0:T(8,128)S(1)}, f32[4,192,192]{2,1,0:T(8,128)S(1)}, u32[]{:S(2)}, u32[]{:S(2)}) collective-permute-start(f32[4,192,192]{2,1,0:T(8,128)S(1)} %constant_dynamic-update-slice_fusion.6), channel_id=1, source_target_pairs={{0,8},{8,0},{16,24},{24,16},{1,9},{9,1},{17,25},{25,17},{2,10},{10... | collective-permute-start | bytes 1769480 | tf_op jit(solution)/shard_map/ppermute | solution.py:35
  83.7 9.5 %copy-start.5 = (f32[16,192]{1,0:T(8,128)S(1)}, f32[16,192]{1,0:T(8,128)}, u32[]{:S(2)}) copy-start(f32[16,192]{1,0:T(8,128)} %param.12) | copy-start | bytes 36868
  93.2 21.4 %copy-start.7 = (s32[16,2]{0,1:T(2,128)S(1)}, s32[16,2]{0,1:T(2,128)}, u32[]{:S(2)}) copy-start(s32[16,2]{0,1:T(2,128)} %param.14) | copy-start | bytes 388
  93.2 22.1 %copy-start.6 = (f32[16,2]{0,1:T(2,128)S(1)}, f32[16,2]{0,1:T(2,128)}, u32[]{:S(2)}) copy-start(f32[16,2]{0,1:T(2,128)} %param.15) | copy-start | bytes 388
  95.2 52.9 %copy-start = (f32[16,192,192]{2,1,0:T(8,128)}, f32[16,192,192]{2,1,0:T(8,128)S(1)}, u32[]{:S(2)}) copy-start(f32[16,192,192]{2,1,0:T(8,128)S(1)} %get-tuple-element.7.refs_1_.refs_4_.refs_10_) | copy-start | bytes 7077892
  95.2 51.8 %collective-permute-start.11 = (f32[16,192,192]{2,1,0:T(8,128)S(1)}, f32[16,192,192]{2,1,0:T(8,128)}, u32[]{:S(2)}, u32[]{:S(2)}) collective-permute-start(f32[16,192,192]{2,1,0:T(8,128)S(1)} %get-tuple-element.7.refs_1_.refs_4_.refs_10_), channel_id=1, source_target_pairs={{1,0},{2,1},{3,2},{4,3},{5,4},{6,5},{7,6},{9,8},{10,9},{11,10},{12... | collective-permute-start | bytes 7077896 | tf_op jit(solution)/shard_map/ppermute | solution.py:18
  97.2 51.0 %collective-permute-start.10 = (f32[16,192,192]{2,1,0:T(8,128)S(1)}, f32[16,192,192]{2,1,0:T(8,128)}, u32[]{:S(2)}, u32[]{:S(2)}) collective-permute-start(f32[16,192,192]{2,1,0:T(8,128)S(1)} %get-tuple-element.7.refs_1_.refs_4_.refs_10_), channel_id=1, source_target_pairs={{0,1},{1,2},{2,3},{3,4},{4,5},{5,6},{6,7},{8,9},{9,10},{10,11},{11... | collective-permute-start | bytes 7077896 | tf_op jit(solution)/shard_map/ppermute | solution.py:17
  166.8 39.7 %collective-permute-start.13 = (f32[16,192,192]{2,1,0:T(8,128)}, f32[16,192,192]{2,1,0:T(8,128)S(1)}, u32[]{:S(2)}, u32[]{:S(2)}) collective-permute-start(f32[16,192,192]{2,1,0:T(8,128)} %shard_map.96.refs_1_.refs_4_.refs_10_), channel_id=1, source_target_pairs={{1,0},{2,1},{3,2},{4,3},{5,4},{6,5},{7,6},{9,8},{10,9},{11,10},{12... | collective-permute-start | bytes 7077896 | tf_op jit(solution)/shard_map/ppermute | solution.py:18
  168.7 39.1 %collective-permute-start.12 = (f32[16,192,192]{2,1,0:T(8,128)}, f32[16,192,192]{2,1,0:T(8,128)}, u32[]{:S(2)}, u32[]{:S(2)}) collective-permute-start(f32[16,192,192]{2,1,0:T(8,128)} %shard_map.96.refs_1_.refs_4_.refs_10_), channel_id=1, source_target_pairs={{0,1},{1,2},{2,3},{3,4},{4,5},{5,6},{6,7},{8,9},{9,10},{10,11},{11... | collective-permute-start | bytes 7077896 | tf_op jit(solution)/shard_map/ppermute | solution.py:17
  206.5 1.7 copy-start.1

commit v3 on v2

--- a/solution.py
+++ b/solution.py
@@ -9,6 +9,7 @@
 
 NPNO = 192
 ITERS = 2
+CLASS_SIZES = (NPNO // 6, NPNO // 3, 2 * NPNO // 3, NPNO)
 
 
 def halo_sources(cells, axis):
@@ -65,18 +66,22 @@
 
 def exchange_kernel(lead_ref, trail_ref, size_ref, x_lead, t_left, t_own, t_right, coef_ref, out_ref, *, occ):
     p = pl.program_id(0)
-    keep = lax.broadcasted_iota(jnp.int32, (NPNO, 1), 0) < size_ref[p]
-    zero = jnp.zeros((), jnp.bfloat16)
-    first = jnp.where(keep, coef_ref[0, 0], zero)
-    second = jnp.where(keep, coef_ref[0, 1], zero)
+    size = size_ref[p]
     source = trail_ref[p] // occ
     x_trail = jnp.where(source == 0, t_left[0], jnp.where(source == 1, t_own[0], t_right[0]))
     transposed = (((1,), (1,)), ((), ()))
-    left_t = lax.dot_general(first, x_lead[0], transposed, preferred_element_type=jnp.float32)
-    right = lax.dot_general(x_trail, second, transposed, preferred_element_type=jnp.float32)
-    out_ref[0] = jnp.dot(
-        left_t.astype(jnp.bfloat16), right.astype(jnp.bfloat16), preferred_element_type=jnp.float32
-    )
+    out_ref[0] = jnp.zeros((NPNO, NPNO), jnp.float32)
+    for m in CLASS_SIZES:
+
+        @pl.when(size == m)
+        def _():
+            first = coef_ref[0, 0, :m, :]
+            second = coef_ref[0, 1, :m, :]
+            left_t = lax.dot_general(first, x_lead[0], transposed, preferred_element_type=jnp.float32)
+            right = lax.dot_general(x_trail, second, transposed, preferred_element_type=jnp.float32)
+            out_ref[0, :m, :m] = jnp.dot(
+                left_t.astype(jnp.bfloat16), right.astype(jnp.bfloat16), preferred_element_type=jnp.float32
+            )
 
 
 def partial_exchange(lead, trail, sizes, sources, coef_t):
@@ -124,25 +129,33 @@
 
 def coupling_kernel(nb_ref, size_ref, fock_ref, *refs, final, width):
     t_refs = refs[:6]
-    margin_ref, ex_ref, col_ref, row_ref, own_ref, out_ref = refs[6:]
+    margin_ref, ex_ref, col_ref, row_ref, own_ref, out_ref, acc_ref = refs[6:]
     p = pl.program_id(0)
-    keep = lax.broadcasted_iota(jnp.int32, (NPNO, 1), 0) < size_ref[p]
-    zero = jnp.zeros((), jnp.bfloat16)
+    size = size_ref[p]
     transposed = (((1,), (1,)), ((), ()))
-    total = None
+    splits = []
     for n in range(2):
         source = nb_ref[2 * p + n] // width
         left, own, right = (t_refs[3 * n + k][0] for k in range(3))
-        t = jnp.where(source == 0, left, jnp.where(source == 1, own, right))
-        side = jnp.where(keep, margin_ref[0, n], zero)
-        t_hi, t_lo = split_bf16(t)
-        inner = mm(side, t_hi) + mm(side, t_lo)
-        w_hi, w_lo = split_bf16(fock_ref[2 * p + n] * inner)
-        outer = mm(w_hi, side, transposed) + mm(w_lo, side, transposed)
-        total = outer if total is None else total + outer
+        splits.append(split_bf16(jnp.where(source == 0, left, jnp.where(source == 1, own, right))))
+    acc_ref[...] = jnp.zeros((NPNO, NPNO), jnp.float32)
+    for m in CLASS_SIZES:
+
+        @pl.when(size == m)
+        def _():
+            total = None
+            for n in range(2):
+                side = margin_ref[0, n, :m, :]
+                t_hi, t_lo = splits[n]
+                inner = mm(side, t_hi) + mm(side, t_lo)
+                w_hi, w_lo = split_bf16(fock_ref[2 * p + n] * inner)
+                outer = mm(w_hi, side, transposed) + mm(w_lo, side, transposed)
+                total = outer if total is None else total + outer
+            acc_ref[:m, :m] = total
+
     denominator = col_ref[0] + row_ref[0]
     amplitudes = own_ref[0]
-    residual = ex_ref[0] + denominator * amplitudes - total
+    residual = ex_ref[0] + denominator * amplitudes - acc_ref[...]
     if final:
         out_ref[0] = residual
     else:
@@ -173,6 +186,7 @@
             own_spec,
         ],
         out_specs=own_spec,
+        scratch_shapes=[pltpu.VMEM((NPNO, NPNO), jnp.float32)],
     )
     flops = pairs * 2 * 4 * 2 * NPNO * NPNO * NPNO
     return pl.pallas_call(

time: 228 us -> 231 us (1.013)
  Pallas kernels: 53.5 us -> 57.3 us
    pallas_call x2, Pallas kernels: 37.4 us -> 41 us  [coupling_step(): pl.pallas_call(functools.partial(coupling_kernel, final=final, width=pair...]
where the time goes in v3:
time: 231 us; the launch traced here: 230 us
  waiting for transfers between devices  112 us (48%)
  Pallas kernels  57.3 us (25%)
  starting transfers between devices  41.6 us (18%)
  local copies, waits for them, and re-layouts  10 us (4%)
  other arithmetic  8.12 us (4%)
    ppermute x3, waiting for transfers between devices, halo_sources(): from_right = lax.ppermute(cells, axis, [(i + 1, i) for i in range(ends)])  66.8 us
    pallas_call x2, Pallas kernels, coupling_step(): pl.pallas_call(functools.partial(coupling_kernel, final=final, width=pair...  41 us
    ppermute x3, starting transfers between devices, halo_sources(): from_left = lax.ppermute(cells, axis, [(i, i + 1) for i in range(ends)])  24.8 us
    ppermute x4, waiting for transfers between devices, halving_stream(): other = lax.ppermute(piece, 'aux', [(i, i ^ bit) for i in range(count)])  17.7 us
    ppermute x4, waiting for transfers between devices, halving_stream(): lax.ppermute(send, 'aux', [(i, i ^ bit) for i in range(count)])  17.2 us
    pallas_call x1, Pallas kernels, partial_exchange(): pl.pallas_call(functools.partial(exchange_kernel, occ=occ), grid_spec=gri...  16.3 us
    ppermute x3, waiting for transfers between devices, halo_sources(): from_left = lax.ppermute(cells, axis, [(i, i + 1) for i in range(ends)])  9.93 us
    ppermute x4, starting transfers between devices, halving_stream(): lax.ppermute(send, 'aux', [(i, i ^ bit) for i in range(count)])  5.95 us
  transfers between devices with their start and end apart: 14, of which 12 were waited for; matrix products, arithmetic and copies ran while one was open for 5% of the time, Pallas kernels for 0%

profile of v3, /device:TPU:1, one launch (start us, length us, event | category | flops | bytes accessed | tf_op | source)
XLA Modules:
  0.0 229.6 jit_solution(957956428017507342)
XLA Ops:
  0.6 4.6 %collective-permute-start = (bf16[4,512,256]{2,1,0:T(8,128)(2,1)}, bf16[4,512,256]{2,1,0:T(8,128)(2,1)S(1)}, u32[]{:S(2)}, u32[]{:S(2)}) collective-permute-start(bf16[4,512,256]{2,1,0:T(8,128)(2,1)} %t_own.1), channel_id=1, source_target_pairs={{0,1},{1,2},{2,3},{3,4},{4,5},{5,6},{6,7},{8,9},{9,10},{10,11},{11... | collective-permute-start | bytes 3145736 | tf_op jit(solution)/shard_map/ppermute | solution.py:18
  5.2 1.9 collective-permute-start.1
  7.2 1.2 compare_select_fusion.2.size_ref
  8.4 0.7 broadcast_subtract_fusion
  9.1 0.6 slice_bitcast_fusion
  9.7 7.6 %collective-permute-done.t_left = bf16[4,512,256]{2,1,0:T(8,128)(2,1)S(1)} collective-permute-done((bf16[4,512,256]{2,1,0:T(8,128)(2,1)}, bf16[4,512,256]{2,1,0:T(8,128)(2,1)S(1)}, u32[]{:S(2)}, u32[]{:S(2)}) %collective-permute-start) | collective-permute-done | bytes 1048608 | tf_op jit(solution)/shard_map/ppermute | solution.py:18
  17.3 4.3 %collective-permute-done.1.t_right = bf16[4,512,256]{2,1,0:T(8,128)(2,1)S(1)} collective-permute-done((bf16[4,512,256]{2,1,0:T(8,128)(2,1)}, bf16[4,512,256]{2,1,0:T(8,128)(2,1)S(1)}, u32[]{:S(2)}, u32[]{:S(2)}) %collective-permute-start.1) | collective-permute-done | bytes 1048608 | tf_op jit(solution)/shard_map/ppermute | solution.py:19
  21.6 1.0 copy-done.4
  22.6 16.3 %shard_map.95 = f32[16,192,192]{2,1,0:T(8,128)} custom-call(s32[16]{0:T(128)} %get-tuple-element.11.lead_ref, s32[16]{0:T(128)} %get-tuple-element.10.trail_ref, s32[16]{0:T(128)} %compare_select_fusion.2.size_ref, bf16[4,512,256]{2,1,0:T(8,128)(2,1)} %t_own.1, bf16[4,512,256]{2,1,0:T(8,128)(2,1)} %copy-done.3, bf16[4,512,256]{2,1,0:T(8,128)(2,1)} %t_own.1, ...), custom_call_target="tpu_custom_call" | custom-call | flops 2214592512 | bytes 13893632 | tf_op jit(solution)/shard_map/pallas_call | solution.py:108
  38.8 2.2 fusion
  41.0 0.9 constant_dynamic-slice_fusion.1
  42.0 1.2 collective-permute-start.6
  43.2 0.9 constant_dynamic-slice_fusion.3
  44.1 1.2 collective-permute-start.2
  45.4 11.2 %collective-permute-done.6 = f32[4,192,192]{2,1,0:T(8,128)} collective-permute-done((f32[4,192,192]{2,1,0:T(8,128)}, f32[4,192,192]{2,1,0:T(8,128)}, u32[]{:S(2)}, u32[]{:S(2)}) %collective-permute-start.6) | collective-permute-done | bytes 589856 | tf_op jit(solution)/shard_map/ppermute | solution.py:33
  56.5 1.2 dynamic-slice_add_fusion
  57.8 1.7 collective-permute-start.7
  59.5 1.2 dynamic-slice_add_fusion.1
  60.8 1.8 collective-permute-start.3
  62.6 6.0 %collective-permute-done.7 = f32[2,192,192]{2,1,0:T(8,128)S(1)} collective-permute-done((f32[2,192,192]{2,1,0:T(8,128)S(1)}, f32[2,192,192]{2,1,0:T(8,128)S(1)}, u32[]{:S(2)}, u32[]{:S(2)}) %collective-permute-start.7) | collective-permute-done | bytes 294944 | tf_op jit(solution)/shard_map/ppermute | solution.py:33
  68.7 1.1 constant_dynamic-update-slice_fusion.3
  69.8 1.2 collective-permute-start.8
  71.1 1.3 collective-permute-start.4
  72.4 7.9 %collective-permute-done.8 = f32[2,192,192]{2,1,0:T(8,128)S(1)} collective-permute-done((f32[2,192,192]{2,1,0:T(8,128)S(1)}, f32[2,192,192]{2,1,0:T(8,128)S(1)}, u32[]{:S(2)}, u32[]{:S(2)}) %collective-permute-start.8) | collective-permute-done | bytes 294944 | tf_op jit(solution)/shard_map/ppermute | solution.py:36
  80.3 1.6 collective-permute-start.9
  81.9 0.4 collective-permute-done.4
  82.4 1.0 collective-permute-start.5
  83.4 0.1 broadcast.30.clone
  83.6 0.1 broadcast.30.clone.1
  83.8 9.1 %collective-permute-done.9 = f32[4,192,192]{2,1,0:T(8,128)S(1)} collective-permute-done((f32[4,192,192]{2,1,0:T(8,128)S(1)}, f32[4,192,192]{2,1,0:T(8,128)S(1)}, u32[]{:S(2)}, u32[]{:S(2)}) %collective-permute-start.9) | collective-permute-done | bytes 589856 | tf_op jit(solution)/shard_map/ppermute | solution.py:36
  93.0 0.3 collective-permute-done.5
  93.4 2.0 pad_maximum_fusion
  95.4 1.9 collective-permute-start.11
  97.3 15.7 %collective-permute-start.10 = (f32[16,192,192]{2,1,0:T(8,128)S(1)}, f32[16,192,192]{2,1,0:T(8,128)}, u32[]{:S(2)}, u32[]{:S(2)}) collective-permute-start(f32[16,192,192]{2,1,0:T(8,128)S(1)} %get-tuple-element.7.refs_1_.refs_4_.refs_10_), channel_id=1, source_target_pairs={{0,1},{1,2},{2,3},{3,4},{4,5},{5,6},{6,7},{8,9},{9,10},{10,11},{11... | collective-permute-start | bytes 7077896 | tf_op jit(solution)/shard_map/ppermute | solution.py:18
  113.0 0.6 broadcast_in_dim.26.refs_9_
  113.7 0.1 copy.12
  113.8 0.7 reshape.18.nb_ref
  114.5 0.6 reshape.19.fock_ref
  115.1 1.7 copy.14.refs_8_
  116.8 29.3 %collective-permute-done.11.refs_2_.refs_5_ = f32[16,192,192]{2,1,0:T(8,128)} collective-permute-done((f32[16,192,192]{2,1,0:T(8,128)S(1)}, f32[16,192,192]{2,1,0:T(8,128)}, u32[]{:S(2)}, u32[]{:S(2)}) %collective-permute-start.11) | collective-permute-done | bytes 2359328 | tf_op jit(solution)/shard_map/ppermute | solution.py:19
  146.2 1.1 collective-permute-done.10.refs_0_.refs_3_
  147.2 20.5 %shard_map.96.refs_1_.refs_4_.refs_10_ = f32[16,192,192]{2,1,0:T(8,128)} custom-call(s32[32]{0:T(128)} %reshape.18.nb_ref, s32[16]{0:T(128)} %compare_select_fusion.2.size_ref, f32[32]{0:T(128)} %reshape.19.fock_ref, f32[16,192,192]{2,1,0:T(8,128)} %collective-permute-done.10.refs_0_.refs_3_, f32[16,192,192]{2,1,0:T(8,128)} %copy-done, ...), custom_call_target="tpu_custom_call" | custom-call | flops 1811939328 | bytes 14155776 | tf_op jit(solution)/shard_map/pallas_call | solution.py:192
  167.8 1.9 collective-permute-start.13
  169.7 4.5 %collective-permute-start.12 = (f32[16,192,192]{2,1,0:T(8,128)}, f32[16,192,192]{2,1,0:T(8,128)}, u32[]{:S(2)}, u32[]{:S(2)}) collective-permute-start(f32[16,192,192]{2,1,0:T(8,128)} %shard_map.96.refs_1_.refs_4_.refs_10_), channel_id=1, source_target_pairs={{0,1},{1,2},{2,3},{3,4},{4,5},{5,6},{6,7},{8,9},{9,10},{10,11},{11... | collective-permute-start | bytes 7077896 | tf_op jit(solution)/shard_map/ppermute | solution.py:18
  174.2 33.2 %collective-permute-done.13.refs_2_.refs_5_ = f32[16,192,192]{2,1,0:T(8,128)S(1)} collective-permute-done((f32[16,192,192]{2,1,0:T(8,128)}, f32[16,192,192]{2,1,0:T(8,128)S(1)}, u32[]{:S(2)}, u32[]{:S(2)}) %collective-permute-start.13) | collective-permute-done | bytes 2359328 | tf_op jit(solution)/shard_map/ppermute | solution.py:19
  207.4 1.3 collective-permute-done.12.refs_0_.refs_3_
  208.7 0.4 copy-done.1
  209.1 20.5 %shard_map.97 = f32[16,192,192]{2,1,0:T(8,128)} custom-call(s32[32]{0:T(128)} %reshape.18.nb_ref, s32[16]{0:T(128)} %compare_select_fusion.2.size_ref, f32[32]{0:T(128)} %reshape.19.fock_ref, f32[16,192,192]{2,1,0:T(8,128)} %collective-permute-done.12.refs_0_.refs_3_, f32[16,192,192]{2,1,0:T(8,128)} %shard_map.96.refs_1_.refs_4_.refs_10_, ...), custom_call_target="tpu_custom_call" | custom-call | flops 1811939328 | bytes 14155776 | tf_op jit(solution)/shard_map/pallas_call | solution.py:192
  (29 shorter events, 0.7 us)
Async XLA Ops:
  0.6 16.6 %collective-permute-start = (bf16[4,512,256]{2,1,0:T(8,128)(2,1)}, bf16[4,512,256]{2,1,0:T(8,128)(2,1)S(1)}, u32[]{:S(2)}, u32[]{:S(2)}) collective-permute-start(bf16[4,512,256]{2,1,0:T(8,128)(2,1)} %t_own.1), channel_id=1, source_target_pairs={{0,1},{1,2},{2,3},{3,4},{4,5},{5,6},{6,7},{8,9},{9,10},{10,11},{11... | collective-permute-start | bytes 3145736 | tf_op jit(solution)/shard_map/ppermute | solution.py:18
  5.2 16.3 %collective-permute-start.1 = (bf16[4,512,256]{2,1,0:T(8,128)(2,1)}, bf16[4,512,256]{2,1,0:T(8,128)(2,1)S(1)}, u32[]{:S(2)}, u32[]{:S(2)}) collective-permute-start(bf16[4,512,256]{2,1,0:T(8,128)(2,1)} %t_own.1), channel_id=1, source_target_pairs={{1,0},{2,1},{3,2},{4,3},{5,4},{6,5},{7,6},{9,8},{10,9},{11,10},{12... | collective-permute-start | bytes 3145736 | tf_op jit(solution)/shard_map/ppermute | solution.py:19
  17.3 4.3 %copy-start.3 = (bf16[4,512,256]{2,1,0:T(8,128)(2,1)}, bf16[4,512,256]{2,1,0:T(8,128)(2,1)S(1)}, u32[]{:S(2)}) copy-start(bf16[4,512,256]{2,1,0:T(8,128)(2,1)S(1)} %collective-permute-done.t_left) | copy-start | bytes 3145732
  21.6 1.0 copy-start.4
  42.0 14.5 %collective-permute-start.6 = (f32[4,192,192]{2,1,0:T(8,128)}, f32[4,192,192]{2,1,0:T(8,128)}, u32[]{:S(2)}, u32[]{:S(2)}) collective-permute-start(f32[4,192,192]{2,1,0:T(8,128)} %constant_dynamic-slice_fusion.1), channel_id=1, source_target_pairs={{0,16},{8,24},{16,0},{24,8},{1,17},{9,25},{17,1},{25,9},{2,18},{10... | collective-permute-start | bytes 1769480 | tf_op jit(solution)/shard_map/ppermute | solution.py:33
  44.1 15.4 %collective-permute-start.2 = (f32[4,192,192]{2,1,0:T(8,128)}, f32[4,192,192]{2,1,0:T(8,128)}, u32[]{:S(2)}, u32[]{:S(2)}) collective-permute-start(f32[4,192,192]{2,1,0:T(8,128)} %constant_dynamic-slice_fusion.3), channel_id=1, source_target_pairs={{0,8},{8,0},{16,24},{24,16},{1,9},{9,1},{17,25},{25,17},{2,10},{10... | collective-permute-start | bytes 1769480 | tf_op jit(solution)/shard_map/ppermute | solution.py:33
  57.7 3.0 %copy-start.2 = (f32[4,192,192]{2,1,0:T(8,128)}, f32[4,192,192]{2,1,0:T(8,128)S(1)}, u32[]{:S(2)}) copy-start(f32[4,192,192]{2,1,0:T(8,128)S(1)} %dynamic-slice_add_fusion) | copy-start | bytes 1769476
  57.8 10.8 %collective-permute-start.7 = (f32[2,192,192]{2,1,0:T(8,128)S(1)}, f32[2,192,192]{2,1,0:T(8,128)S(1)}, u32[]{:S(2)}, u32[]{:S(2)}) collective-permute-start(f32[2,192,192]{2,1,0:T(8,128)S(1)} %constant_dynamic-slice_fusion), channel_id=1, source_target_pairs={{0,8},{8,0},{16,24},{24,16},{1,9},{9,1},{17,25},{25,17},{2,10},{10... | collective-permute-start | bytes 884744 | tf_op jit(solution)/shard_map/ppermute | solution.py:33
  60.8 10.1 %collective-permute-start.3 = (f32[2,192,192]{2,1,0:T(8,128)S(1)}, f32[2,192,192]{2,1,0:T(8,128)S(1)}, u32[]{:S(2)}, u32[]{:S(2)}) collective-permute-start(f32[2,192,192]{2,1,0:T(8,128)S(1)} %constant_dynamic-slice_fusion.2), channel_id=1, source_target_pairs={{0,16},{8,24},{16,0},{24,8},{1,17},{9,25},{17,1},{25,9},{2,18},{10... | collective-permute-start | bytes 884744 | tf_op jit(solution)/shard_map/ppermute | solution.py:33
  69.8 10.5 %collective-permute-start.8 = (f32[2,192,192]{2,1,0:T(8,128)S(1)}, f32[2,192,192]{2,1,0:T(8,128)S(1)}, u32[]{:S(2)}, u32[]{:S(2)}) collective-permute-start(f32[2,192,192]{2,1,0:T(8,128)S(1)} %get-tuple-element.5), channel_id=1, source_target_pairs={{0,8},{8,0},{16,24},{24,16},{1,9},{9,1},{17,25},{25,17},{2,10},{10... | collective-permute-start | bytes 884744 | tf_op jit(solution)/shard_map/ppermute | solution.py:36
  71.1 11.3 %collective-permute-start.4 = (f32[2,192,192]{2,1,0:T(8,128)S(1)}, f32[2,192,192]{2,1,0:T(8,128)S(1)}, u32[]{:S(2)}, u32[]{:S(2)}) collective-permute-start(f32[2,192,192]{2,1,0:T(8,128)S(1)} %get-tuple-element.3), channel_id=1, source_target_pairs={{0,16},{8,24},{16,0},{24,8},{1,17},{9,25},{17,1},{25,9},{2,18},{10... | collective-permute-start | bytes 884744 | tf_op jit(solution)/shard_map/ppermute | solution.py:36
  80.3 12.6 %collective-permute-start.9 = (f32[4,192,192]{2,1,0:T(8,128)S(1)}, f32[4,192,192]{2,1,0:T(8,128)S(1)}, u32[]{:S(2)}, u32[]{:S(2)}) collective-permute-start(f32[4,192,192]{2,1,0:T(8,128)S(1)} %constant_dynamic-update-slice_fusion.2), channel_id=1, source_target_pairs={{0,16},{8,24},{16,0},{24,8},{1,17},{9,25},{17,1},{25,9},{2,18},{10... | collective-permute-start | bytes 1769480 | tf_op jit(solution)/shard_map/ppermute | solution.py:36
  82.4 10.9 %collective-permute-start.5 = (f32[4,192,192]{2,1,0:T(8,128)S(1)}, f32[4,192,192]{2,1,0:T(8,128)S(1)}, u32[]{:S(2)}, u32[]{:S(2)}) collective-permute-start(f32[4,192,192]{2,1,0:T(8,128)S(1)} %constant_dynamic-update-slice_fusion.6), channel_id=1, source_target_pairs={{0,8},{8,0},{16,24},{24,16},{1,9},{9,1},{17,25},{25,17},{2,10},{10... | collective-permute-start | bytes 1769480 | tf_op jit(solution)/shard_map/ppermute | solution.py:36
  83.8 9.6 %copy-start.5 = (f32[16,192]{1,0:T(8,128)S(1)}, f32[16,192]{1,0:T(8,128)}, u32[]{:S(2)}) copy-start(f32[16,192]{1,0:T(8,128)} %param.12) | copy-start | bytes 36868
  93.4 20.3 %copy-start.7 = (s32[16,2]{0,1:T(2,128)S(1)}, s32[16,2]{0,1:T(2,128)}, u32[]{:S(2)}) copy-start(s32[16,2]{0,1:T(2,128)} %param.14) | copy-start | bytes 388
  93.4 21.0 %copy-start.6 = (f32[16,2]{0,1:T(2,128)S(1)}, f32[16,2]{0,1:T(2,128)}, u32[]{:S(2)}) copy-start(f32[16,2]{0,1:T(2,128)} %param.15) | copy-start | bytes 388
  95.4 51.8 %copy-start = (f32[16,192,192]{2,1,0:T(8,128)}, f32[16,192,192]{2,1,0:T(8,128)S(1)}, u32[]{:S(2)}) copy-start(f32[16,192,192]{2,1,0:T(8,128)S(1)} %get-tuple-element.7.refs_1_.refs_4_.refs_10_) | copy-start | bytes 7077892
  95.4 50.7 %collective-permute-start.11 = (f32[16,192,192]{2,1,0:T(8,128)S(1)}, f32[16,192,192]{2,1,0:T(8,128)}, u32[]{:S(2)}, u32[]{:S(2)}) collective-permute-start(f32[16,192,192]{2,1,0:T(8,128)S(1)} %get-tuple-element.7.refs_1_.refs_4_.refs_10_), channel_id=1, source_target_pairs={{1,0},{2,1},{3,2},{4,3},{5,4},{6,5},{7,6},{9,8},{10,9},{11,10},{12... | collective-permute-start | bytes 7077896 | tf_op jit(solution)/shard_map/ppermute | solution.py:19
  97.3 49.9 %collective-permute-start.10 = (f32[16,192,192]{2,1,0:T(8,128)S(1)}, f32[16,192,192]{2,1,0:T(8,128)}, u32[]{:S(2)}, u32[]{:S(2)}) collective-permute-start(f32[16,192,192]{2,1,0:T(8,128)S(1)} %get-tuple-element.7.refs_1_.refs_4_.refs_10_), channel_id=1, source_target_pairs={{0,1},{1,2},{2,3},{3,4},{4,5},{5,6},{6,7},{8,9},{9,10},{10,11},{11... | collective-permute-start | bytes 7077896 | tf_op jit(solution)/shard_map/ppermute | solution.py:18
  167.8 39.6 %collective-permute-start.13 = (f32[16,192,192]{2,1,0:T(8,128)}, f32[16,192,192]{2,1,0:T(8,128)S(1)}, u32[]{:S(2)}, u32[]{:S(2)}) collective-permute-start(f32[16,192,192]{2,1,0:T(8,128)} %shard_map.96.refs_1_.refs_4_.refs_10_), channel_id=1, source_target_pairs={{1,0},{2,1},{3,2},{4,3},{5,4},{6,5},{7,6},{9,8},{10,9},{11,10},{12... | collective-permute-start | bytes 7077896 | tf_op jit(solution)/shard_map/ppermute | solution.py:19
  169.7 39.0 %collective-permute-start.12 = (f32[16,192,192]{2,1,0:T(8,128)}, f32[16,192,192]{2,1,0:T(8,128)}, u32[]{:S(2)}, u32[]{:S(2)}) collective-permute-start(f32[16,192,192]{2,1,0:T(8,128)} %shard_map.96.refs_1_.refs_4_.refs_10_), channel_id=1, source_target_pairs={{0,1},{1,2},{2,3},{3,4},{4,5},{5,6},{6,7},{8,9},{9,10},{10,11},{11... | collective-permute-start | bytes 7077896 | tf_op jit(solution)/shard_map/ppermute | solution.py:18
  207.4 1.7 copy-start.1

commit v4 on v3

--- a/solution.py
+++ b/solution.py
@@ -18,10 +18,6 @@
     from_left = lax.ppermute(cells, axis, [(i, i + 1) for i in range(ends)])
     from_right = lax.ppermute(cells, axis, [(i + 1, i) for i in range(ends)])
     return (from_left, cells, from_right)
-
-
-def source_index(local, width, source):
-    return jnp.where(local // width == source, local % width, 0)
 
 
 def halving_stream(piece, index, count, bits):
@@ -64,11 +60,13 @@
     ).astype(jnp.int32)
 
 
-def exchange_kernel(lead_ref, trail_ref, size_ref, x_lead, t_left, t_own, t_right, coef_ref, out_ref, *, occ):
+def exchange_kernel(lead_ref, trail_ref, size_ref, t_left, t_own, t_right, coef_ref, out_ref, *, occ):
     p = pl.program_id(0)
     size = size_ref[p]
     source = trail_ref[p] // occ
-    x_trail = jnp.where(source == 0, t_left[0], jnp.where(source == 1, t_own[0], t_right[0]))
+    slot = trail_ref[p] % occ
+    x_trail = jnp.where(source == 0, t_left[slot], jnp.where(source == 1, t_own[slot], t_right[slot]))
+    x_lead = t_own[lead_ref[p]]
     transposed = (((1,), (1,)), ((), ()))
     out_ref[0] = jnp.zeros((NPNO, NPNO), jnp.float32)
     for m in CLASS_SIZES:
@@ -77,7 +75,7 @@
         def _():
             first = coef_ref[0, 0, :m, :]
             second = coef_ref[0, 1, :m, :]
-            left_t = lax.dot_general(first, x_lead[0], transposed, preferred_element_type=jnp.float32)
+            left_t = lax.dot_general(first, x_lead, transposed, preferred_element_type=jnp.float32)
             right = lax.dot_general(x_trail, second, transposed, preferred_element_type=jnp.float32)
             out_ref[0, :m, :m] = jnp.dot(
                 left_t.astype(jnp.bfloat16), right.astype(jnp.bfloat16), preferred_element_type=jnp.float32
@@ -87,19 +85,14 @@
 def partial_exchange(lead, trail, sizes, sources, coef_t):
     pairs = coef_t.shape[0]
     occ, nfit, npao = sources[1].shape
-    block = (1, nfit, npao)
-
-    def trail_spec(source):
-        return pl.BlockSpec(block, lambda i, a, b, s: (source_index(b[i], occ, source), 0, 0))
-
+    whole = pl.BlockSpec((occ, nfit, npao), lambda i, a, b, s: (0, 0, 0))
     grid_spec = pltpu.PrefetchScalarGridSpec(
         num_scalar_prefetch=3,
         grid=(pairs,),
         in_specs=[
-            pl.BlockSpec(block, lambda i, a, b, s: (a[i], 0, 0)),
-            trail_spec(0),
-            trail_spec(1),
-            trail_spec(2),
+            whole,
+            whole,
+            whole,
             pl.BlockSpec((1, 2, NPNO, npao), lambda i, a, b, s: (i, 0, 0, 0)),
         ],
         out_specs=pl.BlockSpec((1, NPNO, NPNO), lambda i, a, b, s: (i, 0, 0)),
@@ -114,7 +107,7 @@
             bytes_accessed=pairs * (2 * nfit * npao * 2 + 2 * npao * NPNO * 2 + NPNO * NPNO * 4),
             transcendentals=0,
         ),
-    )(lead, trail, sizes, sources[1], *sources, coef_t)
+    )(lead, trail, sizes, *sources, coef_t)
 
 
 def split_bf16(value):
@@ -128,15 +121,16 @@
 
 
 def coupling_kernel(nb_ref, size_ref, fock_ref, *refs, final, width):
-    t_refs = refs[:6]
-    margin_ref, ex_ref, col_ref, row_ref, own_ref, out_ref, acc_ref = refs[6:]
+    t_refs = refs[:3]
+    margin_ref, ex_ref, col_ref, row_ref, own_ref, out_ref, acc_ref = refs[3:]
     p = pl.program_id(0)
     size = size_ref[p]
     transposed = (((1,), (1,)), ((), ()))
     splits = []
     for n in range(2):
         source = nb_ref[2 * p + n] // width
-        left, own, right = (t_refs[3 * n + k][0] for k in range(3))
+        slot = nb_ref[2 * p + n] % width
+        left, own, right = (t_refs[k][slot] for k in range(3))
         splits.append(split_bf16(jnp.where(source == 0, left, jnp.where(source == 1, own, right))))
     acc_ref[...] = jnp.zeros((NPNO, NPNO), jnp.float32)
     for m in CLASS_SIZES:
@@ -168,16 +162,12 @@
     pairs = own.shape[0]
     block = (1, NPNO, NPNO)
 
-    def t_spec(n, source):
-        return pl.BlockSpec(
-            block, lambda i, q, s, f: (source_index(q[2 * i + n], pairs, source), 0, 0)
-        )
-
+    whole = pl.BlockSpec((pairs, NPNO, NPNO), lambda i, q, s, f: (0, 0, 0))
     own_spec = pl.BlockSpec(block, lambda i, q, s, f: (i, 0, 0))
     grid_spec = pltpu.PrefetchScalarGridSpec(
         num_scalar_prefetch=3,
         grid=(pairs,),
-        in_specs=[t_spec(n, k) for n in range(2) for k in range(3)]
+        in_specs=[whole] * 3
         + [
             pl.BlockSpec((1, 2, NPNO, NPNO), lambda i, q, s, f: (i, 0, 0, 0)),
             own_spec,
@@ -198,7 +188,7 @@
             bytes_accessed=pairs * NPNO * NPNO * (2 * 4 + 2 * 2 + 3 * 4),
             transcendentals=0,
         ),
-    )(nb, sizes, fock, *sources, *sources, margin, exchange, column, row, own)
+    )(nb, sizes, fock, *sources, margin, exchange, column, row, own)
 
 
 def per_device(

time: 231 us -> 231 us (level)
  transfers between devices with their start and end apart: 14 -> 14, of which waited for: 12 -> 13; matrix products, arithmetic and copies ran while one was open for 5% -> 5% of each run, Pallas kernels for 0% -> 0%
where the time goes in v4:
time: 231 us; the launch traced here: 229 us
  waiting for transfers between devices  112 us (48%)
  Pallas kernels  55.8 us (24%)
  starting transfers between devices  41.9 us (18%)
  local copies, waits for them, and re-layouts  10 us (4%)
  other arithmetic  8.12 us (4%)
    ppermute x3, waiting for transfers between devices, halo_sources(): from_right = lax.ppermute(cells, axis, [(i + 1, i) for i in range(ends)])  66.9 us
    pallas_call x2, Pallas kernels, coupling_step(): pl.pallas_call(functools.partial(coupling_kernel, final=final, width=pair...  40.3 us
    ppermute x3, starting transfers between devices, halo_sources(): from_left = lax.ppermute(cells, axis, [(i, i + 1) for i in range(ends)])  25.5 us
    ppermute x4, waiting for transfers between devices, halving_stream(): other = lax.ppermute(piece, 'aux', [(i, i ^ bit) for i in range(count)])  18 us
    ppermute x4, waiting for transfers between devices, halving_stream(): lax.ppermute(send, 'aux', [(i, i ^ bit) for i in range(count)])  17.6 us
    pallas_call x1, Pallas kernels, partial_exchange(): pl.pallas_call(functools.partial(exchange_kernel, occ=occ), grid_spec=gri...  15.5 us
    ppermute x3, waiting for transfers between devices, halo_sources(): from_left = lax.ppermute(cells, axis, [(i, i + 1) for i in range(ends)])  9.93 us
    ppermute x4, starting transfers between devices, halving_stream(): lax.ppermute(send, 'aux', [(i, i ^ bit) for i in range(count)])  5.86 us
  transfers between devices with their start and end apart: 14, of which 13 were waited for; matrix products, arithmetic and copies ran while one was open for 5% of the time, Pallas kernels for 0%

profile of v4, /device:TPU:1, one launch (start us, length us, event | category | flops | bytes accessed | tf_op | source)
XLA Modules:
  0.0 229.2 jit_solution(2619700929913326170)
XLA Ops:
  0.6 4.6 %collective-permute-start = (bf16[4,512,256]{2,1,0:T(8,128)(2,1)}, bf16[4,512,256]{2,1,0:T(8,128)(2,1)S(1)}, u32[]{:S(2)}, u32[]{:S(2)}) collective-permute-start(bf16[4,512,256]{2,1,0:T(8,128)(2,1)} %t_own.1), channel_id=1, source_target_pairs={{0,1},{1,2},{2,3},{3,4},{4,5},{5,6},{6,7},{8,9},{9,10},{10,11},{11... | collective-permute-start | bytes 3145736 | tf_op jit(solution)/shard_map/ppermute | solution.py:18
  5.2 1.9 collective-permute-start.1
  7.2 1.2 compare_select_fusion.2.size_ref
  8.4 0.7 broadcast_subtract_fusion
  9.1 0.6 slice_bitcast_fusion
  9.7 7.6 %collective-permute-done.t_left = bf16[4,512,256]{2,1,0:T(8,128)(2,1)S(1)} collective-permute-done((bf16[4,512,256]{2,1,0:T(8,128)(2,1)}, bf16[4,512,256]{2,1,0:T(8,128)(2,1)S(1)}, u32[]{:S(2)}, u32[]{:S(2)}) %collective-permute-start) | collective-permute-done | bytes 1048608 | tf_op jit(solution)/shard_map/ppermute | solution.py:18
  17.3 4.3 %collective-permute-done.1.t_right = bf16[4,512,256]{2,1,0:T(8,128)(2,1)S(1)} collective-permute-done((bf16[4,512,256]{2,1,0:T(8,128)(2,1)}, bf16[4,512,256]{2,1,0:T(8,128)(2,1)S(1)}, u32[]{:S(2)}, u32[]{:S(2)}) %collective-permute-start.1) | collective-permute-done | bytes 1048608 | tf_op jit(solution)/shard_map/ppermute | solution.py:19
  21.6 1.0 copy-done.4
  22.6 15.5 %shard_map.95 = f32[16,192,192]{2,1,0:T(8,128)} custom-call(s32[16]{0:T(128)} %get-tuple-element.11.lead_ref, s32[16]{0:T(128)} %get-tuple-element.10.trail_ref, s32[16]{0:T(128)} %compare_select_fusion.2.size_ref, bf16[4,512,256]{2,1,0:T(8,128)(2,1)} %copy-done.3, bf16[4,512,256]{2,1,0:T(8,128)(2,1)} %t_own.1, bf16[4,512,256]{2,1,0:T(8,128)(2,1)} %copy-done.4, ...), custom_call_target="tpu_custom_call" | custom-call | flops 2214592512 | bytes 13893632 | tf_op jit(solution)/shard_map/pallas_call | solution.py:101
  38.1 2.2 fusion
  40.3 0.9 constant_dynamic-slice_fusion.1
  41.3 1.2 collective-permute-start.6
  42.5 0.9 constant_dynamic-slice_fusion.3
  43.4 1.2 collective-permute-start.2
  44.6 11.1 %collective-permute-done.6 = f32[4,192,192]{2,1,0:T(8,128)} collective-permute-done((f32[4,192,192]{2,1,0:T(8,128)}, f32[4,192,192]{2,1,0:T(8,128)}, u32[]{:S(2)}, u32[]{:S(2)}) %collective-permute-start.6) | collective-permute-done | bytes 589856 | tf_op jit(solution)/shard_map/ppermute | solution.py:29
  55.7 1.2 dynamic-slice_add_fusion
  57.0 1.7 collective-permute-start.7
  58.7 0.1 collective-permute-done.2
  58.8 1.2 dynamic-slice_add_fusion.1
  60.1 1.7 collective-permute-start.3
  61.8 6.4 %collective-permute-done.7 = f32[2,192,192]{2,1,0:T(8,128)S(1)} collective-permute-done((f32[2,192,192]{2,1,0:T(8,128)S(1)}, f32[2,192,192]{2,1,0:T(8,128)S(1)}, u32[]{:S(2)}, u32[]{:S(2)}) %collective-permute-start.7) | collective-permute-done | bytes 294944 | tf_op jit(solution)/shard_map/ppermute | solution.py:29
  68.3 1.1 constant_dynamic-update-slice_fusion.3
  69.3 1.0 collective-permute-start.8
  70.4 1.3 collective-permute-start.4
  71.8 8.0 %collective-permute-done.8 = f32[2,192,192]{2,1,0:T(8,128)S(1)} collective-permute-done((f32[2,192,192]{2,1,0:T(8,128)S(1)}, f32[2,192,192]{2,1,0:T(8,128)S(1)}, u32[]{:S(2)}, u32[]{:S(2)}) %collective-permute-start.8) | collective-permute-done | bytes 294944 | tf_op jit(solution)/shard_map/ppermute | solution.py:32
  79.8 1.7 collective-permute-start.9
  81.4 0.3 collective-permute-done.4
  81.7 0.8 collective-permute-start.5
  82.6 0.1 broadcast.30.clone
  82.8 0.1 broadcast.30.clone.1
  83.0 9.5 %collective-permute-done.9 = f32[4,192,192]{2,1,0:T(8,128)S(1)} collective-permute-done((f32[4,192,192]{2,1,0:T(8,128)S(1)}, f32[4,192,192]{2,1,0:T(8,128)S(1)}, u32[]{:S(2)}, u32[]{:S(2)}) %collective-permute-start.9) | collective-permute-done | bytes 589856 | tf_op jit(solution)/shard_map/ppermute | solution.py:32
  92.5 0.3 collective-permute-done.5
  93.0 2.0 pad_maximum_fusion
  95.0 1.9 collective-permute-start.11
  96.9 15.7 %collective-permute-start.10 = (f32[16,192,192]{2,1,0:T(8,128)S(1)}, f32[16,192,192]{2,1,0:T(8,128)}, u32[]{:S(2)}, u32[]{:S(2)}) collective-permute-start(f32[16,192,192]{2,1,0:T(8,128)S(1)} %get-tuple-element.7.refs_1_.refs_7_), channel_id=1, source_target_pairs={{0,1},{1,2},{2,3},{3,4},{4,5},{5,6},{6,7},{8,9},{9,10},{10,11},{11... | collective-permute-start | bytes 7077896 | tf_op jit(solution)/shard_map/ppermute | solution.py:18
  112.6 0.6 broadcast_in_dim.26.refs_6_
  113.3 0.7 reshape.18.nb_ref
  114.1 0.6 reshape.19.fock_ref
  114.7 1.7 copy.14.refs_5_
  116.4 29.3 %collective-permute-done.11.refs_2_ = f32[16,192,192]{2,1,0:T(8,128)} collective-permute-done((f32[16,192,192]{2,1,0:T(8,128)S(1)}, f32[16,192,192]{2,1,0:T(8,128)}, u32[]{:S(2)}, u32[]{:S(2)}) %collective-permute-start.11) | collective-permute-done | bytes 2359328 | tf_op jit(solution)/shard_map/ppermute | solution.py:19
  145.7 1.1 collective-permute-done.10.refs_0_
  146.8 20.2 %shard_map.96.refs_1_.refs_7_ = f32[16,192,192]{2,1,0:T(8,128)} custom-call(s32[32]{0:T(128)} %reshape.18.nb_ref, s32[16]{0:T(128)} %compare_select_fusion.2.size_ref, f32[32]{0:T(128)} %reshape.19.fock_ref, f32[16,192,192]{2,1,0:T(8,128)} %collective-permute-done.10.refs_0_, f32[16,192,192]{2,1,0:T(8,128)} %copy-done, ...), custom_call_target="tpu_custom_call" | custom-call | flops 1811939328 | bytes 14155776 | tf_op jit(solution)/shard_map/pallas_call | solution.py:182
  167.0 1.9 collective-permute-start.13
  169.0 5.2 %collective-permute-start.12 = (f32[16,192,192]{2,1,0:T(8,128)}, f32[16,192,192]{2,1,0:T(8,128)}, u32[]{:S(2)}, u32[]{:S(2)}) collective-permute-start(f32[16,192,192]{2,1,0:T(8,128)} %shard_map.96.refs_1_.refs_7_), channel_id=1, source_target_pairs={{0,1},{1,2},{2,3},{3,4},{4,5},{5,6},{6,7},{8,9},{9,10},{10,11},{11... | collective-permute-start | bytes 7077896 | tf_op jit(solution)/shard_map/ppermute | solution.py:18
  174.2 33.2 %collective-permute-done.13.refs_2_ = f32[16,192,192]{2,1,0:T(8,128)S(1)} collective-permute-done((f32[16,192,192]{2,1,0:T(8,128)}, f32[16,192,192]{2,1,0:T(8,128)S(1)}, u32[]{:S(2)}, u32[]{:S(2)}) %collective-permute-start.13) | collective-permute-done | bytes 2359328 | tf_op jit(solution)/shard_map/ppermute | solution.py:19
  207.4 1.3 collective-permute-done.12.refs_0_
  208.7 0.4 copy-done.1
  209.2 20.1 %shard_map.97 = f32[16,192,192]{2,1,0:T(8,128)} custom-call(s32[32]{0:T(128)} %reshape.18.nb_ref, s32[16]{0:T(128)} %compare_select_fusion.2.size_ref, f32[32]{0:T(128)} %reshape.19.fock_ref, f32[16,192,192]{2,1,0:T(8,128)} %collective-permute-done.12.refs_0_, f32[16,192,192]{2,1,0:T(8,128)} %shard_map.96.refs_1_.refs_7_, f32[16,192,192]{2,1,0:T(8,128)} %copy-done.1, ...), custom_call_target="tpu_custom_call" | custom-call | flops 1811939328 | bytes 14155776 | tf_op jit(solution)/shard_map/pallas_call | solution.py:182
  (29 shorter events, 0.7 us)
Async XLA Ops:
  0.6 16.6 %collective-permute-start = (bf16[4,512,256]{2,1,0:T(8,128)(2,1)}, bf16[4,512,256]{2,1,0:T(8,128)(2,1)S(1)}, u32[]{:S(2)}, u32[]{:S(2)}) collective-permute-start(bf16[4,512,256]{2,1,0:T(8,128)(2,1)} %t_own.1), channel_id=1, source_target_pairs={{0,1},{1,2},{2,3},{3,4},{4,5},{5,6},{6,7},{8,9},{9,10},{10,11},{11... | collective-permute-start | bytes 3145736 | tf_op jit(solution)/shard_map/ppermute | solution.py:18
  5.2 16.3 %collective-permute-start.1 = (bf16[4,512,256]{2,1,0:T(8,128)(2,1)}, bf16[4,512,256]{2,1,0:T(8,128)(2,1)S(1)}, u32[]{:S(2)}, u32[]{:S(2)}) collective-permute-start(bf16[4,512,256]{2,1,0:T(8,128)(2,1)} %t_own.1), channel_id=1, source_target_pairs={{1,0},{2,1},{3,2},{4,3},{5,4},{6,5},{7,6},{9,8},{10,9},{11,10},{12... | collective-permute-start | bytes 3145736 | tf_op jit(solution)/shard_map/ppermute | solution.py:19
  17.3 4.3 %copy-start.3 = (bf16[4,512,256]{2,1,0:T(8,128)(2,1)}, bf16[4,512,256]{2,1,0:T(8,128)(2,1)S(1)}, u32[]{:S(2)}) copy-start(bf16[4,512,256]{2,1,0:T(8,128)(2,1)S(1)} %collective-permute-done.t_left) | copy-start | bytes 3145732
  21.6 1.0 copy-start.4
  41.3 14.4 %collective-permute-start.6 = (f32[4,192,192]{2,1,0:T(8,128)}, f32[4,192,192]{2,1,0:T(8,128)}, u32[]{:S(2)}, u32[]{:S(2)}) collective-permute-start(f32[4,192,192]{2,1,0:T(8,128)} %constant_dynamic-slice_fusion.1), channel_id=1, source_target_pairs={{0,16},{8,24},{16,0},{24,8},{1,17},{9,25},{17,1},{25,9},{2,18},{10... | collective-permute-start | bytes 1769480 | tf_op jit(solution)/shard_map/ppermute | solution.py:29
  43.4 15.4 %collective-permute-start.2 = (f32[4,192,192]{2,1,0:T(8,128)}, f32[4,192,192]{2,1,0:T(8,128)}, u32[]{:S(2)}, u32[]{:S(2)}) collective-permute-start(f32[4,192,192]{2,1,0:T(8,128)} %constant_dynamic-slice_fusion.3), channel_id=1, source_target_pairs={{0,8},{8,0},{16,24},{24,16},{1,9},{9,1},{17,25},{25,17},{2,10},{10... | collective-permute-start | bytes 1769480 | tf_op jit(solution)/shard_map/ppermute | solution.py:29
  56.9 3.1 %copy-start.2 = (f32[4,192,192]{2,1,0:T(8,128)}, f32[4,192,192]{2,1,0:T(8,128)S(1)}, u32[]{:S(2)}) copy-start(f32[4,192,192]{2,1,0:T(8,128)S(1)} %dynamic-slice_add_fusion) | copy-start | bytes 1769476
  57.0 11.2 %collective-permute-start.7 = (f32[2,192,192]{2,1,0:T(8,128)S(1)}, f32[2,192,192]{2,1,0:T(8,128)S(1)}, u32[]{:S(2)}, u32[]{:S(2)}) collective-permute-start(f32[2,192,192]{2,1,0:T(8,128)S(1)} %constant_dynamic-slice_fusion), channel_id=1, source_target_pairs={{0,8},{8,0},{16,24},{24,16},{1,9},{9,1},{17,25},{25,17},{2,10},{10... | collective-permute-start | bytes 884744 | tf_op jit(solution)/shard_map/ppermute | solution.py:29
  60.1 10.2 %collective-permute-start.3 = (f32[2,192,192]{2,1,0:T(8,128)S(1)}, f32[2,192,192]{2,1,0:T(8,128)S(1)}, u32[]{:S(2)}, u32[]{:S(2)}) collective-permute-start(f32[2,192,192]{2,1,0:T(8,128)S(1)} %constant_dynamic-slice_fusion.2), channel_id=1, source_target_pairs={{0,16},{8,24},{16,0},{24,8},{1,17},{9,25},{17,1},{25,9},{2,18},{10... | collective-permute-start | bytes 884744 | tf_op jit(solution)/shard_map/ppermute | solution.py:29
  69.3 10.4 %collective-permute-start.8 = (f32[2,192,192]{2,1,0:T(8,128)S(1)}, f32[2,192,192]{2,1,0:T(8,128)S(1)}, u32[]{:S(2)}, u32[]{:S(2)}) collective-permute-start(f32[2,192,192]{2,1,0:T(8,128)S(1)} %get-tuple-element.5), channel_id=1, source_target_pairs={{0,8},{8,0},{16,24},{24,16},{1,9},{9,1},{17,25},{25,17},{2,10},{10... | collective-permute-start | bytes 884744 | tf_op jit(solution)/shard_map/ppermute | solution.py:32
  70.4 11.3 %collective-permute-start.4 = (f32[2,192,192]{2,1,0:T(8,128)S(1)}, f32[2,192,192]{2,1,0:T(8,128)S(1)}, u32[]{:S(2)}, u32[]{:S(2)}) collective-permute-start(f32[2,192,192]{2,1,0:T(8,128)S(1)} %get-tuple-element.3), channel_id=1, source_target_pairs={{0,16},{8,24},{16,0},{24,8},{1,17},{9,25},{17,1},{25,9},{2,18},{10... | collective-permute-start | bytes 884744 | tf_op jit(solution)/shard_map/ppermute | solution.py:32
  79.8 12.7 %collective-permute-start.9 = (f32[4,192,192]{2,1,0:T(8,128)S(1)}, f32[4,192,192]{2,1,0:T(8,128)S(1)}, u32[]{:S(2)}, u32[]{:S(2)}) collective-permute-start(f32[4,192,192]{2,1,0:T(8,128)S(1)} %constant_dynamic-update-slice_fusion.2), channel_id=1, source_target_pairs={{0,16},{8,24},{16,0},{24,8},{1,17},{9,25},{17,1},{25,9},{2,18},{10... | collective-permute-start | bytes 1769480 | tf_op jit(solution)/shard_map/ppermute | solution.py:32
  81.7 11.1 %collective-permute-start.5 = (f32[4,192,192]{2,1,0:T(8,128)S(1)}, f32[4,192,192]{2,1,0:T(8,128)S(1)}, u32[]{:S(2)}, u32[]{:S(2)}) collective-permute-start(f32[4,192,192]{2,1,0:T(8,128)S(1)} %constant_dynamic-update-slice_fusion.6), channel_id=1, source_target_pairs={{0,8},{8,0},{16,24},{24,16},{1,9},{9,1},{17,25},{25,17},{2,10},{10... | collective-permute-start | bytes 1769480 | tf_op jit(solution)/shard_map/ppermute | solution.py:32
  83.0 10.0 %copy-start.5 = (f32[16,192]{1,0:T(8,128)S(1)}, f32[16,192]{1,0:T(8,128)}, u32[]{:S(2)}) copy-start(f32[16,192]{1,0:T(8,128)} %param.12) | copy-start | bytes 36868
  92.9 20.3 %copy-start.7 = (s32[16,2]{0,1:T(2,128)S(1)}, s32[16,2]{0,1:T(2,128)}, u32[]{:S(2)}) copy-start(s32[16,2]{0,1:T(2,128)} %param.14) | copy-start | bytes 388
  92.9 21.0 %copy-start.6 = (f32[16,2]{0,1:T(2,128)S(1)}, f32[16,2]{0,1:T(2,128)}, u32[]{:S(2)}) copy-start(f32[16,2]{0,1:T(2,128)} %param.15) | copy-start | bytes 388
  95.0 51.8 %copy-start = (f32[16,192,192]{2,1,0:T(8,128)}, f32[16,192,192]{2,1,0:T(8,128)S(1)}, u32[]{:S(2)}) copy-start(f32[16,192,192]{2,1,0:T(8,128)S(1)} %get-tuple-element.7.refs_1_.refs_7_) | copy-start | bytes 7077892
  95.0 50.7 %collective-permute-start.11 = (f32[16,192,192]{2,1,0:T(8,128)S(1)}, f32[16,192,192]{2,1,0:T(8,128)}, u32[]{:S(2)}, u32[]{:S(2)}) collective-permute-start(f32[16,192,192]{2,1,0:T(8,128)S(1)} %get-tuple-element.7.refs_1_.refs_7_), channel_id=1, source_target_pairs={{1,0},{2,1},{3,2},{4,3},{5,4},{6,5},{7,6},{9,8},{10,9},{11,10},{12... | collective-permute-start | bytes 7077896 | tf_op jit(solution)/shard_map/ppermute | solution.py:19
  96.9 49.9 %collective-permute-start.10 = (f32[16,192,192]{2,1,0:T(8,128)S(1)}, f32[16,192,192]{2,1,0:T(8,128)}, u32[]{:S(2)}, u32[]{:S(2)}) collective-permute-start(f32[16,192,192]{2,1,0:T(8,128)S(1)} %get-tuple-element.7.refs_1_.refs_7_), channel_id=1, source_target_pairs={{0,1},{1,2},{2,3},{3,4},{4,5},{5,6},{6,7},{8,9},{9,10},{10,11},{11... | collective-permute-start | bytes 7077896 | tf_op jit(solution)/shard_map/ppermute | solution.py:18
  167.0 40.4 %collective-permute-start.13 = (f32[16,192,192]{2,1,0:T(8,128)}, f32[16,192,192]{2,1,0:T(8,128)S(1)}, u32[]{:S(2)}, u32[]{:S(2)}) collective-permute-start(f32[16,192,192]{2,1,0:T(8,128)} %shard_map.96.refs_1_.refs_7_), channel_id=1, source_target_pairs={{1,0},{2,1},{3,2},{4,3},{5,4},{6,5},{7,6},{9,8},{10,9},{11,10},{12... | collective-permute-start | bytes 7077896 | tf_op jit(solution)/shard_map/ppermute | solution.py:19
  169.0 39.7 %collective-permute-start.12 = (f32[16,192,192]{2,1,0:T(8,128)}, f32[16,192,192]{2,1,0:T(8,128)}, u32[]{:S(2)}, u32[]{:S(2)}) collective-permute-start(f32[16,192,192]{2,1,0:T(8,128)} %shard_map.96.refs_1_.refs_7_), channel_id=1, source_target_pairs={{0,1},{1,2},{2,3},{3,4},{4,5},{5,6},{6,7},{8,9},{9,10},{10,11},{11... | collective-permute-start | bytes 7077896 | tf_op jit(solution)/shard_map/ppermute | solution.py:18
  207.4 1.7 copy-start.1

commit v5 on v4

--- a/solution.py
+++ b/solution.py
@@ -120,10 +120,10 @@
     return lax.dot_general(lhs, rhs, dims, preferred_element_type=jnp.float32)
 
 
-def coupling_kernel(nb_ref, size_ref, fock_ref, *refs, final, width):
+def coupling_kernel(nb_ref, size_ref, fock_ref, *refs, final, width, start):
     t_refs = refs[:3]
     margin_ref, ex_ref, col_ref, row_ref, own_ref, out_ref, acc_ref = refs[3:]
-    p = pl.program_id(0)
+    p = pl.program_id(0) + start
     size = size_ref[p]
     transposed = (((1,), (1,)), ((), ()))
     splits = []
@@ -156,39 +156,44 @@
         out_ref[0] = amplitudes - residual / denominator
 
 
-def coupling_step(nb, sizes, fock, sources, margin, exchange, energy, own, final):
-    column = energy.reshape(energy.shape[0], NPNO, 1)
-    row = energy.reshape(energy.shape[0], 1, NPNO)
+def coupling_step(nb, sizes, fock, sources, margin, exchange, energy, own, final, start=0, count=None):
     pairs = own.shape[0]
+    count = pairs if count is None else count
+    column = energy.reshape(pairs, NPNO, 1)
+    row = energy.reshape(pairs, 1, NPNO)
     block = (1, NPNO, NPNO)
-
     whole = pl.BlockSpec((pairs, NPNO, NPNO), lambda i, q, s, f: (0, 0, 0))
-    own_spec = pl.BlockSpec(block, lambda i, q, s, f: (i, 0, 0))
+    own_spec = pl.BlockSpec(block, lambda i, q, s, f: (i + start, 0, 0))
     grid_spec = pltpu.PrefetchScalarGridSpec(
         num_scalar_prefetch=3,
-        grid=(pairs,),
+        grid=(count,),
         in_specs=[whole] * 3
         + [
-            pl.BlockSpec((1, 2, NPNO, NPNO), lambda i, q, s, f: (i, 0, 0, 0)),
+            pl.BlockSpec((1, 2, NPNO, NPNO), lambda i, q, s, f: (i + start, 0, 0, 0)),
             own_spec,
-            pl.BlockSpec((1, NPNO, 1), lambda i, q, s, f: (i, 0, 0)),
-            pl.BlockSpec((1, 1, NPNO), lambda i, q, s, f: (i, 0, 0)),
+            pl.BlockSpec((1, NPNO, 1), lambda i, q, s, f: (i + start, 0, 0)),
+            pl.BlockSpec((1, 1, NPNO), lambda i, q, s, f: (i + start, 0, 0)),
             own_spec,
         ],
-        out_specs=own_spec,
+        out_specs=pl.BlockSpec(block, lambda i, q, s, f: (i, 0, 0)),
         scratch_shapes=[pltpu.VMEM((NPNO, NPNO), jnp.float32)],
     )
-    flops = pairs * 2 * 4 * 2 * NPNO * NPNO * NPNO
+    flops = count * 2 * 4 * 2 * NPNO * NPNO * NPNO
     return pl.pallas_call(
-        functools.partial(coupling_kernel, final=final, width=pairs),
+        functools.partial(coupling_kernel, final=final, width=pairs, start=start),
         grid_spec=grid_spec,
-        out_shape=jax.ShapeDtypeStruct((pairs, NPNO, NPNO), jnp.float32),
+        out_shape=jax.ShapeDtypeStruct((count, NPNO, NPNO), jnp.float32),
         cost_estimate=pl.CostEstimate(
             flops=flops,
-            bytes_accessed=pairs * NPNO * NPNO * (2 * 4 + 2 * 2 + 3 * 4),
+            bytes_accessed=count * NPNO * NPNO * (2 * 4 + 2 * 2 + 3 * 4),
             transcendentals=0,
         ),
     )(nb, sizes, fock, *sources, margin, exchange, column, row, own)
+
+
+def joined_halo(parts, axis):
+    received = [halo_sources(part, axis) for part in parts]
+    return tuple(jnp.concatenate([r[k] for r in received], axis=0) for k in range(3))
 
 
 def per_device(
@@ -220,14 +225,20 @@
     fock = fock_coupling.reshape(-1)
 
     amplitudes = -(exchange_ints / denominator)
+    sources = halo_sources(amplitudes, "pair")
+    half = pair_dev // 2
     for iteration in range(1, ITERS):
-        amplitudes = coupling_step(
-            local_rows, sizes, fock, halo_sources(amplitudes, "pair"), margin, exchange_ints,
-            pno_energy, amplitudes, False,
-        )
+        parts = [
+            coupling_step(
+                local_rows, sizes, fock, sources, margin, exchange_ints, pno_energy, amplitudes,
+                False, start, half,
+            )
+            for start in (0, half)
+        ]
+        sources = joined_halo(parts, "pair")
+        amplitudes = sources[1]
     residual = coupling_step(
-        local_rows, sizes, fock, halo_sources(amplitudes, "pair"), margin, exchange_ints,
-        pno_energy, amplitudes, True,
+        local_rows, sizes, fock, sources, margin, exchange_ints, pno_energy, amplitudes, True
     )
     return (amplitudes, residual)
 

time: 231 us -> 240 us (1.039)
  waiting for transfers between devices: 112 us -> 103 us
  other arithmetic: 8.12 us -> 15.4 us
  Pallas kernels: 55.8 us -> 62.8 us
  starting transfers between devices: 41.9 us -> 47.4 us
    ppermute x3 -> x4, waiting for transfers between devices: 66.9 us -> 46 us  [halo_sources(): from_right = lax.ppermute(cells, axis, [(i + 1, i) for i in range(ends)])]
    ppermute x3 -> x4, waiting for transfers between devices: 9.93 us -> 22.9 us  [halo_sources(): from_left = lax.ppermute(cells, axis, [(i, i + 1) for i in range(ends)])]
    concatenate x0 -> x3, other arithmetic: none -> 7.31 us  [joined_halo(): jnp.concatenate([r[k] for r in received], axis=0)]
    pallas_call x2 -> x3, Pallas kernels: 40.3 us -> 46.9 us  [coupling_step(): pl.pallas_call(functools.partial(coupling_kernel, final=final, width=pair...]
    ppermute x3 -> x4, starting transfers between devices: 25.5 us -> 28 us  [halo_sources(): from_left = lax.ppermute(cells, axis, [(i, i + 1) for i in range(ends)])]
    ppermute x3 -> x4, starting transfers between devices: 5.74 us -> 7.78 us  [halo_sources(): from_right = lax.ppermute(cells, axis, [(i + 1, i) for i in range(ends)])]
  transfers between devices with their start and end apart: 14 -> 16, of which waited for: 13 -> 12; matrix products, arithmetic and copies ran while one was open for 5% -> 7% of each run, Pallas kernels for 0% -> 5%
where the time goes in v5:
time: 240 us; the launch traced here: 239 us
  waiting for transfers between devices  103 us (43%)
  Pallas kernels  62.8 us (26%)
  starting transfers between devices  47.4 us (20%)
  other arithmetic  15.4 us (6%)
  local copies, waits for them, and re-layouts  9.57 us (4%)
    pallas_call x3, Pallas kernels, coupling_step(): pl.pallas_call(functools.partial(coupling_kernel, final=final, width=pair...  46.9 us
    ppermute x4, waiting for transfers between devices, halo_sources(): from_right = lax.ppermute(cells, axis, [(i + 1, i) for i in range(ends)])  46 us
    ppermute x4, starting transfers between devices, halo_sources(): from_left = lax.ppermute(cells, axis, [(i, i + 1) for i in range(ends)])  28 us
    ppermute x4, waiting for transfers between devices, halo_sources(): from_left = lax.ppermute(cells, axis, [(i, i + 1) for i in range(ends)])  22.9 us
    ppermute x4, waiting for transfers between devices, halving_stream(): lax.ppermute(send, 'aux', [(i, i ^ bit) for i in range(count)])  17 us
    ppermute x4, waiting for transfers between devices, halving_stream(): other = lax.ppermute(piece, 'aux', [(i, i ^ bit) for i in range(count)])  16.9 us
    pallas_call x1, Pallas kernels, partial_exchange(): pl.pallas_call(functools.partial(exchange_kernel, occ=occ), grid_spec=gri...  15.8 us
    ppermute x4, starting transfers between devices, halo_sources(): from_right = lax.ppermute(cells, axis, [(i + 1, i) for i in range(ends)])  7.78 us
  transfers between devices with their start and end apart: 16, of which 12 were waited for; matrix products, arithmetic and copies ran while one was open for 7% of the time, Pallas kernels for 5%

profile of v5, /device:TPU:1, one launch (start us, length us, event | category | flops | bytes accessed | tf_op | source)
XLA Modules:
  0.0 238.8 jit_solution(16029504561625935712)
XLA Ops:
  0.6 4.6 %collective-permute-start = (bf16[4,512,256]{2,1,0:T(8,128)(2,1)}, bf16[4,512,256]{2,1,0:T(8,128)(2,1)S(1)}, u32[]{:S(2)}, u32[]{:S(2)}) collective-permute-start(bf16[4,512,256]{2,1,0:T(8,128)(2,1)} %t_own.1), channel_id=1, source_target_pairs={{0,1},{1,2},{2,3},{3,4},{4,5},{5,6},{6,7},{8,9},{9,10},{10,11},{11... | collective-permute-start | bytes 3145736 | tf_op jit(solution)/shard_map/ppermute | solution.py:18
  5.2 1.9 collective-permute-start.1
  7.2 1.2 compare_select_fusion.2.size_ref
  8.4 0.7 broadcast_subtract_fusion
  9.6 7.7 %collective-permute-done.t_left = bf16[4,512,256]{2,1,0:T(8,128)(2,1)S(1)} collective-permute-done((bf16[4,512,256]{2,1,0:T(8,128)(2,1)}, bf16[4,512,256]{2,1,0:T(8,128)(2,1)S(1)}, u32[]{:S(2)}, u32[]{:S(2)}) %collective-permute-start) | collective-permute-done | bytes 1048608 | tf_op jit(solution)/shard_map/ppermute | solution.py:18
  17.3 4.3 %collective-permute-done.1.t_right = bf16[4,512,256]{2,1,0:T(8,128)(2,1)S(1)} collective-permute-done((bf16[4,512,256]{2,1,0:T(8,128)(2,1)}, bf16[4,512,256]{2,1,0:T(8,128)(2,1)S(1)}, u32[]{:S(2)}, u32[]{:S(2)}) %collective-permute-start.1) | collective-permute-done | bytes 1048608 | tf_op jit(solution)/shard_map/ppermute | solution.py:19
  21.6 1.0 copy-done.4
  22.6 15.8 %shard_map.95 = f32[16,192,192]{2,1,0:T(8,128)} custom-call(s32[16]{0:T(128)} %get-tuple-element.11.lead_ref, s32[16]{0:T(128)} %get-tuple-element.10.trail_ref, s32[16]{0:T(128)} %compare_select_fusion.2.size_ref, bf16[4,512,256]{2,1,0:T(8,128)(2,1)} %copy-done.3, bf16[4,512,256]{2,1,0:T(8,128)(2,1)} %t_own.1, bf16[4,512,256]{2,1,0:T(8,128)(2,1)} %copy-done.4, ...), custom_call_target="tpu_custom_call" | custom-call | flops 2214592512 | bytes 13893632 | tf_op jit(solution)/shard_map/pallas_call | solution.py:101
  38.4 2.2 fusion
  40.6 0.9 constant_dynamic-slice_fusion.1
  41.6 1.2 collective-permute-start.6
  42.8 0.9 constant_dynamic-slice_fusion.3
  43.7 1.2 collective-permute-start.2
  44.9 11.5 %collective-permute-done.6 = f32[4,192,192]{2,1,0:T(8,128)} collective-permute-done((f32[4,192,192]{2,1,0:T(8,128)}, f32[4,192,192]{2,1,0:T(8,128)}, u32[]{:S(2)}, u32[]{:S(2)}) %collective-permute-start.6) | collective-permute-done | bytes 589856 | tf_op jit(solution)/shard_map/ppermute | solution.py:29
  56.4 1.2 dynamic-slice_add_fusion
  57.7 1.7 collective-permute-start.7
  59.4 1.2 dynamic-slice_add_fusion.1
  60.7 1.4 collective-permute-start.3
  62.1 5.5 %collective-permute-done.7 = f32[2,192,192]{2,1,0:T(8,128)S(1)} collective-permute-done((f32[2,192,192]{2,1,0:T(8,128)S(1)}, f32[2,192,192]{2,1,0:T(8,128)S(1)}, u32[]{:S(2)}, u32[]{:S(2)}) %collective-permute-start.7) | collective-permute-done | bytes 294944 | tf_op jit(solution)/shard_map/ppermute | solution.py:29
  67.7 1.1 constant_dynamic-update-slice_fusion.3
  68.7 1.3 collective-permute-start.8
  70.2 1.4 collective-permute-start.4
  71.6 7.7 %collective-permute-done.8 = f32[2,192,192]{2,1,0:T(8,128)S(1)} collective-permute-done((f32[2,192,192]{2,1,0:T(8,128)S(1)}, f32[2,192,192]{2,1,0:T(8,128)S(1)}, u32[]{:S(2)}, u32[]{:S(2)}) %collective-permute-start.8) | collective-permute-done | bytes 294944 | tf_op jit(solution)/shard_map/ppermute | solution.py:32
  79.3 2.0 collective-permute-start.9
  81.5 1.3 collective-permute-start.5
  83.1 8.1 %collective-permute-done.9 = f32[4,192,192]{2,1,0:T(8,128)S(1)} collective-permute-done((f32[4,192,192]{2,1,0:T(8,128)S(1)}, f32[4,192,192]{2,1,0:T(8,128)S(1)}, u32[]{:S(2)}, u32[]{:S(2)}) %collective-permute-start.9) | collective-permute-done | bytes 589856 | tf_op jit(solution)/shard_map/ppermute | solution.py:32
  91.3 1.1 collective-permute-done.5
  92.5 2.1 pad_maximum_fusion
  94.6 1.9 collective-permute-start.11
  96.5 16.4 %collective-permute-start.10 = (f32[16,192,192]{2,1,0:T(8,128)S(1)}, f32[16,192,192]{2,1,0:T(8,128)}, u32[]{:S(2)}, u32[]{:S(2)}) collective-permute-start(f32[16,192,192]{2,1,0:T(8,128)S(1)} %get-tuple-element.7.refs_1_.refs_7_), channel_id=1, source_target_pairs={{0,1},{1,2},{2,3},{3,4},{4,5},{5,6},{6,7},{8,9},{9,10},{10,11},{11... | collective-permute-start | bytes 7077896 | tf_op jit(solution)/shard_map/ppermute | solution.py:18
  112.9 0.6 broadcast_in_dim.26.refs_6_
  113.6 0.6 reshape.20.nb_ref
  114.3 0.7 reshape.21.fock_ref
  115.0 1.7 copy.14.refs_5_
  116.7 29.4 %collective-permute-done.11.refs_2_ = f32[16,192,192]{2,1,0:T(8,128)} collective-permute-done((f32[16,192,192]{2,1,0:T(8,128)S(1)}, f32[16,192,192]{2,1,0:T(8,128)}, u32[]{:S(2)}, u32[]{:S(2)}) %collective-permute-start.11) | collective-permute-done | bytes 2359328 | tf_op jit(solution)/shard_map/ppermute | solution.py:19
  146.0 1.1 collective-permute-done.10.refs_0_
  147.1 13.1 %shard_map.96 = f32[8,192,192]{2,1,0:T(8,128)} custom-call(s32[32]{0:T(128)} %reshape.20.nb_ref, s32[16]{0:T(128)} %compare_select_fusion.2.size_ref, f32[32]{0:T(128)} %reshape.21.fock_ref, f32[16,192,192]{2,1,0:T(8,128)} %collective-permute-done.10.refs_0_, f32[16,192,192]{2,1,0:T(8,128)} %copy-done, f32[16,192,192]{2,1,0:T(8,128)} %collective-permute-done.11.refs_2_, ...), custom_call_target="tpu_custom_call" | custom-call | flops 905969664 | bytes 7077888 | tf_op jit(solution)/shard_map/pallas_call | solution.py:182
  160.3 2.0 collective-permute-start.14
  162.3 13.0 %shard_map.97 = f32[8,192,192]{2,1,0:T(8,128)} custom-call(s32[32]{0:T(128)} %reshape.20.nb_ref, s32[16]{0:T(128)} %compare_select_fusion.2.size_ref, f32[32]{0:T(128)} %reshape.21.fock_ref, f32[16,192,192]{2,1,0:T(8,128)} %collective-permute-done.10.refs_0_, f32[16,192,192]{2,1,0:T(8,128)} %copy-done, f32[16,192,192]{2,1,0:T(8,128)} %collective-permute-done.11.refs_2_, ...), custom_call_target="tpu_custom_call" | custom-call | flops 905969664 | bytes 7077888 | tf_op jit(solution)/shard_map/pallas_call | solution.py:182
  175.3 1.9 collective-permute-start.15
  177.2 4.6 %collective-permute-start.12 = (f32[8,192,192]{2,1,0:T(8,128)S(1)}, f32[8,192,192]{2,1,0:T(8,128)S(1)}, u32[]{:S(2)}, u32[]{:S(2)}) collective-permute-start(f32[8,192,192]{2,1,0:T(8,128)S(1)} %copy-done.1), channel_id=1, source_target_pairs={{0,1},{1,2},{2,3},{3,4},{4,5},{5,6},{6,7},{8,9},{9,10},{10,11},{11... | collective-permute-start | bytes 3538952 | tf_op jit(solution)/shard_map/ppermute | solution.py:18
  181.8 2.4 %collective-permute-start.13 = (f32[8,192,192]{2,1,0:T(8,128)}, f32[8,192,192]{2,1,0:T(8,128)S(1)}, u32[]{:S(2)}, u32[]{:S(2)}) collective-permute-start(f32[8,192,192]{2,1,0:T(8,128)} %shard_map.97), channel_id=1, source_target_pairs={{0,1},{1,2},{2,3},{3,4},{4,5},{5,6},{6,7},{8,9},{9,10},{10,11},{11... | collective-permute-start | bytes 3538952 | tf_op jit(solution)/shard_map/ppermute | solution.py:18
  184.2 3.4 %pad_maximum_fusion.1.refs_1_.refs_7_ = f32[16,192,192]{2,1,0:T(8,128)} fusion(f32[8,192,192]{2,1,0:T(8,128)} %shard_map.97, f32[8,192,192]{2,1,0:T(8,128)S(1)} %copy-done.1), kind=kLoop, calls=%fused_computation.1 | loop fusion | flops 589824 | bytes 4718592 | tf_op jit(solution)/shard_map/concatenate | solution.py:196
  187.6 12.4 %collective-permute-done.15 = f32[8,192,192]{2,1,0:T(8,128)S(1)} collective-permute-done((f32[8,192,192]{2,1,0:T(8,128)}, f32[8,192,192]{2,1,0:T(8,128)S(1)}, u32[]{:S(2)}, u32[]{:S(2)}) %collective-permute-start.15) | collective-permute-done | bytes 1179680 | tf_op jit(solution)/shard_map/ppermute | solution.py:19
  200.0 2.0 pad_maximum_fusion.3.refs_2_
  202.0 14.1 %collective-permute-done.13 = f32[8,192,192]{2,1,0:T(8,128)S(1)} collective-permute-done((f32[8,192,192]{2,1,0:T(8,128)}, f32[8,192,192]{2,1,0:T(8,128)S(1)}, u32[]{:S(2)}, u32[]{:S(2)}) %collective-permute-start.13) | collective-permute-done | bytes 1179680 | tf_op jit(solution)/shard_map/ppermute | solution.py:18
  216.1 1.9 pad_maximum_fusion.2.refs_0_
  218.0 20.8 %shard_map.98 = f32[16,192,192]{2,1,0:T(8,128)} custom-call(s32[32]{0:T(128)} %reshape.20.nb_ref, s32[16]{0:T(128)} %compare_select_fusion.2.size_ref, f32[32]{0:T(128)} %reshape.21.fock_ref, f32[16,192,192]{2,1,0:T(8,128)} %pad_maximum_fusion.2.refs_0_, f32[16,192,192]{2,1,0:T(8,128)} %pad_maximum_fusion.1.refs_1_.refs_7_, ...), custom_call_target="tpu_custom_call" | custom-call | flops 1811939328 | bytes 14155776 | tf_op jit(solution)/shard_map/pallas_call | solution.py:182
  (37 shorter events, 1.6 us)
Async XLA Ops:
  0.6 16.6 %collective-permute-start = (bf16[4,512,256]{2,1,0:T(8,128)(2,1)}, bf16[4,512,256]{2,1,0:T(8,128)(2,1)S(1)}, u32[]{:S(2)}, u32[]{:S(2)}) collective-permute-start(bf16[4,512,256]{2,1,0:T(8,128)(2,1)} %t_own.1), channel_id=1, source_target_pairs={{0,1},{1,2},{2,3},{3,4},{4,5},{5,6},{6,7},{8,9},{9,10},{10,11},{11... | collective-permute-start | bytes 3145736 | tf_op jit(solution)/shard_map/ppermute | solution.py:18
  5.2 16.3 %collective-permute-start.1 = (bf16[4,512,256]{2,1,0:T(8,128)(2,1)}, bf16[4,512,256]{2,1,0:T(8,128)(2,1)S(1)}, u32[]{:S(2)}, u32[]{:S(2)}) collective-permute-start(bf16[4,512,256]{2,1,0:T(8,128)(2,1)} %t_own.1), channel_id=1, source_target_pairs={{1,0},{2,1},{3,2},{4,3},{5,4},{6,5},{7,6},{9,8},{10,9},{11,10},{12... | collective-permute-start | bytes 3145736 | tf_op jit(solution)/shard_map/ppermute | solution.py:19
  17.3 4.3 %copy-start.3 = (bf16[4,512,256]{2,1,0:T(8,128)(2,1)}, bf16[4,512,256]{2,1,0:T(8,128)(2,1)S(1)}, u32[]{:S(2)}) copy-start(bf16[4,512,256]{2,1,0:T(8,128)(2,1)S(1)} %collective-permute-done.t_left) | copy-start | bytes 3145732
  21.6 1.0 copy-start.4
  41.6 14.8 %collective-permute-start.6 = (f32[4,192,192]{2,1,0:T(8,128)}, f32[4,192,192]{2,1,0:T(8,128)}, u32[]{:S(2)}, u32[]{:S(2)}) collective-permute-start(f32[4,192,192]{2,1,0:T(8,128)} %constant_dynamic-slice_fusion.1), channel_id=1, source_target_pairs={{0,16},{8,24},{16,0},{24,8},{1,17},{9,25},{17,1},{25,9},{2,18},{10... | collective-permute-start | bytes 1769480 | tf_op jit(solution)/shard_map/ppermute | solution.py:29
  43.7 15.6 %collective-permute-start.2 = (f32[4,192,192]{2,1,0:T(8,128)}, f32[4,192,192]{2,1,0:T(8,128)}, u32[]{:S(2)}, u32[]{:S(2)}) collective-permute-start(f32[4,192,192]{2,1,0:T(8,128)} %constant_dynamic-slice_fusion.3), channel_id=1, source_target_pairs={{0,8},{8,0},{16,24},{24,16},{1,9},{9,1},{17,25},{25,17},{2,10},{10... | collective-permute-start | bytes 1769480 | tf_op jit(solution)/shard_map/ppermute | solution.py:29
  57.6 3.0 %copy-start.2 = (f32[4,192,192]{2,1,0:T(8,128)}, f32[4,192,192]{2,1,0:T(8,128)S(1)}, u32[]{:S(2)}) copy-start(f32[4,192,192]{2,1,0:T(8,128)S(1)} %dynamic-slice_add_fusion) | copy-start | bytes 1769476
  57.7 9.9 %collective-permute-start.7 = (f32[2,192,192]{2,1,0:T(8,128)S(1)}, f32[2,192,192]{2,1,0:T(8,128)S(1)}, u32[]{:S(2)}, u32[]{:S(2)}) collective-permute-start(f32[2,192,192]{2,1,0:T(8,128)S(1)} %constant_dynamic-slice_fusion), channel_id=1, source_target_pairs={{0,8},{8,0},{16,24},{24,16},{1,9},{9,1},{17,25},{25,17},{2,10},{10... | collective-permute-start | bytes 884744 | tf_op jit(solution)/shard_map/ppermute | solution.py:29
  60.7 9.4 %collective-permute-start.3 = (f32[2,192,192]{2,1,0:T(8,128)S(1)}, f32[2,192,192]{2,1,0:T(8,128)S(1)}, u32[]{:S(2)}, u32[]{:S(2)}) collective-permute-start(f32[2,192,192]{2,1,0:T(8,128)S(1)} %constant_dynamic-slice_fusion.2), channel_id=1, source_target_pairs={{0,16},{8,24},{16,0},{24,8},{1,17},{9,25},{17,1},{25,9},{2,18},{10... | collective-permute-start | bytes 884744 | tf_op jit(solution)/shard_map/ppermute | solution.py:29
  68.7 10.5 %collective-permute-start.8 = (f32[2,192,192]{2,1,0:T(8,128)S(1)}, f32[2,192,192]{2,1,0:T(8,128)S(1)}, u32[]{:S(2)}, u32[]{:S(2)}) collective-permute-start(f32[2,192,192]{2,1,0:T(8,128)S(1)} %get-tuple-element.5), channel_id=1, source_target_pairs={{0,8},{8,0},{16,24},{24,16},{1,9},{9,1},{17,25},{25,17},{2,10},{10... | collective-permute-start | bytes 884744 | tf_op jit(solution)/shard_map/ppermute | solution.py:32
  70.2 11.3 %collective-permute-start.4 = (f32[2,192,192]{2,1,0:T(8,128)S(1)}, f32[2,192,192]{2,1,0:T(8,128)S(1)}, u32[]{:S(2)}, u32[]{:S(2)}) collective-permute-start(f32[2,192,192]{2,1,0:T(8,128)S(1)} %get-tuple-element.3), channel_id=1, source_target_pairs={{0,16},{8,24},{16,0},{24,8},{1,17},{9,25},{17,1},{25,9},{2,18},{10... | collective-permute-start | bytes 884744 | tf_op jit(solution)/shard_map/ppermute | solution.py:32
  79.3 11.9 %collective-permute-start.9 = (f32[4,192,192]{2,1,0:T(8,128)S(1)}, f32[4,192,192]{2,1,0:T(8,128)S(1)}, u32[]{:S(2)}, u32[]{:S(2)}) collective-permute-start(f32[4,192,192]{2,1,0:T(8,128)S(1)} %constant_dynamic-update-slice_fusion.2), channel_id=1, source_target_pairs={{0,16},{8,24},{16,0},{24,8},{1,17},{9,25},{17,1},{25,9},{2,18},{10... | collective-permute-start | bytes 1769480 | tf_op jit(solution)/shard_map/ppermute | solution.py:32
  81.5 10.9 %collective-permute-start.5 = (f32[4,192,192]{2,1,0:T(8,128)S(1)}, f32[4,192,192]{2,1,0:T(8,128)S(1)}, u32[]{:S(2)}, u32[]{:S(2)}) collective-permute-start(f32[4,192,192]{2,1,0:T(8,128)S(1)} %constant_dynamic-update-slice_fusion.6), channel_id=1, source_target_pairs={{0,8},{8,0},{16,24},{24,16},{1,9},{9,1},{17,25},{25,17},{2,10},{10... | collective-permute-start | bytes 1769480 | tf_op jit(solution)/shard_map/ppermute | solution.py:32
  83.1 9.3 %copy-start.5 = (f32[16,192]{1,0:T(8,128)S(1)}, f32[16,192]{1,0:T(8,128)}, u32[]{:S(2)}) copy-start(f32[16,192]{1,0:T(8,128)} %param.12) | copy-start | bytes 36868
  92.5 21.1 %copy-start.7 = (s32[16,2]{0,1:T(2,128)S(1)}, s32[16,2]{0,1:T(2,128)}, u32[]{:S(2)}) copy-start(s32[16,2]{0,1:T(2,128)} %param.14) | copy-start | bytes 388
  92.5 21.8 %copy-start.6 = (f32[16,2]{0,1:T(2,128)S(1)}, f32[16,2]{0,1:T(2,128)}, u32[]{:S(2)}) copy-start(f32[16,2]{0,1:T(2,128)} %param.15) | copy-start | bytes 388
  94.6 52.6 %copy-start = (f32[16,192,192]{2,1,0:T(8,128)}, f32[16,192,192]{2,1,0:T(8,128)S(1)}, u32[]{:S(2)}) copy-start(f32[16,192,192]{2,1,0:T(8,128)S(1)} %get-tuple-element.7.refs_1_.refs_7_) | copy-start | bytes 7077892
  94.6 51.5 %collective-permute-start.11 = (f32[16,192,192]{2,1,0:T(8,128)S(1)}, f32[16,192,192]{2,1,0:T(8,128)}, u32[]{:S(2)}, u32[]{:S(2)}) collective-permute-start(f32[16,192,192]{2,1,0:T(8,128)S(1)} %get-tuple-element.7.refs_1_.refs_7_), channel_id=1, source_target_pairs={{1,0},{2,1},{3,2},{4,3},{5,4},{6,5},{7,6},{9,8},{10,9},{11,10},{12... | collective-permute-start | bytes 7077896 | tf_op jit(solution)/shard_map/ppermute | solution.py:19
  96.5 50.6 %collective-permute-start.10 = (f32[16,192,192]{2,1,0:T(8,128)S(1)}, f32[16,192,192]{2,1,0:T(8,128)}, u32[]{:S(2)}, u32[]{:S(2)}) collective-permute-start(f32[16,192,192]{2,1,0:T(8,128)S(1)} %get-tuple-element.7.refs_1_.refs_7_), channel_id=1, source_target_pairs={{0,1},{1,2},{2,3},{3,4},{4,5},{5,6},{6,7},{8,9},{9,10},{10,11},{11... | collective-permute-start | bytes 7077896 | tf_op jit(solution)/shard_map/ppermute | solution.py:18
  160.3 16.9 %copy-start.1 = (f32[8,192,192]{2,1,0:T(8,128)S(1)}, f32[8,192,192]{2,1,0:T(8,128)}, u32[]{:S(2)}) copy-start(f32[8,192,192]{2,1,0:T(8,128)} %shard_map.96) | copy-start | bytes 3538948
  160.3 27.4 %collective-permute-start.14 = (f32[8,192,192]{2,1,0:T(8,128)}, f32[8,192,192]{2,1,0:T(8,128)S(1)}, u32[]{:S(2)}, u32[]{:S(2)}) collective-permute-start(f32[8,192,192]{2,1,0:T(8,128)} %shard_map.96), channel_id=1, source_target_pairs={{1,0},{2,1},{3,2},{4,3},{5,4},{6,5},{7,6},{9,8},{10,9},{11,10},{12... | collective-permute-start | bytes 3538952 | tf_op jit(solution)/shard_map/ppermute | solution.py:19
  175.3 24.7 %collective-permute-start.15 = (f32[8,192,192]{2,1,0:T(8,128)}, f32[8,192,192]{2,1,0:T(8,128)S(1)}, u32[]{:S(2)}, u32[]{:S(2)}) collective-permute-start(f32[8,192,192]{2,1,0:T(8,128)} %shard_map.97), channel_id=1, source_target_pairs={{1,0},{2,1},{3,2},{4,3},{5,4},{6,5},{7,6},{9,8},{10,9},{11,10},{12... | collective-permute-start | bytes 3538952 | tf_op jit(solution)/shard_map/ppermute | solution.py:19
  177.2 24.8 %collective-permute-start.12 = (f32[8,192,192]{2,1,0:T(8,128)S(1)}, f32[8,192,192]{2,1,0:T(8,128)S(1)}, u32[]{:S(2)}, u32[]{:S(2)}) collective-permute-start(f32[8,192,192]{2,1,0:T(8,128)S(1)} %copy-done.1), channel_id=1, source_target_pairs={{0,1},{1,2},{2,3},{3,4},{4,5},{5,6},{6,7},{8,9},{9,10},{10,11},{11... | collective-permute-start | bytes 3538952 | tf_op jit(solution)/shard_map/ppermute | solution.py:18
  181.8 34.3 %collective-permute-start.13 = (f32[8,192,192]{2,1,0:T(8,128)}, f32[8,192,192]{2,1,0:T(8,128)S(1)}, u32[]{:S(2)}, u32[]{:S(2)}) collective-permute-start(f32[8,192,192]{2,1,0:T(8,128)} %shard_map.97), channel_id=1, source_target_pairs={{0,1},{1,2},{2,3},{3,4},{4,5},{5,6},{6,7},{8,9},{9,10},{10,11},{11... | collective-permute-start | bytes 3538952 | tf_op jit(solution)/shard_map/ppermute | solution.py:18

commit v6 on v4

--- a/solution.py
+++ b/solution.py
@@ -60,13 +60,35 @@
     ).astype(jnp.int32)
 
 
-def exchange_kernel(lead_ref, trail_ref, size_ref, t_left, t_own, t_right, coef_ref, out_ref, *, occ):
-    p = pl.program_id(0)
-    size = size_ref[p]
-    source = trail_ref[p] // occ
-    slot = trail_ref[p] % occ
-    x_trail = jnp.where(source == 0, t_left[slot], jnp.where(source == 1, t_own[slot], t_right[slot]))
-    x_lead = t_own[lead_ref[p]]
+def fetch_block(sources, width, local, dst, sem):
+    source = local // width
+    block = local % width
+    conditions = (source == 0, (source != 0) & (source != 2), source == 2)
+    for src, condition in zip(sources, conditions):
+
+        @pl.when(condition)
+        def _():
+            pltpu.make_async_copy(src.at[block], dst, sem).start()
+
+
+def exchange_kernel(
+    lead_ref, trail_ref, size_ref, x_lead, t_left, t_own, t_right, coef_ref, out_ref, xbuf, sems, *, occ
+):
+    i = pl.program_id(0)
+    steps = pl.num_programs(0)
+    sources = (t_left, t_own, t_right)
+
+    @pl.when(i == 0)
+    def _():
+        fetch_block(sources, occ, trail_ref[0], xbuf.at[0], sems.at[0])
+
+    @pl.when(i + 1 < steps)
+    def _():
+        fetch_block(sources, occ, trail_ref[i + 1], xbuf.at[(i + 1) % 2], sems.at[(i + 1) % 2])
+
+    slot = i % 2
+    pltpu.make_async_copy(t_own.at[0], xbuf.at[slot], sems.at[slot]).wait()
+    size = size_ref[i]
     transposed = (((1,), (1,)), ((), ()))
     out_ref[0] = jnp.zeros((NPNO, NPNO), jnp.float32)
     for m in CLASS_SIZES:
@@ -75,8 +97,8 @@
         def _():
             first = coef_ref[0, 0, :m, :]
             second = coef_ref[0, 1, :m, :]
-            left_t = lax.dot_general(first, x_lead, transposed, preferred_element_type=jnp.float32)
-            right = lax.dot_general(x_trail, second, transposed, preferred_element_type=jnp.float32)
+            left_t = lax.dot_general(first, x_lead[0], transposed, preferred_element_type=jnp.float32)
+            right = lax.dot_general(xbuf[slot], second, transposed, preferred_element_type=jnp.float32)
             out_ref[0, :m, :m] = jnp.dot(
                 left_t.astype(jnp.bfloat16), right.astype(jnp.bfloat16), preferred_element_type=jnp.float32
             )
@@ -85,17 +107,22 @@
 def partial_exchange(lead, trail, sizes, sources, coef_t):
     pairs = coef_t.shape[0]
     occ, nfit, npao = sources[1].shape
-    whole = pl.BlockSpec((occ, nfit, npao), lambda i, a, b, s: (0, 0, 0))
+    hbm = pl.BlockSpec(memory_space=pl.ANY)
     grid_spec = pltpu.PrefetchScalarGridSpec(
         num_scalar_prefetch=3,
         grid=(pairs,),
         in_specs=[
-            whole,
-            whole,
-            whole,
+            pl.BlockSpec((1, nfit, npao), lambda i, a, b, s: (a[i], 0, 0)),
+            hbm,
+            hbm,
+            hbm,
             pl.BlockSpec((1, 2, NPNO, npao), lambda i, a, b, s: (i, 0, 0, 0)),
         ],
         out_specs=pl.BlockSpec((1, NPNO, NPNO), lambda i, a, b, s: (i, 0, 0)),
+        scratch_shapes=[
+            pltpu.VMEM((2, nfit, npao), sources[1].dtype),
+            pltpu.SemaphoreType.DMA((2,)),
+        ],
     )
     flops = pairs * (2 * 2 * nfit * npao * NPNO + 2 * nfit * NPNO * NPNO)
     return pl.pallas_call(
@@ -107,7 +134,7 @@
             bytes_accessed=pairs * (2 * nfit * npao * 2 + 2 * npao * NPNO * 2 + NPNO * NPNO * 4),
             transcendentals=0,
         ),
-    )(lead, trail, sizes, *sources, coef_t)
+    )(lead, trail, sizes, sources[1], *sources, coef_t)
 
 
 def split_bf16(value):
@@ -121,17 +148,30 @@
 
 
 def coupling_kernel(nb_ref, size_ref, fock_ref, *refs, final, width):
-    t_refs = refs[:3]
-    margin_ref, ex_ref, col_ref, row_ref, own_ref, out_ref, acc_ref = refs[3:]
-    p = pl.program_id(0)
-    size = size_ref[p]
-    transposed = (((1,), (1,)), ((), ()))
+    sources = refs[:3]
+    margin_ref, ex_ref, col_ref, row_ref, own_ref, out_ref, tbuf, sems, acc_ref = refs[3:]
+    i = pl.program_id(0)
+    steps = pl.num_programs(0)
+
+    def fetch(step, slot):
+        for n in range(2):
+            fetch_block(sources, width, nb_ref[2 * step + n], tbuf.at[slot, n], sems.at[slot, n])
+
+    @pl.when(i == 0)
+    def _():
+        fetch(0, 0)
+
+    @pl.when(i + 1 < steps)
+    def _():
+        fetch(i + 1, (i + 1) % 2)
+
+    slot = i % 2
     splits = []
     for n in range(2):
-        source = nb_ref[2 * p + n] // width
-        slot = nb_ref[2 * p + n] % width
-        left, own, right = (t_refs[k][slot] for k in range(3))
-        splits.append(split_bf16(jnp.where(source == 0, left, jnp.where(source == 1, own, right))))
+        pltpu.make_async_copy(sources[1].at[0], tbuf.at[slot, n], sems.at[slot, n]).wait()
+        splits.append(split_bf16(tbuf[slot, n]))
+    size = size_ref[i]
+    transposed = (((1,), (1,)), ((), ()))
     acc_ref[...] = jnp.zeros((NPNO, NPNO), jnp.float32)
     for m in CLASS_SIZES:
 
@@ -142,7 +182,7 @@
                 side = margin_ref[0, n, :m, :]
                 t_hi, t_lo = splits[n]
                 inner = mm(side, t_hi) + mm(side, t_lo)
-                w_hi, w_lo = split_bf16(fock_ref[2 * p + n] * inner)
+                w_hi, w_lo = split_bf16(fock_ref[2 * i + n] * inner)
                 outer = mm(w_hi, side, transposed) + mm(w_lo, side, transposed)
                 total = outer if total is None else total + outer
             acc_ref[:m, :m] = total
@@ -157,17 +197,16 @@
 
 
 def coupling_step(nb, sizes, fock, sources, margin, exchange, energy, own, final):
-    column = energy.reshape(energy.shape[0], NPNO, 1)
-    row = energy.reshape(energy.shape[0], 1, NPNO)
     pairs = own.shape[0]
+    column = energy.reshape(pairs, NPNO, 1)
+    row = energy.reshape(pairs, 1, NPNO)
     block = (1, NPNO, NPNO)
-
-    whole = pl.BlockSpec((pairs, NPNO, NPNO), lambda i, q, s, f: (0, 0, 0))
+    hbm = pl.BlockSpec(memory_space=pl.ANY)
     own_spec = pl.BlockSpec(block, lambda i, q, s, f: (i, 0, 0))
     grid_spec = pltpu.PrefetchScalarGridSpec(
         num_scalar_prefetch=3,
         grid=(pairs,),
-        in_specs=[whole] * 3
+        in_specs=[hbm] * 3
         + [
             pl.BlockSpec((1, 2, NPNO, NPNO), lambda i, q, s, f: (i, 0, 0, 0)),
             own_spec,
@@ -176,7 +215,11 @@
             own_spec,
         ],
         out_specs=own_spec,
-        scratch_shapes=[pltpu.VMEM((NPNO, NPNO), jnp.float32)],
+        scratch_shapes=[
+            pltpu.VMEM((2, 2, NPNO, NPNO), jnp.float32),
+            pltpu.SemaphoreType.DMA((2, 2)),
+            pltpu.VMEM((NPNO, NPNO), jnp.float32),
+        ],
     )
     flops = pairs * 2 * 4 * 2 * NPNO * NPNO * NPNO
     return pl.pallas_call(

time: 231 us -> 229 us (level)
    pallas_call x2, Pallas kernels: 40.3 us -> 37.2 us  [coupling_step(): pl.pallas_call(functools.partial(coupling_kernel, final=final, width=pair...]
  transfers between devices with their start and end apart: 14 -> 14, of which waited for: 13 -> 12; matrix products, arithmetic and copies ran while one was open for 5% -> 5% of each run, Pallas kernels for 0% -> 0%
where the time goes in v6:
time: 229 us; the launch traced here: 227 us
  waiting for transfers between devices  111 us (48%)
  Pallas kernels  53.8 us (23%)
  starting transfers between devices  43.1 us (19%)
  local copies, waits for them, and re-layouts  10 us (4%)
  other arithmetic  8.12 us (4%)
    ppermute x3, waiting for transfers between devices, halo_sources(): from_right = lax.ppermute(cells, axis, [(i + 1, i) for i in range(ends)])  66.8 us
    pallas_call x2, Pallas kernels, coupling_step(): pl.pallas_call(functools.partial(coupling_kernel, final=final, width=pair...  37.2 us
    ppermute x3, starting transfers between devices, halo_sources(): from_left = lax.ppermute(cells, axis, [(i, i + 1) for i in range(ends)])  25 us
    ppermute x4, waiting for transfers between devices, halving_stream(): lax.ppermute(send, 'aux', [(i, i ^ bit) for i in range(count)])  17.6 us
    pallas_call x1, Pallas kernels, partial_exchange(): pl.pallas_call(functools.partial(exchange_kernel, occ=occ), grid_spec=gri...  16.6 us
    ppermute x4, waiting for transfers between devices, halving_stream(): other = lax.ppermute(piece, 'aux', [(i, i ^ bit) for i in range(count)])  16.4 us
    ppermute x3, waiting for transfers between devices, halo_sources(): from_left = lax.ppermute(cells, axis, [(i, i + 1) for i in range(ends)])  9.93 us
    ppermute x4, starting transfers between devices, halving_stream(): other = lax.ppermute(piece, 'aux', [(i, i ^ bit) for i in range(count)])  6.66 us
  transfers between devices with their start and end apart: 14, of which 12 were waited for; matrix products, arithmetic and copies ran while one was open for 5% of the time, Pallas kernels for 0%

profile of v6, /device:TPU:1, one launch (start us, length us, event | category | flops | bytes accessed | tf_op | source)
XLA Modules:
  0.0 226.8 jit_solution(13619695328527871541)
XLA Ops:
  0.6 4.6 %collective-permute-start = (bf16[4,512,256]{2,1,0:T(8,128)(2,1)}, bf16[4,512,256]{2,1,0:T(8,128)(2,1)S(1)}, u32[]{:S(2)}, u32[]{:S(2)}) collective-permute-start(bf16[4,512,256]{2,1,0:T(8,128)(2,1)} %t_own.1), channel_id=1, source_target_pairs={{0,1},{1,2},{2,3},{3,4},{4,5},{5,6},{6,7},{8,9},{9,10},{10,11},{11... | collective-permute-start | bytes 3145736 | tf_op jit(solution)/shard_map/ppermute | solution.py:18
  5.2 1.9 collective-permute-start.1
  7.2 1.2 compare_select_fusion.2.size_ref
  8.4 0.7 broadcast_subtract_fusion
  9.1 0.6 slice_bitcast_fusion
  9.7 7.6 %collective-permute-done.t_left = bf16[4,512,256]{2,1,0:T(8,128)(2,1)S(1)} collective-permute-done((bf16[4,512,256]{2,1,0:T(8,128)(2,1)}, bf16[4,512,256]{2,1,0:T(8,128)(2,1)S(1)}, u32[]{:S(2)}, u32[]{:S(2)}) %collective-permute-start) | collective-permute-done | bytes 1048608 | tf_op jit(solution)/shard_map/ppermute | solution.py:18
  17.3 4.3 %collective-permute-done.1.t_right = bf16[4,512,256]{2,1,0:T(8,128)(2,1)S(1)} collective-permute-done((bf16[4,512,256]{2,1,0:T(8,128)(2,1)}, bf16[4,512,256]{2,1,0:T(8,128)(2,1)S(1)}, u32[]{:S(2)}, u32[]{:S(2)}) %collective-permute-start.1) | collective-permute-done | bytes 1048608 | tf_op jit(solution)/shard_map/ppermute | solution.py:19
  21.6 1.0 copy-done.4
  22.6 16.6 %shard_map.95 = f32[16,192,192]{2,1,0:T(8,128)} custom-call(s32[16]{0:T(128)} %get-tuple-element.11.lead_ref, s32[16]{0:T(128)} %get-tuple-element.10.trail_ref, s32[16]{0:T(128)} %compare_select_fusion.2.size_ref, bf16[4,512,256]{2,1,0:T(8,128)(2,1)} %t_own.1, bf16[4,512,256]{2,1,0:T(8,128)(2,1)} %copy-done.3, bf16[4,512,256]{2,1,0:T(8,128)(2,1)} %t_own.1, ...), custom_call_target="tpu_custom_call" | custom-call | flops 2214592512 | bytes 13893632 | tf_op jit(solution)/shard_map/pallas_call | solution.py:128
  39.2 2.2 fusion
  41.4 0.9 constant_dynamic-slice_fusion.1
  42.3 1.2 collective-permute-start.6
  43.6 0.9 constant_dynamic-slice_fusion.3
  44.5 1.2 collective-permute-start.2
  45.7 10.9 %collective-permute-done.6 = f32[4,192,192]{2,1,0:T(8,128)} collective-permute-done((f32[4,192,192]{2,1,0:T(8,128)}, f32[4,192,192]{2,1,0:T(8,128)}, u32[]{:S(2)}, u32[]{:S(2)}) %collective-permute-start.6) | collective-permute-done | bytes 589856 | tf_op jit(solution)/shard_map/ppermute | solution.py:29
  56.6 1.2 dynamic-slice_add_fusion
  57.9 1.7 collective-permute-start.7
  59.6 0.3 collective-permute-done.2
  59.9 1.2 dynamic-slice_add_fusion.1
  61.2 1.6 collective-permute-start.3
  62.7 6.4 %collective-permute-done.7 = f32[2,192,192]{2,1,0:T(8,128)S(1)} collective-permute-done((f32[2,192,192]{2,1,0:T(8,128)S(1)}, f32[2,192,192]{2,1,0:T(8,128)S(1)}, u32[]{:S(2)}, u32[]{:S(2)}) %collective-permute-start.7) | collective-permute-done | bytes 294944 | tf_op jit(solution)/shard_map/ppermute | solution.py:29
  69.2 1.1 constant_dynamic-update-slice_fusion.3
  70.2 1.4 collective-permute-start.8
  71.8 1.3 collective-permute-start.4
  73.1 6.8 %collective-permute-done.8 = f32[2,192,192]{2,1,0:T(8,128)S(1)} collective-permute-done((f32[2,192,192]{2,1,0:T(8,128)S(1)}, f32[2,192,192]{2,1,0:T(8,128)S(1)}, u32[]{:S(2)}, u32[]{:S(2)}) %collective-permute-start.8) | collective-permute-done | bytes 294944 | tf_op jit(solution)/shard_map/ppermute | solution.py:32
  79.9 3.2 %collective-permute-start.9 = (f32[4,192,192]{2,1,0:T(8,128)S(1)}, f32[4,192,192]{2,1,0:T(8,128)S(1)}, u32[]{:S(2)}, u32[]{:S(2)}) collective-permute-start(f32[4,192,192]{2,1,0:T(8,128)S(1)} %constant_dynamic-update-slice_fusion.2), channel_id=1, source_target_pairs={{0,16},{8,24},{16,0},{24,8},{1,17},{9,25},{17,1},{25,9},{2,18},{10... | collective-permute-start | bytes 1769480 | tf_op jit(solution)/shard_map/ppermute | solution.py:32
  83.1 0.8 collective-permute-start.5
  83.9 0.1 broadcast.30.clone
  84.1 0.1 broadcast.30.clone.1
  84.3 9.4 %collective-permute-done.9 = f32[4,192,192]{2,1,0:T(8,128)S(1)} collective-permute-done((f32[4,192,192]{2,1,0:T(8,128)S(1)}, f32[4,192,192]{2,1,0:T(8,128)S(1)}, u32[]{:S(2)}, u32[]{:S(2)}) %collective-permute-start.9) | collective-permute-done | bytes 589856 | tf_op jit(solution)/shard_map/ppermute | solution.py:32
  93.8 0.3 collective-permute-done.5
  94.1 2.0 pad_maximum_fusion
  96.1 1.9 collective-permute-start.11
  98.1 15.6 %collective-permute-start.10 = (f32[16,192,192]{2,1,0:T(8,128)S(1)}, f32[16,192,192]{2,1,0:T(8,128)}, u32[]{:S(2)}, u32[]{:S(2)}) collective-permute-start(f32[16,192,192]{2,1,0:T(8,128)S(1)} %get-tuple-element.7.refs_1_.refs_7_), channel_id=1, source_target_pairs={{0,1},{1,2},{2,3},{3,4},{4,5},{5,6},{6,7},{8,9},{9,10},{10,11},{11... | collective-permute-start | bytes 7077896 | tf_op jit(solution)/shard_map/ppermute | solution.py:18
  113.7 0.6 broadcast_in_dim.26.refs_6_
  114.3 0.1 copy.12
  114.4 0.7 reshape.18.nb_ref
  115.1 0.6 reshape.19.fock_ref
  115.8 1.7 copy.14.refs_5_
  117.5 29.3 %collective-permute-done.11.refs_2_ = f32[16,192,192]{2,1,0:T(8,128)} collective-permute-done((f32[16,192,192]{2,1,0:T(8,128)S(1)}, f32[16,192,192]{2,1,0:T(8,128)}, u32[]{:S(2)}, u32[]{:S(2)}) %collective-permute-start.11) | collective-permute-done | bytes 2359328 | tf_op jit(solution)/shard_map/ppermute | solution.py:19
  146.8 1.1 collective-permute-done.10.refs_0_
  147.9 18.7 %shard_map.96.refs_1_.refs_7_ = f32[16,192,192]{2,1,0:T(8,128)} custom-call(s32[32]{0:T(128)} %reshape.18.nb_ref, s32[16]{0:T(128)} %compare_select_fusion.2.size_ref, f32[32]{0:T(128)} %reshape.19.fock_ref, f32[16,192,192]{2,1,0:T(8,128)} %collective-permute-done.10.refs_0_, f32[16,192,192]{2,1,0:T(8,128)} %copy-done, ...), custom_call_target="tpu_custom_call" | custom-call | flops 1811939328 | bytes 14155776 | tf_op jit(solution)/shard_map/pallas_call | solution.py:225
  166.5 1.9 collective-permute-start.13
  168.5 4.8 %collective-permute-start.12 = (f32[16,192,192]{2,1,0:T(8,128)}, f32[16,192,192]{2,1,0:T(8,128)}, u32[]{:S(2)}, u32[]{:S(2)}) collective-permute-start(f32[16,192,192]{2,1,0:T(8,128)} %shard_map.96.refs_1_.refs_7_), channel_id=1, source_target_pairs={{0,1},{1,2},{2,3},{3,4},{4,5},{5,6},{6,7},{8,9},{9,10},{10,11},{11... | collective-permute-start | bytes 7077896 | tf_op jit(solution)/shard_map/ppermute | solution.py:18
  173.3 33.2 %collective-permute-done.13.refs_2_ = f32[16,192,192]{2,1,0:T(8,128)S(1)} collective-permute-done((f32[16,192,192]{2,1,0:T(8,128)}, f32[16,192,192]{2,1,0:T(8,128)S(1)}, u32[]{:S(2)}, u32[]{:S(2)}) %collective-permute-start.13) | collective-permute-done | bytes 2359328 | tf_op jit(solution)/shard_map/ppermute | solution.py:19
  206.5 1.3 collective-permute-done.12.refs_0_
  207.8 0.4 copy-done.1
  208.2 18.5 %shard_map.97 = f32[16,192,192]{2,1,0:T(8,128)} custom-call(s32[32]{0:T(128)} %reshape.18.nb_ref, s32[16]{0:T(128)} %compare_select_fusion.2.size_ref, f32[32]{0:T(128)} %reshape.19.fock_ref, f32[16,192,192]{2,1,0:T(8,128)} %collective-permute-done.12.refs_0_, f32[16,192,192]{2,1,0:T(8,128)} %shard_map.96.refs_1_.refs_7_, f32[16,192,192]{2,1,0:T(8,128)} %copy-done.1, ...), custom_call_target="tpu_custom_call" | custom-call | flops 1811939328 | bytes 14155776 | tf_op jit(solution)/shard_map/pallas_call | solution.py:225
  (29 shorter events, 0.7 us)
Async XLA Ops:
  0.6 16.6 %collective-permute-start = (bf16[4,512,256]{2,1,0:T(8,128)(2,1)}, bf16[4,512,256]{2,1,0:T(8,128)(2,1)S(1)}, u32[]{:S(2)}, u32[]{:S(2)}) collective-permute-start(bf16[4,512,256]{2,1,0:T(8,128)(2,1)} %t_own.1), channel_id=1, source_target_pairs={{0,1},{1,2},{2,3},{3,4},{4,5},{5,6},{6,7},{8,9},{9,10},{10,11},{11... | collective-permute-start | bytes 3145736 | tf_op jit(solution)/shard_map/ppermute | solution.py:18
  5.2 16.3 %collective-permute-start.1 = (bf16[4,512,256]{2,1,0:T(8,128)(2,1)}, bf16[4,512,256]{2,1,0:T(8,128)(2,1)S(1)}, u32[]{:S(2)}, u32[]{:S(2)}) collective-permute-start(bf16[4,512,256]{2,1,0:T(8,128)(2,1)} %t_own.1), channel_id=1, source_target_pairs={{1,0},{2,1},{3,2},{4,3},{5,4},{6,5},{7,6},{9,8},{10,9},{11,10},{12... | collective-permute-start | bytes 3145736 | tf_op jit(solution)/shard_map/ppermute | solution.py:19
  17.3 4.3 %copy-start.3 = (bf16[4,512,256]{2,1,0:T(8,128)(2,1)}, bf16[4,512,256]{2,1,0:T(8,128)(2,1)S(1)}, u32[]{:S(2)}) copy-start(bf16[4,512,256]{2,1,0:T(8,128)(2,1)S(1)} %collective-permute-done.t_left) | copy-start | bytes 3145732
  21.6 1.0 copy-start.4
  42.3 14.2 %collective-permute-start.6 = (f32[4,192,192]{2,1,0:T(8,128)}, f32[4,192,192]{2,1,0:T(8,128)}, u32[]{:S(2)}, u32[]{:S(2)}) collective-permute-start(f32[4,192,192]{2,1,0:T(8,128)} %constant_dynamic-slice_fusion.1), channel_id=1, source_target_pairs={{0,16},{8,24},{16,0},{24,8},{1,17},{9,25},{17,1},{25,9},{2,18},{10... | collective-permute-start | bytes 1769480 | tf_op jit(solution)/shard_map/ppermute | solution.py:29
  44.5 15.4 %collective-permute-start.2 = (f32[4,192,192]{2,1,0:T(8,128)}, f32[4,192,192]{2,1,0:T(8,128)}, u32[]{:S(2)}, u32[]{:S(2)}) collective-permute-start(f32[4,192,192]{2,1,0:T(8,128)} %constant_dynamic-slice_fusion.3), channel_id=1, source_target_pairs={{0,8},{8,0},{16,24},{24,16},{1,9},{9,1},{17,25},{25,17},{2,10},{10... | collective-permute-start | bytes 1769480 | tf_op jit(solution)/shard_map/ppermute | solution.py:29
  57.8 3.3 %copy-start.2 = (f32[4,192,192]{2,1,0:T(8,128)}, f32[4,192,192]{2,1,0:T(8,128)S(1)}, u32[]{:S(2)}) copy-start(f32[4,192,192]{2,1,0:T(8,128)S(1)} %dynamic-slice_add_fusion) | copy-start | bytes 1769476
  57.9 11.2 %collective-permute-start.7 = (f32[2,192,192]{2,1,0:T(8,128)S(1)}, f32[2,192,192]{2,1,0:T(8,128)S(1)}, u32[]{:S(2)}, u32[]{:S(2)}) collective-permute-start(f32[2,192,192]{2,1,0:T(8,128)S(1)} %constant_dynamic-slice_fusion), channel_id=1, source_target_pairs={{0,8},{8,0},{16,24},{24,16},{1,9},{9,1},{17,25},{25,17},{2,10},{10... | collective-permute-start | bytes 884744 | tf_op jit(solution)/shard_map/ppermute | solution.py:29
  61.2 10.5 %collective-permute-start.3 = (f32[2,192,192]{2,1,0:T(8,128)S(1)}, f32[2,192,192]{2,1,0:T(8,128)S(1)}, u32[]{:S(2)}, u32[]{:S(2)}) collective-permute-start(f32[2,192,192]{2,1,0:T(8,128)S(1)} %constant_dynamic-slice_fusion.2), channel_id=1, source_target_pairs={{0,16},{8,24},{16,0},{24,8},{1,17},{9,25},{17,1},{25,9},{2,18},{10... | collective-permute-start | bytes 884744 | tf_op jit(solution)/shard_map/ppermute | solution.py:29
  70.2 9.6 %collective-permute-start.8 = (f32[2,192,192]{2,1,0:T(8,128)S(1)}, f32[2,192,192]{2,1,0:T(8,128)S(1)}, u32[]{:S(2)}, u32[]{:S(2)}) collective-permute-start(f32[2,192,192]{2,1,0:T(8,128)S(1)} %get-tuple-element.5), channel_id=1, source_target_pairs={{0,8},{8,0},{16,24},{24,16},{1,9},{9,1},{17,25},{25,17},{2,10},{10... | collective-permute-start | bytes 884744 | tf_op jit(solution)/shard_map/ppermute | solution.py:32
  71.8 11.3 %collective-permute-start.4 = (f32[2,192,192]{2,1,0:T(8,128)S(1)}, f32[2,192,192]{2,1,0:T(8,128)S(1)}, u32[]{:S(2)}, u32[]{:S(2)}) collective-permute-start(f32[2,192,192]{2,1,0:T(8,128)S(1)} %get-tuple-element.3), channel_id=1, source_target_pairs={{0,16},{8,24},{16,0},{24,8},{1,17},{9,25},{17,1},{25,9},{2,18},{10... | collective-permute-start | bytes 884744 | tf_op jit(solution)/shard_map/ppermute | solution.py:32
  79.9 13.8 %collective-permute-start.9 = (f32[4,192,192]{2,1,0:T(8,128)S(1)}, f32[4,192,192]{2,1,0:T(8,128)S(1)}, u32[]{:S(2)}, u32[]{:S(2)}) collective-permute-start(f32[4,192,192]{2,1,0:T(8,128)S(1)} %constant_dynamic-update-slice_fusion.2), channel_id=1, source_target_pairs={{0,16},{8,24},{16,0},{24,8},{1,17},{9,25},{17,1},{25,9},{2,18},{10... | collective-permute-start | bytes 1769480 | tf_op jit(solution)/shard_map/ppermute | solution.py:32
  83.1 10.9 %collective-permute-start.5 = (f32[4,192,192]{2,1,0:T(8,128)S(1)}, f32[4,192,192]{2,1,0:T(8,128)S(1)}, u32[]{:S(2)}, u32[]{:S(2)}) collective-permute-start(f32[4,192,192]{2,1,0:T(8,128)S(1)} %constant_dynamic-update-slice_fusion.6), channel_id=1, source_target_pairs={{0,8},{8,0},{16,24},{24,16},{1,9},{9,1},{17,25},{25,17},{2,10},{10... | collective-permute-start | bytes 1769480 | tf_op jit(solution)/shard_map/ppermute | solution.py:32
  84.3 9.8 %copy-start.5 = (f32[16,192]{1,0:T(8,128)S(1)}, f32[16,192]{1,0:T(8,128)}, u32[]{:S(2)}) copy-start(f32[16,192]{1,0:T(8,128)} %param.12) | copy-start | bytes 36868
  94.1 20.2 %copy-start.7 = (s32[16,2]{0,1:T(2,128)S(1)}, s32[16,2]{0,1:T(2,128)}, u32[]{:S(2)}) copy-start(s32[16,2]{0,1:T(2,128)} %param.14) | copy-start | bytes 388
  94.1 21.0 %copy-start.6 = (f32[16,2]{0,1:T(2,128)S(1)}, f32[16,2]{0,1:T(2,128)}, u32[]{:S(2)}) copy-start(f32[16,2]{0,1:T(2,128)} %param.15) | copy-start | bytes 388
  96.1 51.7 %copy-start = (f32[16,192,192]{2,1,0:T(8,128)}, f32[16,192,192]{2,1,0:T(8,128)S(1)}, u32[]{:S(2)}) copy-start(f32[16,192,192]{2,1,0:T(8,128)S(1)} %get-tuple-element.7.refs_1_.refs_7_) | copy-start | bytes 7077892
  96.1 50.6 %collective-permute-start.11 = (f32[16,192,192]{2,1,0:T(8,128)S(1)}, f32[16,192,192]{2,1,0:T(8,128)}, u32[]{:S(2)}, u32[]{:S(2)}) collective-permute-start(f32[16,192,192]{2,1,0:T(8,128)S(1)} %get-tuple-element.7.refs_1_.refs_7_), channel_id=1, source_target_pairs={{1,0},{2,1},{3,2},{4,3},{5,4},{6,5},{7,6},{9,8},{10,9},{11,10},{12... | collective-permute-start | bytes 7077896 | tf_op jit(solution)/shard_map/ppermute | solution.py:19
  98.1 49.8 %collective-permute-start.10 = (f32[16,192,192]{2,1,0:T(8,128)S(1)}, f32[16,192,192]{2,1,0:T(8,128)}, u32[]{:S(2)}, u32[]{:S(2)}) collective-permute-start(f32[16,192,192]{2,1,0:T(8,128)S(1)} %get-tuple-element.7.refs_1_.refs_7_), channel_id=1, source_target_pairs={{0,1},{1,2},{2,3},{3,4},{4,5},{5,6},{6,7},{8,9},{9,10},{10,11},{11... | collective-permute-start | bytes 7077896 | tf_op jit(solution)/shard_map/ppermute | solution.py:18
  166.5 39.9 %collective-permute-start.13 = (f32[16,192,192]{2,1,0:T(8,128)}, f32[16,192,192]{2,1,0:T(8,128)S(1)}, u32[]{:S(2)}, u32[]{:S(2)}) collective-permute-start(f32[16,192,192]{2,1,0:T(8,128)} %shard_map.96.refs_1_.refs_7_), channel_id=1, source_target_pairs={{1,0},{2,1},{3,2},{4,3},{5,4},{6,5},{7,6},{9,8},{10,9},{11,10},{12... | collective-permute-start | bytes 7077896 | tf_op jit(solution)/shard_map/ppermute | solution.py:19
  168.5 39.3 %collective-permute-start.12 = (f32[16,192,192]{2,1,0:T(8,128)}, f32[16,192,192]{2,1,0:T(8,128)}, u32[]{:S(2)}, u32[]{:S(2)}) collective-permute-start(f32[16,192,192]{2,1,0:T(8,128)} %shard_map.96.refs_1_.refs_7_), channel_id=1, source_target_pairs={{0,1},{1,2},{2,3},{3,4},{4,5},{5,6},{6,7},{8,9},{9,10},{10,11},{11... | collective-permute-start | bytes 7077896 | tf_op jit(solution)/shard_map/ppermute | solution.py:18
  206.5 1.7 copy-start.1

commit v7 on v6

--- a/solution.py
+++ b/solution.py
@@ -147,83 +147,86 @@
     return lax.dot_general(lhs, rhs, dims, preferred_element_type=jnp.float32)
 
 
-def coupling_kernel(nb_ref, size_ref, fock_ref, *refs, final, width):
+def coupling_kernel(nb_ref, size_ref, fock_ref, *refs, final, width, group):
     sources = refs[:3]
     margin_ref, ex_ref, col_ref, row_ref, own_ref, out_ref, tbuf, sems, acc_ref = refs[3:]
     i = pl.program_id(0)
     steps = pl.num_programs(0)
 
     def fetch(step, slot):
+        for k in range(2 * group):
+            fetch_block(sources, width, nb_ref[2 * group * step + k], tbuf.at[slot, k], sems.at[slot, k])
+
+    @pl.when(i == 0)
+    def _():
+        fetch(0, 0)
+
+    @pl.when(i + 1 < steps)
+    def _():
+        fetch(i + 1, (i + 1) % 2)
+
+    slot = i % 2
+    transposed = (((1,), (1,)), ((), ()))
+    for g in range(group):
+        p = i * group + g
+        splits = []
         for n in range(2):
-            fetch_block(sources, width, nb_ref[2 * step + n], tbuf.at[slot, n], sems.at[slot, n])
-
-    @pl.when(i == 0)
-    def _():
-        fetch(0, 0)
-
-    @pl.when(i + 1 < steps)
-    def _():
-        fetch(i + 1, (i + 1) % 2)
-
-    slot = i % 2
-    splits = []
-    for n in range(2):
-        pltpu.make_async_copy(sources[1].at[0], tbuf.at[slot, n], sems.at[slot, n]).wait()
-        splits.append(split_bf16(tbuf[slot, n]))
-    size = size_ref[i]
-    transposed = (((1,), (1,)), ((), ()))
-    acc_ref[...] = jnp.zeros((NPNO, NPNO), jnp.float32)
-    for m in CLASS_SIZES:
-
-        @pl.when(size == m)
-        def _():
-            total = None
-            for n in range(2):
-                side = margin_ref[0, n, :m, :]
-                t_hi, t_lo = splits[n]
-                inner = mm(side, t_hi) + mm(side, t_lo)
-                w_hi, w_lo = split_bf16(fock_ref[2 * i + n] * inner)
-                outer = mm(w_hi, side, transposed) + mm(w_lo, side, transposed)
-                total = outer if total is None else total + outer
-            acc_ref[:m, :m] = total
-
-    denominator = col_ref[0] + row_ref[0]
-    amplitudes = own_ref[0]
-    residual = ex_ref[0] + denominator * amplitudes - acc_ref[...]
-    if final:
-        out_ref[0] = residual
-    else:
-        out_ref[0] = amplitudes - residual / denominator
+            k = 2 * g + n
+            pltpu.make_async_copy(sources[1].at[0], tbuf.at[slot, k], sems.at[slot, k]).wait()
+            splits.append(split_bf16(tbuf[slot, k]))
+        size = size_ref[p]
+        acc_ref[...] = jnp.zeros((NPNO, NPNO), jnp.float32)
+        for m in CLASS_SIZES:
+
+            @pl.when(size == m)
+            def _():
+                total = None
+                for n in range(2):
+                    side = margin_ref[g, n, :m, :]
+                    t_hi, t_lo = splits[n]
+                    inner = mm(side, t_hi) + mm(side, t_lo)
+                    w_hi, w_lo = split_bf16(fock_ref[2 * p + n] * inner)
+                    outer = mm(w_hi, side, transposed) + mm(w_lo, side, transposed)
+                    total = outer if total is None else total + outer
+                acc_ref[:m, :m] = total
+
+        denominator = col_ref[g] + row_ref[g]
+        amplitudes = own_ref[g]
+        residual = ex_ref[g] + denominator * amplitudes - acc_ref[...]
+        if final:
+            out_ref[g] = residual
+        else:
+            out_ref[g] = amplitudes - residual / denominator
 
 
 def coupling_step(nb, sizes, fock, sources, margin, exchange, energy, own, final):
     pairs = own.shape[0]
+    group = next(g for g in (4, 2, 1) if pairs % g == 0)
     column = energy.reshape(pairs, NPNO, 1)
     row = energy.reshape(pairs, 1, NPNO)
-    block = (1, NPNO, NPNO)
     hbm = pl.BlockSpec(memory_space=pl.ANY)
-    own_spec = pl.BlockSpec(block, lambda i, q, s, f: (i, 0, 0))
+    own_spec = pl.BlockSpec((group, NPNO, NPNO), lambda i, q, s, f: (i, 0, 0))
     grid_spec = pltpu.PrefetchScalarGridSpec(
         num_scalar_prefetch=3,
-        grid=(pairs,),
+        grid=(pairs // group,),
         in_specs=[hbm] * 3
         + [
-            pl.BlockSpec((1, 2, NPNO, NPNO), lambda i, q, s, f: (i, 0, 0, 0)),
+            pl.BlockSpec((group, 2, NPNO, NPNO), lambda i, q, s, f: (i, 0, 0, 0)),
             own_spec,
-            pl.BlockSpec((1, NPNO, 1), lambda i, q, s, f: (i, 0, 0)),
-            pl.BlockSpec((1, 1, NPNO), lambda i, q, s, f: (i, 0, 0)),
+            pl.BlockSpec((group, NPNO, 1), lambda i, q, s, f: (i, 0, 0)),
+            pl.BlockSpec((group, 1, NPNO), lambda i, q, s, f: (i, 0, 0)),
             own_spec,
         ],
         out_specs=own_spec,
         scratch_shapes=[
-            pltpu.VMEM((2, 2, NPNO, NPNO), jnp.float32),
-            pltpu.SemaphoreType.DMA((2, 2)),
+            pltpu.VMEM((2, 2 * group, NPNO, NPNO), jnp.float32),
+            pltpu.SemaphoreType.DMA((2, 2 * group)),
             pltpu.VMEM((NPNO, NPNO), jnp.float32),
         ],
     )
     flops = pairs * 2 * 4 * 2 * NPNO * NPNO * NPNO
     return pl.pallas_call(
-        functools.partial(coupling_kernel, final=final, width=pairs),
+        functools.partial(coupling_kernel, final=final, width=pairs, group=group),
         grid_spec=grid_spec,
         out_shape=jax.ShapeDtypeStruct((pairs, NPNO, NPNO), jnp.float32),
         cost_estimate=pl.CostEstimate(

time: 229 us -> 220 us (0.961)
  Pallas kernels: 53.8 us -> 46.1 us
    pallas_call x2, Pallas kernels: 37.2 us -> 29.1 us  [coupling_step(): pl.pallas_call(functools.partial(coupling_kernel, final=final, width=pair...]
where the time goes in v7:
time: 220 us; the launch traced here: 218 us
  waiting for transfers between devices  111 us (50%)
  Pallas kernels  46.1 us (21%)
  starting transfers between devices  42.2 us (19%)
  local copies, waits for them, and re-layouts  10 us (5%)
  other arithmetic  8.12 us (4%)
    ppermute x3, waiting for transfers between devices, halo_sources(): from_right = lax.ppermute(cells, axis, [(i + 1, i) for i in range(ends)])  66.7 us
    pallas_call x2, Pallas kernels, coupling_step(): pl.pallas_call(functools.partial(coupling_kernel, final=final, width=pair...  29.1 us
    ppermute x3, starting transfers between devices, halo_sources(): from_left = lax.ppermute(cells, axis, [(i, i + 1) for i in range(ends)])  25 us
    ppermute x4, waiting for transfers between devices, halving_stream(): other = lax.ppermute(piece, 'aux', [(i, i ^ bit) for i in range(count)])  17.2 us
    ppermute x4, waiting for transfers between devices, halving_stream(): lax.ppermute(send, 'aux', [(i, i ^ bit) for i in range(count)])  17.1 us
    pallas_call x1, Pallas kernels, partial_exchange(): pl.pallas_call(functools.partial(exchange_kernel, occ=occ), grid_spec=gri...  17 us
    ppermute x3, waiting for transfers between devices, halo_sources(): from_left = lax.ppermute(cells, axis, [(i, i + 1) for i in range(ends)])  9.93 us
    ppermute x4, starting transfers between devices, halving_stream(): other = lax.ppermute(piece, 'aux', [(i, i ^ bit) for i in range(count)])  5.75 us
  transfers between devices with their start and end apart: 14, of which 12 were waited for; matrix products, arithmetic and copies ran while one was open for 5% of the time, Pallas kernels for 0%

profile of v7, /device:TPU:1, one launch (start us, length us, event | category | flops | bytes accessed | tf_op | source)
XLA Modules:
  0.0 218.4 jit_solution(13491800075041015857)
XLA Ops:
  0.6 4.6 %collective-permute-start = (bf16[4,512,256]{2,1,0:T(8,128)(2,1)}, bf16[4,512,256]{2,1,0:T(8,128)(2,1)S(1)}, u32[]{:S(2)}, u32[]{:S(2)}) collective-permute-start(bf16[4,512,256]{2,1,0:T(8,128)(2,1)} %t_own.1), channel_id=1, source_target_pairs={{0,1},{1,2},{2,3},{3,4},{4,5},{5,6},{6,7},{8,9},{9,10},{10,11},{11... | collective-permute-start | bytes 3145736 | tf_op jit(solution)/shard_map/ppermute | solution.py:18
  5.2 1.9 collective-permute-start.1
  7.2 1.2 compare_select_fusion.2.size_ref
  8.4 0.7 broadcast_subtract_fusion
  9.1 0.6 slice_bitcast_fusion
  9.7 7.6 %collective-permute-done.t_left = bf16[4,512,256]{2,1,0:T(8,128)(2,1)S(1)} collective-permute-done((bf16[4,512,256]{2,1,0:T(8,128)(2,1)}, bf16[4,512,256]{2,1,0:T(8,128)(2,1)S(1)}, u32[]{:S(2)}, u32[]{:S(2)}) %collective-permute-start) | collective-permute-done | bytes 1048608 | tf_op jit(solution)/shard_map/ppermute | solution.py:18
  17.3 4.3 %collective-permute-done.1.t_right = bf16[4,512,256]{2,1,0:T(8,128)(2,1)S(1)} collective-permute-done((bf16[4,512,256]{2,1,0:T(8,128)(2,1)}, bf16[4,512,256]{2,1,0:T(8,128)(2,1)S(1)}, u32[]{:S(2)}, u32[]{:S(2)}) %collective-permute-start.1) | collective-permute-done | bytes 1048608 | tf_op jit(solution)/shard_map/ppermute | solution.py:19
  21.6 1.0 copy-done.4
  22.6 17.0 %shard_map.95 = f32[16,192,192]{2,1,0:T(8,128)} custom-call(s32[16]{0:T(128)} %get-tuple-element.11.lead_ref, s32[16]{0:T(128)} %get-tuple-element.10.trail_ref, s32[16]{0:T(128)} %compare_select_fusion.2.size_ref, bf16[4,512,256]{2,1,0:T(8,128)(2,1)} %t_own.1, bf16[4,512,256]{2,1,0:T(8,128)(2,1)} %copy-done.3, bf16[4,512,256]{2,1,0:T(8,128)(2,1)} %t_own.1, ...), custom_call_target="tpu_custom_call" | custom-call | flops 2214592512 | bytes 13893632 | tf_op jit(solution)/shard_map/pallas_call | solution.py:128
  39.6 2.2 %fusion = (f32[8,192,192]{2,1,0:T(8,128)S(1)}, f32[8,192,192]{2,1,0:T(8,128)S(1)}) fusion(f32[16,192,192]{2,1,0:T(8,128)} %shard_map.95), kind=kLoop, calls=%fused_computation.25 | loop fusion | bytes 4718592 | tf_op jit(solution)/shard_map/slice | solution.py:46
  41.8 0.9 constant_dynamic-slice_fusion.1
  42.7 1.2 collective-permute-start.6
  44.0 0.9 constant_dynamic-slice_fusion.3
  44.9 1.2 collective-permute-start.2
  46.1 11.4 %collective-permute-done.6 = f32[4,192,192]{2,1,0:T(8,128)} collective-permute-done((f32[4,192,192]{2,1,0:T(8,128)}, f32[4,192,192]{2,1,0:T(8,128)}, u32[]{:S(2)}, u32[]{:S(2)}) %collective-permute-start.6) | collective-permute-done | bytes 589856 | tf_op jit(solution)/shard_map/ppermute | solution.py:29
  57.5 1.2 dynamic-slice_add_fusion
  58.8 1.7 collective-permute-start.7
  60.5 1.2 dynamic-slice_add_fusion.1
  61.7 1.6 collective-permute-start.3
  63.3 5.7 %collective-permute-done.7 = f32[2,192,192]{2,1,0:T(8,128)S(1)} collective-permute-done((f32[2,192,192]{2,1,0:T(8,128)S(1)}, f32[2,192,192]{2,1,0:T(8,128)S(1)}, u32[]{:S(2)}, u32[]{:S(2)}) %collective-permute-start.7) | collective-permute-done | bytes 294944 | tf_op jit(solution)/shard_map/ppermute | solution.py:29
  69.1 1.1 constant_dynamic-update-slice_fusion.3
  70.1 1.3 collective-permute-start.8
  71.6 1.4 collective-permute-start.4
  72.9 7.8 %collective-permute-done.8 = f32[2,192,192]{2,1,0:T(8,128)S(1)} collective-permute-done((f32[2,192,192]{2,1,0:T(8,128)S(1)}, f32[2,192,192]{2,1,0:T(8,128)S(1)}, u32[]{:S(2)}, u32[]{:S(2)}) %collective-permute-start.8) | collective-permute-done | bytes 294944 | tf_op jit(solution)/shard_map/ppermute | solution.py:32
  80.7 2.0 collective-permute-start.9
  82.7 0.1 collective-permute-done.4
  82.9 1.1 collective-permute-start.5
  84.0 0.1 broadcast.30.clone
  84.2 0.1 broadcast.30.clone.1
  84.4 8.6 %collective-permute-done.9 = f32[4,192,192]{2,1,0:T(8,128)S(1)} collective-permute-done((f32[4,192,192]{2,1,0:T(8,128)S(1)}, f32[4,192,192]{2,1,0:T(8,128)S(1)}, u32[]{:S(2)}, u32[]{:S(2)}) %collective-permute-start.9) | collective-permute-done | bytes 589856 | tf_op jit(solution)/shard_map/ppermute | solution.py:32
  93.0 0.7 collective-permute-done.5
  93.9 2.0 pad_maximum_fusion
  95.9 1.9 collective-permute-start.11
  97.8 15.9 %collective-permute-start.10 = (f32[16,192,192]{2,1,0:T(8,128)S(1)}, f32[16,192,192]{2,1,0:T(8,128)}, u32[]{:S(2)}, u32[]{:S(2)}) collective-permute-start(f32[16,192,192]{2,1,0:T(8,128)S(1)} %get-tuple-element.7.refs_1_.refs_7_), channel_id=1, source_target_pairs={{0,1},{1,2},{2,3},{3,4},{4,5},{5,6},{6,7},{8,9},{9,10},{10,11},{11... | collective-permute-start | bytes 7077896 | tf_op jit(solution)/shard_map/ppermute | solution.py:18
  113.7 0.6 broadcast_in_dim.26.refs_6_
  114.4 0.1 copy.12
  114.5 0.7 reshape.18.nb_ref
  115.2 0.6 reshape.19.fock_ref
  115.8 1.7 copy.14.refs_5_
  117.5 29.3 %collective-permute-done.11.refs_2_ = f32[16,192,192]{2,1,0:T(8,128)} collective-permute-done((f32[16,192,192]{2,1,0:T(8,128)S(1)}, f32[16,192,192]{2,1,0:T(8,128)}, u32[]{:S(2)}, u32[]{:S(2)}) %collective-permute-start.11) | collective-permute-done | bytes 2359328 | tf_op jit(solution)/shard_map/ppermute | solution.py:19
  146.9 1.1 collective-permute-done.10.refs_0_
  147.9 14.7 %shard_map.96.refs_1_.refs_7_ = f32[16,192,192]{2,1,0:T(8,128)} custom-call(s32[32]{0:T(128)} %reshape.18.nb_ref, s32[16]{0:T(128)} %compare_select_fusion.2.size_ref, f32[32]{0:T(128)} %reshape.19.fock_ref, f32[16,192,192]{2,1,0:T(8,128)} %collective-permute-done.10.refs_0_, f32[16,192,192]{2,1,0:T(8,128)} %copy-done, ...), custom_call_target="tpu_custom_call" | custom-call | flops 1811939328 | bytes 14155776 | tf_op jit(solution)/shard_map/pallas_call | solution.py:228
  162.6 1.9 collective-permute-start.13
  164.6 4.5 %collective-permute-start.12 = (f32[16,192,192]{2,1,0:T(8,128)}, f32[16,192,192]{2,1,0:T(8,128)}, u32[]{:S(2)}, u32[]{:S(2)}) collective-permute-start(f32[16,192,192]{2,1,0:T(8,128)} %shard_map.96.refs_1_.refs_7_), channel_id=1, source_target_pairs={{0,1},{1,2},{2,3},{3,4},{4,5},{5,6},{6,7},{8,9},{9,10},{10,11},{11... | collective-permute-start | bytes 7077896 | tf_op jit(solution)/shard_map/ppermute | solution.py:18
  169.1 33.0 %collective-permute-done.13.refs_2_ = f32[16,192,192]{2,1,0:T(8,128)S(1)} collective-permute-done((f32[16,192,192]{2,1,0:T(8,128)}, f32[16,192,192]{2,1,0:T(8,128)S(1)}, u32[]{:S(2)}, u32[]{:S(2)}) %collective-permute-start.13) | collective-permute-done | bytes 2359328 | tf_op jit(solution)/shard_map/ppermute | solution.py:19
  202.1 1.3 collective-permute-done.12.refs_0_
  203.4 0.4 copy-done.1
  203.9 14.4 %shard_map.97 = f32[16,192,192]{2,1,0:T(8,128)} custom-call(s32[32]{0:T(128)} %reshape.18.nb_ref, s32[16]{0:T(128)} %compare_select_fusion.2.size_ref, f32[32]{0:T(128)} %reshape.19.fock_ref, f32[16,192,192]{2,1,0:T(8,128)} %collective-permute-done.12.refs_0_, f32[16,192,192]{2,1,0:T(8,128)} %shard_map.96.refs_1_.refs_7_, f32[16,192,192]{2,1,0:T(8,128)} %copy-done.1, ...), custom_call_target="tpu_custom_call" | custom-call | flops 1811939328 | bytes 14155776 | tf_op jit(solution)/shard_map/pallas_call | solution.py:228
  (29 shorter events, 0.7 us)
Async XLA Ops:
  0.6 16.6 %collective-permute-start = (bf16[4,512,256]{2,1,0:T(8,128)(2,1)}, bf16[4,512,256]{2,1,0:T(8,128)(2,1)S(1)}, u32[]{:S(2)}, u32[]{:S(2)}) collective-permute-start(bf16[4,512,256]{2,1,0:T(8,128)(2,1)} %t_own.1), channel_id=1, source_target_pairs={{0,1},{1,2},{2,3},{3,4},{4,5},{5,6},{6,7},{8,9},{9,10},{10,11},{11... | collective-permute-start | bytes 3145736 | tf_op jit(solution)/shard_map/ppermute | solution.py:18
  5.2 16.3 %collective-permute-start.1 = (bf16[4,512,256]{2,1,0:T(8,128)(2,1)}, bf16[4,512,256]{2,1,0:T(8,128)(2,1)S(1)}, u32[]{:S(2)}, u32[]{:S(2)}) collective-permute-start(bf16[4,512,256]{2,1,0:T(8,128)(2,1)} %t_own.1), channel_id=1, source_target_pairs={{1,0},{2,1},{3,2},{4,3},{5,4},{6,5},{7,6},{9,8},{10,9},{11,10},{12... | collective-permute-start | bytes 3145736 | tf_op jit(solution)/shard_map/ppermute | solution.py:19
  17.3 4.3 %copy-start.3 = (bf16[4,512,256]{2,1,0:T(8,128)(2,1)}, bf16[4,512,256]{2,1,0:T(8,128)(2,1)S(1)}, u32[]{:S(2)}) copy-start(bf16[4,512,256]{2,1,0:T(8,128)(2,1)S(1)} %collective-permute-done.t_left) | copy-start | bytes 3145732
  21.6 1.0 copy-start.4
  42.7 14.7 %collective-permute-start.6 = (f32[4,192,192]{2,1,0:T(8,128)}, f32[4,192,192]{2,1,0:T(8,128)}, u32[]{:S(2)}, u32[]{:S(2)}) collective-permute-start(f32[4,192,192]{2,1,0:T(8,128)} %constant_dynamic-slice_fusion.1), channel_id=1, source_target_pairs={{0,16},{8,24},{16,0},{24,8},{1,17},{9,25},{17,1},{25,9},{2,18},{10... | collective-permute-start | bytes 1769480 | tf_op jit(solution)/shard_map/ppermute | solution.py:29
  44.9 15.5 %collective-permute-start.2 = (f32[4,192,192]{2,1,0:T(8,128)}, f32[4,192,192]{2,1,0:T(8,128)}, u32[]{:S(2)}, u32[]{:S(2)}) collective-permute-start(f32[4,192,192]{2,1,0:T(8,128)} %constant_dynamic-slice_fusion.3), channel_id=1, source_target_pairs={{0,8},{8,0},{16,24},{24,16},{1,9},{9,1},{17,25},{25,17},{2,10},{10... | collective-permute-start | bytes 1769480 | tf_op jit(solution)/shard_map/ppermute | solution.py:29
  58.7 3.0 %copy-start.2 = (f32[4,192,192]{2,1,0:T(8,128)}, f32[4,192,192]{2,1,0:T(8,128)S(1)}, u32[]{:S(2)}) copy-start(f32[4,192,192]{2,1,0:T(8,128)S(1)} %dynamic-slice_add_fusion) | copy-start | bytes 1769476
  58.8 10.2 %collective-permute-start.7 = (f32[2,192,192]{2,1,0:T(8,128)S(1)}, f32[2,192,192]{2,1,0:T(8,128)S(1)}, u32[]{:S(2)}, u32[]{:S(2)}) collective-permute-start(f32[2,192,192]{2,1,0:T(8,128)S(1)} %constant_dynamic-slice_fusion), channel_id=1, source_target_pairs={{0,8},{8,0},{16,24},{24,16},{1,9},{9,1},{17,25},{25,17},{2,10},{10... | collective-permute-start | bytes 884744 | tf_op jit(solution)/shard_map/ppermute | solution.py:29
  61.7 9.7 %collective-permute-start.3 = (f32[2,192,192]{2,1,0:T(8,128)S(1)}, f32[2,192,192]{2,1,0:T(8,128)S(1)}, u32[]{:S(2)}, u32[]{:S(2)}) collective-permute-start(f32[2,192,192]{2,1,0:T(8,128)S(1)} %constant_dynamic-slice_fusion.2), channel_id=1, source_target_pairs={{0,16},{8,24},{16,0},{24,8},{1,17},{9,25},{17,1},{25,9},{2,18},{10... | collective-permute-start | bytes 884744 | tf_op jit(solution)/shard_map/ppermute | solution.py:29
  70.1 10.5 %collective-permute-start.8 = (f32[2,192,192]{2,1,0:T(8,128)S(1)}, f32[2,192,192]{2,1,0:T(8,128)S(1)}, u32[]{:S(2)}, u32[]{:S(2)}) collective-permute-start(f32[2,192,192]{2,1,0:T(8,128)S(1)} %get-tuple-element.5), channel_id=1, source_target_pairs={{0,8},{8,0},{16,24},{24,16},{1,9},{9,1},{17,25},{25,17},{2,10},{10... | collective-permute-start | bytes 884744 | tf_op jit(solution)/shard_map/ppermute | solution.py:32
  71.6 11.3 %collective-permute-start.4 = (f32[2,192,192]{2,1,0:T(8,128)S(1)}, f32[2,192,192]{2,1,0:T(8,128)S(1)}, u32[]{:S(2)}, u32[]{:S(2)}) collective-permute-start(f32[2,192,192]{2,1,0:T(8,128)S(1)} %get-tuple-element.3), channel_id=1, source_target_pairs={{0,16},{8,24},{16,0},{24,8},{1,17},{9,25},{17,1},{25,9},{2,18},{10... | collective-permute-start | bytes 884744 | tf_op jit(solution)/shard_map/ppermute | solution.py:32
  80.7 12.3 %collective-permute-start.9 = (f32[4,192,192]{2,1,0:T(8,128)S(1)}, f32[4,192,192]{2,1,0:T(8,128)S(1)}, u32[]{:S(2)}, u32[]{:S(2)}) collective-permute-start(f32[4,192,192]{2,1,0:T(8,128)S(1)} %constant_dynamic-update-slice_fusion.2), channel_id=1, source_target_pairs={{0,16},{8,24},{16,0},{24,8},{1,17},{9,25},{17,1},{25,9},{2,18},{10... | collective-permute-start | bytes 1769480 | tf_op jit(solution)/shard_map/ppermute | solution.py:32
  82.9 10.9 %collective-permute-start.5 = (f32[4,192,192]{2,1,0:T(8,128)S(1)}, f32[4,192,192]{2,1,0:T(8,128)S(1)}, u32[]{:S(2)}, u32[]{:S(2)}) collective-permute-start(f32[4,192,192]{2,1,0:T(8,128)S(1)} %constant_dynamic-update-slice_fusion.6), channel_id=1, source_target_pairs={{0,8},{8,0},{16,24},{24,16},{1,9},{9,1},{17,25},{25,17},{2,10},{10... | collective-permute-start | bytes 1769480 | tf_op jit(solution)/shard_map/ppermute | solution.py:32
  84.4 9.5 %copy-start.5 = (f32[16,192]{1,0:T(8,128)S(1)}, f32[16,192]{1,0:T(8,128)}, u32[]{:S(2)}) copy-start(f32[16,192]{1,0:T(8,128)} %param.12) | copy-start | bytes 36868
  93.8 20.5 %copy-start.7 = (s32[16,2]{0,1:T(2,128)S(1)}, s32[16,2]{0,1:T(2,128)}, u32[]{:S(2)}) copy-start(s32[16,2]{0,1:T(2,128)} %param.14) | copy-start | bytes 388
  93.9 21.3 %copy-start.6 = (f32[16,2]{0,1:T(2,128)S(1)}, f32[16,2]{0,1:T(2,128)}, u32[]{:S(2)}) copy-start(f32[16,2]{0,1:T(2,128)} %param.15) | copy-start | bytes 388
  95.9 52.1 %copy-start = (f32[16,192,192]{2,1,0:T(8,128)}, f32[16,192,192]{2,1,0:T(8,128)S(1)}, u32[]{:S(2)}) copy-start(f32[16,192,192]{2,1,0:T(8,128)S(1)} %get-tuple-element.7.refs_1_.refs_7_) | copy-start | bytes 7077892
  95.9 51.0 %collective-permute-start.11 = (f32[16,192,192]{2,1,0:T(8,128)S(1)}, f32[16,192,192]{2,1,0:T(8,128)}, u32[]{:S(2)}, u32[]{:S(2)}) collective-permute-start(f32[16,192,192]{2,1,0:T(8,128)S(1)} %get-tuple-element.7.refs_1_.refs_7_), channel_id=1, source_target_pairs={{1,0},{2,1},{3,2},{4,3},{5,4},{6,5},{7,6},{9,8},{10,9},{11,10},{12... | collective-permute-start | bytes 7077896 | tf_op jit(solution)/shard_map/ppermute | solution.py:19
  97.8 50.1 %collective-permute-start.10 = (f32[16,192,192]{2,1,0:T(8,128)S(1)}, f32[16,192,192]{2,1,0:T(8,128)}, u32[]{:S(2)}, u32[]{:S(2)}) collective-permute-start(f32[16,192,192]{2,1,0:T(8,128)S(1)} %get-tuple-element.7.refs_1_.refs_7_), channel_id=1, source_target_pairs={{0,1},{1,2},{2,3},{3,4},{4,5},{5,6},{6,7},{8,9},{9,10},{10,11},{11... | collective-permute-start | bytes 7077896 | tf_op jit(solution)/shard_map/ppermute | solution.py:18
  162.6 39.5 %collective-permute-start.13 = (f32[16,192,192]{2,1,0:T(8,128)}, f32[16,192,192]{2,1,0:T(8,128)S(1)}, u32[]{:S(2)}, u32[]{:S(2)}) collective-permute-start(f32[16,192,192]{2,1,0:T(8,128)} %shard_map.96.refs_1_.refs_7_), channel_id=1, source_target_pairs={{1,0},{2,1},{3,2},{4,3},{5,4},{6,5},{7,6},{9,8},{10,9},{11,10},{12... | collective-permute-start | bytes 7077896 | tf_op jit(solution)/shard_map/ppermute | solution.py:19
  164.6 38.8 %collective-permute-start.12 = (f32[16,192,192]{2,1,0:T(8,128)}, f32[16,192,192]{2,1,0:T(8,128)}, u32[]{:S(2)}, u32[]{:S(2)}) collective-permute-start(f32[16,192,192]{2,1,0:T(8,128)} %shard_map.96.refs_1_.refs_7_), channel_id=1, source_target_pairs={{0,1},{1,2},{2,3},{3,4},{4,5},{5,6},{6,7},{8,9},{9,10},{10,11},{11... | collective-permute-start | bytes 7077896 | tf_op jit(solution)/shard_map/ppermute | solution.py:18
  202.1 1.7 copy-start.1

commit v8 on v7

--- a/solution.py
+++ b/solution.py
@@ -72,61 +72,71 @@
 
 
 def exchange_kernel(
-    lead_ref, trail_ref, size_ref, x_lead, t_left, t_own, t_right, coef_ref, out_ref, xbuf, sems, *, occ
+    lead_ref, trail_ref, size_ref, t_left, t_own, t_right, coef_ref, out_ref, lbuf, tbuf, sems, *, occ, group
 ):
     i = pl.program_id(0)
     steps = pl.num_programs(0)
     sources = (t_left, t_own, t_right)
 
+    def fetch(step, slot):
+        for g in range(group):
+            p = step * group + g
+            pltpu.make_async_copy(t_own.at[lead_ref[p] % occ], lbuf.at[slot, g], sems.at[slot, 0, g]).start()
+            fetch_block(sources, occ, trail_ref[p], tbuf.at[slot, g], sems.at[slot, 1, g])
+
     @pl.when(i == 0)
     def _():
-        fetch_block(sources, occ, trail_ref[0], xbuf.at[0], sems.at[0])
+        fetch(0, 0)
 
     @pl.when(i + 1 < steps)
     def _():
-        fetch_block(sources, occ, trail_ref[i + 1], xbuf.at[(i + 1) % 2], sems.at[(i + 1) % 2])
+        fetch(i + 1, (i + 1) % 2)
 
     slot = i % 2
-    pltpu.make_async_copy(t_own.at[0], xbuf.at[slot], sems.at[slot]).wait()
-    size = size_ref[i]
     transposed = (((1,), (1,)), ((), ()))
-    out_ref[0] = jnp.zeros((NPNO, NPNO), jnp.float32)
-    for m in CLASS_SIZES:
-
-        @pl.when(size == m)
-        def _():
-            first = coef_ref[0, 0, :m, :]
-            second = coef_ref[0, 1, :m, :]
-            left_t = lax.dot_general(first, x_lead[0], transposed, preferred_element_type=jnp.float32)
-            right = lax.dot_general(xbuf[slot], second, transposed, preferred_element_type=jnp.float32)
-            out_ref[0, :m, :m] = jnp.dot(
-                left_t.astype(jnp.bfloat16), right.astype(jnp.bfloat16), preferred_element_type=jnp.float32
-            )
+    for g in range(group):
+        p = i * group + g
+        pltpu.make_async_copy(t_own.at[0], lbuf.at[slot, g], sems.at[slot, 0, g]).wait()
+        pltpu.make_async_copy(t_own.at[0], tbuf.at[slot, g], sems.at[slot, 1, g]).wait()
+        size = size_ref[p]
+        out_ref[g] = jnp.zeros((NPNO, NPNO), jnp.float32)
+        for m in CLASS_SIZES:
+
+            @pl.when(size == m)
+            def _():
+                first = coef_ref[g, 0, :m, :]
+                second = coef_ref[g, 1, :m, :]
+                left_t = lax.dot_general(first, lbuf[slot, g], transposed, preferred_element_type=jnp.float32)
+                right = lax.dot_general(tbuf[slot, g], second, transposed, preferred_element_type=jnp.float32)
+                out_ref[g, :m, :m] = jnp.dot(
+                    left_t.astype(jnp.bfloat16), right.astype(jnp.bfloat16), preferred_element_type=jnp.float32
+                )
 
 
 def partial_exchange(lead, trail, sizes, sources, coef_t):
     pairs = coef_t.shape[0]
+    group = next(g for g in (4, 2, 1) if pairs % g == 0)
     occ, nfit, npao = sources[1].shape
     hbm = pl.BlockSpec(memory_space=pl.ANY)
     grid_spec = pltpu.PrefetchScalarGridSpec(
         num_scalar_prefetch=3,
-        grid=(pairs,),
+        grid=(pairs // group,),
         in_specs=[
-            pl.BlockSpec((1, nfit, npao), lambda i, a, b, s: (a[i], 0, 0)),
             hbm,
             hbm,
             hbm,
-            pl.BlockSpec((1, 2, NPNO, npao), lambda i, a, b, s: (i, 0, 0, 0)),
+            pl.BlockSpec((group, 2, NPNO, npao), lambda i, a, b, s: (i, 0, 0, 0)),
         ],
-        out_specs=pl.BlockSpec((1, NPNO, NPNO), lambda i, a, b, s: (i, 0, 0)),
+        out_specs=pl.BlockSpec((group, NPNO, NPNO), lambda i, a, b, s: (i, 0, 0)),
         scratch_shapes=[
-            pltpu.VMEM((2, nfit, npao), sources[1].dtype),
-            pltpu.SemaphoreType.DMA((2,)),
+            pltpu.VMEM((2, group, nfit, npao), sources[1].dtype),
+            pltpu.VMEM((2, group, nfit, npao), sources[1].dtype),
+            pltpu.SemaphoreType.DMA((2, 2, group)),
         ],
     )
     flops = pairs * (2 * 2 * nfit * npao * NPNO + 2 * nfit * NPNO * NPNO)
     return pl.pallas_call(
-        functools.partial(exchange_kernel, occ=occ),
+        functools.partial(exchange_kernel, occ=occ, group=group),
         grid_spec=grid_spec,
         out_shape=jax.ShapeDtypeStruct((pairs, NPNO, NPNO), jnp.float32),
         cost_estimate=pl.CostEstimate(
@@ -134,7 +144,7 @@
             bytes_accessed=pairs * (2 * nfit * npao * 2 + 2 * npao * NPNO * 2 + NPNO * NPNO * 4),
             transcendentals=0,
         ),
-    )(lead, trail, sizes, sources[1], *sources, coef_t)
+    )(lead, trail, sizes, *sources, coef_t)
 
 
 def split_bf16(value):

time: 220 us -> 215 us (0.977)
  Pallas kernels: 46.1 us -> 42.1 us
    pallas_call x1, Pallas kernels: 17 us -> 12.1 us  [partial_exchange(): pl.pallas_call(functools.partial(exchange_kernel, occ=occ, group=group),...]
  transfers between devices with their start and end apart: 14 -> 14, of which waited for: 12 -> 11; matrix products, arithmetic and copies ran while one was open for 5% -> 5% of each run, Pallas kernels for 0% -> 0%
where the time goes in v8:
time: 215 us
  waiting for transfers between devices  111 us (52%)
  starting transfers between devices  42.9 us (20%)
  Pallas kernels  42.1 us (20%)
  local copies, waits for them, and re-layouts  10 us (5%)
  other arithmetic  8.12 us (4%)
    ppermute x3, waiting for transfers between devices, halo_sources(): from_right = lax.ppermute(cells, axis, [(i + 1, i) for i in range(ends)])  66.7 us
    pallas_call x2, Pallas kernels, coupling_step(): pl.pallas_call(functools.partial(coupling_kernel, final=final, width=pair...  29.9 us
    ppermute x3, starting transfers between devices, halo_sources(): from_left = lax.ppermute(cells, axis, [(i, i + 1) for i in range(ends)])  25.6 us
    ppermute x4, waiting for transfers between devices, halving_stream(): lax.ppermute(send, 'aux', [(i, i ^ bit) for i in range(count)])  17.1 us
    ppermute x4, waiting for transfers between devices, halving_stream(): other = lax.ppermute(piece, 'aux', [(i, i ^ bit) for i in range(count)])  17 us
    pallas_call x1, Pallas kernels, partial_exchange(): pl.pallas_call(functools.partial(exchange_kernel, occ=occ, group=group),...  12.1 us
    ppermute x3, waiting for transfers between devices, halo_sources(): from_left = lax.ppermute(cells, axis, [(i, i + 1) for i in range(ends)])  9.93 us
    ppermute x4, starting transfers between devices, halving_stream(): other = lax.ppermute(piece, 'aux', [(i, i ^ bit) for i in range(count)])  5.91 us
  transfers between devices with their start and end apart: 14, of which 11 were waited for; matrix products, arithmetic and copies ran while one was open for 5% of the time, Pallas kernels for 0%

profile of v8, /device:TPU:1, one launch (start us, length us, event | category | flops | bytes accessed | tf_op | source)
XLA Modules:
  0.0 214.8 jit_solution(2300480017350693700)
XLA Ops:
  0.6 4.6 %collective-permute-start = (bf16[4,512,256]{2,1,0:T(8,128)(2,1)}, bf16[4,512,256]{2,1,0:T(8,128)(2,1)S(1)}, u32[]{:S(2)}, u32[]{:S(2)}) collective-permute-start(bf16[4,512,256]{2,1,0:T(8,128)(2,1)} %t_own.1), channel_id=1, source_target_pairs={{0,1},{1,2},{2,3},{3,4},{4,5},{5,6},{6,7},{8,9},{9,10},{10,11},{11... | collective-permute-start | bytes 3145736 | tf_op jit(solution)/shard_map/ppermute | solution.py:18
  5.2 1.9 collective-permute-start.1
  7.2 1.2 compare_select_fusion.2.size_ref
  8.4 0.7 broadcast_subtract_fusion
  9.1 0.6 slice_bitcast_fusion
  9.7 7.6 %collective-permute-done.t_left = bf16[4,512,256]{2,1,0:T(8,128)(2,1)S(1)} collective-permute-done((bf16[4,512,256]{2,1,0:T(8,128)(2,1)}, bf16[4,512,256]{2,1,0:T(8,128)(2,1)S(1)}, u32[]{:S(2)}, u32[]{:S(2)}) %collective-permute-start) | collective-permute-done | bytes 1048608 | tf_op jit(solution)/shard_map/ppermute | solution.py:18
  17.3 4.3 %collective-permute-done.1.t_right = bf16[4,512,256]{2,1,0:T(8,128)(2,1)S(1)} collective-permute-done((bf16[4,512,256]{2,1,0:T(8,128)(2,1)}, bf16[4,512,256]{2,1,0:T(8,128)(2,1)S(1)}, u32[]{:S(2)}, u32[]{:S(2)}) %collective-permute-start.1) | collective-permute-done | bytes 1048608 | tf_op jit(solution)/shard_map/ppermute | solution.py:19
  21.6 1.0 copy-done.4
  22.6 12.1 %shard_map.95 = f32[16,192,192]{2,1,0:T(8,128)} custom-call(s32[16]{0:T(128)} %get-tuple-element.11.lead_ref, s32[16]{0:T(128)} %get-tuple-element.10.trail_ref, s32[16]{0:T(128)} %compare_select_fusion.2.size_ref, bf16[4,512,256]{2,1,0:T(8,128)(2,1)} %copy-done.3, bf16[4,512,256]{2,1,0:T(8,128)(2,1)} %t_own.1, bf16[4,512,256]{2,1,0:T(8,128)(2,1)} %copy-done.4, ...), custom_call_target="tpu_custom_call" | custom-call | flops 2214592512 | bytes 13893632 | tf_op jit(solution)/shard_map/pallas_call | solution.py:138
  34.7 2.2 %fusion = (f32[8,192,192]{2,1,0:T(8,128)S(1)}, f32[8,192,192]{2,1,0:T(8,128)S(1)}) fusion(f32[16,192,192]{2,1,0:T(8,128)} %shard_map.95), kind=kLoop, calls=%fused_computation.25 | loop fusion | bytes 4718592 | tf_op jit(solution)/shard_map/slice | solution.py:46
  36.9 0.9 constant_dynamic-slice_fusion.1
  37.9 1.2 collective-permute-start.6
  39.1 0.9 constant_dynamic-slice_fusion.3
  40.0 1.2 collective-permute-start.2
  41.2 11.4 %collective-permute-done.6 = f32[4,192,192]{2,1,0:T(8,128)} collective-permute-done((f32[4,192,192]{2,1,0:T(8,128)}, f32[4,192,192]{2,1,0:T(8,128)}, u32[]{:S(2)}, u32[]{:S(2)}) %collective-permute-start.6) | collective-permute-done | bytes 589856 | tf_op jit(solution)/shard_map/ppermute | solution.py:29
  52.6 1.2 dynamic-slice_add_fusion
  53.9 1.7 collective-permute-start.7
  55.6 1.2 dynamic-slice_add_fusion.1
  56.9 1.5 collective-permute-start.3
  58.4 5.7 %collective-permute-done.7 = f32[2,192,192]{2,1,0:T(8,128)S(1)} collective-permute-done((f32[2,192,192]{2,1,0:T(8,128)S(1)}, f32[2,192,192]{2,1,0:T(8,128)S(1)}, u32[]{:S(2)}, u32[]{:S(2)}) %collective-permute-start.7) | collective-permute-done | bytes 294944 | tf_op jit(solution)/shard_map/ppermute | solution.py:29
  64.1 1.1 constant_dynamic-update-slice_fusion.3
  65.2 1.3 collective-permute-start.8
  66.6 1.4 collective-permute-start.4
  68.0 7.7 %collective-permute-done.8 = f32[2,192,192]{2,1,0:T(8,128)S(1)} collective-permute-done((f32[2,192,192]{2,1,0:T(8,128)S(1)}, f32[2,192,192]{2,1,0:T(8,128)S(1)}, u32[]{:S(2)}, u32[]{:S(2)}) %collective-permute-start.8) | collective-permute-done | bytes 294944 | tf_op jit(solution)/shard_map/ppermute | solution.py:32
  75.8 2.1 collective-permute-start.9
  77.9 1.2 collective-permute-start.5
  79.1 0.1 broadcast.30.clone
  79.3 0.1 broadcast.30.clone.1
  79.5 8.4 %collective-permute-done.9 = f32[4,192,192]{2,1,0:T(8,128)S(1)} collective-permute-done((f32[4,192,192]{2,1,0:T(8,128)S(1)}, f32[4,192,192]{2,1,0:T(8,128)S(1)}, u32[]{:S(2)}, u32[]{:S(2)}) %collective-permute-start.9) | collective-permute-done | bytes 589856 | tf_op jit(solution)/shard_map/ppermute | solution.py:32
  88.0 0.8 collective-permute-done.5
  88.9 2.0 pad_maximum_fusion
  90.9 1.9 collective-permute-start.11
  92.8 16.0 %collective-permute-start.10 = (f32[16,192,192]{2,1,0:T(8,128)S(1)}, f32[16,192,192]{2,1,0:T(8,128)}, u32[]{:S(2)}, u32[]{:S(2)}) collective-permute-start(f32[16,192,192]{2,1,0:T(8,128)S(1)} %get-tuple-element.7.refs_1_.refs_7_), channel_id=1, source_target_pairs={{0,1},{1,2},{2,3},{3,4},{4,5},{5,6},{6,7},{8,9},{9,10},{10,11},{11... | collective-permute-start | bytes 7077896 | tf_op jit(solution)/shard_map/ppermute | solution.py:18
  108.8 0.6 broadcast_in_dim.26.refs_6_
  109.5 0.1 copy.12
  109.5 0.7 reshape.18.nb_ref
  110.2 0.1 copy.13
  110.3 0.6 reshape.19.fock_ref
  110.9 1.7 copy.14.refs_5_
  112.6 29.3 %collective-permute-done.11.refs_2_ = f32[16,192,192]{2,1,0:T(8,128)} collective-permute-done((f32[16,192,192]{2,1,0:T(8,128)S(1)}, f32[16,192,192]{2,1,0:T(8,128)}, u32[]{:S(2)}, u32[]{:S(2)}) %collective-permute-start.11) | collective-permute-done | bytes 2359328 | tf_op jit(solution)/shard_map/ppermute | solution.py:19
  142.0 1.1 collective-permute-done.10.refs_0_
  143.0 15.1 %shard_map.96.refs_1_.refs_7_ = f32[16,192,192]{2,1,0:T(8,128)} custom-call(s32[32]{0:T(128)} %reshape.18.nb_ref, s32[16]{0:T(128)} %compare_select_fusion.2.size_ref, f32[32]{0:T(128)} %reshape.19.fock_ref, f32[16,192,192]{2,1,0:T(8,128)} %collective-permute-done.10.refs_0_, f32[16,192,192]{2,1,0:T(8,128)} %copy-done, ...), custom_call_target="tpu_custom_call" | custom-call | flops 1811939328 | bytes 14155776 | tf_op jit(solution)/shard_map/pallas_call | solution.py:238
  158.2 1.9 collective-permute-start.13
  160.1 5.0 %collective-permute-start.12 = (f32[16,192,192]{2,1,0:T(8,128)}, f32[16,192,192]{2,1,0:T(8,128)}, u32[]{:S(2)}, u32[]{:S(2)}) collective-permute-start(f32[16,192,192]{2,1,0:T(8,128)} %shard_map.96.refs_1_.refs_7_), channel_id=1, source_target_pairs={{0,1},{1,2},{2,3},{3,4},{4,5},{5,6},{6,7},{8,9},{9,10},{10,11},{11... | collective-permute-start | bytes 7077896 | tf_op jit(solution)/shard_map/ppermute | solution.py:18
  165.1 33.0 %collective-permute-done.13.refs_2_ = f32[16,192,192]{2,1,0:T(8,128)S(1)} collective-permute-done((f32[16,192,192]{2,1,0:T(8,128)}, f32[16,192,192]{2,1,0:T(8,128)S(1)}, u32[]{:S(2)}, u32[]{:S(2)}) %collective-permute-start.13) | collective-permute-done | bytes 2359328 | tf_op jit(solution)/shard_map/ppermute | solution.py:19
  198.1 1.3 collective-permute-done.12.refs_0_
  199.4 0.4 copy-done.1
  199.8 14.8 %shard_map.97 = f32[16,192,192]{2,1,0:T(8,128)} custom-call(s32[32]{0:T(128)} %reshape.18.nb_ref, s32[16]{0:T(128)} %compare_select_fusion.2.size_ref, f32[32]{0:T(128)} %reshape.19.fock_ref, f32[16,192,192]{2,1,0:T(8,128)} %collective-permute-done.12.refs_0_, f32[16,192,192]{2,1,0:T(8,128)} %shard_map.96.refs_1_.refs_7_, f32[16,192,192]{2,1,0:T(8,128)} %copy-done.1, ...), custom_call_target="tpu_custom_call" | custom-call | flops 1811939328 | bytes 14155776 | tf_op jit(solution)/shard_map/pallas_call | solution.py:238
  (29 shorter events, 0.6 us)
Async XLA Ops:
  0.6 16.6 %collective-permute-start = (bf16[4,512,256]{2,1,0:T(8,128)(2,1)}, bf16[4,512,256]{2,1,0:T(8,128)(2,1)S(1)}, u32[]{:S(2)}, u32[]{:S(2)}) collective-permute-start(bf16[4,512,256]{2,1,0:T(8,128)(2,1)} %t_own.1), channel_id=1, source_target_pairs={{0,1},{1,2},{2,3},{3,4},{4,5},{5,6},{6,7},{8,9},{9,10},{10,11},{11... | collective-permute-start | bytes 3145736 | tf_op jit(solution)/shard_map/ppermute | solution.py:18
  5.2 16.3 %collective-permute-start.1 = (bf16[4,512,256]{2,1,0:T(8,128)(2,1)}, bf16[4,512,256]{2,1,0:T(8,128)(2,1)S(1)}, u32[]{:S(2)}, u32[]{:S(2)}) collective-permute-start(bf16[4,512,256]{2,1,0:T(8,128)(2,1)} %t_own.1), channel_id=1, source_target_pairs={{1,0},{2,1},{3,2},{4,3},{5,4},{6,5},{7,6},{9,8},{10,9},{11,10},{12... | collective-permute-start | bytes 3145736 | tf_op jit(solution)/shard_map/ppermute | solution.py:19
  17.3 4.3 %copy-start.3 = (bf16[4,512,256]{2,1,0:T(8,128)(2,1)}, bf16[4,512,256]{2,1,0:T(8,128)(2,1)S(1)}, u32[]{:S(2)}) copy-start(bf16[4,512,256]{2,1,0:T(8,128)(2,1)S(1)} %collective-permute-done.t_left) | copy-start | bytes 3145732
  21.6 1.0 copy-start.4
  37.9 14.8 %collective-permute-start.6 = (f32[4,192,192]{2,1,0:T(8,128)}, f32[4,192,192]{2,1,0:T(8,128)}, u32[]{:S(2)}, u32[]{:S(2)}) collective-permute-start(f32[4,192,192]{2,1,0:T(8,128)} %constant_dynamic-slice_fusion.1), channel_id=1, source_target_pairs={{0,16},{8,24},{16,0},{24,8},{1,17},{9,25},{17,1},{25,9},{2,18},{10... | collective-permute-start | bytes 1769480 | tf_op jit(solution)/shard_map/ppermute | solution.py:29
  40.0 15.6 %collective-permute-start.2 = (f32[4,192,192]{2,1,0:T(8,128)}, f32[4,192,192]{2,1,0:T(8,128)}, u32[]{:S(2)}, u32[]{:S(2)}) collective-permute-start(f32[4,192,192]{2,1,0:T(8,128)} %constant_dynamic-slice_fusion.3), channel_id=1, source_target_pairs={{0,8},{8,0},{16,24},{24,16},{1,9},{9,1},{17,25},{25,17},{2,10},{10... | collective-permute-start | bytes 1769480 | tf_op jit(solution)/shard_map/ppermute | solution.py:29
  53.9 3.0 %copy-start.2 = (f32[4,192,192]{2,1,0:T(8,128)}, f32[4,192,192]{2,1,0:T(8,128)S(1)}, u32[]{:S(2)}) copy-start(f32[4,192,192]{2,1,0:T(8,128)S(1)} %dynamic-slice_add_fusion) | copy-start | bytes 1769476
  53.9 10.1 %collective-permute-start.7 = (f32[2,192,192]{2,1,0:T(8,128)S(1)}, f32[2,192,192]{2,1,0:T(8,128)S(1)}, u32[]{:S(2)}, u32[]{:S(2)}) collective-permute-start(f32[2,192,192]{2,1,0:T(8,128)S(1)} %constant_dynamic-slice_fusion), channel_id=1, source_target_pairs={{0,8},{8,0},{16,24},{24,16},{1,9},{9,1},{17,25},{25,17},{2,10},{10... | collective-permute-start | bytes 884744 | tf_op jit(solution)/shard_map/ppermute | solution.py:29
  56.9 9.6 %collective-permute-start.3 = (f32[2,192,192]{2,1,0:T(8,128)S(1)}, f32[2,192,192]{2,1,0:T(8,128)S(1)}, u32[]{:S(2)}, u32[]{:S(2)}) collective-permute-start(f32[2,192,192]{2,1,0:T(8,128)S(1)} %constant_dynamic-slice_fusion.2), channel_id=1, source_target_pairs={{0,16},{8,24},{16,0},{24,8},{1,17},{9,25},{17,1},{25,9},{2,18},{10... | collective-permute-start | bytes 884744 | tf_op jit(solution)/shard_map/ppermute | solution.py:29
  65.2 10.5 %collective-permute-start.8 = (f32[2,192,192]{2,1,0:T(8,128)S(1)}, f32[2,192,192]{2,1,0:T(8,128)S(1)}, u32[]{:S(2)}, u32[]{:S(2)}) collective-permute-start(f32[2,192,192]{2,1,0:T(8,128)S(1)} %get-tuple-element.5), channel_id=1, source_target_pairs={{0,8},{8,0},{16,24},{24,16},{1,9},{9,1},{17,25},{25,17},{2,10},{10... | collective-permute-start | bytes 884744 | tf_op jit(solution)/shard_map/ppermute | solution.py:32
  66.6 11.3 %collective-permute-start.4 = (f32[2,192,192]{2,1,0:T(8,128)S(1)}, f32[2,192,192]{2,1,0:T(8,128)S(1)}, u32[]{:S(2)}, u32[]{:S(2)}) collective-permute-start(f32[2,192,192]{2,1,0:T(8,128)S(1)} %get-tuple-element.3), channel_id=1, source_target_pairs={{0,16},{8,24},{16,0},{24,8},{1,17},{9,25},{17,1},{25,9},{2,18},{10... | collective-permute-start | bytes 884744 | tf_op jit(solution)/shard_map/ppermute | solution.py:32
  75.8 12.2 %collective-permute-start.9 = (f32[4,192,192]{2,1,0:T(8,128)S(1)}, f32[4,192,192]{2,1,0:T(8,128)S(1)}, u32[]{:S(2)}, u32[]{:S(2)}) collective-permute-start(f32[4,192,192]{2,1,0:T(8,128)S(1)} %constant_dynamic-update-slice_fusion.2), channel_id=1, source_target_pairs={{0,16},{8,24},{16,0},{24,8},{1,17},{9,25},{17,1},{25,9},{2,18},{10... | collective-permute-start | bytes 1769480 | tf_op jit(solution)/shard_map/ppermute | solution.py:32
  77.9 10.9 %collective-permute-start.5 = (f32[4,192,192]{2,1,0:T(8,128)S(1)}, f32[4,192,192]{2,1,0:T(8,128)S(1)}, u32[]{:S(2)}, u32[]{:S(2)}) collective-permute-start(f32[4,192,192]{2,1,0:T(8,128)S(1)} %constant_dynamic-update-slice_fusion.6), channel_id=1, source_target_pairs={{0,8},{8,0},{16,24},{24,16},{1,9},{9,1},{17,25},{25,17},{2,10},{10... | collective-permute-start | bytes 1769480 | tf_op jit(solution)/shard_map/ppermute | solution.py:32
  79.5 9.4 %copy-start.5 = (f32[16,192]{1,0:T(8,128)S(1)}, f32[16,192]{1,0:T(8,128)}, u32[]{:S(2)}) copy-start(f32[16,192]{1,0:T(8,128)} %param.12) | copy-start | bytes 36868
  88.9 20.6 %copy-start.7 = (s32[16,2]{0,1:T(2,128)S(1)}, s32[16,2]{0,1:T(2,128)}, u32[]{:S(2)}) copy-start(s32[16,2]{0,1:T(2,128)} %param.14) | copy-start | bytes 388
  88.9 21.4 %copy-start.6 = (f32[16,2]{0,1:T(2,128)S(1)}, f32[16,2]{0,1:T(2,128)}, u32[]{:S(2)}) copy-start(f32[16,2]{0,1:T(2,128)} %param.15) | copy-start | bytes 388
  90.9 52.1 %copy-start = (f32[16,192,192]{2,1,0:T(8,128)}, f32[16,192,192]{2,1,0:T(8,128)S(1)}, u32[]{:S(2)}) copy-start(f32[16,192,192]{2,1,0:T(8,128)S(1)} %get-tuple-element.7.refs_1_.refs_7_) | copy-start | bytes 7077892
  90.9 51.0 %collective-permute-start.11 = (f32[16,192,192]{2,1,0:T(8,128)S(1)}, f32[16,192,192]{2,1,0:T(8,128)}, u32[]{:S(2)}, u32[]{:S(2)}) collective-permute-start(f32[16,192,192]{2,1,0:T(8,128)S(1)} %get-tuple-element.7.refs_1_.refs_7_), channel_id=1, source_target_pairs={{1,0},{2,1},{3,2},{4,3},{5,4},{6,5},{7,6},{9,8},{10,9},{11,10},{12... | collective-permute-start | bytes 7077896 | tf_op jit(solution)/shard_map/ppermute | solution.py:19
  92.8 50.2 %collective-permute-start.10 = (f32[16,192,192]{2,1,0:T(8,128)S(1)}, f32[16,192,192]{2,1,0:T(8,128)}, u32[]{:S(2)}, u32[]{:S(2)}) collective-permute-start(f32[16,192,192]{2,1,0:T(8,128)S(1)} %get-tuple-element.7.refs_1_.refs_7_), channel_id=1, source_target_pairs={{0,1},{1,2},{2,3},{3,4},{4,5},{5,6},{6,7},{8,9},{9,10},{10,11},{11... | collective-permute-start | bytes 7077896 | tf_op jit(solution)/shard_map/ppermute | solution.py:18
  158.2 39.9 %collective-permute-start.13 = (f32[16,192,192]{2,1,0:T(8,128)}, f32[16,192,192]{2,1,0:T(8,128)S(1)}, u32[]{:S(2)}, u32[]{:S(2)}) collective-permute-start(f32[16,192,192]{2,1,0:T(8,128)} %shard_map.96.refs_1_.refs_7_), channel_id=1, source_target_pairs={{1,0},{2,1},{3,2},{4,3},{5,4},{6,5},{7,6},{9,8},{10,9},{11,10},{12... | collective-permute-start | bytes 7077896 | tf_op jit(solution)/shard_map/ppermute | solution.py:19
  160.1 39.3 %collective-permute-start.12 = (f32[16,192,192]{2,1,0:T(8,128)}, f32[16,192,192]{2,1,0:T(8,128)}, u32[]{:S(2)}, u32[]{:S(2)}) collective-permute-start(f32[16,192,192]{2,1,0:T(8,128)} %shard_map.96.refs_1_.refs_7_), channel_id=1, source_target_pairs={{0,1},{1,2},{2,3},{3,4},{4,5},{5,6},{6,7},{8,9},{9,10},{10,11},{11... | collective-permute-start | bytes 7077896 | tf_op jit(solution)/shard_map/ppermute | solution.py:18
  198.1 1.7 copy-start.1

commit v9 on v8

--- a/solution.py
+++ b/solution.py
@@ -37,15 +37,24 @@
     return piece
 
 
-def sum_over_aux(partial):
+def reduce_chunks(partial):
     count = lax.axis_size("aux")
-    if count != 4 or partial.shape[0] % 8:
-        return lax.psum(partial, "aux")
+    pairs = partial.shape[0]
+    if count != 4 or pairs % 16:
+        return [lax.psum(partial, "aux")]
     index = lax.axis_index("aux")
-    half = partial.shape[0] // 2
-    first = halving_stream(partial[:half], index, count, (1, 2))
-    second = halving_stream(partial[half:], index, count, (2, 1))
-    return jnp.concatenate([first, second], axis=0)
+    chunk = pairs // 2
+    stream = chunk // 2
+    results = []
+    pending = partial
+    for c in range(2):
+        part = pending[c * chunk:(c + 1) * chunk]
+        first = halving_stream(part[:stream], index, count, (1, 2))
+        second = halving_stream(part[stream:], index, count, (2, 1))
+        results.append(jnp.concatenate([first, second], axis=0))
+        if c == 0:
+            results[0], pending = lax.optimization_barrier((results[0], pending))
+    return results
 
 
 def class_size(natural_orbital_class):
@@ -61,14 +70,13 @@
 
 
 def fetch_block(sources, width, local, dst, sem):
-    source = local // width
-    block = local % width
-    conditions = (source == 0, (source != 0) & (source != 2), source == 2)
-    for src, condition in zip(sources, conditions):
-
-        @pl.when(condition)
+    index = jnp.clip(local // width, 0, len(sources) - 1)
+    row = local % width
+    for k, src in enumerate(sources):
+
+        @pl.when(index == k)
         def _():
-            pltpu.make_async_copy(src.at[block], dst, sem).start()
+            pltpu.make_async_copy(src.at[row], dst, sem).start()
 
 
 def exchange_kernel(
@@ -157,15 +165,15 @@
     return lax.dot_general(lhs, rhs, dims, preferred_element_type=jnp.float32)
 
 
-def coupling_kernel(nb_ref, size_ref, fock_ref, *refs, final, width, group):
-    sources = refs[:3]
-    margin_ref, ex_ref, col_ref, row_ref, own_ref, out_ref, tbuf, sems, acc_ref = refs[3:]
+def coupling_kernel(nb_ref, size_ref, fock_ref, *refs, final, width, group, start, nsrc):
+    sources = refs[:nsrc]
+    margin_ref, ex_ref, col_ref, row_ref, own_ref, out_ref, tbuf, sems, acc_ref = refs[nsrc:]
     i = pl.program_id(0)
     steps = pl.num_programs(0)
 
     def fetch(step, slot):
         for k in range(2 * group):
-            fetch_block(sources, width, nb_ref[2 * group * step + k], tbuf.at[slot, k], sems.at[slot, k])
+            fetch_block(sources, width, nb_ref[2 * (start + group * step) + k], tbuf.at[slot, k], sems.at[slot, k])
 
     @pl.when(i == 0)
     def _():
@@ -178,11 +186,11 @@
     slot = i % 2
     transposed = (((1,), (1,)), ((), ()))
     for g in range(group):
-        p = i * group + g
+        p = start + i * group + g
         splits = []
         for n in range(2):
             k = 2 * g + n
-            pltpu.make_async_copy(sources[1].at[0], tbuf.at[slot, k], sems.at[slot, k]).wait()
+            pltpu.make_async_copy(sources[0].at[0], tbuf.at[slot, k], sems.at[slot, k]).wait()
             splits.append(split_bf16(tbuf[slot, k]))
         size = size_ref[p]
         acc_ref[...] = jnp.zeros((NPNO, NPNO), jnp.float32)
@@ -209,42 +217,52 @@
             out_ref[g] = amplitudes - residual / denominator
 
 
-def coupling_step(nb, sizes, fock, sources, margin, exchange, energy, own, final):
+def coupling_step(nb, sizes, fock, sources, margin, exchange, energy, own, final, start=0, count=None):
     pairs = own.shape[0]
-    group = next(g for g in (4, 2, 1) if pairs % g == 0)
+    count = pairs if count is None else count
+    group = next(g for g in (4, 2, 1) if count % g == 0 and start % g == 0)
+    base = start // group
     column = energy.reshape(pairs, NPNO, 1)
     row = energy.reshape(pairs, 1, NPNO)
     hbm = pl.BlockSpec(memory_space=pl.ANY)
-    own_spec = pl.BlockSpec((group, NPNO, NPNO), lambda i, q, s, f: (i, 0, 0))
+    own_spec = pl.BlockSpec((group, NPNO, NPNO), lambda i, q, s, f: (i + base, 0, 0))
     grid_spec = pltpu.PrefetchScalarGridSpec(
         num_scalar_prefetch=3,
-        grid=(pairs // group,),
-        in_specs=[hbm] * 3
+        grid=(count // group,),
+        in_specs=[hbm] * len(sources)
         + [
-            pl.BlockSpec((group, 2, NPNO, NPNO), lambda i, q, s, f: (i, 0, 0, 0)),
+            pl.BlockSpec((group, 2, NPNO, NPNO), lambda i, q, s, f: (i + base, 0, 0, 0)),
             own_spec,
-            pl.BlockSpec((group, NPNO, 1), lambda i, q, s, f: (i, 0, 0)),
-            pl.BlockSpec((group, 1, NPNO), lambda i, q, s, f: (i, 0, 0)),
+            pl.BlockSpec((group, NPNO, 1), lambda i, q, s, f: (i + base, 0, 0)),
+            pl.BlockSpec((group, 1, NPNO), lambda i, q, s, f: (i + base, 0, 0)),
             own_spec,
         ],
-        out_specs=own_spec,
+        out_specs=pl.BlockSpec((group, NPNO, NPNO), lambda i, q, s, f: (i, 0, 0)),
         scratch_shapes=[
             pltpu.VMEM((2, 2 * group, NPNO, NPNO), jnp.float32),
             pltpu.SemaphoreType.DMA((2, 2 * group)),
             pltpu.VMEM((NPNO, NPNO), jnp.float32),
         ],
     )
-    flops = pairs * 2 * 4 * 2 * NPNO * NPNO * NPNO
+    flops = count * 2 * 4 * 2 * NPNO * NPNO * NPNO
+    kernel = functools.partial(
+        coupling_kernel, final=final, width=sources[0].shape[0], group=group, start=start, nsrc=len(sources)
+    )
     return pl.pallas_call(
-        functools.partial(coupling_kernel, final=final, width=pairs, group=group),
+        kernel,
         grid_spec=grid_spec,
-        out_shape=jax.ShapeDtypeStruct((pairs, NPNO, NPNO), jnp.float32),
+        out_shape=jax.ShapeDtypeStruct((count, NPNO, NPNO), jnp.float32),
         cost_estimate=pl.CostEstimate(
             flops=flops,
-            bytes_accessed=pairs * NPNO * NPNO * (2 * 4 + 2 * 2 + 3 * 4),
+            bytes_accessed=count * NPNO * NPNO * (2 * 4 + 2 * 2 + 3 * 4),
             transcendentals=0,
         ),
     )(nb, sizes, fock, *sources, margin, exchange, column, row, own)
+
+
+def chunked_halo(chunks):
+    received = [halo_sources(chunk, "pair") for chunk in chunks]
+    return [r[k] for k in range(3) for r in received]
 
 
 def per_device(
@@ -270,20 +288,30 @@
         blocks,
         jnp.swapaxes(pno_coef, 2, 3),
     )
-    exchange_ints = sum_over_aux(partial_ints)
+    exchange_chunks = reduce_chunks(partial_ints)
+    exchange_ints = jnp.concatenate(exchange_chunks, axis=0)
     denominator = pno_energy[:, :, None] + pno_energy[:, None, :]
     local_rows = (neighbour_pairs - (position - 1) * pair_dev).astype(jnp.int32).reshape(-1)
     fock = fock_coupling.reshape(-1)
 
-    amplitudes = -(exchange_ints / denominator)
+    chunk = exchange_chunks[0].shape[0]
+    parts = [
+        -(part / denominator[c * chunk:(c + 1) * chunk]) for c, part in enumerate(exchange_chunks)
+    ]
+    sources = chunked_halo(parts)
+    amplitudes = jnp.concatenate(parts, axis=0)
     for iteration in range(1, ITERS):
-        amplitudes = coupling_step(
-            local_rows, sizes, fock, halo_sources(amplitudes, "pair"), margin, exchange_ints,
-            pno_energy, amplitudes, False,
-        )
+        parts = [
+            coupling_step(
+                local_rows, sizes, fock, sources, margin, exchange_ints, pno_energy, amplitudes,
+                False, c * chunk, chunk,
+            )
+            for c in range(len(parts))
+        ]
+        sources = chunked_halo(parts)
+        amplitudes = jnp.concatenate(parts, axis=0)
     residual = coupling_step(
-        local_rows, sizes, fock, halo_sources(amplitudes, "pair"), margin, exchange_ints,
-        pno_energy, amplitudes, True,
+        local_rows, sizes, fock, sources, margin, exchange_ints, pno_energy, amplitudes, True
     )
     return (amplitudes, residual)
 

time: 215 us -> 220 us (1.023)
  waiting for transfers between devices: 111 us -> 97.4 us
  starting transfers between devices: 42.9 us -> 52.4 us
  Pallas kernels: 42.1 us -> 46.6 us
  other arithmetic: 8.12 us -> 12.5 us
    ppermute x3 -> x5, waiting for transfers between devices: 66.7 us -> 17.5 us  [halo_sources(): from_right = lax.ppermute(cells, axis, [(i + 1, i) for i in range(ends)])]
    ppermute x3 -> x5, waiting for transfers between devices: 9.93 us -> 37.7 us  [halo_sources(): from_left = lax.ppermute(cells, axis, [(i, i + 1) for i in range(ends)])]
    concatenate x1 -> x3, other arithmetic: 2.02 us -> 8.76 us  [the longest x1 5.18 us: per_device(): exchange_ints = jnp.concatenate(exchange_chunks, axis=0)]
    ppermute x4 -> x8, waiting for transfers between devices: 17.1 us -> 23.8 us  [halving_stream(): lax.ppermute(send, 'aux', [(i, i ^ bit) for i in range(count)])]
    ppermute x3 -> x5, starting transfers between devices: 5.75 us -> 12.3 us  [halo_sources(): from_right = lax.ppermute(cells, axis, [(i + 1, i) for i in range(ends)])]
    pallas_call x2 -> x3, Pallas kernels: 29.9 us -> 34.3 us  [coupling_step(): pl.pallas_call(kernel, grid_spec=grid_spec, out_shape=jax.ShapeDtypeStruc...]
    ppermute x4 -> x8, starting transfers between devices: 5.91 us -> 8.27 us  [halving_stream(): other = lax.ppermute(piece, 'aux', [(i, i ^ bit) for i in range(count)])]
    add x2 -> x4, other arithmetic: 2.47 us -> 0.21 us  [halving_stream(): keep + lax.ppermute(send, 'aux', [(i, i ^ bit) for i in range(count)])]
  transfers between devices with their start and end apart: 14 -> 26, of which waited for: 11 -> 23; matrix products, arithmetic and copies ran while one was open for 5% -> 7% of each run, Pallas kernels for 0% -> 4%
where the time goes in v9:
time: 220 us
  waiting for transfers between devices  97.4 us (44%)
  starting transfers between devices  52.4 us (24%)
  Pallas kernels  46.6 us (21%)
  other arithmetic  12.5 us (6%)
  local copies, waits for them, and re-layouts  9.4 us (4%)
    ppermute x5, waiting for transfers between devices, halo_sources(): from_left = lax.ppermute(cells, axis, [(i, i + 1) for i in range(ends)])  37.7 us
    pallas_call x3, Pallas kernels, coupling_step(): pl.pallas_call(kernel, grid_spec=grid_spec, out_shape=jax.ShapeDtypeStruc...  34.3 us
    ppermute x5, starting transfers between devices, halo_sources(): from_left = lax.ppermute(cells, axis, [(i, i + 1) for i in range(ends)])  24 us
    ppermute x8, waiting for transfers between devices, halving_stream(): lax.ppermute(send, 'aux', [(i, i ^ bit) for i in range(count)])  23.8 us
    ppermute x8, waiting for transfers between devices, halving_stream(): other = lax.ppermute(piece, 'aux', [(i, i ^ bit) for i in range(count)])  18.4 us
    ppermute x5, waiting for transfers between devices, halo_sources(): from_right = lax.ppermute(cells, axis, [(i + 1, i) for i in range(ends)])  17.5 us
    ppermute x5, starting transfers between devices, halo_sources(): from_right = lax.ppermute(cells, axis, [(i + 1, i) for i in range(ends)])  12.3 us
    pallas_call x1, Pallas kernels, partial_exchange(): pl.pallas_call(functools.partial(exchange_kernel, occ=occ, group=group),...  12.3 us
  transfers between devices with their start and end apart: 26, of which 23 were waited for; matrix products, arithmetic and copies ran while one was open for 7% of the time, Pallas kernels for 4%

profile of v9, /device:TPU:1, one launch (start us, length us, event | category | flops | bytes accessed | tf_op | source)
XLA Modules:
  0.0 219.6 jit_solution(10769360927802499810)
XLA Ops:
  0.6 4.6 %collective-permute-start = (bf16[4,512,256]{2,1,0:T(8,128)(2,1)}, bf16[4,512,256]{2,1,0:T(8,128)(2,1)S(1)}, u32[]{:S(2)}, u32[]{:S(2)}) collective-permute-start(bf16[4,512,256]{2,1,0:T(8,128)(2,1)} %t_own.1), channel_id=1, source_target_pairs={{0,1},{1,2},{2,3},{3,4},{4,5},{5,6},{6,7},{8,9},{9,10},{10,11},{11... | collective-permute-start | bytes 3145736 | tf_op jit(solution)/shard_map/ppermute | solution.py:18
  5.2 1.9 collective-permute-start.1
  7.2 1.2 compare_select_fusion.2.size_ref
  9.7 7.6 %collective-permute-done.t_left = bf16[4,512,256]{2,1,0:T(8,128)(2,1)S(1)} collective-permute-done((bf16[4,512,256]{2,1,0:T(8,128)(2,1)}, bf16[4,512,256]{2,1,0:T(8,128)(2,1)S(1)}, u32[]{:S(2)}, u32[]{:S(2)}) %collective-permute-start) | collective-permute-done | bytes 1048608 | tf_op jit(solution)/shard_map/ppermute | solution.py:18
  17.3 4.3 %collective-permute-done.1.t_right = bf16[4,512,256]{2,1,0:T(8,128)(2,1)S(1)} collective-permute-done((bf16[4,512,256]{2,1,0:T(8,128)(2,1)}, bf16[4,512,256]{2,1,0:T(8,128)(2,1)S(1)}, u32[]{:S(2)}, u32[]{:S(2)}) %collective-permute-start.1) | collective-permute-done | bytes 1048608 | tf_op jit(solution)/shard_map/ppermute | solution.py:19
  22.6 12.3 %shard_map.95 = f32[16,192,192]{2,1,0:T(8,128)} custom-call(s32[16]{0:T(128)} %get-tuple-element.21.lead_ref, s32[16]{0:T(128)} %get-tuple-element.20.trail_ref, s32[16]{0:T(128)} %compare_select_fusion.2.size_ref, bf16[4,512,256]{2,1,0:T(8,128)(2,1)} %copy-done.8, bf16[4,512,256]{2,1,0:T(8,128)(2,1)} %t_own.1, bf16[4,512,256]{2,1,0:T(8,128)(2,1)} %copy-done.9, ...), custom_call_target="tpu_custom_call" | custom-call | flops 2214592512 | bytes 13893632 | tf_op jit(solution)/shard_map/pallas_call | solution.py:146
  34.8 1.5 fusion.3
  36.4 1.3 collective-permute-start.2
  37.7 1.3 collective-permute-start.6
  39.0 4.9 %collective-permute-done.2 = f32[2,192,192]{2,1,0:T(8,128)S(1)} collective-permute-done((f32[2,192,192]{2,1,0:T(8,128)S(1)}, f32[2,192,192]{2,1,0:T(8,128)S(1)}, u32[]{:S(2)}, u32[]{:S(2)}) %collective-permute-start.2) | collective-permute-done | bytes 294944 | tf_op jit(solution)/shard_map/ppermute | solution.py:29
  44.0 1.3 collective-permute-start.3
  45.3 1.2 collective-permute-done.6
  47.3 1.3 collective-permute-done.3
  48.7 1.3 collective-permute-start.4
  50.0 3.6 %collective-permute-done.7 = f32[1,192,192]{2,1,0:T(8,128)S(1)} collective-permute-done((f32[1,192,192]{2,1,0:T(8,128)S(1)}, f32[1,192,192]{2,1,0:T(8,128)S(1)}, u32[]{:S(2)}, u32[]{:S(2)}) %collective-permute-start.7) | collective-permute-done | bytes 147488 | tf_op jit(solution)/shard_map/ppermute | solution.py:29
  53.8 1.8 collective-permute-done.4
  55.6 1.8 collective-permute-start.5
  58.3 1.3 collective-permute-start.9
  59.8 3.6 %collective-permute-done.5 = f32[2,192,192]{2,1,0:T(8,128)S(1)} collective-permute-done((f32[2,192,192]{2,1,0:T(8,128)S(1)}, f32[2,192,192]{2,1,0:T(8,128)S(1)}, u32[]{:S(2)}, u32[]{:S(2)}) %collective-permute-start.5) | collective-permute-done | bytes 294944 | tf_op jit(solution)/shard_map/ppermute | solution.py:32
  63.4 3.6 %collective-permute-done.9 = f32[2,192,192]{2,1,0:T(8,128)S(1)} collective-permute-done((f32[2,192,192]{2,1,0:T(8,128)S(1)}, f32[2,192,192]{2,1,0:T(8,128)S(1)}, u32[]{:S(2)}, u32[]{:S(2)}) %collective-permute-start.9) | collective-permute-done | bytes 294944 | tf_op jit(solution)/shard_map/ppermute | solution.py:32
  67.2 1.7 copy-done.4
  69.2 1.5 collective-permute-start.15
  70.7 7.4 %collective-permute-done.11 = f32[2,192,192]{2,1,0:T(8,128)S(1)} collective-permute-done((f32[2,192,192]{2,1,0:T(8,128)S(1)}, f32[2,192,192]{2,1,0:T(8,128)S(1)}, u32[]{:S(2)}, u32[]{:S(2)}) %collective-permute-start.11) | collective-permute-done | bytes 294944 | tf_op jit(solution)/shard_map/ppermute | solution.py:29
  78.3 1.5 collective-permute-start.12
  80.0 3.2 %collective-permute-done.12 = f32[1,192,192]{2,1,0:T(8,128)S(1)} collective-permute-done((f32[1,192,192]{2,1,0:T(8,128)S(1)}, f32[1,192,192]{2,1,0:T(8,128)S(1)}, u32[]{:S(2)}, u32[]{:S(2)}) %collective-permute-start.12) | collective-permute-done | bytes 147488 | tf_op jit(solution)/shard_map/ppermute | solution.py:29
  83.2 1.5 collective-permute-start.13
  84.8 2.2 %collective-permute-done.16 = f32[1,192,192]{2,1,0:T(8,128)S(1)} collective-permute-done((f32[1,192,192]{2,1,0:T(8,128)S(1)}, f32[1,192,192]{2,1,0:T(8,128)S(1)}, u32[]{:S(2)}, u32[]{:S(2)}) %collective-permute-start.16) | collective-permute-done | bytes 147488 | tf_op jit(solution)/shard_map/ppermute | solution.py:29
  89.2 2.8 %collective-permute-done.17 = f32[1,192,192]{2,1,0:T(8,128)S(1)} collective-permute-done((f32[1,192,192]{2,1,0:T(8,128)S(1)}, f32[1,192,192]{2,1,0:T(8,128)S(1)}, u32[]{:S(2)}, u32[]{:S(2)}) %collective-permute-start.17) | collective-permute-done | bytes 147488 | tf_op jit(solution)/shard_map/ppermute | solution.py:32
  93.2 2.6 %collective-permute-done.14 = f32[2,192,192]{2,1,0:T(8,128)S(1)} collective-permute-done((f32[2,192,192]{2,1,0:T(8,128)S(1)}, f32[2,192,192]{2,1,0:T(8,128)S(1)}, u32[]{:S(2)}, u32[]{:S(2)}) %collective-permute-start.14) | collective-permute-done | bytes 294944 | tf_op jit(solution)/shard_map/ppermute | solution.py:32
  95.9 2.7 %collective-permute-done.18 = f32[2,192,192]{2,1,0:T(8,128)S(1)} collective-permute-done((f32[2,192,192]{2,1,0:T(8,128)S(1)}, f32[2,192,192]{2,1,0:T(8,128)S(1)}, u32[]{:S(2)}, u32[]{:S(2)}) %collective-permute-start.18) | collective-permute-done | bytes 294944 | tf_op jit(solution)/shard_map/ppermute | solution.py:32
  99.6 11.8 %collective-permute-start.10 = (f32[8,192,192]{2,1,0:T(8,128)S(1)}, f32[8,192,192]{2,1,0:T(8,128)}, u32[]{:S(2)}, u32[]{:S(2)}) collective-permute-start(f32[8,192,192]{2,1,0:T(8,128)S(1)} %get-tuple-element.15.refs_2_), channel_id=1, source_target_pairs={{0,1},{1,2},{2,3},{3,4},{4,5},{5,6},{6,7},{8,9},{9,10},{10,11},{11... | collective-permute-start | bytes 3538952 | tf_op jit(solution)/shard_map/ppermute | solution.py:18
  111.4 1.9 collective-permute-start.19
  113.3 3.6 %collective-permute-start.20 = (f32[8,192,192]{2,1,0:T(8,128)S(1)}, f32[8,192,192]{2,1,0:T(8,128)}, u32[]{:S(2)}, u32[]{:S(2)}) collective-permute-start(f32[8,192,192]{2,1,0:T(8,128)S(1)} %get-tuple-element.15.refs_2_), channel_id=1, source_target_pairs={{1,0},{2,1},{3,2},{4,3},{5,4},{6,5},{7,6},{9,8},{10,9},{11,10},{12... | collective-permute-start | bytes 3538952 | tf_op jit(solution)/shard_map/ppermute | solution.py:19
  117.0 2.1 collective-permute-start.21
  120.4 1.7 copy.14.refs_8_
  122.8 5.2 %pad_maximum_fusion = (f32[16,192,192]{2,1,0:T(8,128)}, f32[16,192,192]{2,1,0:T(8,128)}) fusion(f32[4,192,192]{2,1,0:T(8,128)} %copy-done.5, f32[4,192,192]{2,1,0:T(8,128)} %copy-done.6, f32[8,192,192]{2,1,0:T(8,128)} %copy-done.2, f32[8,192,192]{2,1,0:T(8,128)S(1)} %get-tuple-element.14.refs_3_, f32[8,192,192]{2,1,0:T(8,128)S(1)} %get-tuple-element.15.refs_2_), kind=kLoop, calls=%fused_computation | loop fusion | flops 1769472 | bytes 9437184 | tf_op jit(solution)/shard_map/concatenate | solution.py:292
  128.8 16.9 %collective-permute-done.19.refs_1_ = f32[8,192,192]{2,1,0:T(8,128)} collective-permute-done((f32[8,192,192]{2,1,0:T(8,128)S(1)}, f32[8,192,192]{2,1,0:T(8,128)}, u32[]{:S(2)}, u32[]{:S(2)}) %collective-permute-start.19) | collective-permute-done | bytes 1179680 | tf_op jit(solution)/shard_map/ppermute | solution.py:18
  145.6 8.1 %collective-permute-done.21.refs_5_ = f32[8,192,192]{2,1,0:T(8,128)} collective-permute-done((f32[8,192,192]{2,1,0:T(8,128)S(1)}, f32[8,192,192]{2,1,0:T(8,128)}, u32[]{:S(2)}, u32[]{:S(2)}) %collective-permute-start.21) | collective-permute-done | bytes 1179680 | tf_op jit(solution)/shard_map/ppermute | solution.py:19
  153.7 9.8 %shard_map.96.refs_2_ = f32[8,192,192]{2,1,0:T(8,128)} custom-call(s32[32]{0:T(128)} %reshape.20.nb_ref, s32[16]{0:T(128)} %compare_select_fusion.2.size_ref, f32[32]{0:T(128)} %reshape.21.fock_ref, f32[8,192,192]{2,1,0:T(8,128)} %collective-permute-done.10.refs_0_, f32[8,192,192]{2,1,0:T(8,128)} %collective-permute-done.19.refs_1_, ...), custom_call_target="tpu_custom_call" | custom-call | flops 905969664 | bytes 7077888 | tf_op jit(solution)/shard_map/pallas_call | solution.py:251
  163.5 2.2 collective-permute-start.22
  165.7 2.4 %collective-permute-start.24 = (f32[8,192,192]{2,1,0:T(8,128)}, f32[8,192,192]{2,1,0:T(8,128)}, u32[]{:S(2)}, u32[]{:S(2)}) collective-permute-start(f32[8,192,192]{2,1,0:T(8,128)} %shard_map.96.refs_2_), channel_id=1, source_target_pairs={{1,0},{2,1},{3,2},{4,3},{5,4},{6,5},{7,6},{9,8},{10,9},{11,10},{12... | collective-permute-start | bytes 3538952 | tf_op jit(solution)/shard_map/ppermute | solution.py:19
  168.1 9.8 %shard_map.97.refs_3_ = f32[8,192,192]{2,1,0:T(8,128)} custom-call(s32[32]{0:T(128)} %reshape.20.nb_ref, s32[16]{0:T(128)} %compare_select_fusion.2.size_ref, f32[32]{0:T(128)} %reshape.21.fock_ref, f32[8,192,192]{2,1,0:T(8,128)} %collective-permute-done.10.refs_0_, f32[8,192,192]{2,1,0:T(8,128)} %collective-permute-done.19.refs_1_, ...), custom_call_target="tpu_custom_call" | custom-call | flops 905969664 | bytes 7077888 | tf_op jit(solution)/shard_map/pallas_call | solution.py:251
  177.9 3.5 %collective-permute-start.23 = (f32[8,192,192]{2,1,0:T(8,128)}, f32[8,192,192]{2,1,0:T(8,128)}, u32[]{:S(2)}, u32[]{:S(2)}) collective-permute-start(f32[8,192,192]{2,1,0:T(8,128)} %shard_map.97.refs_3_), channel_id=1, source_target_pairs={{0,1},{1,2},{2,3},{3,4},{4,5},{5,6},{6,7},{8,9},{9,10},{10,11},{11... | collective-permute-start | bytes 3538952 | tf_op jit(solution)/shard_map/ppermute | solution.py:18
  181.4 2.3 %collective-permute-start.25 = (f32[8,192,192]{2,1,0:T(8,128)}, f32[8,192,192]{2,1,0:T(8,128)}, u32[]{:S(2)}, u32[]{:S(2)}) collective-permute-start(f32[8,192,192]{2,1,0:T(8,128)} %shard_map.97.refs_3_), channel_id=1, source_target_pairs={{1,0},{2,1},{3,2},{4,3},{5,4},{6,5},{7,6},{9,8},{10,9},{11,10},{12... | collective-permute-start | bytes 3538952 | tf_op jit(solution)/shard_map/ppermute | solution.py:19
  183.7 3.4 %pad_maximum_fusion.2.refs_10_ = f32[16,192,192]{2,1,0:T(8,128)} fusion(f32[8,192,192]{2,1,0:T(8,128)} %shard_map.97.refs_3_, f32[8,192,192]{2,1,0:T(8,128)S(1)} %copy-done.3), kind=kLoop, calls=%fused_computation.2 | loop fusion | flops 589824 | bytes 4718592 | tf_op jit(solution)/shard_map/concatenate | solution.py:312
  187.8 12.5 %collective-permute-done.23.refs_1_ = f32[8,192,192]{2,1,0:T(8,128)} collective-permute-done((f32[8,192,192]{2,1,0:T(8,128)}, f32[8,192,192]{2,1,0:T(8,128)}, u32[]{:S(2)}, u32[]{:S(2)}) %collective-permute-start.23) | collective-permute-done | bytes 1179680 | tf_op jit(solution)/shard_map/ppermute | solution.py:18
  200.2 4.4 %collective-permute-done.25.refs_5_ = f32[8,192,192]{2,1,0:T(8,128)} collective-permute-done((f32[8,192,192]{2,1,0:T(8,128)}, f32[8,192,192]{2,1,0:T(8,128)}, u32[]{:S(2)}, u32[]{:S(2)}) %collective-permute-start.25) | collective-permute-done | bytes 1179680 | tf_op jit(solution)/shard_map/ppermute | solution.py:19
  204.6 14.8 %shard_map.98 = f32[16,192,192]{2,1,0:T(8,128)} custom-call(s32[32]{0:T(128)} %reshape.20.nb_ref, s32[16]{0:T(128)} %compare_select_fusion.2.size_ref, f32[32]{0:T(128)} %reshape.21.fock_ref, f32[8,192,192]{2,1,0:T(8,128)} %copy-done.7, f32[8,192,192]{2,1,0:T(8,128)} %collective-permute-done.23.refs_1_, f32[8,192,192]{2,1,0:T(8,128)} %shard_map.96.refs_2_, ...), custom_call_target="tpu_custom_call" | custom-call | flops 1811939328 | bytes 14155776 | tf_op jit(solution)/shard_map/pallas_call | solution.py:251
  (87 shorter events, 13.1 us)
Async XLA Ops:
  0.6 16.6 %collective-permute-start = (bf16[4,512,256]{2,1,0:T(8,128)(2,1)}, bf16[4,512,256]{2,1,0:T(8,128)(2,1)S(1)}, u32[]{:S(2)}, u32[]{:S(2)}) collective-permute-start(bf16[4,512,256]{2,1,0:T(8,128)(2,1)} %t_own.1), channel_id=1, source_target_pairs={{0,1},{1,2},{2,3},{3,4},{4,5},{5,6},{6,7},{8,9},{9,10},{10,11},{11... | collective-permute-start | bytes 3145736 | tf_op jit(solution)/shard_map/ppermute | solution.py:18
  5.2 16.3 %collective-permute-start.1 = (bf16[4,512,256]{2,1,0:T(8,128)(2,1)}, bf16[4,512,256]{2,1,0:T(8,128)(2,1)S(1)}, u32[]{:S(2)}, u32[]{:S(2)}) collective-permute-start(bf16[4,512,256]{2,1,0:T(8,128)(2,1)} %t_own.1), channel_id=1, source_target_pairs={{1,0},{2,1},{3,2},{4,3},{5,4},{6,5},{7,6},{9,8},{10,9},{11,10},{12... | collective-permute-start | bytes 3145736 | tf_op jit(solution)/shard_map/ppermute | solution.py:19
  17.3 4.3 %copy-start.8 = (bf16[4,512,256]{2,1,0:T(8,128)(2,1)}, bf16[4,512,256]{2,1,0:T(8,128)(2,1)S(1)}, u32[]{:S(2)}) copy-start(bf16[4,512,256]{2,1,0:T(8,128)(2,1)S(1)} %collective-permute-done.t_left) | copy-start | bytes 3145732
  21.6 1.0 copy-start.9
  36.4 7.5 %collective-permute-start.2 = (f32[2,192,192]{2,1,0:T(8,128)S(1)}, f32[2,192,192]{2,1,0:T(8,128)S(1)}, u32[]{:S(2)}, u32[]{:S(2)}) collective-permute-start(f32[2,192,192]{2,1,0:T(8,128)S(1)} %constant_dynamic-slice_fusion.7), channel_id=1, source_target_pairs={{0,8},{8,0},{16,24},{24,16},{1,9},{9,1},{17,25},{25,17},{2,10},{10... | collective-permute-start | bytes 884744 | tf_op jit(solution)/shard_map/ppermute | solution.py:29
  37.7 8.8 %collective-permute-start.6 = (f32[2,192,192]{2,1,0:T(8,128)S(1)}, f32[2,192,192]{2,1,0:T(8,128)S(1)}, u32[]{:S(2)}, u32[]{:S(2)}) collective-permute-start(f32[2,192,192]{2,1,0:T(8,128)S(1)} %constant_dynamic-slice_fusion.5), channel_id=1, source_target_pairs={{0,16},{8,24},{16,0},{24,8},{1,17},{9,25},{17,1},{25,9},{2,18},{10... | collective-permute-start | bytes 884744 | tf_op jit(solution)/shard_map/ppermute | solution.py:29
  44.0 4.6 %collective-permute-start.3 = (f32[1,192,192]{2,1,0:T(8,128)S(1)}, f32[1,192,192]{2,1,0:T(8,128)S(1)}, u32[]{:S(2)}, u32[]{:S(2)}) collective-permute-start(f32[1,192,192]{2,1,0:T(8,128)S(1)} %constant_dynamic-slice_fusion.6), channel_id=1, source_target_pairs={{0,16},{8,24},{16,0},{24,8},{1,17},{9,25},{17,1},{25,9},{2,18},{10... | collective-permute-start | bytes 442376 | tf_op jit(solution)/shard_map/ppermute | solution.py:29
  46.6 7.0 %collective-permute-start.7 = (f32[1,192,192]{2,1,0:T(8,128)S(1)}, f32[1,192,192]{2,1,0:T(8,128)S(1)}, u32[]{:S(2)}, u32[]{:S(2)}) collective-permute-start(f32[1,192,192]{2,1,0:T(8,128)S(1)} %constant_dynamic-slice_fusion.4), channel_id=1, source_target_pairs={{0,8},{8,0},{16,24},{24,16},{1,9},{9,1},{17,25},{25,17},{2,10},{10... | collective-permute-start | bytes 442376 | tf_op jit(solution)/shard_map/ppermute | solution.py:29
  48.7 6.9 %collective-permute-start.4 = (f32[1,192,192]{2,1,0:T(8,128)S(1)}, f32[1,192,192]{2,1,0:T(8,128)S(1)}, u32[]{:S(2)}, u32[]{:S(2)}) collective-permute-start(f32[1,192,192]{2,1,0:T(8,128)S(1)} %get-tuple-element.11), channel_id=1, source_target_pairs={{0,16},{8,24},{16,0},{24,8},{1,17},{9,25},{17,1},{25,9},{2,18},{10... | collective-permute-start | bytes 442376 | tf_op jit(solution)/shard_map/ppermute | solution.py:32
  53.7 4.6 %collective-permute-start.8 = (f32[1,192,192]{2,1,0:T(8,128)S(1)}, f32[1,192,192]{2,1,0:T(8,128)S(1)}, u32[]{:S(2)}, u32[]{:S(2)}) collective-permute-start(f32[1,192,192]{2,1,0:T(8,128)S(1)} %get-tuple-element.13), channel_id=1, source_target_pairs={{0,8},{8,0},{16,24},{24,16},{1,9},{9,1},{17,25},{25,17},{2,10},{10... | collective-permute-start | bytes 442376 | tf_op jit(solution)/shard_map/ppermute | solution.py:32
  55.6 7.8 %collective-permute-start.5 = (f32[2,192,192]{2,1,0:T(8,128)S(1)}, f32[2,192,192]{2,1,0:T(8,128)S(1)}, u32[]{:S(2)}, u32[]{:S(2)}) collective-permute-start(f32[2,192,192]{2,1,0:T(8,128)S(1)} %constant_dynamic-update-slice_fusion.14), channel_id=1, source_target_pairs={{0,8},{8,0},{16,24},{24,16},{1,9},{9,1},{17,25},{25,17},{2,10},{10... | collective-permute-start | bytes 884744 | tf_op jit(solution)/shard_map/ppermute | solution.py:32
  58.3 8.7 %collective-permute-start.9 = (f32[2,192,192]{2,1,0:T(8,128)S(1)}, f32[2,192,192]{2,1,0:T(8,128)S(1)}, u32[]{:S(2)}, u32[]{:S(2)}) collective-permute-start(f32[2,192,192]{2,1,0:T(8,128)S(1)} %constant_dynamic-update-slice_fusion.10), channel_id=1, source_target_pairs={{0,16},{8,24},{16,0},{24,8},{1,17},{9,25},{17,1},{25,9},{2,18},{10... | collective-permute-start | bytes 884744 | tf_op jit(solution)/shard_map/ppermute | solution.py:32
  67.0 1.9 copy-start.4
  68.9 29.7 %copy-start.2 = (f32[8,192,192]{2,1,0:T(8,128)}, f32[8,192,192]{2,1,0:T(8,128)S(1)}, u32[]{:S(2)}) copy-start(f32[8,192,192]{2,1,0:T(8,128)S(1)} %pad_maximum_fusion.3) | copy-start | bytes 3538948
  69.1 9.1 %collective-permute-start.11 = (f32[2,192,192]{2,1,0:T(8,128)S(1)}, f32[2,192,192]{2,1,0:T(8,128)S(1)}, u32[]{:S(2)}, u32[]{:S(2)}) collective-permute-start(f32[2,192,192]{2,1,0:T(8,128)S(1)} %constant_dynamic-slice_fusion.3), channel_id=1, source_target_pairs={{0,8},{8,0},{16,24},{24,16},{1,9},{9,1},{17,25},{25,17},{2,10},{10... | collective-permute-start | bytes 884744 | tf_op jit(solution)/shard_map/ppermute | solution.py:29
  69.2 10.6 %collective-permute-start.15 = (f32[2,192,192]{2,1,0:T(8,128)S(1)}, f32[2,192,192]{2,1,0:T(8,128)S(1)}, u32[]{:S(2)}, u32[]{:S(2)}) collective-permute-start(f32[2,192,192]{2,1,0:T(8,128)S(1)} %constant_dynamic-slice_fusion.1), channel_id=1, source_target_pairs={{0,16},{8,24},{16,0},{24,8},{1,17},{9,25},{17,1},{25,9},{2,18},{10... | collective-permute-start | bytes 884744 | tf_op jit(solution)/shard_map/ppermute | solution.py:29
  78.3 4.9 %collective-permute-start.12 = (f32[1,192,192]{2,1,0:T(8,128)S(1)}, f32[1,192,192]{2,1,0:T(8,128)S(1)}, u32[]{:S(2)}, u32[]{:S(2)}) collective-permute-start(f32[1,192,192]{2,1,0:T(8,128)S(1)} %constant_dynamic-slice_fusion.2), channel_id=1, source_target_pairs={{0,16},{8,24},{16,0},{24,8},{1,17},{9,25},{17,1},{25,9},{2,18},{10... | collective-permute-start | bytes 442376 | tf_op jit(solution)/shard_map/ppermute | solution.py:29
  79.9 7.3 %copy-start.10 = (f32[16,192]{1,0:T(8,128)S(1)}, f32[16,192]{1,0:T(8,128)}, u32[]{:S(2)}) copy-start(f32[16,192]{1,0:T(8,128)} %param.12) | copy-start | bytes 36868
  79.9 7.1 %collective-permute-start.16 = (f32[1,192,192]{2,1,0:T(8,128)S(1)}, f32[1,192,192]{2,1,0:T(8,128)S(1)}, u32[]{:S(2)}, u32[]{:S(2)}) collective-permute-start(f32[1,192,192]{2,1,0:T(8,128)S(1)} %constant_dynamic-slice_fusion), channel_id=1, source_target_pairs={{0,8},{8,0},{16,24},{24,16},{1,9},{9,1},{17,25},{25,17},{2,10},{10... | collective-permute-start | bytes 442376 | tf_op jit(solution)/shard_map/ppermute | solution.py:29
  83.2 4.9 %collective-permute-start.13 = (f32[1,192,192]{2,1,0:T(8,128)S(1)}, f32[1,192,192]{2,1,0:T(8,128)S(1)}, u32[]{:S(2)}, u32[]{:S(2)}) collective-permute-start(f32[1,192,192]{2,1,0:T(8,128)S(1)} %get-tuple-element.7), channel_id=1, source_target_pairs={{0,16},{8,24},{16,0},{24,8},{1,17},{9,25},{17,1},{25,9},{2,18},{10... | collective-permute-start | bytes 442376 | tf_op jit(solution)/shard_map/ppermute | solution.py:32
  87.0 4.9 %collective-permute-start.17 = (f32[1,192,192]{2,1,0:T(8,128)S(1)}, f32[1,192,192]{2,1,0:T(8,128)S(1)}, u32[]{:S(2)}, u32[]{:S(2)}) collective-permute-start(f32[1,192,192]{2,1,0:T(8,128)S(1)} %get-tuple-element.9), channel_id=1, source_target_pairs={{0,8},{8,0},{16,24},{24,16},{1,9},{9,1},{17,25},{25,17},{2,10},{10... | collective-permute-start | bytes 442376 | tf_op jit(solution)/shard_map/ppermute | solution.py:32
  88.1 7.7 %collective-permute-start.14 = (f32[2,192,192]{2,1,0:T(8,128)S(1)}, f32[2,192,192]{2,1,0:T(8,128)S(1)}, u32[]{:S(2)}, u32[]{:S(2)}) collective-permute-start(f32[2,192,192]{2,1,0:T(8,128)S(1)} %constant_dynamic-update-slice_fusion.6), channel_id=1, source_target_pairs={{0,8},{8,0},{16,24},{24,16},{1,9},{9,1},{17,25},{25,17},{2,10},{10... | collective-permute-start | bytes 884744 | tf_op jit(solution)/shard_map/ppermute | solution.py:32
  91.9 6.7 %collective-permute-start.18 = (f32[2,192,192]{2,1,0:T(8,128)S(1)}, f32[2,192,192]{2,1,0:T(8,128)S(1)}, u32[]{:S(2)}, u32[]{:S(2)}) collective-permute-start(f32[2,192,192]{2,1,0:T(8,128)S(1)} %constant_dynamic-update-slice_fusion.2), channel_id=1, source_target_pairs={{0,16},{8,24},{16,0},{24,8},{1,17},{9,25},{17,1},{25,9},{2,18},{10... | collective-permute-start | bytes 884744 | tf_op jit(solution)/shard_map/ppermute | solution.py:32
  95.9 3.3 %copy-start.6 = (f32[4,192,192]{2,1,0:T(8,128)}, f32[4,192,192]{2,1,0:T(8,128)S(1)}, u32[]{:S(2)}) copy-start(f32[4,192,192]{2,1,0:T(8,128)S(1)} %constant_dynamic-update-slice_fusion.4) | copy-start | bytes 1769476
  98.7 0.9 copy-start.5
  98.7 21.0 %copy-start.12 = (s32[16,2]{0,1:T(2,128)S(1)}, s32[16,2]{0,1:T(2,128)}, u32[]{:S(2)}) copy-start(s32[16,2]{0,1:T(2,128)} %param.14) | copy-start | bytes 388
  99.6 28.4 %copy-start = (f32[8,192,192]{2,1,0:T(8,128)}, f32[8,192,192]{2,1,0:T(8,128)S(1)}, u32[]{:S(2)}) copy-start(f32[8,192,192]{2,1,0:T(8,128)S(1)} %get-tuple-element.14.refs_3_) | copy-start | bytes 3538948
  99.6 28.4 %copy-start.1 = (f32[8,192,192]{2,1,0:T(8,128)}, f32[8,192,192]{2,1,0:T(8,128)S(1)}, u32[]{:S(2)}) copy-start(f32[8,192,192]{2,1,0:T(8,128)S(1)} %get-tuple-element.15.refs_2_) | copy-start | bytes 3538948
  99.6 22.5 %copy-start.11 = (f32[16,2]{0,1:T(2,128)S(1)}, f32[16,2]{0,1:T(2,128)}, u32[]{:S(2)}) copy-start(f32[16,2]{0,1:T(2,128)} %param.15) | copy-start | bytes 388
  99.6 29.2 %collective-permute-start.10 = (f32[8,192,192]{2,1,0:T(8,128)S(1)}, f32[8,192,192]{2,1,0:T(8,128)}, u32[]{:S(2)}, u32[]{:S(2)}) collective-permute-start(f32[8,192,192]{2,1,0:T(8,128)S(1)} %get-tuple-element.15.refs_2_), channel_id=1, source_target_pairs={{0,1},{1,2},{2,3},{3,4},{4,5},{5,6},{6,7},{8,9},{9,10},{10,11},{11... | collective-permute-start | bytes 3538952 | tf_op jit(solution)/shard_map/ppermute | solution.py:18
  111.4 34.2 %collective-permute-start.19 = (f32[8,192,192]{2,1,0:T(8,128)S(1)}, f32[8,192,192]{2,1,0:T(8,128)}, u32[]{:S(2)}, u32[]{:S(2)}) collective-permute-start(f32[8,192,192]{2,1,0:T(8,128)S(1)} %get-tuple-element.14.refs_3_), channel_id=1, source_target_pairs={{0,1},{1,2},{2,3},{3,4},{4,5},{5,6},{6,7},{8,9},{9,10},{10,11},{11... | collective-permute-start | bytes 3538952 | tf_op jit(solution)/shard_map/ppermute | solution.py:18
  113.3 32.3 %collective-permute-start.20 = (f32[8,192,192]{2,1,0:T(8,128)S(1)}, f32[8,192,192]{2,1,0:T(8,128)}, u32[]{:S(2)}, u32[]{:S(2)}) collective-permute-start(f32[8,192,192]{2,1,0:T(8,128)S(1)} %get-tuple-element.15.refs_2_), channel_id=1, source_target_pairs={{1,0},{2,1},{3,2},{4,3},{5,4},{6,5},{7,6},{9,8},{10,9},{11,10},{12... | collective-permute-start | bytes 3538952 | tf_op jit(solution)/shard_map/ppermute | solution.py:19
  117.0 36.7 %collective-permute-start.21 = (f32[8,192,192]{2,1,0:T(8,128)S(1)}, f32[8,192,192]{2,1,0:T(8,128)}, u32[]{:S(2)}, u32[]{:S(2)}) collective-permute-start(f32[8,192,192]{2,1,0:T(8,128)S(1)} %get-tuple-element.14.refs_3_), channel_id=1, source_target_pairs={{1,0},{2,1},{3,2},{4,3},{5,4},{6,5},{7,6},{9,8},{10,9},{11,10},{12... | collective-permute-start | bytes 3538952 | tf_op jit(solution)/shard_map/ppermute | solution.py:19
  163.5 20.1 %copy-start.3 = (f32[8,192,192]{2,1,0:T(8,128)S(1)}, f32[8,192,192]{2,1,0:T(8,128)}, u32[]{:S(2)}) copy-start(f32[8,192,192]{2,1,0:T(8,128)} %shard_map.96.refs_2_) | copy-start | bytes 3538948
  163.5 23.5 %collective-permute-start.22 = (f32[8,192,192]{2,1,0:T(8,128)}, f32[8,192,192]{2,1,0:T(8,128)S(1)}, u32[]{:S(2)}, u32[]{:S(2)}) collective-permute-start(f32[8,192,192]{2,1,0:T(8,128)} %shard_map.96.refs_2_), channel_id=1, source_target_pairs={{0,1},{1,2},{2,3},{3,4},{4,5},{5,6},{6,7},{8,9},{9,10},{10,11},{11... | collective-permute-start | bytes 3538952 | tf_op jit(solution)/shard_map/ppermute | solution.py:18
  165.7 22.1 %collective-permute-start.24 = (f32[8,192,192]{2,1,0:T(8,128)}, f32[8,192,192]{2,1,0:T(8,128)}, u32[]{:S(2)}, u32[]{:S(2)}) collective-permute-start(f32[8,192,192]{2,1,0:T(8,128)} %shard_map.96.refs_2_), channel_id=1, source_target_pairs={{1,0},{2,1},{3,2},{4,3},{5,4},{6,5},{7,6},{9,8},{10,9},{11,10},{12... | collective-permute-start | bytes 3538952 | tf_op jit(solution)/shard_map/ppermute | solution.py:19
  177.9 22.4 %collective-permute-start.23 = (f32[8,192,192]{2,1,0:T(8,128)}, f32[8,192,192]{2,1,0:T(8,128)}, u32[]{:S(2)}, u32[]{:S(2)}) collective-permute-start(f32[8,192,192]{2,1,0:T(8,128)} %shard_map.97.refs_3_), channel_id=1, source_target_pairs={{0,1},{1,2},{2,3},{3,4},{4,5},{5,6},{6,7},{8,9},{9,10},{10,11},{11... | collective-permute-start | bytes 3538952 | tf_op jit(solution)/shard_map/ppermute | solution.py:18
  181.4 23.3 %collective-permute-start.25 = (f32[8,192,192]{2,1,0:T(8,128)}, f32[8,192,192]{2,1,0:T(8,128)}, u32[]{:S(2)}, u32[]{:S(2)}) collective-permute-start(f32[8,192,192]{2,1,0:T(8,128)} %shard_map.97.refs_3_), channel_id=1, source_target_pairs={{1,0},{2,1},{3,2},{4,3},{5,4},{6,5},{7,6},{9,8},{10,9},{11,10},{12... | collective-permute-start | bytes 3538952 | tf_op jit(solution)/shard_map/ppermute | solution.py:19
  187.1 17.5 %copy-start.7 = (f32[8,192,192]{2,1,0:T(8,128)}, f32[8,192,192]{2,1,0:T(8,128)S(1)}, u32[]{:S(2)}) copy-start(f32[8,192,192]{2,1,0:T(8,128)S(1)} %collective-permute-done.22.refs_0_) | copy-start | bytes 3538948

commit v10 on v9

--- a/solution.py
+++ b/solution.py
@@ -37,24 +37,15 @@
     return piece
 
 
-def reduce_chunks(partial):
+def sum_over_aux(partial):
     count = lax.axis_size("aux")
-    pairs = partial.shape[0]
-    if count != 4 or pairs % 16:
-        return [lax.psum(partial, "aux")]
+    if count != 4 or partial.shape[0] % 8:
+        return lax.psum(partial, "aux")
     index = lax.axis_index("aux")
-    chunk = pairs // 2
-    stream = chunk // 2
-    results = []
-    pending = partial
-    for c in range(2):
-        part = pending[c * chunk:(c + 1) * chunk]
-        first = halving_stream(part[:stream], index, count, (1, 2))
-        second = halving_stream(part[stream:], index, count, (2, 1))
-        results.append(jnp.concatenate([first, second], axis=0))
-        if c == 0:
-            results[0], pending = lax.optimization_barrier((results[0], pending))
-    return results
+    half = partial.shape[0] // 2
+    first = halving_stream(partial[:half], index, count, (1, 2))
+    second = halving_stream(partial[half:], index, count, (2, 1))
+    return jnp.concatenate([first, second], axis=0)
 
 
 def class_size(natural_orbital_class):
@@ -288,16 +279,13 @@
         blocks,
         jnp.swapaxes(pno_coef, 2, 3),
     )
-    exchange_chunks = reduce_chunks(partial_ints)
-    exchange_ints = jnp.concatenate(exchange_chunks, axis=0)
+    exchange_ints = sum_over_aux(partial_ints)
     denominator = pno_energy[:, :, None] + pno_energy[:, None, :]
     local_rows = (neighbour_pairs - (position - 1) * pair_dev).astype(jnp.int32).reshape(-1)
     fock = fock_coupling.reshape(-1)
 
-    chunk = exchange_chunks[0].shape[0]
-    parts = [
-        -(part / denominator[c * chunk:(c + 1) * chunk]) for c, part in enumerate(exchange_chunks)
-    ]
+    chunk = pair_dev // 2 if pair_dev % 8 == 0 else pair_dev
+    parts = [-(exchange_ints / denominator)]
     sources = chunked_halo(parts)
     amplitudes = jnp.concatenate(parts, axis=0)
     for iteration in range(1, ITERS):
@@ -306,7 +294,7 @@
                 local_rows, sizes, fock, sources, margin, exchange_ints, pno_energy, amplitudes,
                 False, c * chunk, chunk,
             )
-            for c in range(len(parts))
+            for c in range(pair_dev // chunk)
         ]
         sources = chunked_halo(parts)
         amplitudes = jnp.concatenate(parts, axis=0)

time: 220 us -> 209 us (0.950)
  waiting for transfers between devices: 97.4 us -> 93.2 us
  starting transfers between devices: 52.4 us -> 48.2 us
    ppermute x5 -> x4, waiting for transfers between devices: 17.5 us -> 48.3 us  [halo_sources(): from_right = lax.ppermute(cells, axis, [(i + 1, i) for i in range(ends)])]
    ppermute x5 -> x4, waiting for transfers between devices: 37.7 us -> 9.95 us  [halo_sources(): from_left = lax.ppermute(cells, axis, [(i, i + 1) for i in range(ends)])]
    ppermute x8 -> x4, waiting for transfers between devices: 23.8 us -> 17.6 us  [halving_stream(): lax.ppermute(send, 'aux', [(i, i ^ bit) for i in range(count)])]
    ppermute x5 -> x4, starting transfers between devices: 24 us -> 29.1 us  [halo_sources(): from_left = lax.ppermute(cells, axis, [(i, i + 1) for i in range(ends)])]
    ppermute x5 -> x4, starting transfers between devices: 12.3 us -> 7.81 us  [halo_sources(): from_right = lax.ppermute(cells, axis, [(i + 1, i) for i in range(ends)])]
    concatenate x2 -> x1, other arithmetic: 5.34 us -> 2.03 us  [sum_over_aux(): return jnp.concatenate([first, second], axis=0)]
    ppermute x8 -> x4, starting transfers between devices: 8.27 us -> 5.58 us  [halving_stream(): other = lax.ppermute(piece, 'aux', [(i, i ^ bit) for i in range(count)])]
    add x4 -> x2, other arithmetic: 0.21 us -> 2.47 us  [halving_stream(): keep + lax.ppermute(send, 'aux', [(i, i ^ bit) for i in range(count)])]
  transfers between devices with their start and end apart: 26 -> 16, of which waited for: 23 -> 13; matrix products, arithmetic and copies ran while one was open for 7% -> 7% of each run, Pallas kernels for 4% -> 5%
where the time goes in v10:
time: 209 us
  waiting for transfers between devices  93.2 us (45%)
  starting transfers between devices  48.2 us (23%)
  Pallas kernels  45.4 us (22%)
  other arithmetic  11.4 us (5%)
  local copies, waits for them, and re-layouts  9.47 us (5%)
    ppermute x4, waiting for transfers between devices, halo_sources(): from_right = lax.ppermute(cells, axis, [(i + 1, i) for i in range(ends)])  48.3 us
    pallas_call x3, Pallas kernels, coupling_step(): pl.pallas_call(kernel, grid_spec=grid_spec, out_shape=jax.ShapeDtypeStruc...  33.5 us
    ppermute x4, starting transfers between devices, halo_sources(): from_left = lax.ppermute(cells, axis, [(i, i + 1) for i in range(ends)])  29.1 us
    ppermute x4, waiting for transfers between devices, halving_stream(): lax.ppermute(send, 'aux', [(i, i ^ bit) for i in range(count)])  17.6 us
    ppermute x4, waiting for transfers between devices, halving_stream(): other = lax.ppermute(piece, 'aux', [(i, i ^ bit) for i in range(count)])  17.3 us
    pallas_call x1, Pallas kernels, partial_exchange(): pl.pallas_call(functools.partial(exchange_kernel, occ=occ, group=group),...  11.9 us
    ppermute x4, waiting for transfers between devices, halo_sources(): from_left = lax.ppermute(cells, axis, [(i, i + 1) for i in range(ends)])  9.95 us
    ppermute x4, starting transfers between devices, halo_sources(): from_right = lax.ppermute(cells, axis, [(i + 1, i) for i in range(ends)])  7.81 us
  transfers between devices with their start and end apart: 16, of which 13 were waited for; matrix products, arithmetic and copies ran while one was open for 7% of the time, Pallas kernels for 5%

profile of v10, /device:TPU:1, one launch (start us, length us, event | category | flops | bytes accessed | tf_op | source)
XLA Modules:
  0.0 208.8 jit_solution(2932834881080378128)
XLA Ops:
  0.6 4.6 %collective-permute-start = (bf16[4,512,256]{2,1,0:T(8,128)(2,1)}, bf16[4,512,256]{2,1,0:T(8,128)(2,1)S(1)}, u32[]{:S(2)}, u32[]{:S(2)}) collective-permute-start(bf16[4,512,256]{2,1,0:T(8,128)(2,1)} %t_own.1), channel_id=1, source_target_pairs={{0,1},{1,2},{2,3},{3,4},{4,5},{5,6},{6,7},{8,9},{9,10},{10,11},{11... | collective-permute-start | bytes 3145736 | tf_op jit(solution)/shard_map/ppermute | solution.py:18
  5.2 1.9 collective-permute-start.1
  7.2 1.2 compare_select_fusion.2.size_ref
  8.4 0.7 broadcast_subtract_fusion
  9.1 0.5 slice_bitcast_fusion
  9.6 7.7 %collective-permute-done.t_left = bf16[4,512,256]{2,1,0:T(8,128)(2,1)S(1)} collective-permute-done((bf16[4,512,256]{2,1,0:T(8,128)(2,1)}, bf16[4,512,256]{2,1,0:T(8,128)(2,1)S(1)}, u32[]{:S(2)}, u32[]{:S(2)}) %collective-permute-start) | collective-permute-done | bytes 1048608 | tf_op jit(solution)/shard_map/ppermute | solution.py:18
  17.3 4.3 %collective-permute-done.1.t_right = bf16[4,512,256]{2,1,0:T(8,128)(2,1)S(1)} collective-permute-done((bf16[4,512,256]{2,1,0:T(8,128)(2,1)}, bf16[4,512,256]{2,1,0:T(8,128)(2,1)S(1)}, u32[]{:S(2)}, u32[]{:S(2)}) %collective-permute-start.1) | collective-permute-done | bytes 1048608 | tf_op jit(solution)/shard_map/ppermute | solution.py:19
  21.6 1.0 copy-done.5
  22.6 11.9 %shard_map.95 = f32[16,192,192]{2,1,0:T(8,128)} custom-call(s32[16]{0:T(128)} %get-tuple-element.11.lead_ref, s32[16]{0:T(128)} %get-tuple-element.10.trail_ref, s32[16]{0:T(128)} %compare_select_fusion.2.size_ref, bf16[4,512,256]{2,1,0:T(8,128)(2,1)} %copy-done.4, bf16[4,512,256]{2,1,0:T(8,128)(2,1)} %t_own.1, bf16[4,512,256]{2,1,0:T(8,128)(2,1)} %copy-done.5, ...), custom_call_target="tpu_custom_call" | custom-call | flops 2214592512 | bytes 13893632 | tf_op jit(solution)/shard_map/pallas_call | solution.py:137
  34.5 2.2 %fusion = (f32[8,192,192]{2,1,0:T(8,128)S(1)}, f32[8,192,192]{2,1,0:T(8,128)S(1)}) fusion(f32[16,192,192]{2,1,0:T(8,128)} %shard_map.95), kind=kLoop, calls=%fused_computation.26 | loop fusion | bytes 4718592 | tf_op jit(solution)/shard_map/slice | solution.py:46
  36.7 0.9 constant_dynamic-slice_fusion.1
  37.6 1.2 collective-permute-start.6
  38.9 0.9 constant_dynamic-slice_fusion.3
  39.8 1.2 collective-permute-start.2
  41.0 10.9 %collective-permute-done.6 = f32[4,192,192]{2,1,0:T(8,128)} collective-permute-done((f32[4,192,192]{2,1,0:T(8,128)}, f32[4,192,192]{2,1,0:T(8,128)}, u32[]{:S(2)}, u32[]{:S(2)}) %collective-permute-start.6) | collective-permute-done | bytes 589856 | tf_op jit(solution)/shard_map/ppermute | solution.py:29
  52.0 1.2 dynamic-slice_add_fusion
  53.2 1.7 collective-permute-start.7
  54.9 0.3 collective-permute-done.2
  55.2 1.2 dynamic-slice_add_fusion.1
  56.5 1.6 collective-permute-start.3
  58.1 6.5 %collective-permute-done.7 = f32[2,192,192]{2,1,0:T(8,128)S(1)} collective-permute-done((f32[2,192,192]{2,1,0:T(8,128)S(1)}, f32[2,192,192]{2,1,0:T(8,128)S(1)}, u32[]{:S(2)}, u32[]{:S(2)}) %collective-permute-start.7) | collective-permute-done | bytes 294944 | tf_op jit(solution)/shard_map/ppermute | solution.py:29
  64.6 1.1 constant_dynamic-update-slice_fusion.3
  65.7 1.2 collective-permute-start.8
  67.0 1.3 collective-permute-start.4
  68.3 7.4 %collective-permute-done.8 = f32[2,192,192]{2,1,0:T(8,128)S(1)} collective-permute-done((f32[2,192,192]{2,1,0:T(8,128)S(1)}, f32[2,192,192]{2,1,0:T(8,128)S(1)}, u32[]{:S(2)}, u32[]{:S(2)}) %collective-permute-start.8) | collective-permute-done | bytes 294944 | tf_op jit(solution)/shard_map/ppermute | solution.py:32
  75.7 2.4 %collective-permute-start.9 = (f32[4,192,192]{2,1,0:T(8,128)S(1)}, f32[4,192,192]{2,1,0:T(8,128)S(1)}, u32[]{:S(2)}, u32[]{:S(2)}) collective-permute-start(f32[4,192,192]{2,1,0:T(8,128)S(1)} %constant_dynamic-update-slice_fusion.2), channel_id=1, source_target_pairs={{0,16},{8,24},{16,0},{24,8},{1,17},{9,25},{17,1},{25,9},{2,18},{10... | collective-permute-start | bytes 1769480 | tf_op jit(solution)/shard_map/ppermute | solution.py:32
  78.1 0.2 collective-permute-done.4
  78.3 0.7 collective-permute-start.5
  79.5 9.6 %collective-permute-done.9 = f32[4,192,192]{2,1,0:T(8,128)S(1)} collective-permute-done((f32[4,192,192]{2,1,0:T(8,128)S(1)}, f32[4,192,192]{2,1,0:T(8,128)S(1)}, u32[]{:S(2)}, u32[]{:S(2)}) %collective-permute-start.9) | collective-permute-done | bytes 589856 | tf_op jit(solution)/shard_map/ppermute | solution.py:32
  89.3 2.0 pad_maximum_fusion
  91.3 1.9 collective-permute-start.11
  93.3 16.2 %collective-permute-start.10 = (f32[16,192,192]{2,1,0:T(8,128)S(1)}, f32[16,192,192]{2,1,0:T(8,128)}, u32[]{:S(2)}, u32[]{:S(2)}) collective-permute-start(f32[16,192,192]{2,1,0:T(8,128)S(1)} %get-tuple-element.7.refs_1_.refs_7_), channel_id=1, source_target_pairs={{0,1},{1,2},{2,3},{3,4},{4,5},{5,6},{6,7},{8,9},{9,10},{10,11},{11... | collective-permute-start | bytes 7077896 | tf_op jit(solution)/shard_map/ppermute | solution.py:18
  109.5 0.6 broadcast_in_dim.26.refs_6_.refs_9_
  110.2 0.6 reshape.20.nb_ref
  110.9 0.6 reshape.21.fock_ref
  111.5 1.7 copy.14.refs_5_.refs_8_
  113.2 29.4 %collective-permute-done.11.refs_2_ = f32[16,192,192]{2,1,0:T(8,128)} collective-permute-done((f32[16,192,192]{2,1,0:T(8,128)S(1)}, f32[16,192,192]{2,1,0:T(8,128)}, u32[]{:S(2)}, u32[]{:S(2)}) %collective-permute-start.11) | collective-permute-done | bytes 2359328 | tf_op jit(solution)/shard_map/ppermute | solution.py:19
  142.6 1.1 collective-permute-done.10.refs_0_
  143.7 9.5 %shard_map.96.refs_2_ = f32[8,192,192]{2,1,0:T(8,128)} custom-call(s32[32]{0:T(128)} %reshape.20.nb_ref, s32[16]{0:T(128)} %compare_select_fusion.2.size_ref, f32[32]{0:T(128)} %reshape.21.fock_ref, f32[16,192,192]{2,1,0:T(8,128)} %collective-permute-done.10.refs_0_, f32[16,192,192]{2,1,0:T(8,128)} %copy-done, ...), custom_call_target="tpu_custom_call" | custom-call | flops 905969664 | bytes 7077888 | tf_op jit(solution)/shard_map/pallas_call | solution.py:242
  153.2 2.1 collective-permute-start.14
  155.2 4.6 %collective-permute-start.12 = (f32[8,192,192]{2,1,0:T(8,128)}, f32[8,192,192]{2,1,0:T(8,128)}, u32[]{:S(2)}, u32[]{:S(2)}) collective-permute-start(f32[8,192,192]{2,1,0:T(8,128)} %shard_map.96.refs_2_), channel_id=1, source_target_pairs={{0,1},{1,2},{2,3},{3,4},{4,5},{5,6},{6,7},{8,9},{9,10},{10,11},{11... | collective-permute-start | bytes 3538952 | tf_op jit(solution)/shard_map/ppermute | solution.py:18
  159.9 9.6 %shard_map.97.refs_3_ = f32[8,192,192]{2,1,0:T(8,128)} custom-call(s32[32]{0:T(128)} %reshape.20.nb_ref, s32[16]{0:T(128)} %compare_select_fusion.2.size_ref, f32[32]{0:T(128)} %reshape.21.fock_ref, f32[16,192,192]{2,1,0:T(8,128)} %collective-permute-done.10.refs_0_, f32[16,192,192]{2,1,0:T(8,128)} %copy-done, ...), custom_call_target="tpu_custom_call" | custom-call | flops 905969664 | bytes 7077888 | tf_op jit(solution)/shard_map/pallas_call | solution.py:242
  169.4 1.9 collective-permute-start.15
  171.4 3.6 %collective-permute-start.13 = (f32[8,192,192]{2,1,0:T(8,128)}, f32[8,192,192]{2,1,0:T(8,128)}, u32[]{:S(2)}, u32[]{:S(2)}) collective-permute-start(f32[8,192,192]{2,1,0:T(8,128)} %shard_map.97.refs_3_), channel_id=1, source_target_pairs={{0,1},{1,2},{2,3},{3,4},{4,5},{5,6},{6,7},{8,9},{9,10},{10,11},{11... | collective-permute-start | bytes 3538952 | tf_op jit(solution)/shard_map/ppermute | solution.py:18
  175.0 3.4 %pad_maximum_fusion.1.refs_10_ = f32[16,192,192]{2,1,0:T(8,128)} fusion(f32[8,192,192]{2,1,0:T(8,128)} %shard_map.97.refs_3_, f32[8,192,192]{2,1,0:T(8,128)S(1)} %copy-done.1), kind=kLoop, calls=%fused_computation.1 | loop fusion | flops 589824 | bytes 4718592 | tf_op jit(solution)/shard_map/concatenate | solution.py:300
  178.5 14.6 %collective-permute-done.15.refs_5_ = f32[8,192,192]{2,1,0:T(8,128)} collective-permute-done((f32[8,192,192]{2,1,0:T(8,128)}, f32[8,192,192]{2,1,0:T(8,128)}, u32[]{:S(2)}, u32[]{:S(2)}) %collective-permute-start.15) | collective-permute-done | bytes 1179680 | tf_op jit(solution)/shard_map/ppermute | solution.py:19
  193.0 1.2 collective-permute-done.13.refs_1_
  194.2 14.5 %shard_map.98 = f32[16,192,192]{2,1,0:T(8,128)} custom-call(s32[32]{0:T(128)} %reshape.20.nb_ref, s32[16]{0:T(128)} %compare_select_fusion.2.size_ref, f32[32]{0:T(128)} %reshape.21.fock_ref, f32[8,192,192]{2,1,0:T(8,128)} %collective-permute-done.12.refs_0_, f32[8,192,192]{2,1,0:T(8,128)} %collective-permute-done.13.refs_1_, ...), custom_call_target="tpu_custom_call" | custom-call | flops 1811939328 | bytes 14155776 | tf_op jit(solution)/shard_map/pallas_call | solution.py:242
  (37 shorter events, 1.1 us)
Async XLA Ops:
  0.6 16.6 %collective-permute-start = (bf16[4,512,256]{2,1,0:T(8,128)(2,1)}, bf16[4,512,256]{2,1,0:T(8,128)(2,1)S(1)}, u32[]{:S(2)}, u32[]{:S(2)}) collective-permute-start(bf16[4,512,256]{2,1,0:T(8,128)(2,1)} %t_own.1), channel_id=1, source_target_pairs={{0,1},{1,2},{2,3},{3,4},{4,5},{5,6},{6,7},{8,9},{9,10},{10,11},{11... | collective-permute-start | bytes 3145736 | tf_op jit(solution)/shard_map/ppermute | solution.py:18
  5.2 16.3 %collective-permute-start.1 = (bf16[4,512,256]{2,1,0:T(8,128)(2,1)}, bf16[4,512,256]{2,1,0:T(8,128)(2,1)S(1)}, u32[]{:S(2)}, u32[]{:S(2)}) collective-permute-start(bf16[4,512,256]{2,1,0:T(8,128)(2,1)} %t_own.1), channel_id=1, source_target_pairs={{1,0},{2,1},{3,2},{4,3},{5,4},{6,5},{7,6},{9,8},{10,9},{11,10},{12... | collective-permute-start | bytes 3145736 | tf_op jit(solution)/shard_map/ppermute | solution.py:19
  17.3 4.3 %copy-start.4 = (bf16[4,512,256]{2,1,0:T(8,128)(2,1)}, bf16[4,512,256]{2,1,0:T(8,128)(2,1)S(1)}, u32[]{:S(2)}) copy-start(bf16[4,512,256]{2,1,0:T(8,128)(2,1)S(1)} %collective-permute-done.t_left) | copy-start | bytes 3145732
  21.6 1.0 copy-start.5
  37.6 14.3 %collective-permute-start.6 = (f32[4,192,192]{2,1,0:T(8,128)}, f32[4,192,192]{2,1,0:T(8,128)}, u32[]{:S(2)}, u32[]{:S(2)}) collective-permute-start(f32[4,192,192]{2,1,0:T(8,128)} %constant_dynamic-slice_fusion.1), channel_id=1, source_target_pairs={{0,16},{8,24},{16,0},{24,8},{1,17},{9,25},{17,1},{25,9},{2,18},{10... | collective-permute-start | bytes 1769480 | tf_op jit(solution)/shard_map/ppermute | solution.py:29
  39.8 15.4 %collective-permute-start.2 = (f32[4,192,192]{2,1,0:T(8,128)}, f32[4,192,192]{2,1,0:T(8,128)}, u32[]{:S(2)}, u32[]{:S(2)}) collective-permute-start(f32[4,192,192]{2,1,0:T(8,128)} %constant_dynamic-slice_fusion.3), channel_id=1, source_target_pairs={{0,8},{8,0},{16,24},{24,16},{1,9},{9,1},{17,25},{25,17},{2,10},{10... | collective-permute-start | bytes 1769480 | tf_op jit(solution)/shard_map/ppermute | solution.py:29
  53.2 3.2 %copy-start.2 = (f32[4,192,192]{2,1,0:T(8,128)}, f32[4,192,192]{2,1,0:T(8,128)S(1)}, u32[]{:S(2)}) copy-start(f32[4,192,192]{2,1,0:T(8,128)S(1)} %dynamic-slice_add_fusion) | copy-start | bytes 1769476
  53.2 11.3 %collective-permute-start.7 = (f32[2,192,192]{2,1,0:T(8,128)S(1)}, f32[2,192,192]{2,1,0:T(8,128)S(1)}, u32[]{:S(2)}, u32[]{:S(2)}) collective-permute-start(f32[2,192,192]{2,1,0:T(8,128)S(1)} %constant_dynamic-slice_fusion), channel_id=1, source_target_pairs={{0,8},{8,0},{16,24},{24,16},{1,9},{9,1},{17,25},{25,17},{2,10},{10... | collective-permute-start | bytes 884744 | tf_op jit(solution)/shard_map/ppermute | solution.py:29
  56.5 10.4 %collective-permute-start.3 = (f32[2,192,192]{2,1,0:T(8,128)S(1)}, f32[2,192,192]{2,1,0:T(8,128)S(1)}, u32[]{:S(2)}, u32[]{:S(2)}) collective-permute-start(f32[2,192,192]{2,1,0:T(8,128)S(1)} %constant_dynamic-slice_fusion.2), channel_id=1, source_target_pairs={{0,16},{8,24},{16,0},{24,8},{1,17},{9,25},{17,1},{25,9},{2,18},{10... | collective-permute-start | bytes 884744 | tf_op jit(solution)/shard_map/ppermute | solution.py:29
  65.7 10.0 %collective-permute-start.8 = (f32[2,192,192]{2,1,0:T(8,128)S(1)}, f32[2,192,192]{2,1,0:T(8,128)S(1)}, u32[]{:S(2)}, u32[]{:S(2)}) collective-permute-start(f32[2,192,192]{2,1,0:T(8,128)S(1)} %get-tuple-element.5), channel_id=1, source_target_pairs={{0,8},{8,0},{16,24},{24,16},{1,9},{9,1},{17,25},{25,17},{2,10},{10... | collective-permute-start | bytes 884744 | tf_op jit(solution)/shard_map/ppermute | solution.py:32
  67.0 11.3 %collective-permute-start.4 = (f32[2,192,192]{2,1,0:T(8,128)S(1)}, f32[2,192,192]{2,1,0:T(8,128)S(1)}, u32[]{:S(2)}, u32[]{:S(2)}) collective-permute-start(f32[2,192,192]{2,1,0:T(8,128)S(1)} %get-tuple-element.3), channel_id=1, source_target_pairs={{0,16},{8,24},{16,0},{24,8},{1,17},{9,25},{17,1},{25,9},{2,18},{10... | collective-permute-start | bytes 884744 | tf_op jit(solution)/shard_map/ppermute | solution.py:32
  75.7 13.3 %collective-permute-start.9 = (f32[4,192,192]{2,1,0:T(8,128)S(1)}, f32[4,192,192]{2,1,0:T(8,128)S(1)}, u32[]{:S(2)}, u32[]{:S(2)}) collective-permute-start(f32[4,192,192]{2,1,0:T(8,128)S(1)} %constant_dynamic-update-slice_fusion.2), channel_id=1, source_target_pairs={{0,16},{8,24},{16,0},{24,8},{1,17},{9,25},{17,1},{25,9},{2,18},{10... | collective-permute-start | bytes 1769480 | tf_op jit(solution)/shard_map/ppermute | solution.py:32
  78.3 10.9 %collective-permute-start.5 = (f32[4,192,192]{2,1,0:T(8,128)S(1)}, f32[4,192,192]{2,1,0:T(8,128)S(1)}, u32[]{:S(2)}, u32[]{:S(2)}) collective-permute-start(f32[4,192,192]{2,1,0:T(8,128)S(1)} %constant_dynamic-update-slice_fusion.6), channel_id=1, source_target_pairs={{0,8},{8,0},{16,24},{24,16},{1,9},{9,1},{17,25},{25,17},{2,10},{10... | collective-permute-start | bytes 1769480 | tf_op jit(solution)/shard_map/ppermute | solution.py:32
  79.4 9.8 %copy-start.6 = (f32[16,192]{1,0:T(8,128)S(1)}, f32[16,192]{1,0:T(8,128)}, u32[]{:S(2)}) copy-start(f32[16,192]{1,0:T(8,128)} %param.12) | copy-start | bytes 36868
  89.3 20.8 %copy-start.8 = (s32[16,2]{0,1:T(2,128)S(1)}, s32[16,2]{0,1:T(2,128)}, u32[]{:S(2)}) copy-start(s32[16,2]{0,1:T(2,128)} %param.14) | copy-start | bytes 388
  89.3 21.5 %copy-start.7 = (f32[16,2]{0,1:T(2,128)S(1)}, f32[16,2]{0,1:T(2,128)}, u32[]{:S(2)}) copy-start(f32[16,2]{0,1:T(2,128)} %param.15) | copy-start | bytes 388
  91.3 52.3 %copy-start = (f32[16,192,192]{2,1,0:T(8,128)}, f32[16,192,192]{2,1,0:T(8,128)S(1)}, u32[]{:S(2)}) copy-start(f32[16,192,192]{2,1,0:T(8,128)S(1)} %get-tuple-element.7.refs_1_.refs_7_) | copy-start | bytes 7077892
  91.3 51.3 %collective-permute-start.11 = (f32[16,192,192]{2,1,0:T(8,128)S(1)}, f32[16,192,192]{2,1,0:T(8,128)}, u32[]{:S(2)}, u32[]{:S(2)}) collective-permute-start(f32[16,192,192]{2,1,0:T(8,128)S(1)} %get-tuple-element.7.refs_1_.refs_7_), channel_id=1, source_target_pairs={{1,0},{2,1},{3,2},{4,3},{5,4},{6,5},{7,6},{9,8},{10,9},{11,10},{12... | collective-permute-start | bytes 7077896 | tf_op jit(solution)/shard_map/ppermute | solution.py:19
  93.3 50.4 %collective-permute-start.10 = (f32[16,192,192]{2,1,0:T(8,128)S(1)}, f32[16,192,192]{2,1,0:T(8,128)}, u32[]{:S(2)}, u32[]{:S(2)}) collective-permute-start(f32[16,192,192]{2,1,0:T(8,128)S(1)} %get-tuple-element.7.refs_1_.refs_7_), channel_id=1, source_target_pairs={{0,1},{1,2},{2,3},{3,4},{4,5},{5,6},{6,7},{8,9},{9,10},{10,11},{11... | collective-permute-start | bytes 7077896 | tf_op jit(solution)/shard_map/ppermute | solution.py:18
  153.2 21.8 %copy-start.1 = (f32[8,192,192]{2,1,0:T(8,128)S(1)}, f32[8,192,192]{2,1,0:T(8,128)}, u32[]{:S(2)}) copy-start(f32[8,192,192]{2,1,0:T(8,128)} %shard_map.96.refs_2_) | copy-start | bytes 3538948
  153.2 25.3 %collective-permute-start.14 = (f32[8,192,192]{2,1,0:T(8,128)}, f32[8,192,192]{2,1,0:T(8,128)S(1)}, u32[]{:S(2)}, u32[]{:S(2)}) collective-permute-start(f32[8,192,192]{2,1,0:T(8,128)} %shard_map.96.refs_2_), channel_id=1, source_target_pairs={{1,0},{2,1},{3,2},{4,3},{5,4},{6,5},{7,6},{9,8},{10,9},{11,10},{12... | collective-permute-start | bytes 3538952 | tf_op jit(solution)/shard_map/ppermute | solution.py:19
  155.2 23.2 %collective-permute-start.12 = (f32[8,192,192]{2,1,0:T(8,128)}, f32[8,192,192]{2,1,0:T(8,128)}, u32[]{:S(2)}, u32[]{:S(2)}) collective-permute-start(f32[8,192,192]{2,1,0:T(8,128)} %shard_map.96.refs_2_), channel_id=1, source_target_pairs={{0,1},{1,2},{2,3},{3,4},{4,5},{5,6},{6,7},{8,9},{9,10},{10,11},{11... | collective-permute-start | bytes 3538952 | tf_op jit(solution)/shard_map/ppermute | solution.py:18
  169.4 23.6 %collective-permute-start.15 = (f32[8,192,192]{2,1,0:T(8,128)}, f32[8,192,192]{2,1,0:T(8,128)}, u32[]{:S(2)}, u32[]{:S(2)}) collective-permute-start(f32[8,192,192]{2,1,0:T(8,128)} %shard_map.97.refs_3_), channel_id=1, source_target_pairs={{1,0},{2,1},{3,2},{4,3},{5,4},{6,5},{7,6},{9,8},{10,9},{11,10},{12... | collective-permute-start | bytes 3538952 | tf_op jit(solution)/shard_map/ppermute | solution.py:19
  171.4 22.8 %collective-permute-start.13 = (f32[8,192,192]{2,1,0:T(8,128)}, f32[8,192,192]{2,1,0:T(8,128)}, u32[]{:S(2)}, u32[]{:S(2)}) collective-permute-start(f32[8,192,192]{2,1,0:T(8,128)} %shard_map.97.refs_3_), channel_id=1, source_target_pairs={{0,1},{1,2},{2,3},{3,4},{4,5},{5,6},{6,7},{8,9},{9,10},{10,11},{11... | collective-permute-start | bytes 3538952 | tf_op jit(solution)/shard_map/ppermute | solution.py:18
  178.5 15.7 %copy-start.3 = (f32[8,192,192]{2,1,0:T(8,128)}, f32[8,192,192]{2,1,0:T(8,128)S(1)}, u32[]{:S(2)}) copy-start(f32[8,192,192]{2,1,0:T(8,128)S(1)} %collective-permute-done.14.refs_4_) | copy-start | bytes 3538948

commit v11 on v10

--- a/solution.py
+++ b/solution.py
@@ -37,14 +37,13 @@
     return piece
 
 
-def sum_over_aux(partial):
+def sum_over_aux(halves):
     count = lax.axis_size("aux")
-    if count != 4 or partial.shape[0] % 8:
-        return lax.psum(partial, "aux")
+    if count != 4 or halves[0].shape[0] % 4:
+        return lax.psum(jnp.concatenate(halves, axis=0), "aux")
     index = lax.axis_index("aux")
-    half = partial.shape[0] // 2
-    first = halving_stream(partial[:half], index, count, (1, 2))
-    second = halving_stream(partial[half:], index, count, (2, 1))
+    first = halving_stream(halves[0], index, count, (1, 2))
+    second = halving_stream(halves[1], index, count, (2, 1))
     return jnp.concatenate([first, second], axis=0)
 
 
@@ -71,7 +70,7 @@
 
 
 def exchange_kernel(
-    lead_ref, trail_ref, size_ref, t_left, t_own, t_right, coef_ref, out_ref, lbuf, tbuf, sems, *, occ, group
+    lead_ref, trail_ref, size_ref, t_left, t_own, t_right, coef_ref, out_ref, lbuf, tbuf, sems, *, occ, group, start
 ):
     i = pl.program_id(0)
     steps = pl.num_programs(0)
@@ -79,7 +78,7 @@
 
     def fetch(step, slot):
         for g in range(group):
-            p = step * group + g
+            p = start + step * group + g
             pltpu.make_async_copy(t_own.at[lead_ref[p] % occ], lbuf.at[slot, g], sems.at[slot, 0, g]).start()
             fetch_block(sources, occ, trail_ref[p], tbuf.at[slot, g], sems.at[slot, 1, g])
 
@@ -94,7 +93,7 @@
     slot = i % 2
     transposed = (((1,), (1,)), ((), ()))
     for g in range(group):
-        p = i * group + g
+        p = start + i * group + g
         pltpu.make_async_copy(t_own.at[0], lbuf.at[slot, g], sems.at[slot, 0, g]).wait()
         pltpu.make_async_copy(t_own.at[0], tbuf.at[slot, g], sems.at[slot, 1, g]).wait()
         size = size_ref[p]
@@ -112,19 +111,21 @@
                 )
 
 
-def partial_exchange(lead, trail, sizes, sources, coef_t):
+def partial_exchange(lead, trail, sizes, sources, coef_t, start=0, count=None):
     pairs = coef_t.shape[0]
-    group = next(g for g in (4, 2, 1) if pairs % g == 0)
+    count = pairs if count is None else count
+    group = next(g for g in (4, 2, 1) if count % g == 0 and start % g == 0)
+    base = start // group
     occ, nfit, npao = sources[1].shape
     hbm = pl.BlockSpec(memory_space=pl.ANY)
     grid_spec = pltpu.PrefetchScalarGridSpec(
         num_scalar_prefetch=3,
-        grid=(pairs // group,),
+        grid=(count // group,),
         in_specs=[
             hbm,
             hbm,
             hbm,
-            pl.BlockSpec((group, 2, NPNO, npao), lambda i, a, b, s: (i, 0, 0, 0)),
+            pl.BlockSpec((group, 2, NPNO, npao), lambda i, a, b, s: (i + base, 0, 0, 0)),
         ],
         out_specs=pl.BlockSpec((group, NPNO, NPNO), lambda i, a, b, s: (i, 0, 0)),
         scratch_shapes=[
@@ -133,14 +134,14 @@
             pltpu.SemaphoreType.DMA((2, 2, group)),
         ],
     )
-    flops = pairs * (2 * 2 * nfit * npao * NPNO + 2 * nfit * NPNO * NPNO)
+    flops = count * (2 * 2 * nfit * npao * NPNO + 2 * nfit * NPNO * NPNO)
     return pl.pallas_call(
-        functools.partial(exchange_kernel, occ=occ, group=group),
+        functools.partial(exchange_kernel, occ=occ, group=group, start=start),
         grid_spec=grid_spec,
-        out_shape=jax.ShapeDtypeStruct((pairs, NPNO, NPNO), jnp.float32),
+        out_shape=jax.ShapeDtypeStruct((count, NPNO, NPNO), jnp.float32),
         cost_estimate=pl.CostEstimate(
             flops=flops,
-            bytes_accessed=pairs * (2 * nfit * npao * 2 + 2 * npao * NPNO * 2 + NPNO * NPNO * 4),
+            bytes_accessed=count * (2 * nfit * npao * 2 + 2 * npao * NPNO * 2 + NPNO * NPNO * 4),
             transcendentals=0,
         ),
     )(lead, trail, sizes, *sources, coef_t)
@@ -272,14 +273,20 @@
     sizes = class_size(natural_orbital_class)
     blocks = halo_sources(three_index, "pair")
     local_orbitals = (pair_orbitals - (position - 1) * occ_dev).astype(jnp.int32)
-    partial_ints = partial_exchange(
-        local_orbitals[:, 0] - occ_dev,
-        local_orbitals[:, 1],
-        sizes,
-        blocks,
-        jnp.swapaxes(pno_coef, 2, 3),
-    )
-    exchange_ints = sum_over_aux(partial_ints)
+    half = pair_dev // 2
+    halves = [
+        partial_exchange(
+            local_orbitals[:, 0] - occ_dev,
+            local_orbitals[:, 1],
+            sizes,
+            blocks,
+            jnp.swapaxes(pno_coef, 2, 3),
+            start,
+            half,
+        )
+        for start in (0, half)
+    ]
+    exchange_ints = sum_over_aux(halves)
     denominator = pno_energy[:, :, None] + pno_energy[:, None, :]
     local_rows = (neighbour_pairs - (position - 1) * pair_dev).astype(jnp.int32).reshape(-1)
     fock = fock_coupling.reshape(-1)

time: 209 us -> 206 us (0.986)
  starting transfers between devices: 48.2 us -> 39.5 us
  Pallas kernels: 45.4 us -> 49.8 us
  waiting for transfers between devices: 93.2 us -> 96.5 us
    ppermute x4, waiting for transfers between devices: 9.95 us -> 3.55 us  [halo_sources(): from_left = lax.ppermute(cells, axis, [(i, i + 1) for i in range(ends)])]
    pallas_call x1 -> x2, Pallas kernels: 11.9 us -> 15.8 us  [partial_exchange(): pl.pallas_call(functools.partial(exchange_kernel, occ=occ, group=group, s...]
    ppermute x4, waiting for transfers between devices: 48.3 us -> 52.1 us  [halo_sources(): from_right = lax.ppermute(cells, axis, [(i + 1, i) for i in range(ends)])]
    ppermute x4, waiting for transfers between devices: 17.3 us -> 20.7 us  [halving_stream(): other = lax.ppermute(piece, 'aux', [(i, i ^ bit) for i in range(count)])]
    ppermute x4, starting transfers between devices: 5.58 us -> 2.23 us  [halving_stream(): other = lax.ppermute(piece, 'aux', [(i, i ^ bit) for i in range(count)])]
    ppermute x4, starting transfers between devices: 5.77 us -> 2.91 us  [halving_stream(): lax.ppermute(send, 'aux', [(i, i ^ bit) for i in range(count)])]
    ppermute x4, starting transfers between devices: 29.1 us -> 26.5 us  [halo_sources(): from_left = lax.ppermute(cells, axis, [(i, i + 1) for i in range(ends)])]
    ppermute x4, waiting for transfers between devices: 17.6 us -> 20.1 us  [halving_stream(): lax.ppermute(send, 'aux', [(i, i ^ bit) for i in range(count)])]
  transfers between devices with their start and end apart: 16 -> 16, of which waited for: 13 -> 11; matrix products, arithmetic and copies ran while one was open for 7% -> 7% of each run, Pallas kernels for 5% -> 9%
where the time goes in v11:
time: 206 us; the launch traced here: 205 us
  waiting for transfers between devices  96.5 us (47%)
  Pallas kernels  49.8 us (24%)
  starting transfers between devices  39.5 us (19%)
  other arithmetic  9.36 us (5%)
  local copies, waits for them, and re-layouts  8.82 us (4%)
    ppermute x4, waiting for transfers between devices, halo_sources(): from_right = lax.ppermute(cells, axis, [(i + 1, i) for i in range(ends)])  52.1 us
    pallas_call x3, Pallas kernels, coupling_step(): pl.pallas_call(kernel, grid_spec=grid_spec, out_shape=jax.ShapeDtypeStruc...  34 us
    ppermute x4, starting transfers between devices, halo_sources(): from_left = lax.ppermute(cells, axis, [(i, i + 1) for i in range(ends)])  26.5 us
    ppermute x4, waiting for transfers between devices, halving_stream(): other = lax.ppermute(piece, 'aux', [(i, i ^ bit) for i in range(count)])  20.7 us
    ppermute x4, waiting for transfers between devices, halving_stream(): lax.ppermute(send, 'aux', [(i, i ^ bit) for i in range(count)])  20.1 us
    pallas_call x2, Pallas kernels, partial_exchange(): pl.pallas_call(functools.partial(exchange_kernel, occ=occ, group=group, s...  15.8 us
    ppermute x4, starting transfers between devices, halo_sources(): from_right = lax.ppermute(cells, axis, [(i + 1, i) for i in range(ends)])  7.85 us
  transfers between devices with their start and end apart: 16, of which 11 were waited for; matrix products, arithmetic and copies ran while one was open for 7% of the time, Pallas kernels for 9%

profile of v11, /device:TPU:1, one launch (start us, length us, event | category | flops | bytes accessed | tf_op | source)
XLA Modules:
  0.0 205.2 jit_solution(15363770845605412847)
XLA Ops:
  0.6 2.0 collective-permute-start.1
  2.6 4.6 %collective-permute-start = (bf16[4,512,256]{2,1,0:T(8,128)(2,1)}, bf16[4,512,256]{2,1,0:T(8,128)(2,1)S(1)}, u32[]{:S(2)}, u32[]{:S(2)}) collective-permute-start(bf16[4,512,256]{2,1,0:T(8,128)(2,1)} %t_own.3), channel_id=1, source_target_pairs={{0,1},{1,2},{2,3},{3,4},{4,5},{5,6},{6,7},{8,9},{9,10},{10,11},{11... | collective-permute-start | bytes 3145736 | tf_op jit(solution)/shard_map/ppermute | solution.py:18
  7.2 1.2 compare_select_fusion.2.size_ref
  8.4 0.7 broadcast_subtract_fusion
  9.1 0.6 slice_bitcast_fusion
  9.7 8.3 %collective-permute-done.1.t_right = bf16[4,512,256]{2,1,0:T(8,128)(2,1)S(1)} collective-permute-done((bf16[4,512,256]{2,1,0:T(8,128)(2,1)}, bf16[4,512,256]{2,1,0:T(8,128)(2,1)S(1)}, u32[]{:S(2)}, u32[]{:S(2)}) %collective-permute-start.1) | collective-permute-done | bytes 1048608 | tf_op jit(solution)/shard_map/ppermute | solution.py:19
  17.9 1.3 collective-permute-done.t_left
  19.2 1.0 copy-done.5
  20.2 7.7 %shard_map.96 = f32[8,192,192]{2,1,0:T(8,128)} custom-call(s32[16]{0:T(128)} %get-tuple-element.9.lead_ref, s32[16]{0:T(128)} %get-tuple-element.8.trail_ref, s32[16]{0:T(128)} %compare_select_fusion.2.size_ref, bf16[4,512,256]{2,1,0:T(8,128)(2,1)} %copy-done.5, bf16[4,512,256]{2,1,0:T(8,128)(2,1)} %t_own.3, bf16[4,512,256]{2,1,0:T(8,128)(2,1)} %copy-done.4, ...), custom_call_target="tpu_custom_call" | custom-call | flops 1107296256 | bytes 6946816 | tf_op jit(solution)/shard_map/pallas_call | solution.py:138
  27.9 1.2 constant_dynamic-slice_fusion.1
  29.1 1.3 collective-permute-start.6
  30.5 8.0 %shard_map.95 = f32[8,192,192]{2,1,0:T(8,128)} custom-call(s32[16]{0:T(128)} %get-tuple-element.9.lead_ref, s32[16]{0:T(128)} %get-tuple-element.8.trail_ref, s32[16]{0:T(128)} %compare_select_fusion.2.size_ref, bf16[4,512,256]{2,1,0:T(8,128)(2,1)} %copy-done.5, bf16[4,512,256]{2,1,0:T(8,128)(2,1)} %t_own.3, bf16[4,512,256]{2,1,0:T(8,128)(2,1)} %copy-done.4, ...), custom_call_target="tpu_custom_call" | custom-call | flops 1107296256 | bytes 6946816 | tf_op jit(solution)/shard_map/pallas_call | solution.py:138
  38.5 2.2 %constant_dynamic-slice_fusion.3 = f32[4,192,192]{2,1,0:T(8,128)} fusion(f32[8,192,192]{2,1,0:T(8,128)} %shard_map.95, s32[]{:T(128)S(6)} %select_n.82), kind=kLoop, calls=%fused_computation.18 | loop fusion | bytes 1179652 | tf_op jit(solution)/shard_map/dynamic_slice | solution.py:28
  40.7 1.2 collective-permute-start.2
  41.9 0.1 dynamic-slice_add_fusion
  42.1 0.3 collective-permute-start.7
  42.4 14.3 %collective-permute-done.2 = f32[4,192,192]{2,1,0:T(8,128)} collective-permute-done((f32[4,192,192]{2,1,0:T(8,128)}, f32[4,192,192]{2,1,0:T(8,128)}, u32[]{:S(2)}, u32[]{:S(2)}) %collective-permute-start.2) | collective-permute-done | bytes 589856 | tf_op jit(solution)/shard_map/ppermute | solution.py:29
  56.7 1.2 dynamic-slice_add_fusion.1
  58.1 5.8 %collective-permute-done.7 = f32[2,192,192]{2,1,0:T(8,128)S(1)} collective-permute-done((f32[2,192,192]{2,1,0:T(8,128)S(1)}, f32[2,192,192]{2,1,0:T(8,128)S(1)}, u32[]{:S(2)}, u32[]{:S(2)}) %collective-permute-start.7) | collective-permute-done | bytes 294944 | tf_op jit(solution)/shard_map/ppermute | solution.py:29
  64.0 1.3 collective-permute-start.8
  65.4 0.3 collective-permute-start.4
  65.7 9.3 %collective-permute-done.8 = f32[2,192,192]{2,1,0:T(8,128)S(1)} collective-permute-done((f32[2,192,192]{2,1,0:T(8,128)S(1)}, f32[2,192,192]{2,1,0:T(8,128)S(1)}, u32[]{:S(2)}, u32[]{:S(2)}) %collective-permute-start.8) | collective-permute-done | bytes 294944 | tf_op jit(solution)/shard_map/ppermute | solution.py:32
  75.1 1.5 collective-permute-done.4
  76.7 0.6 collective-permute-start.5
  77.3 0.1 broadcast.30.clone
  77.5 0.1 broadcast.30.clone.1
  77.7 9.9 %collective-permute-done.9 = f32[4,192,192]{2,1,0:T(8,128)S(1)} collective-permute-done((f32[4,192,192]{2,1,0:T(8,128)S(1)}, f32[4,192,192]{2,1,0:T(8,128)S(1)}, u32[]{:S(2)}, u32[]{:S(2)}) %collective-permute-start.9) | collective-permute-done | bytes 589856 | tf_op jit(solution)/shard_map/ppermute | solution.py:32
  87.8 2.0 pad_maximum_fusion
  89.8 1.9 collective-permute-start.11
  91.8 13.7 %collective-permute-start.10 = (f32[16,192,192]{2,1,0:T(8,128)S(1)}, f32[16,192,192]{2,1,0:T(8,128)}, u32[]{:S(2)}, u32[]{:S(2)}) collective-permute-start(f32[16,192,192]{2,1,0:T(8,128)S(1)} %get-tuple-element.7.refs_1_.refs_7_), channel_id=1, source_target_pairs={{0,1},{1,2},{2,3},{3,4},{4,5},{5,6},{6,7},{8,9},{9,10},{10,11},{11... | collective-permute-start | bytes 7077896 | tf_op jit(solution)/shard_map/ppermute | solution.py:18
  105.4 0.6 broadcast_in_dim.26.refs_6_.refs_9_
  106.1 0.1 copy.12
  106.2 0.6 reshape.20.nb_ref
  106.8 0.1 copy.13
  106.9 0.6 reshape.21.fock_ref
  107.4 1.7 copy.14.refs_5_.refs_8_
  109.1 29.3 %collective-permute-done.11.refs_2_ = f32[16,192,192]{2,1,0:T(8,128)} collective-permute-done((f32[16,192,192]{2,1,0:T(8,128)S(1)}, f32[16,192,192]{2,1,0:T(8,128)}, u32[]{:S(2)}, u32[]{:S(2)}) %collective-permute-start.11) | collective-permute-done | bytes 2359328 | tf_op jit(solution)/shard_map/ppermute | solution.py:19
  138.4 1.1 collective-permute-done.10.refs_0_
  139.5 9.8 %shard_map.97.refs_2_ = f32[8,192,192]{2,1,0:T(8,128)} custom-call(s32[32]{0:T(128)} %reshape.20.nb_ref, s32[16]{0:T(128)} %compare_select_fusion.2.size_ref, f32[32]{0:T(128)} %reshape.21.fock_ref, f32[16,192,192]{2,1,0:T(8,128)} %collective-permute-done.10.refs_0_, f32[16,192,192]{2,1,0:T(8,128)} %copy-done, ...), custom_call_target="tpu_custom_call" | custom-call | flops 905969664 | bytes 7077888 | tf_op jit(solution)/shard_map/pallas_call | solution.py:243
  149.3 2.1 collective-permute-start.14
  151.4 4.4 %collective-permute-start.12 = (f32[8,192,192]{2,1,0:T(8,128)}, f32[8,192,192]{2,1,0:T(8,128)}, u32[]{:S(2)}, u32[]{:S(2)}) collective-permute-start(f32[8,192,192]{2,1,0:T(8,128)} %shard_map.97.refs_2_), channel_id=1, source_target_pairs={{0,1},{1,2},{2,3},{3,4},{4,5},{5,6},{6,7},{8,9},{9,10},{10,11},{11... | collective-permute-start | bytes 3538952 | tf_op jit(solution)/shard_map/ppermute | solution.py:18
  155.8 9.5 %shard_map.98.refs_3_ = f32[8,192,192]{2,1,0:T(8,128)} custom-call(s32[32]{0:T(128)} %reshape.20.nb_ref, s32[16]{0:T(128)} %compare_select_fusion.2.size_ref, f32[32]{0:T(128)} %reshape.21.fock_ref, f32[16,192,192]{2,1,0:T(8,128)} %collective-permute-done.10.refs_0_, f32[16,192,192]{2,1,0:T(8,128)} %copy-done, ...), custom_call_target="tpu_custom_call" | custom-call | flops 905969664 | bytes 7077888 | tf_op jit(solution)/shard_map/pallas_call | solution.py:243
  165.2 1.9 collective-permute-start.15
  167.2 3.9 %collective-permute-start.13 = (f32[8,192,192]{2,1,0:T(8,128)}, f32[8,192,192]{2,1,0:T(8,128)}, u32[]{:S(2)}, u32[]{:S(2)}) collective-permute-start(f32[8,192,192]{2,1,0:T(8,128)} %shard_map.98.refs_3_), channel_id=1, source_target_pairs={{0,1},{1,2},{2,3},{3,4},{4,5},{5,6},{6,7},{8,9},{9,10},{10,11},{11... | collective-permute-start | bytes 3538952 | tf_op jit(solution)/shard_map/ppermute | solution.py:18
  171.1 3.4 %pad_maximum_fusion.1.refs_10_ = f32[16,192,192]{2,1,0:T(8,128)} fusion(f32[8,192,192]{2,1,0:T(8,128)} %shard_map.98.refs_3_, f32[8,192,192]{2,1,0:T(8,128)S(1)} %copy-done.1), kind=kLoop, calls=%fused_computation.1 | loop fusion | flops 589824 | bytes 4718592 | tf_op jit(solution)/shard_map/concatenate | solution.py:307
  174.5 14.6 %collective-permute-done.15.refs_5_ = f32[8,192,192]{2,1,0:T(8,128)} collective-permute-done((f32[8,192,192]{2,1,0:T(8,128)}, f32[8,192,192]{2,1,0:T(8,128)}, u32[]{:S(2)}, u32[]{:S(2)}) %collective-permute-start.15) | collective-permute-done | bytes 1179680 | tf_op jit(solution)/shard_map/ppermute | solution.py:19
  189.1 1.2 collective-permute-done.13.refs_1_
  190.3 14.7 %shard_map.99 = f32[16,192,192]{2,1,0:T(8,128)} custom-call(s32[32]{0:T(128)} %reshape.20.nb_ref, s32[16]{0:T(128)} %compare_select_fusion.2.size_ref, f32[32]{0:T(128)} %reshape.21.fock_ref, f32[8,192,192]{2,1,0:T(8,128)} %collective-permute-done.12.refs_0_, f32[8,192,192]{2,1,0:T(8,128)} %collective-permute-done.13.refs_1_, ...), custom_call_target="tpu_custom_call" | custom-call | flops 1811939328 | bytes 14155776 | tf_op jit(solution)/shard_map/pallas_call | solution.py:243
  (39 shorter events, 0.8 us)
Async XLA Ops:
  0.6 17.3 %collective-permute-start.1 = (bf16[4,512,256]{2,1,0:T(8,128)(2,1)}, bf16[4,512,256]{2,1,0:T(8,128)(2,1)S(1)}, u32[]{:S(2)}, u32[]{:S(2)}) collective-permute-start(bf16[4,512,256]{2,1,0:T(8,128)(2,1)} %t_own.3), channel_id=1, source_target_pairs={{1,0},{2,1},{3,2},{4,3},{5,4},{6,5},{7,6},{9,8},{10,9},{11,10},{12... | collective-permute-start | bytes 3145736 | tf_op jit(solution)/shard_map/ppermute | solution.py:19
  2.6 16.6 %collective-permute-start = (bf16[4,512,256]{2,1,0:T(8,128)(2,1)}, bf16[4,512,256]{2,1,0:T(8,128)(2,1)S(1)}, u32[]{:S(2)}, u32[]{:S(2)}) collective-permute-start(bf16[4,512,256]{2,1,0:T(8,128)(2,1)} %t_own.3), channel_id=1, source_target_pairs={{0,1},{1,2},{2,3},{3,4},{4,5},{5,6},{6,7},{8,9},{9,10},{10,11},{11... | collective-permute-start | bytes 3145736 | tf_op jit(solution)/shard_map/ppermute | solution.py:18
  17.9 1.3 copy-start.4
  19.2 1.0 copy-start.5
  29.1 12.8 %collective-permute-start.6 = (f32[4,192,192]{2,1,0:T(8,128)S(1)}, f32[4,192,192]{2,1,0:T(8,128)S(1)}, u32[]{:S(2)}, u32[]{:S(2)}) collective-permute-start(f32[4,192,192]{2,1,0:T(8,128)S(1)} %constant_dynamic-slice_fusion.1), channel_id=1, source_target_pairs={{0,16},{8,24},{16,0},{24,8},{1,17},{9,25},{17,1},{25,9},{2,18},{10... | collective-permute-start | bytes 1769480 | tf_op jit(solution)/shard_map/ppermute | solution.py:29
  38.5 3.4 %copy-start.2 = (f32[8,192,192]{2,1,0:T(8,128)S(1)}, f32[8,192,192]{2,1,0:T(8,128)}, u32[]{:S(2)}) copy-start(f32[8,192,192]{2,1,0:T(8,128)} %shard_map.96) | copy-start | bytes 3538948
  40.7 16.0 %collective-permute-start.2 = (f32[4,192,192]{2,1,0:T(8,128)}, f32[4,192,192]{2,1,0:T(8,128)}, u32[]{:S(2)}, u32[]{:S(2)}) collective-permute-start(f32[4,192,192]{2,1,0:T(8,128)} %constant_dynamic-slice_fusion.3), channel_id=1, source_target_pairs={{0,8},{8,0},{16,24},{24,16},{1,9},{9,1},{17,25},{25,17},{2,10},{10... | collective-permute-start | bytes 1769480 | tf_op jit(solution)/shard_map/ppermute | solution.py:29
  41.9 14.8 %copy-start.3 = (f32[8,192,192]{2,1,0:T(8,128)S(1)}, f32[8,192,192]{2,1,0:T(8,128)}, u32[]{:S(2)}) copy-start(f32[8,192,192]{2,1,0:T(8,128)} %shard_map.95) | copy-start | bytes 3538948
  42.1 21.8 %collective-permute-start.7 = (f32[2,192,192]{2,1,0:T(8,128)S(1)}, f32[2,192,192]{2,1,0:T(8,128)S(1)}, u32[]{:S(2)}, u32[]{:S(2)}) collective-permute-start(f32[2,192,192]{2,1,0:T(8,128)S(1)} %constant_dynamic-slice_fusion), channel_id=1, source_target_pairs={{0,8},{8,0},{16,24},{24,16},{1,9},{9,1},{17,25},{25,17},{2,10},{10... | collective-permute-start | bytes 884744 | tf_op jit(solution)/shard_map/ppermute | solution.py:29
  58.0 7.3 %collective-permute-start.3 = (f32[2,192,192]{2,1,0:T(8,128)S(1)}, f32[2,192,192]{2,1,0:T(8,128)S(1)}, u32[]{:S(2)}, u32[]{:S(2)}) collective-permute-start(f32[2,192,192]{2,1,0:T(8,128)S(1)} %constant_dynamic-slice_fusion.2), channel_id=1, source_target_pairs={{0,16},{8,24},{16,0},{24,8},{1,17},{9,25},{17,1},{25,9},{2,18},{10... | collective-permute-start | bytes 884744 | tf_op jit(solution)/shard_map/ppermute | solution.py:29
  64.0 11.0 %collective-permute-start.8 = (f32[2,192,192]{2,1,0:T(8,128)S(1)}, f32[2,192,192]{2,1,0:T(8,128)S(1)}, u32[]{:S(2)}, u32[]{:S(2)}) collective-permute-start(f32[2,192,192]{2,1,0:T(8,128)S(1)} %get-tuple-element.5), channel_id=1, source_target_pairs={{0,8},{8,0},{16,24},{24,16},{1,9},{9,1},{17,25},{25,17},{2,10},{10... | collective-permute-start | bytes 884744 | tf_op jit(solution)/shard_map/ppermute | solution.py:32
  65.4 11.2 %collective-permute-start.4 = (f32[2,192,192]{2,1,0:T(8,128)S(1)}, f32[2,192,192]{2,1,0:T(8,128)S(1)}, u32[]{:S(2)}, u32[]{:S(2)}) collective-permute-start(f32[2,192,192]{2,1,0:T(8,128)S(1)} %get-tuple-element.3), channel_id=1, source_target_pairs={{0,16},{8,24},{16,0},{24,8},{1,17},{9,25},{17,1},{25,9},{2,18},{10... | collective-permute-start | bytes 884744 | tf_op jit(solution)/shard_map/ppermute | solution.py:32
  75.0 12.6 %collective-permute-start.9 = (f32[4,192,192]{2,1,0:T(8,128)S(1)}, f32[4,192,192]{2,1,0:T(8,128)S(1)}, u32[]{:S(2)}, u32[]{:S(2)}) collective-permute-start(f32[4,192,192]{2,1,0:T(8,128)S(1)} %constant_dynamic-update-slice_fusion.2), channel_id=1, source_target_pairs={{0,16},{8,24},{16,0},{24,8},{1,17},{9,25},{17,1},{25,9},{2,18},{10... | collective-permute-start | bytes 1769480 | tf_op jit(solution)/shard_map/ppermute | solution.py:32
  76.7 11.0 %collective-permute-start.5 = (f32[4,192,192]{2,1,0:T(8,128)S(1)}, f32[4,192,192]{2,1,0:T(8,128)S(1)}, u32[]{:S(2)}, u32[]{:S(2)}) collective-permute-start(f32[4,192,192]{2,1,0:T(8,128)S(1)} %constant_dynamic-update-slice_fusion.6), channel_id=1, source_target_pairs={{0,8},{8,0},{16,24},{24,16},{1,9},{9,1},{17,25},{25,17},{2,10},{10... | collective-permute-start | bytes 1769480 | tf_op jit(solution)/shard_map/ppermute | solution.py:32
  77.7 10.1 %copy-start.7 = (f32[16,192]{1,0:T(8,128)S(1)}, f32[16,192]{1,0:T(8,128)}, u32[]{:S(2)}) copy-start(f32[16,192]{1,0:T(8,128)} %param.12) | copy-start | bytes 36868
  87.8 18.3 %copy-start.9 = (s32[16,2]{0,1:T(2,128)S(1)}, s32[16,2]{0,1:T(2,128)}, u32[]{:S(2)}) copy-start(s32[16,2]{0,1:T(2,128)} %param.14) | copy-start | bytes 388
  87.8 19.0 %copy-start.8 = (f32[16,2]{0,1:T(2,128)S(1)}, f32[16,2]{0,1:T(2,128)}, u32[]{:S(2)}) copy-start(f32[16,2]{0,1:T(2,128)} %param.15) | copy-start | bytes 388
  89.8 49.6 %copy-start = (f32[16,192,192]{2,1,0:T(8,128)}, f32[16,192,192]{2,1,0:T(8,128)S(1)}, u32[]{:S(2)}) copy-start(f32[16,192,192]{2,1,0:T(8,128)S(1)} %get-tuple-element.7.refs_1_.refs_7_) | copy-start | bytes 7077892
  89.8 48.5 %collective-permute-start.11 = (f32[16,192,192]{2,1,0:T(8,128)S(1)}, f32[16,192,192]{2,1,0:T(8,128)}, u32[]{:S(2)}, u32[]{:S(2)}) collective-permute-start(f32[16,192,192]{2,1,0:T(8,128)S(1)} %get-tuple-element.7.refs_1_.refs_7_), channel_id=1, source_target_pairs={{1,0},{2,1},{3,2},{4,3},{5,4},{6,5},{7,6},{9,8},{10,9},{11,10},{12... | collective-permute-start | bytes 7077896 | tf_op jit(solution)/shard_map/ppermute | solution.py:19
  91.8 47.7 %collective-permute-start.10 = (f32[16,192,192]{2,1,0:T(8,128)S(1)}, f32[16,192,192]{2,1,0:T(8,128)}, u32[]{:S(2)}, u32[]{:S(2)}) collective-permute-start(f32[16,192,192]{2,1,0:T(8,128)S(1)} %get-tuple-element.7.refs_1_.refs_7_), channel_id=1, source_target_pairs={{0,1},{1,2},{2,3},{3,4},{4,5},{5,6},{6,7},{8,9},{9,10},{10,11},{11... | collective-permute-start | bytes 7077896 | tf_op jit(solution)/shard_map/ppermute | solution.py:18
  149.3 21.7 %copy-start.1 = (f32[8,192,192]{2,1,0:T(8,128)S(1)}, f32[8,192,192]{2,1,0:T(8,128)}, u32[]{:S(2)}) copy-start(f32[8,192,192]{2,1,0:T(8,128)} %shard_map.97.refs_2_) | copy-start | bytes 3538948
  149.3 25.2 %collective-permute-start.14 = (f32[8,192,192]{2,1,0:T(8,128)}, f32[8,192,192]{2,1,0:T(8,128)S(1)}, u32[]{:S(2)}, u32[]{:S(2)}) collective-permute-start(f32[8,192,192]{2,1,0:T(8,128)} %shard_map.97.refs_2_), channel_id=1, source_target_pairs={{1,0},{2,1},{3,2},{4,3},{5,4},{6,5},{7,6},{9,8},{10,9},{11,10},{12... | collective-permute-start | bytes 3538952 | tf_op jit(solution)/shard_map/ppermute | solution.py:19
  151.4 23.1 %collective-permute-start.12 = (f32[8,192,192]{2,1,0:T(8,128)}, f32[8,192,192]{2,1,0:T(8,128)}, u32[]{:S(2)}, u32[]{:S(2)}) collective-permute-start(f32[8,192,192]{2,1,0:T(8,128)} %shard_map.97.refs_2_), channel_id=1, source_target_pairs={{0,1},{1,2},{2,3},{3,4},{4,5},{5,6},{6,7},{8,9},{9,10},{10,11},{11... | collective-permute-start | bytes 3538952 | tf_op jit(solution)/shard_map/ppermute | solution.py:18
  165.2 23.9 %collective-permute-start.15 = (f32[8,192,192]{2,1,0:T(8,128)}, f32[8,192,192]{2,1,0:T(8,128)}, u32[]{:S(2)}, u32[]{:S(2)}) collective-permute-start(f32[8,192,192]{2,1,0:T(8,128)} %shard_map.98.refs_3_), channel_id=1, source_target_pairs={{1,0},{2,1},{3,2},{4,3},{5,4},{6,5},{7,6},{9,8},{10,9},{11,10},{12... | collective-permute-start | bytes 3538952 | tf_op jit(solution)/shard_map/ppermute | solution.py:19
  167.2 23.1 %collective-permute-start.13 = (f32[8,192,192]{2,1,0:T(8,128)}, f32[8,192,192]{2,1,0:T(8,128)}, u32[]{:S(2)}, u32[]{:S(2)}) collective-permute-start(f32[8,192,192]{2,1,0:T(8,128)} %shard_map.98.refs_3_), channel_id=1, source_target_pairs={{0,1},{1,2},{2,3},{3,4},{4,5},{5,6},{6,7},{8,9},{9,10},{10,11},{11... | collective-permute-start | bytes 3538952 | tf_op jit(solution)/shard_map/ppermute | solution.py:18
  174.5 15.8 %copy-start.6 = (f32[8,192,192]{2,1,0:T(8,128)}, f32[8,192,192]{2,1,0:T(8,128)S(1)}, u32[]{:S(2)}) copy-start(f32[8,192,192]{2,1,0:T(8,128)S(1)} %collective-permute-done.14.refs_4_) | copy-start | bytes 3538948

commit v12 on v11

--- a/solution.py
+++ b/solution.py
@@ -157,15 +157,39 @@
     return lax.dot_general(lhs, rhs, dims, preferred_element_type=jnp.float32)
 
 
-def coupling_kernel(nb_ref, size_ref, fock_ref, *refs, final, width, group, start, nsrc):
+def coupling_kernel(nb_ref, size_ref, fock_ref, *refs, mode, final, width, group, start, nsrc):
     sources = refs[:nsrc]
-    margin_ref, ex_ref, col_ref, row_ref, own_ref, out_ref, tbuf, sems, acc_ref = refs[nsrc:]
+    margin_ref = refs[nsrc]
+    if mode == "local":
+        out_ref, tbuf, sems, acc_ref = refs[nsrc + 1:]
+    else:
+        ex_ref, col_ref, row_ref, own_ref = refs[nsrc + 1:nsrc + 5]
+        partial_ref = refs[nsrc + 5] if mode == "remote" else None
+        out_ref, tbuf, sems, acc_ref = refs[-4:]
     i = pl.program_id(0)
     steps = pl.num_programs(0)
 
+    def taken(q):
+        if mode == "local":
+            return q // width == 1
+        if mode == "remote":
+            return q // width != 1
+        return None
+
+    def when(condition, body):
+        if condition is None:
+            body()
+        else:
+            pl.when(condition)(body)
+
     def fetch(step, slot):
         for k in range(2 * group):
-            fetch_block(sources, width, nb_ref[2 * (start + group * step) + k], tbuf.at[slot, k], sems.at[slot, k])
+            q = nb_ref[2 * (start + group * step) + k]
+            if mode == "local":
+                copy = pltpu.make_async_copy(sources[0].at[q % width], tbuf.at[slot, k], sems.at[slot, k])
+                when(taken(q), copy.start)
+            else:
+                when(taken(q), functools.partial(fetch_block, sources, width, q, tbuf.at[slot, k], sems.at[slot, k]))
 
     @pl.when(i == 0)
     def _():
@@ -179,27 +203,31 @@
     transposed = (((1,), (1,)), ((), ()))
     for g in range(group):
         p = start + i * group + g
-        splits = []
+        size = size_ref[p]
+        if mode == "remote":
+            acc_ref[...] = partial_ref[g]
+        else:
+            acc_ref[...] = jnp.zeros((NPNO, NPNO), jnp.float32)
         for n in range(2):
             k = 2 * g + n
-            pltpu.make_async_copy(sources[0].at[0], tbuf.at[slot, k], sems.at[slot, k]).wait()
-            splits.append(split_bf16(tbuf[slot, k]))
-        size = size_ref[p]
-        acc_ref[...] = jnp.zeros((NPNO, NPNO), jnp.float32)
-        for m in CLASS_SIZES:
-
-            @pl.when(size == m)
-            def _():
-                total = None
-                for n in range(2):
-                    side = margin_ref[g, n, :m, :]
-                    t_hi, t_lo = splits[n]
-                    inner = mm(side, t_hi) + mm(side, t_lo)
-                    w_hi, w_lo = split_bf16(fock_ref[2 * p + n] * inner)
-                    outer = mm(w_hi, side, transposed) + mm(w_lo, side, transposed)
-                    total = outer if total is None else total + outer
-                acc_ref[:m, :m] = total
-
+
+            def term(g=g, n=n, k=k, p=p, size=size):
+                pltpu.make_async_copy(sources[0].at[0], tbuf.at[slot, k], sems.at[slot, k]).wait()
+                t_hi, t_lo = split_bf16(tbuf[slot, k])
+                for m in CLASS_SIZES:
+
+                    @pl.when(size == m)
+                    def _():
+                        side = margin_ref[g, n, :m, :]
+                        inner = mm(side, t_hi) + mm(side, t_lo)
+                        w_hi, w_lo = split_bf16(fock_ref[2 * p + n] * inner)
+                        acc_ref[:m, :m] += mm(w_hi, side, transposed) + mm(w_lo, side, transposed)
+
+            when(taken(nb_ref[2 * p + n]), term)
+
+        if mode == "local":
+            out_ref[g] = acc_ref[...]
+            continue
         denominator = col_ref[g] + row_ref[g]
         amplitudes = own_ref[g]
         residual = ex_ref[g] + denominator * amplitudes - acc_ref[...]
@@ -209,26 +237,34 @@
             out_ref[g] = amplitudes - residual / denominator
 
 
-def coupling_step(nb, sizes, fock, sources, margin, exchange, energy, own, final, start=0, count=None):
-    pairs = own.shape[0]
+def coupling_step(
+    nb, sizes, fock, sources, margin, exchange, energy, own, final, start=0, count=None, mode="all", partial=None
+):
+    pairs = margin.shape[0]
     count = pairs if count is None else count
     group = next(g for g in (4, 2, 1) if count % g == 0 and start % g == 0)
     base = start // group
-    column = energy.reshape(pairs, NPNO, 1)
-    row = energy.reshape(pairs, 1, NPNO)
     hbm = pl.BlockSpec(memory_space=pl.ANY)
     own_spec = pl.BlockSpec((group, NPNO, NPNO), lambda i, q, s, f: (i + base, 0, 0))
-    grid_spec = pltpu.PrefetchScalarGridSpec(
-        num_scalar_prefetch=3,
-        grid=(count // group,),
-        in_specs=[hbm] * len(sources)
-        + [
-            pl.BlockSpec((group, 2, NPNO, NPNO), lambda i, q, s, f: (i + base, 0, 0, 0)),
+    in_specs = [hbm] * len(sources) + [
+        pl.BlockSpec((group, 2, NPNO, NPNO), lambda i, q, s, f: (i + base, 0, 0, 0))
+    ]
+    operands = [*sources, margin]
+    if mode != "local":
+        in_specs += [
             own_spec,
             pl.BlockSpec((group, NPNO, 1), lambda i, q, s, f: (i + base, 0, 0)),
             pl.BlockSpec((group, 1, NPNO), lambda i, q, s, f: (i + base, 0, 0)),
             own_spec,
-        ],
+        ]
+        operands += [exchange, energy.reshape(pairs, NPNO, 1), energy.reshape(pairs, 1, NPNO), own]
+    if mode == "remote":
+        in_specs.append(pl.BlockSpec((group, NPNO, NPNO), lambda i, q, s, f: (i, 0, 0)))
+        operands.append(partial)
+    grid_spec = pltpu.PrefetchScalarGridSpec(
+        num_scalar_prefetch=3,
+        grid=(count // group,),
+        in_specs=in_specs,
         out_specs=pl.BlockSpec((group, NPNO, NPNO), lambda i, q, s, f: (i, 0, 0)),
         scratch_shapes=[
             pltpu.VMEM((2, 2 * group, NPNO, NPNO), jnp.float32),
@@ -238,7 +274,13 @@
     )
     flops = count * 2 * 4 * 2 * NPNO * NPNO * NPNO
     kernel = functools.partial(
-        coupling_kernel, final=final, width=sources[0].shape[0], group=group, start=start, nsrc=len(sources)
+        coupling_kernel,
+        mode=mode,
+        final=final,
+        width=sources[0].shape[0],
+        group=group,
+        start=start,
+        nsrc=len(sources),
     )
     return pl.pallas_call(
         kernel,
@@ -249,7 +291,7 @@
             bytes_accessed=count * NPNO * NPNO * (2 * 4 + 2 * 2 + 3 * 4),
             transcendentals=0,
         ),
-    )(nb, sizes, fock, *sources, margin, exchange, column, row, own)
+    )(nb, sizes, fock, *operands)
 
 
 def chunked_halo(chunks):
@@ -292,14 +334,16 @@
     fock = fock_coupling.reshape(-1)
 
     chunk = pair_dev // 2 if pair_dev % 8 == 0 else pair_dev
-    parts = [-(exchange_ints / denominator)]
-    sources = chunked_halo(parts)
-    amplitudes = jnp.concatenate(parts, axis=0)
+    amplitudes = -(exchange_ints / denominator)
+    sources = chunked_halo([amplitudes])
     for iteration in range(1, ITERS):
+        local = coupling_step(
+            local_rows, sizes, fock, [amplitudes], margin, None, None, None, False, mode="local"
+        )
         parts = [
             coupling_step(
                 local_rows, sizes, fock, sources, margin, exchange_ints, pno_energy, amplitudes,
-                False, c * chunk, chunk,
+                False, c * chunk, chunk, mode="remote", partial=local[c * chunk:(c + 1) * chunk],
             )
             for c in range(pair_dev // chunk)
         ]

time: 206 us -> 211 us (1.024)
  Pallas kernels: 49.8 us -> 62.8 us
  waiting for transfers between devices: 96.5 us -> 84 us
  local copies, waits for them, and re-layouts: 8.82 us -> 12.8 us
    pallas_call x3 -> x4, Pallas kernels: 34 us -> 47.1 us  [coupling_step(): pl.pallas_call(kernel, grid_spec=grid_spec, out_shape=jax.ShapeDtypeStruc...]
    ppermute x4, waiting for transfers between devices: 52.1 us -> 40.2 us  [halo_sources(): from_right = lax.ppermute(cells, axis, [(i + 1, i) for i in range(ends)])]
    slice x0 -> x1, local copies, waits for them, and re-layouts: none -> 3.81 us  [per_device(): local[c * chunk:(c + 1) * chunk]]
  transfers between devices with their start and end apart: 16 -> 16, of which waited for: 11 -> 12; matrix products, arithmetic and copies ran while one was open for 7% -> 9% of each run, Pallas kernels for 9% -> 12%
where the time goes in v12:
time: 211 us; the launch traced here: 209 us
  waiting for transfers between devices  84 us (40%)
  Pallas kernels  62.8 us (30%)
  starting transfers between devices  38.7 us (18%)
  local copies, waits for them, and re-layouts  12.8 us (6%)
  other arithmetic  9.39 us (4%)
    pallas_call x4, Pallas kernels, coupling_step(): pl.pallas_call(kernel, grid_spec=grid_spec, out_shape=jax.ShapeDtypeStruc...  47.1 us
    ppermute x4, waiting for transfers between devices, halo_sources(): from_right = lax.ppermute(cells, axis, [(i + 1, i) for i in range(ends)])  40.2 us
    ppermute x4, starting transfers between devices, halo_sources(): from_left = lax.ppermute(cells, axis, [(i, i + 1) for i in range(ends)])  25.6 us
    ppermute x4, waiting for transfers between devices, halving_stream(): other = lax.ppermute(piece, 'aux', [(i, i ^ bit) for i in range(count)])  20.4 us
    ppermute x4, waiting for transfers between devices, halving_stream(): lax.ppermute(send, 'aux', [(i, i ^ bit) for i in range(count)])  19.8 us
    pallas_call x2, Pallas kernels, partial_exchange(): pl.pallas_call(functools.partial(exchange_kernel, occ=occ, group=group, s...  15.7 us
    ppermute x4, starting transfers between devices, halo_sources(): from_right = lax.ppermute(cells, axis, [(i + 1, i) for i in range(ends)])  7.72 us
  transfers between devices with their start and end apart: 16, of which 12 were waited for; matrix products, arithmetic and copies ran while one was open for 9% of the time, Pallas kernels for 12%

profile of v12, /device:TPU:1, one launch (start us, length us, event | category | flops | bytes accessed | tf_op | source)
XLA Modules:
  0.0 208.9 jit_solution(387816941978263584)
XLA Ops:
  0.6 2.0 collective-permute-start.1
  2.6 4.6 %collective-permute-start = (bf16[4,512,256]{2,1,0:T(8,128)(2,1)}, bf16[4,512,256]{2,1,0:T(8,128)(2,1)S(1)}, u32[]{:S(2)}, u32[]{:S(2)}) collective-permute-start(bf16[4,512,256]{2,1,0:T(8,128)(2,1)} %t_own.3), channel_id=1, source_target_pairs={{0,1},{1,2},{2,3},{3,4},{4,5},{5,6},{6,7},{8,9},{9,10},{10,11},{11... | collective-permute-start | bytes 3145736 | tf_op jit(solution)/shard_map/ppermute | solution.py:18
  7.2 1.2 compare_select_fusion.2.size_ref
  8.4 0.7 broadcast_subtract_fusion
  9.1 0.6 slice_bitcast_fusion
  9.7 8.3 %collective-permute-done.1.t_right = bf16[4,512,256]{2,1,0:T(8,128)(2,1)S(1)} collective-permute-done((bf16[4,512,256]{2,1,0:T(8,128)(2,1)}, bf16[4,512,256]{2,1,0:T(8,128)(2,1)S(1)}, u32[]{:S(2)}, u32[]{:S(2)}) %collective-permute-start.1) | collective-permute-done | bytes 1048608 | tf_op jit(solution)/shard_map/ppermute | solution.py:19
  17.9 1.3 collective-permute-done.t_left
  19.2 1.0 copy-done.5
  20.2 7.8 %shard_map.96 = f32[8,192,192]{2,1,0:T(8,128)} custom-call(s32[16]{0:T(128)} %get-tuple-element.11.lead_ref, s32[16]{0:T(128)} %get-tuple-element.10.trail_ref, s32[16]{0:T(128)} %compare_select_fusion.2.size_ref, bf16[4,512,256]{2,1,0:T(8,128)(2,1)} %copy-done.5, bf16[4,512,256]{2,1,0:T(8,128)(2,1)} %t_own.3, bf16[4,512,256]{2,1,0:T(8,128)(2,1)} %copy-done.4, ...), custom_call_target="tpu_custom_call" | custom-call | flops 1107296256 | bytes 6946816 | tf_op jit(solution)/shard_map/pallas_call | solution.py:138
  28.0 1.2 constant_dynamic-slice_fusion.1
  29.2 1.3 collective-permute-start.6
  30.5 7.9 %shard_map.95 = f32[8,192,192]{2,1,0:T(8,128)} custom-call(s32[16]{0:T(128)} %get-tuple-element.11.lead_ref, s32[16]{0:T(128)} %get-tuple-element.10.trail_ref, s32[16]{0:T(128)} %compare_select_fusion.2.size_ref, bf16[4,512,256]{2,1,0:T(8,128)(2,1)} %copy-done.5, bf16[4,512,256]{2,1,0:T(8,128)(2,1)} %t_own.3, bf16[4,512,256]{2,1,0:T(8,128)(2,1)} %copy-done.4, ...), custom_call_target="tpu_custom_call" | custom-call | flops 1107296256 | bytes 6946816 | tf_op jit(solution)/shard_map/pallas_call | solution.py:138
  38.4 2.2 %constant_dynamic-slice_fusion.3 = f32[4,192,192]{2,1,0:T(8,128)} fusion(f32[8,192,192]{2,1,0:T(8,128)} %shard_map.95, s32[]{:T(128)S(6)} %select_n.82), kind=kLoop, calls=%fused_computation.18 | loop fusion | bytes 1179652 | tf_op jit(solution)/shard_map/dynamic_slice | solution.py:28
  40.6 1.2 collective-permute-start.2
  42.0 0.3 collective-permute-start.7
  42.3 14.3 %collective-permute-done.2 = f32[4,192,192]{2,1,0:T(8,128)} collective-permute-done((f32[4,192,192]{2,1,0:T(8,128)}, f32[4,192,192]{2,1,0:T(8,128)}, u32[]{:S(2)}, u32[]{:S(2)}) %collective-permute-start.2) | collective-permute-done | bytes 589856 | tf_op jit(solution)/shard_map/ppermute | solution.py:29
  56.6 1.2 dynamic-slice_add_fusion.1
  58.0 5.5 %collective-permute-done.7 = f32[2,192,192]{2,1,0:T(8,128)S(1)} collective-permute-done((f32[2,192,192]{2,1,0:T(8,128)S(1)}, f32[2,192,192]{2,1,0:T(8,128)S(1)}, u32[]{:S(2)}, u32[]{:S(2)}) %collective-permute-start.7) | collective-permute-done | bytes 294944 | tf_op jit(solution)/shard_map/ppermute | solution.py:29
  63.7 1.3 collective-permute-start.8
  65.1 0.3 collective-permute-start.4
  65.4 9.5 %collective-permute-done.8 = f32[2,192,192]{2,1,0:T(8,128)S(1)} collective-permute-done((f32[2,192,192]{2,1,0:T(8,128)S(1)}, f32[2,192,192]{2,1,0:T(8,128)S(1)}, u32[]{:S(2)}, u32[]{:S(2)}) %collective-permute-start.8) | collective-permute-done | bytes 294944 | tf_op jit(solution)/shard_map/ppermute | solution.py:32
  75.0 1.4 collective-permute-done.4
  76.4 0.9 collective-permute-start.5
  77.3 0.1 broadcast.30.clone
  77.5 0.1 broadcast.30.clone.1
  77.7 9.3 %collective-permute-done.9 = f32[4,192,192]{2,1,0:T(8,128)S(1)} collective-permute-done((f32[4,192,192]{2,1,0:T(8,128)S(1)}, f32[4,192,192]{2,1,0:T(8,128)S(1)}, u32[]{:S(2)}, u32[]{:S(2)}) %collective-permute-start.9) | collective-permute-done | bytes 589856 | tf_op jit(solution)/shard_map/ppermute | solution.py:32
  87.1 0.2 collective-permute-done.5
  87.4 2.1 pad_maximum_fusion
  89.4 1.9 collective-permute-start.11
  91.3 13.5 %collective-permute-start.10 = (f32[16,192,192]{2,1,0:T(8,128)S(1)}, f32[16,192,192]{2,1,0:T(8,128)}, u32[]{:S(2)}, u32[]{:S(2)}) collective-permute-start(f32[16,192,192]{2,1,0:T(8,128)S(1)} %get-tuple-element.9.refs_0_.refs_1_.refs_7_), channel_id=1, source_target_pairs={{0,1},{1,2},{2,3},{3,4},{4,5},{5,6},{6,7},{8,9},{9,10},{10,11},{11... | collective-permute-start | bytes 7077896 | tf_op jit(solution)/shard_map/ppermute | solution.py:18
  104.9 0.6 broadcast_in_dim.26.refs_6_.refs_9_
  105.6 0.7 reshape.20.nb_ref
  106.3 0.7 reshape.21.fock_ref
  107.0 1.7 copy.14.refs_5_.refs_8_
  108.7 6.6 %shard_map.97 = f32[16,192,192]{2,1,0:T(8,128)} custom-call(s32[32]{0:T(128)} %reshape.20.nb_ref, s32[16]{0:T(128)} %compare_select_fusion.2.size_ref, f32[32]{0:T(128)} %reshape.21.fock_ref, f32[16,192,192]{2,1,0:T(8,128)} %copy-done, bf16[16,2,192,192]{3,2,1,0:T(8,128)(2,1)} %refs_6_.1), custom_call_target="tpu_custom_call" | custom-call | flops 1811939328 | bytes 14155776 | tf_op jit(solution)/shard_map/pallas_call | solution.py:285
  115.3 3.8 %fusion = (f32[8,192,192]{2,1,0:T(8,128)}, f32[8,192,192]{2,1,0:T(8,128)}) fusion(f32[16,192,192]{2,1,0:T(8,128)} %shard_map.97), kind=kLoop, calls=%fused_computation.26 | loop fusion | bytes 4718592 | tf_op jit(solution)/shard_map/slice | solution.py:346
  119.1 18.7 %collective-permute-done.11.refs_2_ = f32[16,192,192]{2,1,0:T(8,128)} collective-permute-done((f32[16,192,192]{2,1,0:T(8,128)S(1)}, f32[16,192,192]{2,1,0:T(8,128)}, u32[]{:S(2)}, u32[]{:S(2)}) %collective-permute-start.11) | collective-permute-done | bytes 2359328 | tf_op jit(solution)/shard_map/ppermute | solution.py:19
  137.8 1.1 collective-permute-done.10.refs_0_
  138.9 11.6 %shard_map.98.refs_2_ = f32[8,192,192]{2,1,0:T(8,128)} custom-call(s32[32]{0:T(128)} %reshape.20.nb_ref, s32[16]{0:T(128)} %compare_select_fusion.2.size_ref, f32[32]{0:T(128)} %reshape.21.fock_ref, f32[16,192,192]{2,1,0:T(8,128)} %collective-permute-done.10.refs_0_, f32[16,192,192]{2,1,0:T(8,128)} %copy-done, ...), custom_call_target="tpu_custom_call" | custom-call | flops 905969664 | bytes 7077888 | tf_op jit(solution)/shard_map/pallas_call | solution.py:285
  150.5 1.9 collective-permute-start.14
  152.4 3.9 %collective-permute-start.12 = (f32[8,192,192]{2,1,0:T(8,128)}, f32[8,192,192]{2,1,0:T(8,128)}, u32[]{:S(2)}, u32[]{:S(2)}) collective-permute-start(f32[8,192,192]{2,1,0:T(8,128)} %shard_map.98.refs_2_), channel_id=1, source_target_pairs={{0,1},{1,2},{2,3},{3,4},{4,5},{5,6},{6,7},{8,9},{9,10},{10,11},{11... | collective-permute-start | bytes 3538952 | tf_op jit(solution)/shard_map/ppermute | solution.py:18
  156.3 10.8 %shard_map.99.refs_3_ = f32[8,192,192]{2,1,0:T(8,128)} custom-call(s32[32]{0:T(128)} %reshape.20.nb_ref, s32[16]{0:T(128)} %compare_select_fusion.2.size_ref, f32[32]{0:T(128)} %reshape.21.fock_ref, f32[16,192,192]{2,1,0:T(8,128)} %collective-permute-done.10.refs_0_, f32[16,192,192]{2,1,0:T(8,128)} %copy-done, ...), custom_call_target="tpu_custom_call" | custom-call | flops 905969664 | bytes 7077888 | tf_op jit(solution)/shard_map/pallas_call | solution.py:285
  167.1 1.9 collective-permute-start.15
  169.1 3.6 %collective-permute-start.13 = (f32[8,192,192]{2,1,0:T(8,128)}, f32[8,192,192]{2,1,0:T(8,128)}, u32[]{:S(2)}, u32[]{:S(2)}) collective-permute-start(f32[8,192,192]{2,1,0:T(8,128)} %shard_map.99.refs_3_), channel_id=1, source_target_pairs={{0,1},{1,2},{2,3},{3,4},{4,5},{5,6},{6,7},{8,9},{9,10},{10,11},{11... | collective-permute-start | bytes 3538952 | tf_op jit(solution)/shard_map/ppermute | solution.py:18
  172.7 3.4 %pad_maximum_fusion.1.refs_10_ = f32[16,192,192]{2,1,0:T(8,128)} fusion(f32[8,192,192]{2,1,0:T(8,128)} %shard_map.99.refs_3_, f32[8,192,192]{2,1,0:T(8,128)S(1)} %copy-done.1), kind=kLoop, calls=%fused_computation.1 | loop fusion | flops 589824 | bytes 4718592 | tf_op jit(solution)/shard_map/concatenate | solution.py:351
  176.2 13.2 %collective-permute-done.15.refs_5_ = f32[8,192,192]{2,1,0:T(8,128)} collective-permute-done((f32[8,192,192]{2,1,0:T(8,128)}, f32[8,192,192]{2,1,0:T(8,128)}, u32[]{:S(2)}, u32[]{:S(2)}) %collective-permute-start.15) | collective-permute-done | bytes 1179680 | tf_op jit(solution)/shard_map/ppermute | solution.py:19
  189.4 1.2 collective-permute-done.13.refs_1_
  190.6 18.1 %shard_map.100 = f32[16,192,192]{2,1,0:T(8,128)} custom-call(s32[32]{0:T(128)} %reshape.20.nb_ref, s32[16]{0:T(128)} %compare_select_fusion.2.size_ref, f32[32]{0:T(128)} %reshape.21.fock_ref, f32[8,192,192]{2,1,0:T(8,128)} %collective-permute-done.12.refs_0_, f32[8,192,192]{2,1,0:T(8,128)} %collective-permute-done.13.refs_1_, ...), custom_call_target="tpu_custom_call" | custom-call | flops 1811939328 | bytes 14155776 | tf_op jit(solution)/shard_map/pallas_call | solution.py:285
  (41 shorter events, 1.1 us)
Async XLA Ops:
  0.6 17.3 %collective-permute-start.1 = (bf16[4,512,256]{2,1,0:T(8,128)(2,1)}, bf16[4,512,256]{2,1,0:T(8,128)(2,1)S(1)}, u32[]{:S(2)}, u32[]{:S(2)}) collective-permute-start(bf16[4,512,256]{2,1,0:T(8,128)(2,1)} %t_own.3), channel_id=1, source_target_pairs={{1,0},{2,1},{3,2},{4,3},{5,4},{6,5},{7,6},{9,8},{10,9},{11,10},{12... | collective-permute-start | bytes 3145736 | tf_op jit(solution)/shard_map/ppermute | solution.py:19
  2.6 16.6 %collective-permute-start = (bf16[4,512,256]{2,1,0:T(8,128)(2,1)}, bf16[4,512,256]{2,1,0:T(8,128)(2,1)S(1)}, u32[]{:S(2)}, u32[]{:S(2)}) collective-permute-start(bf16[4,512,256]{2,1,0:T(8,128)(2,1)} %t_own.3), channel_id=1, source_target_pairs={{0,1},{1,2},{2,3},{3,4},{4,5},{5,6},{6,7},{8,9},{9,10},{10,11},{11... | collective-permute-start | bytes 3145736 | tf_op jit(solution)/shard_map/ppermute | solution.py:18
  17.9 1.3 copy-start.4
  19.2 1.0 copy-start.5
  29.2 12.6 %collective-permute-start.6 = (f32[4,192,192]{2,1,0:T(8,128)S(1)}, f32[4,192,192]{2,1,0:T(8,128)S(1)}, u32[]{:S(2)}, u32[]{:S(2)}) collective-permute-start(f32[4,192,192]{2,1,0:T(8,128)S(1)} %constant_dynamic-slice_fusion.1), channel_id=1, source_target_pairs={{0,16},{8,24},{16,0},{24,8},{1,17},{9,25},{17,1},{25,9},{2,18},{10... | collective-permute-start | bytes 1769480 | tf_op jit(solution)/shard_map/ppermute | solution.py:29
  38.4 3.4 %copy-start.2 = (f32[8,192,192]{2,1,0:T(8,128)S(1)}, f32[8,192,192]{2,1,0:T(8,128)}, u32[]{:S(2)}) copy-start(f32[8,192,192]{2,1,0:T(8,128)} %shard_map.96) | copy-start | bytes 3538948
  40.6 16.0 %collective-permute-start.2 = (f32[4,192,192]{2,1,0:T(8,128)}, f32[4,192,192]{2,1,0:T(8,128)}, u32[]{:S(2)}, u32[]{:S(2)}) collective-permute-start(f32[4,192,192]{2,1,0:T(8,128)} %constant_dynamic-slice_fusion.3), channel_id=1, source_target_pairs={{0,8},{8,0},{16,24},{24,16},{1,9},{9,1},{17,25},{25,17},{2,10},{10... | collective-permute-start | bytes 1769480 | tf_op jit(solution)/shard_map/ppermute | solution.py:29
  41.8 14.8 %copy-start.3 = (f32[8,192,192]{2,1,0:T(8,128)S(1)}, f32[8,192,192]{2,1,0:T(8,128)}, u32[]{:S(2)}) copy-start(f32[8,192,192]{2,1,0:T(8,128)} %shard_map.95) | copy-start | bytes 3538948
  42.0 21.5 %collective-permute-start.7 = (f32[2,192,192]{2,1,0:T(8,128)S(1)}, f32[2,192,192]{2,1,0:T(8,128)S(1)}, u32[]{:S(2)}, u32[]{:S(2)}) collective-permute-start(f32[2,192,192]{2,1,0:T(8,128)S(1)} %constant_dynamic-slice_fusion), channel_id=1, source_target_pairs={{0,8},{8,0},{16,24},{24,16},{1,9},{9,1},{17,25},{25,17},{2,10},{10... | collective-permute-start | bytes 884744 | tf_op jit(solution)/shard_map/ppermute | solution.py:29
  57.9 7.0 %collective-permute-start.3 = (f32[2,192,192]{2,1,0:T(8,128)S(1)}, f32[2,192,192]{2,1,0:T(8,128)S(1)}, u32[]{:S(2)}, u32[]{:S(2)}) collective-permute-start(f32[2,192,192]{2,1,0:T(8,128)S(1)} %constant_dynamic-slice_fusion.2), channel_id=1, source_target_pairs={{0,16},{8,24},{16,0},{24,8},{1,17},{9,25},{17,1},{25,9},{2,18},{10... | collective-permute-start | bytes 884744 | tf_op jit(solution)/shard_map/ppermute | solution.py:29
  63.7 11.2 %collective-permute-start.8 = (f32[2,192,192]{2,1,0:T(8,128)S(1)}, f32[2,192,192]{2,1,0:T(8,128)S(1)}, u32[]{:S(2)}, u32[]{:S(2)}) collective-permute-start(f32[2,192,192]{2,1,0:T(8,128)S(1)} %get-tuple-element.5), channel_id=1, source_target_pairs={{0,8},{8,0},{16,24},{24,16},{1,9},{9,1},{17,25},{25,17},{2,10},{10... | collective-permute-start | bytes 884744 | tf_op jit(solution)/shard_map/ppermute | solution.py:32
  65.1 11.3 %collective-permute-start.4 = (f32[2,192,192]{2,1,0:T(8,128)S(1)}, f32[2,192,192]{2,1,0:T(8,128)S(1)}, u32[]{:S(2)}, u32[]{:S(2)}) collective-permute-start(f32[2,192,192]{2,1,0:T(8,128)S(1)} %get-tuple-element.3), channel_id=1, source_target_pairs={{0,16},{8,24},{16,0},{24,8},{1,17},{9,25},{17,1},{25,9},{2,18},{10... | collective-permute-start | bytes 884744 | tf_op jit(solution)/shard_map/ppermute | solution.py:32
  74.9 12.1 %collective-permute-start.9 = (f32[4,192,192]{2,1,0:T(8,128)S(1)}, f32[4,192,192]{2,1,0:T(8,128)S(1)}, u32[]{:S(2)}, u32[]{:S(2)}) collective-permute-start(f32[4,192,192]{2,1,0:T(8,128)S(1)} %constant_dynamic-update-slice_fusion.2), channel_id=1, source_target_pairs={{0,16},{8,24},{16,0},{24,8},{1,17},{9,25},{17,1},{25,9},{2,18},{10... | collective-permute-start | bytes 1769480 | tf_op jit(solution)/shard_map/ppermute | solution.py:32
  76.4 10.9 %collective-permute-start.5 = (f32[4,192,192]{2,1,0:T(8,128)S(1)}, f32[4,192,192]{2,1,0:T(8,128)S(1)}, u32[]{:S(2)}, u32[]{:S(2)}) collective-permute-start(f32[4,192,192]{2,1,0:T(8,128)S(1)} %constant_dynamic-update-slice_fusion.6), channel_id=1, source_target_pairs={{0,8},{8,0},{16,24},{24,16},{1,9},{9,1},{17,25},{25,17},{2,10},{10... | collective-permute-start | bytes 1769480 | tf_op jit(solution)/shard_map/ppermute | solution.py:32
  77.7 9.6 %copy-start.7 = (f32[16,192]{1,0:T(8,128)S(1)}, f32[16,192]{1,0:T(8,128)}, u32[]{:S(2)}) copy-start(f32[16,192]{1,0:T(8,128)} %param.12) | copy-start | bytes 36868
  87.3 18.1 %copy-start.9 = (s32[16,2]{0,1:T(2,128)S(1)}, s32[16,2]{0,1:T(2,128)}, u32[]{:S(2)}) copy-start(s32[16,2]{0,1:T(2,128)} %param.14) | copy-start | bytes 388
  87.4 18.9 %copy-start.8 = (f32[16,2]{0,1:T(2,128)S(1)}, f32[16,2]{0,1:T(2,128)}, u32[]{:S(2)}) copy-start(f32[16,2]{0,1:T(2,128)} %param.15) | copy-start | bytes 388
  89.4 19.3 %copy-start = (f32[16,192,192]{2,1,0:T(8,128)}, f32[16,192,192]{2,1,0:T(8,128)S(1)}, u32[]{:S(2)}) copy-start(f32[16,192,192]{2,1,0:T(8,128)S(1)} %get-tuple-element.9.refs_0_.refs_1_.refs_7_) | copy-start | bytes 7077892
  89.4 48.4 %collective-permute-start.11 = (f32[16,192,192]{2,1,0:T(8,128)S(1)}, f32[16,192,192]{2,1,0:T(8,128)}, u32[]{:S(2)}, u32[]{:S(2)}) collective-permute-start(f32[16,192,192]{2,1,0:T(8,128)S(1)} %get-tuple-element.9.refs_0_.refs_1_.refs_7_), channel_id=1, source_target_pairs={{1,0},{2,1},{3,2},{4,3},{5,4},{6,5},{7,6},{9,8},{10,9},{11,10},{12... | collective-permute-start | bytes 7077896 | tf_op jit(solution)/shard_map/ppermute | solution.py:19
  91.3 47.5 %collective-permute-start.10 = (f32[16,192,192]{2,1,0:T(8,128)S(1)}, f32[16,192,192]{2,1,0:T(8,128)}, u32[]{:S(2)}, u32[]{:S(2)}) collective-permute-start(f32[16,192,192]{2,1,0:T(8,128)S(1)} %get-tuple-element.9.refs_0_.refs_1_.refs_7_), channel_id=1, source_target_pairs={{0,1},{1,2},{2,3},{3,4},{4,5},{5,6},{6,7},{8,9},{9,10},{10,11},{11... | collective-permute-start | bytes 7077896 | tf_op jit(solution)/shard_map/ppermute | solution.py:18
  150.5 25.7 %collective-permute-start.14 = (f32[8,192,192]{2,1,0:T(8,128)}, f32[8,192,192]{2,1,0:T(8,128)S(1)}, u32[]{:S(2)}, u32[]{:S(2)}) collective-permute-start(f32[8,192,192]{2,1,0:T(8,128)} %shard_map.98.refs_2_), channel_id=1, source_target_pairs={{1,0},{2,1},{3,2},{4,3},{5,4},{6,5},{7,6},{9,8},{10,9},{11,10},{12... | collective-permute-start | bytes 3538952 | tf_op jit(solution)/shard_map/ppermute | solution.py:19
  152.4 23.7 %collective-permute-start.12 = (f32[8,192,192]{2,1,0:T(8,128)}, f32[8,192,192]{2,1,0:T(8,128)}, u32[]{:S(2)}, u32[]{:S(2)}) collective-permute-start(f32[8,192,192]{2,1,0:T(8,128)} %shard_map.98.refs_2_), channel_id=1, source_target_pairs={{0,1},{1,2},{2,3},{3,4},{4,5},{5,6},{6,7},{8,9},{9,10},{10,11},{11... | collective-permute-start | bytes 3538952 | tf_op jit(solution)/shard_map/ppermute | solution.py:18
  156.3 16.4 %copy-start.1 = (f32[8,192,192]{2,1,0:T(8,128)S(1)}, f32[8,192,192]{2,1,0:T(8,128)}, u32[]{:S(2)}) copy-start(f32[8,192,192]{2,1,0:T(8,128)} %shard_map.98.refs_2_) | copy-start | bytes 3538948
  167.1 22.2 %collective-permute-start.15 = (f32[8,192,192]{2,1,0:T(8,128)}, f32[8,192,192]{2,1,0:T(8,128)}, u32[]{:S(2)}, u32[]{:S(2)}) collective-permute-start(f32[8,192,192]{2,1,0:T(8,128)} %shard_map.99.refs_3_), channel_id=1, source_target_pairs={{1,0},{2,1},{3,2},{4,3},{5,4},{6,5},{7,6},{9,8},{10,9},{11,10},{12... | collective-permute-start | bytes 3538952 | tf_op jit(solution)/shard_map/ppermute | solution.py:19
  169.1 21.5 %collective-permute-start.13 = (f32[8,192,192]{2,1,0:T(8,128)}, f32[8,192,192]{2,1,0:T(8,128)}, u32[]{:S(2)}, u32[]{:S(2)}) collective-permute-start(f32[8,192,192]{2,1,0:T(8,128)} %shard_map.99.refs_3_), channel_id=1, source_target_pairs={{0,1},{1,2},{2,3},{3,4},{4,5},{5,6},{6,7},{8,9},{9,10},{10,11},{11... | collective-permute-start | bytes 3538952 | tf_op jit(solution)/shard_map/ppermute | solution.py:18
  176.2 14.4 %copy-start.6 = (f32[8,192,192]{2,1,0:T(8,128)}, f32[8,192,192]{2,1,0:T(8,128)S(1)}, u32[]{:S(2)}) copy-start(f32[8,192,192]{2,1,0:T(8,128)S(1)} %collective-permute-done.14.refs_4_) | copy-start | bytes 3538948

commit v13 on v11

--- a/solution.py
+++ b/solution.py
@@ -159,7 +159,7 @@
 
 def coupling_kernel(nb_ref, size_ref, fock_ref, *refs, final, width, group, start, nsrc):
     sources = refs[:nsrc]
-    margin_ref, ex_ref, col_ref, row_ref, own_ref, out_ref, tbuf, sems, acc_ref = refs[nsrc:]
+    margin_ref, ex_ref, col_ref, row_ref, own_ref, out_ref, tbuf, sems = refs[nsrc:]
     i = pl.program_id(0)
     steps = pl.num_programs(0)
 
@@ -185,7 +185,7 @@
             pltpu.make_async_copy(sources[0].at[0], tbuf.at[slot, k], sems.at[slot, k]).wait()
             splits.append(split_bf16(tbuf[slot, k]))
         size = size_ref[p]
-        acc_ref[...] = jnp.zeros((NPNO, NPNO), jnp.float32)
+        out_ref[g] = jnp.zeros((NPNO, NPNO), jnp.float32)
         for m in CLASS_SIZES:
 
             @pl.when(size == m)
@@ -198,15 +198,13 @@
                     w_hi, w_lo = split_bf16(fock_ref[2 * p + n] * inner)
                     outer = mm(w_hi, side, transposed) + mm(w_lo, side, transposed)
                     total = outer if total is None else total + outer
-                acc_ref[:m, :m] = total
-
-        denominator = col_ref[g] + row_ref[g]
-        amplitudes = own_ref[g]
-        residual = ex_ref[g] + denominator * amplitudes - acc_ref[...]
-        if final:
-            out_ref[g] = residual
-        else:
-            out_ref[g] = amplitudes - residual / denominator
+                denominator = col_ref[g, :m, :] + row_ref[g, :, :m]
+                amplitudes = own_ref[g, :m, :m]
+                residual = ex_ref[g, :m, :m] + denominator * amplitudes - total
+                if final:
+                    out_ref[g, :m, :m] = residual
+                else:
+                    out_ref[g, :m, :m] = amplitudes - residual / denominator
 
 
 def coupling_step(nb, sizes, fock, sources, margin, exchange, energy, own, final, start=0, count=None):
@@ -233,7 +231,6 @@
         scratch_shapes=[
             pltpu.VMEM((2, 2 * group, NPNO, NPNO), jnp.float32),
             pltpu.SemaphoreType.DMA((2, 2 * group)),
-            pltpu.VMEM((NPNO, NPNO), jnp.float32),
         ],
     )
     flops = count * 2 * 4 * 2 * NPNO * NPNO * NPNO

time: 206 us -> 204 us (level)
  Pallas kernels: 49.8 us -> 47 us
    pallas_call x3, Pallas kernels: 34 us -> 31.2 us  [coupling_step(): pl.pallas_call(kernel, grid_spec=grid_spec, out_shape=jax.ShapeDtypeStruc...]
  transfers between devices with their start and end apart: 16 -> 16, of which waited for: 11 -> 11; matrix products, arithmetic and copies ran while one was open for 7% -> 7% of each run, Pallas kernels for 9% -> 8%
where the time goes in v13:
time: 204 us; the launch traced here: 202 us
  waiting for transfers between devices  96.8 us (47%)
  Pallas kernels  47 us (23%)
  starting transfers between devices  38.5 us (19%)
  other arithmetic  9.36 us (5%)
  local copies, waits for them, and re-layouts  8.82 us (4%)
    ppermute x4, waiting for transfers between devices, halo_sources(): from_right = lax.ppermute(cells, axis, [(i + 1, i) for i in range(ends)])  52.6 us
    pallas_call x3, Pallas kernels, coupling_step(): pl.pallas_call(kernel, grid_spec=grid_spec, out_shape=jax.ShapeDtypeStruc...  31.2 us
    ppermute x4, starting transfers between devices, halo_sources(): from_left = lax.ppermute(cells, axis, [(i, i + 1) for i in range(ends)])  25.5 us
    ppermute x4, waiting for transfers between devices, halving_stream(): other = lax.ppermute(piece, 'aux', [(i, i ^ bit) for i in range(count)])  20.6 us
    ppermute x4, waiting for transfers between devices, halving_stream(): lax.ppermute(send, 'aux', [(i, i ^ bit) for i in range(count)])  20 us
    pallas_call x2, Pallas kernels, partial_exchange(): pl.pallas_call(functools.partial(exchange_kernel, occ=occ, group=group, s...  15.9 us
    ppermute x4, starting transfers between devices, halo_sources(): from_right = lax.ppermute(cells, axis, [(i + 1, i) for i in range(ends)])  7.85 us
  transfers between devices with their start and end apart: 16, of which 11 were waited for; matrix products, arithmetic and copies ran while one was open for 7% of the time, Pallas kernels for 8%

profile of v13, /device:TPU:1, one launch (start us, length us, event | category | flops | bytes accessed | tf_op | source)
XLA Modules:
  0.0 201.7 jit_solution(17548411936223185070)
XLA Ops:
  0.6 2.0 collective-permute-start.1
  2.6 4.6 %collective-permute-start = (bf16[4,512,256]{2,1,0:T(8,128)(2,1)}, bf16[4,512,256]{2,1,0:T(8,128)(2,1)S(1)}, u32[]{:S(2)}, u32[]{:S(2)}) collective-permute-start(bf16[4,512,256]{2,1,0:T(8,128)(2,1)} %t_own.3), channel_id=1, source_target_pairs={{0,1},{1,2},{2,3},{3,4},{4,5},{5,6},{6,7},{8,9},{9,10},{10,11},{11... | collective-permute-start | bytes 3145736 | tf_op jit(solution)/shard_map/ppermute | solution.py:18
  7.2 1.2 compare_select_fusion.2.size_ref
  8.4 0.7 broadcast_subtract_fusion
  9.1 0.6 slice_bitcast_fusion
  9.7 8.3 %collective-permute-done.1.t_right = bf16[4,512,256]{2,1,0:T(8,128)(2,1)S(1)} collective-permute-done((bf16[4,512,256]{2,1,0:T(8,128)(2,1)}, bf16[4,512,256]{2,1,0:T(8,128)(2,1)S(1)}, u32[]{:S(2)}, u32[]{:S(2)}) %collective-permute-start.1) | collective-permute-done | bytes 1048608 | tf_op jit(solution)/shard_map/ppermute | solution.py:19
  17.9 1.3 collective-permute-done.t_left
  19.2 1.0 copy-done.5
  20.2 8.0 %shard_map.96 = f32[8,192,192]{2,1,0:T(8,128)} custom-call(s32[16]{0:T(128)} %get-tuple-element.9.lead_ref, s32[16]{0:T(128)} %get-tuple-element.8.trail_ref, s32[16]{0:T(128)} %compare_select_fusion.2.size_ref, bf16[4,512,256]{2,1,0:T(8,128)(2,1)} %copy-done.5, bf16[4,512,256]{2,1,0:T(8,128)(2,1)} %t_own.3, bf16[4,512,256]{2,1,0:T(8,128)(2,1)} %copy-done.4, ...), custom_call_target="tpu_custom_call" | custom-call | flops 1107296256 | bytes 6946816 | tf_op jit(solution)/shard_map/pallas_call | solution.py:138
  28.2 1.2 constant_dynamic-slice_fusion.1
  29.4 1.3 collective-permute-start.6
  30.7 7.9 %shard_map.95 = f32[8,192,192]{2,1,0:T(8,128)} custom-call(s32[16]{0:T(128)} %get-tuple-element.9.lead_ref, s32[16]{0:T(128)} %get-tuple-element.8.trail_ref, s32[16]{0:T(128)} %compare_select_fusion.2.size_ref, bf16[4,512,256]{2,1,0:T(8,128)(2,1)} %copy-done.5, bf16[4,512,256]{2,1,0:T(8,128)(2,1)} %t_own.3, bf16[4,512,256]{2,1,0:T(8,128)(2,1)} %copy-done.4, ...), custom_call_target="tpu_custom_call" | custom-call | flops 1107296256 | bytes 6946816 | tf_op jit(solution)/shard_map/pallas_call | solution.py:138
  38.6 2.2 %constant_dynamic-slice_fusion.3 = f32[4,192,192]{2,1,0:T(8,128)} fusion(f32[8,192,192]{2,1,0:T(8,128)} %shard_map.95, s32[]{:T(128)S(6)} %select_n.82), kind=kLoop, calls=%fused_computation.18 | loop fusion | bytes 1179652 | tf_op jit(solution)/shard_map/dynamic_slice | solution.py:28
  40.8 1.2 collective-permute-start.2
  42.0 0.1 dynamic-slice_add_fusion
  42.1 0.3 collective-permute-start.7
  42.5 14.3 %collective-permute-done.2 = f32[4,192,192]{2,1,0:T(8,128)} collective-permute-done((f32[4,192,192]{2,1,0:T(8,128)}, f32[4,192,192]{2,1,0:T(8,128)}, u32[]{:S(2)}, u32[]{:S(2)}) %collective-permute-start.2) | collective-permute-done | bytes 589856 | tf_op jit(solution)/shard_map/ppermute | solution.py:29
  56.8 1.2 dynamic-slice_add_fusion.1
  58.2 5.7 %collective-permute-done.7 = f32[2,192,192]{2,1,0:T(8,128)S(1)} collective-permute-done((f32[2,192,192]{2,1,0:T(8,128)S(1)}, f32[2,192,192]{2,1,0:T(8,128)S(1)}, u32[]{:S(2)}, u32[]{:S(2)}) %collective-permute-start.7) | collective-permute-done | bytes 294944 | tf_op jit(solution)/shard_map/ppermute | solution.py:29
  64.0 1.3 collective-permute-start.8
  65.4 0.3 collective-permute-start.4
  65.7 9.4 %collective-permute-done.8 = f32[2,192,192]{2,1,0:T(8,128)S(1)} collective-permute-done((f32[2,192,192]{2,1,0:T(8,128)S(1)}, f32[2,192,192]{2,1,0:T(8,128)S(1)}, u32[]{:S(2)}, u32[]{:S(2)}) %collective-permute-start.8) | collective-permute-done | bytes 294944 | tf_op jit(solution)/shard_map/ppermute | solution.py:32
  75.2 1.5 collective-permute-done.4
  76.7 0.7 collective-permute-start.5
  77.4 0.1 broadcast.30.clone
  77.6 0.1 broadcast.30.clone.1
  77.8 9.7 %collective-permute-done.9 = f32[4,192,192]{2,1,0:T(8,128)S(1)} collective-permute-done((f32[4,192,192]{2,1,0:T(8,128)S(1)}, f32[4,192,192]{2,1,0:T(8,128)S(1)}, u32[]{:S(2)}, u32[]{:S(2)}) %collective-permute-start.9) | collective-permute-done | bytes 589856 | tf_op jit(solution)/shard_map/ppermute | solution.py:32
  87.7 2.0 %pad_maximum_fusion = (f32[16,192,192]{2,1,0:T(8,128)}, f32[16,192,192]{2,1,0:T(8,128)S(1)}) fusion(f32[8,192,192]{2,1,0:T(8,128)S(1)} %constant_dynamic-update-slice_fusion, f32[8,192,192]{2,1,0:T(8,128)S(1)} %constant_dynamic-update-slice_fusion.4, f32[16,192]{1,0:T(8,128)S(1)} %copy-done.7), kind=kLoop, calls=%fused_computation | loop fusion | flops 2359296 | bytes 7090176 | tf_op jit(solution)/shard_map/concatenate | solution.py:47
  89.8 1.9 collective-permute-start.11
  91.7 12.9 %collective-permute-start.10 = (f32[16,192,192]{2,1,0:T(8,128)S(1)}, f32[16,192,192]{2,1,0:T(8,128)}, u32[]{:S(2)}, u32[]{:S(2)}) collective-permute-start(f32[16,192,192]{2,1,0:T(8,128)S(1)} %get-tuple-element.7.refs_1_.refs_7_), channel_id=1, source_target_pairs={{0,1},{1,2},{2,3},{3,4},{4,5},{5,6},{6,7},{8,9},{9,10},{10,11},{11... | collective-permute-start | bytes 7077896 | tf_op jit(solution)/shard_map/ppermute | solution.py:18
  104.6 0.6 broadcast_in_dim.26.refs_6_.refs_9_
  105.2 0.1 copy.12
  105.3 0.6 reshape.20.nb_ref
  105.9 0.1 copy.13
  106.0 0.6 reshape.21.fock_ref
  106.6 1.7 copy.14.refs_5_.refs_8_
  108.3 29.3 %collective-permute-done.11.refs_2_ = f32[16,192,192]{2,1,0:T(8,128)} collective-permute-done((f32[16,192,192]{2,1,0:T(8,128)S(1)}, f32[16,192,192]{2,1,0:T(8,128)}, u32[]{:S(2)}, u32[]{:S(2)}) %collective-permute-start.11) | collective-permute-done | bytes 2359328 | tf_op jit(solution)/shard_map/ppermute | solution.py:19
  137.5 1.1 collective-permute-done.10.refs_0_
  138.6 8.8 %shard_map.97.refs_2_ = f32[8,192,192]{2,1,0:T(8,128)} custom-call(s32[32]{0:T(128)} %reshape.20.nb_ref, s32[16]{0:T(128)} %compare_select_fusion.2.size_ref, f32[32]{0:T(128)} %reshape.21.fock_ref, f32[16,192,192]{2,1,0:T(8,128)} %collective-permute-done.10.refs_0_, f32[16,192,192]{2,1,0:T(8,128)} %copy-done, ...), custom_call_target="tpu_custom_call" | custom-call | flops 905969664 | bytes 7077888 | tf_op jit(solution)/shard_map/pallas_call | solution.py:240
  147.4 2.1 %collective-permute-start.14 = (f32[8,192,192]{2,1,0:T(8,128)}, f32[8,192,192]{2,1,0:T(8,128)S(1)}, u32[]{:S(2)}, u32[]{:S(2)}) collective-permute-start(f32[8,192,192]{2,1,0:T(8,128)} %shard_map.97.refs_2_), channel_id=1, source_target_pairs={{1,0},{2,1},{3,2},{4,3},{5,4},{6,5},{7,6},{9,8},{10,9},{11,10},{12... | collective-permute-start | bytes 3538952 | tf_op jit(solution)/shard_map/ppermute | solution.py:19
  149.5 4.1 %collective-permute-start.12 = (f32[8,192,192]{2,1,0:T(8,128)}, f32[8,192,192]{2,1,0:T(8,128)}, u32[]{:S(2)}, u32[]{:S(2)}) collective-permute-start(f32[8,192,192]{2,1,0:T(8,128)} %shard_map.97.refs_2_), channel_id=1, source_target_pairs={{0,1},{1,2},{2,3},{3,4},{4,5},{5,6},{6,7},{8,9},{9,10},{10,11},{11... | collective-permute-start | bytes 3538952 | tf_op jit(solution)/shard_map/ppermute | solution.py:18
  153.6 9.0 %shard_map.98.refs_3_ = f32[8,192,192]{2,1,0:T(8,128)} custom-call(s32[32]{0:T(128)} %reshape.20.nb_ref, s32[16]{0:T(128)} %compare_select_fusion.2.size_ref, f32[32]{0:T(128)} %reshape.21.fock_ref, f32[16,192,192]{2,1,0:T(8,128)} %collective-permute-done.10.refs_0_, f32[16,192,192]{2,1,0:T(8,128)} %copy-done, ...), custom_call_target="tpu_custom_call" | custom-call | flops 905969664 | bytes 7077888 | tf_op jit(solution)/shard_map/pallas_call | solution.py:240
  162.6 1.9 collective-permute-start.15
  164.6 3.9 %collective-permute-start.13 = (f32[8,192,192]{2,1,0:T(8,128)}, f32[8,192,192]{2,1,0:T(8,128)}, u32[]{:S(2)}, u32[]{:S(2)}) collective-permute-start(f32[8,192,192]{2,1,0:T(8,128)} %shard_map.98.refs_3_), channel_id=1, source_target_pairs={{0,1},{1,2},{2,3},{3,4},{4,5},{5,6},{6,7},{8,9},{9,10},{10,11},{11... | collective-permute-start | bytes 3538952 | tf_op jit(solution)/shard_map/ppermute | solution.py:18
  168.4 3.4 %pad_maximum_fusion.1.refs_10_ = f32[16,192,192]{2,1,0:T(8,128)} fusion(f32[8,192,192]{2,1,0:T(8,128)} %shard_map.98.refs_3_, f32[8,192,192]{2,1,0:T(8,128)S(1)} %copy-done.1), kind=kLoop, calls=%fused_computation.1 | loop fusion | flops 589824 | bytes 4718592 | tf_op jit(solution)/shard_map/concatenate | solution.py:304
  171.9 15.1 %collective-permute-done.15.refs_5_ = f32[8,192,192]{2,1,0:T(8,128)} collective-permute-done((f32[8,192,192]{2,1,0:T(8,128)}, f32[8,192,192]{2,1,0:T(8,128)}, u32[]{:S(2)}, u32[]{:S(2)}) %collective-permute-start.15) | collective-permute-done | bytes 1179680 | tf_op jit(solution)/shard_map/ppermute | solution.py:19
  186.9 1.2 collective-permute-done.13.refs_1_
  188.1 13.4 %shard_map.99 = f32[16,192,192]{2,1,0:T(8,128)} custom-call(s32[32]{0:T(128)} %reshape.20.nb_ref, s32[16]{0:T(128)} %compare_select_fusion.2.size_ref, f32[32]{0:T(128)} %reshape.21.fock_ref, f32[8,192,192]{2,1,0:T(8,128)} %collective-permute-done.12.refs_0_, f32[8,192,192]{2,1,0:T(8,128)} %collective-permute-done.13.refs_1_, ...), custom_call_target="tpu_custom_call" | custom-call | flops 1811939328 | bytes 14155776 | tf_op jit(solution)/shard_map/pallas_call | solution.py:240
  (39 shorter events, 0.8 us)
Async XLA Ops:
  0.6 17.3 %collective-permute-start.1 = (bf16[4,512,256]{2,1,0:T(8,128)(2,1)}, bf16[4,512,256]{2,1,0:T(8,128)(2,1)S(1)}, u32[]{:S(2)}, u32[]{:S(2)}) collective-permute-start(bf16[4,512,256]{2,1,0:T(8,128)(2,1)} %t_own.3), channel_id=1, source_target_pairs={{1,0},{2,1},{3,2},{4,3},{5,4},{6,5},{7,6},{9,8},{10,9},{11,10},{12... | collective-permute-start | bytes 3145736 | tf_op jit(solution)/shard_map/ppermute | solution.py:19
  2.6 16.6 %collective-permute-start = (bf16[4,512,256]{2,1,0:T(8,128)(2,1)}, bf16[4,512,256]{2,1,0:T(8,128)(2,1)S(1)}, u32[]{:S(2)}, u32[]{:S(2)}) collective-permute-start(bf16[4,512,256]{2,1,0:T(8,128)(2,1)} %t_own.3), channel_id=1, source_target_pairs={{0,1},{1,2},{2,3},{3,4},{4,5},{5,6},{6,7},{8,9},{9,10},{10,11},{11... | collective-permute-start | bytes 3145736 | tf_op jit(solution)/shard_map/ppermute | solution.py:18
  17.9 1.3 copy-start.4
  19.2 1.0 copy-start.5
  29.4 12.6 %collective-permute-start.6 = (f32[4,192,192]{2,1,0:T(8,128)S(1)}, f32[4,192,192]{2,1,0:T(8,128)S(1)}, u32[]{:S(2)}, u32[]{:S(2)}) collective-permute-start(f32[4,192,192]{2,1,0:T(8,128)S(1)} %constant_dynamic-slice_fusion.1), channel_id=1, source_target_pairs={{0,16},{8,24},{16,0},{24,8},{1,17},{9,25},{17,1},{25,9},{2,18},{10... | collective-permute-start | bytes 1769480 | tf_op jit(solution)/shard_map/ppermute | solution.py:29
  38.6 3.4 %copy-start.2 = (f32[8,192,192]{2,1,0:T(8,128)S(1)}, f32[8,192,192]{2,1,0:T(8,128)}, u32[]{:S(2)}) copy-start(f32[8,192,192]{2,1,0:T(8,128)} %shard_map.96) | copy-start | bytes 3538948
  40.8 16.0 %collective-permute-start.2 = (f32[4,192,192]{2,1,0:T(8,128)}, f32[4,192,192]{2,1,0:T(8,128)}, u32[]{:S(2)}, u32[]{:S(2)}) collective-permute-start(f32[4,192,192]{2,1,0:T(8,128)} %constant_dynamic-slice_fusion.3), channel_id=1, source_target_pairs={{0,8},{8,0},{16,24},{24,16},{1,9},{9,1},{17,25},{25,17},{2,10},{10... | collective-permute-start | bytes 1769480 | tf_op jit(solution)/shard_map/ppermute | solution.py:29
  42.0 14.8 %copy-start.3 = (f32[8,192,192]{2,1,0:T(8,128)S(1)}, f32[8,192,192]{2,1,0:T(8,128)}, u32[]{:S(2)}) copy-start(f32[8,192,192]{2,1,0:T(8,128)} %shard_map.95) | copy-start | bytes 3538948
  42.1 21.7 %collective-permute-start.7 = (f32[2,192,192]{2,1,0:T(8,128)S(1)}, f32[2,192,192]{2,1,0:T(8,128)S(1)}, u32[]{:S(2)}, u32[]{:S(2)}) collective-permute-start(f32[2,192,192]{2,1,0:T(8,128)S(1)} %constant_dynamic-slice_fusion), channel_id=1, source_target_pairs={{0,8},{8,0},{16,24},{24,16},{1,9},{9,1},{17,25},{25,17},{2,10},{10... | collective-permute-start | bytes 884744 | tf_op jit(solution)/shard_map/ppermute | solution.py:29
  58.1 7.2 %collective-permute-start.3 = (f32[2,192,192]{2,1,0:T(8,128)S(1)}, f32[2,192,192]{2,1,0:T(8,128)S(1)}, u32[]{:S(2)}, u32[]{:S(2)}) collective-permute-start(f32[2,192,192]{2,1,0:T(8,128)S(1)} %constant_dynamic-slice_fusion.2), channel_id=1, source_target_pairs={{0,16},{8,24},{16,0},{24,8},{1,17},{9,25},{17,1},{25,9},{2,18},{10... | collective-permute-start | bytes 884744 | tf_op jit(solution)/shard_map/ppermute | solution.py:29
  64.0 11.1 %collective-permute-start.8 = (f32[2,192,192]{2,1,0:T(8,128)S(1)}, f32[2,192,192]{2,1,0:T(8,128)S(1)}, u32[]{:S(2)}, u32[]{:S(2)}) collective-permute-start(f32[2,192,192]{2,1,0:T(8,128)S(1)} %get-tuple-element.5), channel_id=1, source_target_pairs={{0,8},{8,0},{16,24},{24,16},{1,9},{9,1},{17,25},{25,17},{2,10},{10... | collective-permute-start | bytes 884744 | tf_op jit(solution)/shard_map/ppermute | solution.py:32
  65.4 11.3 %collective-permute-start.4 = (f32[2,192,192]{2,1,0:T(8,128)S(1)}, f32[2,192,192]{2,1,0:T(8,128)S(1)}, u32[]{:S(2)}, u32[]{:S(2)}) collective-permute-start(f32[2,192,192]{2,1,0:T(8,128)S(1)} %get-tuple-element.3), channel_id=1, source_target_pairs={{0,16},{8,24},{16,0},{24,8},{1,17},{9,25},{17,1},{25,9},{2,18},{10... | collective-permute-start | bytes 884744 | tf_op jit(solution)/shard_map/ppermute | solution.py:32
  75.1 12.4 %collective-permute-start.9 = (f32[4,192,192]{2,1,0:T(8,128)S(1)}, f32[4,192,192]{2,1,0:T(8,128)S(1)}, u32[]{:S(2)}, u32[]{:S(2)}) collective-permute-start(f32[4,192,192]{2,1,0:T(8,128)S(1)} %constant_dynamic-update-slice_fusion.2), channel_id=1, source_target_pairs={{0,16},{8,24},{16,0},{24,8},{1,17},{9,25},{17,1},{25,9},{2,18},{10... | collective-permute-start | bytes 1769480 | tf_op jit(solution)/shard_map/ppermute | solution.py:32
  76.7 10.9 %collective-permute-start.5 = (f32[4,192,192]{2,1,0:T(8,128)S(1)}, f32[4,192,192]{2,1,0:T(8,128)S(1)}, u32[]{:S(2)}, u32[]{:S(2)}) collective-permute-start(f32[4,192,192]{2,1,0:T(8,128)S(1)} %constant_dynamic-update-slice_fusion.6), channel_id=1, source_target_pairs={{0,8},{8,0},{16,24},{24,16},{1,9},{9,1},{17,25},{25,17},{2,10},{10... | collective-permute-start | bytes 1769480 | tf_op jit(solution)/shard_map/ppermute | solution.py:32
  77.8 9.9 %copy-start.7 = (f32[16,192]{1,0:T(8,128)S(1)}, f32[16,192]{1,0:T(8,128)}, u32[]{:S(2)}) copy-start(f32[16,192]{1,0:T(8,128)} %param.12) | copy-start | bytes 36868
  87.7 17.5 %copy-start.9 = (s32[16,2]{0,1:T(2,128)S(1)}, s32[16,2]{0,1:T(2,128)}, u32[]{:S(2)}) copy-start(s32[16,2]{0,1:T(2,128)} %param.14) | copy-start | bytes 388
  87.7 18.2 %copy-start.8 = (f32[16,2]{0,1:T(2,128)S(1)}, f32[16,2]{0,1:T(2,128)}, u32[]{:S(2)}) copy-start(f32[16,2]{0,1:T(2,128)} %param.15) | copy-start | bytes 388
  89.8 48.8 %copy-start = (f32[16,192,192]{2,1,0:T(8,128)}, f32[16,192,192]{2,1,0:T(8,128)S(1)}, u32[]{:S(2)}) copy-start(f32[16,192,192]{2,1,0:T(8,128)S(1)} %get-tuple-element.7.refs_1_.refs_7_) | copy-start | bytes 7077892
  89.8 47.8 %collective-permute-start.11 = (f32[16,192,192]{2,1,0:T(8,128)S(1)}, f32[16,192,192]{2,1,0:T(8,128)}, u32[]{:S(2)}, u32[]{:S(2)}) collective-permute-start(f32[16,192,192]{2,1,0:T(8,128)S(1)} %get-tuple-element.7.refs_1_.refs_7_), channel_id=1, source_target_pairs={{1,0},{2,1},{3,2},{4,3},{5,4},{6,5},{7,6},{9,8},{10,9},{11,10},{12... | collective-permute-start | bytes 7077896 | tf_op jit(solution)/shard_map/ppermute | solution.py:19
  91.7 46.9 %collective-permute-start.10 = (f32[16,192,192]{2,1,0:T(8,128)S(1)}, f32[16,192,192]{2,1,0:T(8,128)}, u32[]{:S(2)}, u32[]{:S(2)}) collective-permute-start(f32[16,192,192]{2,1,0:T(8,128)S(1)} %get-tuple-element.7.refs_1_.refs_7_), channel_id=1, source_target_pairs={{0,1},{1,2},{2,3},{3,4},{4,5},{5,6},{6,7},{8,9},{9,10},{10,11},{11... | collective-permute-start | bytes 7077896 | tf_op jit(solution)/shard_map/ppermute | solution.py:18
  147.4 21.0 %copy-start.1 = (f32[8,192,192]{2,1,0:T(8,128)S(1)}, f32[8,192,192]{2,1,0:T(8,128)}, u32[]{:S(2)}) copy-start(f32[8,192,192]{2,1,0:T(8,128)} %shard_map.97.refs_2_) | copy-start | bytes 3538948
  147.4 24.4 %collective-permute-start.14 = (f32[8,192,192]{2,1,0:T(8,128)}, f32[8,192,192]{2,1,0:T(8,128)S(1)}, u32[]{:S(2)}, u32[]{:S(2)}) collective-permute-start(f32[8,192,192]{2,1,0:T(8,128)} %shard_map.97.refs_2_), channel_id=1, source_target_pairs={{1,0},{2,1},{3,2},{4,3},{5,4},{6,5},{7,6},{9,8},{10,9},{11,10},{12... | collective-permute-start | bytes 3538952 | tf_op jit(solution)/shard_map/ppermute | solution.py:19
  149.5 22.4 %collective-permute-start.12 = (f32[8,192,192]{2,1,0:T(8,128)}, f32[8,192,192]{2,1,0:T(8,128)}, u32[]{:S(2)}, u32[]{:S(2)}) collective-permute-start(f32[8,192,192]{2,1,0:T(8,128)} %shard_map.97.refs_2_), channel_id=1, source_target_pairs={{0,1},{1,2},{2,3},{3,4},{4,5},{5,6},{6,7},{8,9},{9,10},{10,11},{11... | collective-permute-start | bytes 3538952 | tf_op jit(solution)/shard_map/ppermute | solution.py:18
  162.6 24.3 %collective-permute-start.15 = (f32[8,192,192]{2,1,0:T(8,128)}, f32[8,192,192]{2,1,0:T(8,128)}, u32[]{:S(2)}, u32[]{:S(2)}) collective-permute-start(f32[8,192,192]{2,1,0:T(8,128)} %shard_map.98.refs_3_), channel_id=1, source_target_pairs={{1,0},{2,1},{3,2},{4,3},{5,4},{6,5},{7,6},{9,8},{10,9},{11,10},{12... | collective-permute-start | bytes 3538952 | tf_op jit(solution)/shard_map/ppermute | solution.py:19
  164.6 23.6 %collective-permute-start.13 = (f32[8,192,192]{2,1,0:T(8,128)}, f32[8,192,192]{2,1,0:T(8,128)}, u32[]{:S(2)}, u32[]{:S(2)}) collective-permute-start(f32[8,192,192]{2,1,0:T(8,128)} %shard_map.98.refs_3_), channel_id=1, source_target_pairs={{0,1},{1,2},{2,3},{3,4},{4,5},{5,6},{6,7},{8,9},{9,10},{10,11},{11... | collective-permute-start | bytes 3538952 | tf_op jit(solution)/shard_map/ppermute | solution.py:18
  171.9 16.3 %copy-start.6 = (f32[8,192,192]{2,1,0:T(8,128)}, f32[8,192,192]{2,1,0:T(8,128)S(1)}, u32[]{:S(2)}) copy-start(f32[8,192,192]{2,1,0:T(8,128)S(1)} %collective-permute-done.14.refs_4_) | copy-start | bytes 3538948

commit v14 on v13

--- a/solution.py
+++ b/solution.py
@@ -40,11 +40,12 @@
 def sum_over_aux(halves):
     count = lax.axis_size("aux")
     if count != 4 or halves[0].shape[0] % 4:
-        return lax.psum(jnp.concatenate(halves, axis=0), "aux")
+        return [lax.psum(half, "aux") for half in halves]
     index = lax.axis_index("aux")
-    first = halving_stream(halves[0], index, count, (1, 2))
-    second = halving_stream(halves[1], index, count, (2, 1))
-    return jnp.concatenate([first, second], axis=0)
+    return [
+        halving_stream(halves[0], index, count, (1, 2)),
+        halving_stream(halves[1], index, count, (2, 1)),
+    ]
 
 
 def class_size(natural_orbital_class):
@@ -283,13 +284,16 @@
         )
         for start in (0, half)
     ]
-    exchange_ints = sum_over_aux(halves)
+    exchange_halves = sum_over_aux(halves)
+    exchange_ints = jnp.concatenate(exchange_halves, axis=0)
     denominator = pno_energy[:, :, None] + pno_energy[:, None, :]
     local_rows = (neighbour_pairs - (position - 1) * pair_dev).astype(jnp.int32).reshape(-1)
     fock = fock_coupling.reshape(-1)
 
     chunk = pair_dev // 2 if pair_dev % 8 == 0 else pair_dev
-    parts = [-(exchange_ints / denominator)]
+    parts = [
+        -(part / denominator[c * half:(c + 1) * half]) for c, part in enumerate(exchange_halves)
+    ]
     sources = chunked_halo(parts)
     amplitudes = jnp.concatenate(parts, axis=0)
     for iteration in range(1, ITERS):

time: 204 us -> 213 us (1.044)
  starting transfers between devices: 38.5 us -> 47.9 us
  waiting for transfers between devices: 96.8 us -> 92.2 us
  other arithmetic: 9.36 us -> 13.6 us
    ppermute x4 -> x5, waiting for transfers between devices: 52.6 us -> 31.6 us  [halo_sources(): from_right = lax.ppermute(cells, axis, [(i + 1, i) for i in range(ends)])]
    ppermute x4 -> x5, waiting for transfers between devices: 3.55 us -> 20.8 us  [halo_sources(): from_left = lax.ppermute(cells, axis, [(i, i + 1) for i in range(ends)])]
    ppermute x4 -> x5, starting transfers between devices: 25.5 us -> 30.7 us  [halo_sources(): from_left = lax.ppermute(cells, axis, [(i, i + 1) for i in range(ends)])]
    concatenate x1, other arithmetic: 2.03 us -> 5.17 us  [per_device(): exchange_ints = jnp.concatenate(exchange_halves, axis=0)]
    ppermute x4 -> x5, starting transfers between devices: 7.85 us -> 11 us  [halo_sources(): from_right = lax.ppermute(cells, axis, [(i + 1, i) for i in range(ends)])]
    ppermute x4, waiting for transfers between devices: 20.6 us -> 17.5 us  [halving_stream(): other = lax.ppermute(piece, 'aux', [(i, i ^ bit) for i in range(count)])]
    ppermute x4, waiting for transfers between devices: 20 us -> 22.3 us  [halving_stream(): lax.ppermute(send, 'aux', [(i, i ^ bit) for i in range(count)])]
  transfers between devices with their start and end apart: 16 -> 18, of which waited for: 11 -> 15; matrix products, arithmetic and copies ran while one was open for 7% -> 9% of each run, Pallas kernels for 8% -> 8%
where the time goes in v14:
time: 213 us; the launch traced here: 212 us
  waiting for transfers between devices  92.2 us (43%)
  starting transfers between devices  47.9 us (22%)
  Pallas kernels  47.4 us (22%)
  other arithmetic  13.6 us (6%)
  local copies, waits for them, and re-layouts  9.52 us (4%)
    ppermute x5, waiting for transfers between devices, halo_sources(): from_right = lax.ppermute(cells, axis, [(i + 1, i) for i in range(ends)])  31.6 us
    pallas_call x3, Pallas kernels, coupling_step(): pl.pallas_call(kernel, grid_spec=grid_spec, out_shape=jax.ShapeDtypeStruc...  31.3 us
    ppermute x5, starting transfers between devices, halo_sources(): from_left = lax.ppermute(cells, axis, [(i, i + 1) for i in range(ends)])  30.7 us
    ppermute x4, waiting for transfers between devices, halving_stream(): lax.ppermute(send, 'aux', [(i, i ^ bit) for i in range(count)])  22.3 us
    ppermute x5, waiting for transfers between devices, halo_sources(): from_left = lax.ppermute(cells, axis, [(i, i + 1) for i in range(ends)])  20.8 us
    ppermute x4, waiting for transfers between devices, halving_stream(): other = lax.ppermute(piece, 'aux', [(i, i ^ bit) for i in range(count)])  17.5 us
    pallas_call x2, Pallas kernels, partial_exchange(): pl.pallas_call(functools.partial(exchange_kernel, occ=occ, group=group, s...  16.1 us
    ppermute x5, starting transfers between devices, halo_sources(): from_right = lax.ppermute(cells, axis, [(i + 1, i) for i in range(ends)])  11 us
  transfers between devices with their start and end apart: 18, of which 15 were waited for; matrix products, arithmetic and copies ran while one was open for 9% of the time, Pallas kernels for 8%

profile of v14, /device:TPU:1, one launch (start us, length us, event | category | flops | bytes accessed | tf_op | source)
XLA Modules:
  0.0 211.8 jit_solution(1914369051334158269)
XLA Ops:
  0.6 4.6 %collective-permute-start = (bf16[4,512,256]{2,1,0:T(8,128)(2,1)}, bf16[4,512,256]{2,1,0:T(8,128)(2,1)S(1)}, u32[]{:S(2)}, u32[]{:S(2)}) collective-permute-start(bf16[4,512,256]{2,1,0:T(8,128)(2,1)} %t_own.3), channel_id=1, source_target_pairs={{0,1},{1,2},{2,3},{3,4},{4,5},{5,6},{6,7},{8,9},{9,10},{10,11},{11... | collective-permute-start | bytes 3145736 | tf_op jit(solution)/shard_map/ppermute | solution.py:18
  5.2 1.9 collective-permute-start.1
  7.2 1.2 compare_select_fusion.2.size_ref
  8.3 0.7 broadcast_subtract_fusion
  9.0 0.6 slice_bitcast_fusion
  9.6 7.6 %collective-permute-done.t_left = bf16[4,512,256]{2,1,0:T(8,128)(2,1)S(1)} collective-permute-done((bf16[4,512,256]{2,1,0:T(8,128)(2,1)}, bf16[4,512,256]{2,1,0:T(8,128)(2,1)S(1)}, u32[]{:S(2)}, u32[]{:S(2)}) %collective-permute-start) | collective-permute-done | bytes 1048608 | tf_op jit(solution)/shard_map/ppermute | solution.py:18
  17.3 4.3 %collective-permute-done.1.t_right = bf16[4,512,256]{2,1,0:T(8,128)(2,1)S(1)} collective-permute-done((bf16[4,512,256]{2,1,0:T(8,128)(2,1)}, bf16[4,512,256]{2,1,0:T(8,128)(2,1)S(1)}, u32[]{:S(2)}, u32[]{:S(2)}) %collective-permute-start.1) | collective-permute-done | bytes 1048608 | tf_op jit(solution)/shard_map/ppermute | solution.py:19
  21.6 1.0 copy-done.8
  22.5 8.0 %shard_map.95 = f32[8,192,192]{2,1,0:T(8,128)} custom-call(s32[16]{0:T(128)} %get-tuple-element.9.lead_ref, s32[16]{0:T(128)} %get-tuple-element.8.trail_ref, s32[16]{0:T(128)} %compare_select_fusion.2.size_ref, bf16[4,512,256]{2,1,0:T(8,128)(2,1)} %copy-done.7, bf16[4,512,256]{2,1,0:T(8,128)(2,1)} %t_own.3, bf16[4,512,256]{2,1,0:T(8,128)(2,1)} %copy-done.8, ...), custom_call_target="tpu_custom_call" | custom-call | flops 1107296256 | bytes 6946816 | tf_op jit(solution)/shard_map/pallas_call | solution.py:139
  30.5 1.2 constant_dynamic-slice_fusion.3
  31.7 1.3 collective-permute-start.2
  33.0 8.1 %shard_map.96 = f32[8,192,192]{2,1,0:T(8,128)} custom-call(s32[16]{0:T(128)} %get-tuple-element.9.lead_ref, s32[16]{0:T(128)} %get-tuple-element.8.trail_ref, s32[16]{0:T(128)} %compare_select_fusion.2.size_ref, bf16[4,512,256]{2,1,0:T(8,128)(2,1)} %copy-done.7, bf16[4,512,256]{2,1,0:T(8,128)(2,1)} %t_own.3, bf16[4,512,256]{2,1,0:T(8,128)(2,1)} %copy-done.8, ...), custom_call_target="tpu_custom_call" | custom-call | flops 1107296256 | bytes 6946816 | tf_op jit(solution)/shard_map/pallas_call | solution.py:139
  41.2 2.2 %constant_dynamic-slice_fusion.1 = f32[4,192,192]{2,1,0:T(8,128)} fusion(f32[8,192,192]{2,1,0:T(8,128)} %shard_map.96, s32[]{:T(128)S(6)} %select_n.88), kind=kLoop, calls=%fused_computation.17 | loop fusion | bytes 1179652 | tf_op jit(solution)/shard_map/dynamic_slice | solution.py:28
  43.4 1.2 collective-permute-start.7
  45.1 14.3 %collective-permute-done.7 = f32[4,192,192]{2,1,0:T(8,128)} collective-permute-done((f32[4,192,192]{2,1,0:T(8,128)}, f32[4,192,192]{2,1,0:T(8,128)}, u32[]{:S(2)}, u32[]{:S(2)}) %collective-permute-start.7) | collective-permute-done | bytes 589856 | tf_op jit(solution)/shard_map/ppermute | solution.py:29
  59.4 1.2 dynamic-slice_add_fusion
  61.0 3.2 %collective-permute-done.3 = f32[2,192,192]{2,1,0:T(8,128)S(1)} collective-permute-done((f32[2,192,192]{2,1,0:T(8,128)S(1)}, f32[2,192,192]{2,1,0:T(8,128)S(1)}, u32[]{:S(2)}, u32[]{:S(2)}) %collective-permute-start.3) | collective-permute-done | bytes 294944 | tf_op jit(solution)/shard_map/ppermute | solution.py:29
  64.3 1.3 collective-permute-start.4
  65.6 4.8 %collective-permute-done.8 = f32[2,192,192]{2,1,0:T(8,128)S(1)} collective-permute-done((f32[2,192,192]{2,1,0:T(8,128)S(1)}, f32[2,192,192]{2,1,0:T(8,128)S(1)}, u32[]{:S(2)}, u32[]{:S(2)}) %collective-permute-start.8) | collective-permute-done | bytes 294944 | tf_op jit(solution)/shard_map/ppermute | solution.py:29
  70.9 4.7 %collective-permute-done.4 = f32[2,192,192]{2,1,0:T(8,128)S(1)} collective-permute-done((f32[2,192,192]{2,1,0:T(8,128)S(1)}, f32[2,192,192]{2,1,0:T(8,128)S(1)}, u32[]{:S(2)}, u32[]{:S(2)}) %collective-permute-start.4) | collective-permute-done | bytes 294944 | tf_op jit(solution)/shard_map/ppermute | solution.py:32
  75.8 4.2 %collective-permute-done.9 = f32[2,192,192]{2,1,0:T(8,128)S(1)} collective-permute-done((f32[2,192,192]{2,1,0:T(8,128)S(1)}, f32[2,192,192]{2,1,0:T(8,128)S(1)}, u32[]{:S(2)}, u32[]{:S(2)}) %collective-permute-start.9) | collective-permute-done | bytes 294944 | tf_op jit(solution)/shard_map/ppermute | solution.py:32
  80.0 1.3 collective-permute-start.10
  82.2 6.2 %collective-permute-done.5 = f32[4,192,192]{2,1,0:T(8,128)S(1)} collective-permute-done((f32[4,192,192]{2,1,0:T(8,128)S(1)}, f32[4,192,192]{2,1,0:T(8,128)S(1)}, u32[]{:S(2)}, u32[]{:S(2)}) %collective-permute-start.5) | collective-permute-done | bytes 589856 | tf_op jit(solution)/shard_map/ppermute | solution.py:32
  88.5 2.4 %collective-permute-done.10 = f32[4,192,192]{2,1,0:T(8,128)S(1)} collective-permute-done((f32[4,192,192]{2,1,0:T(8,128)S(1)}, f32[4,192,192]{2,1,0:T(8,128)S(1)}, u32[]{:S(2)}, u32[]{:S(2)}) %collective-permute-start.10) | collective-permute-done | bytes 589856 | tf_op jit(solution)/shard_map/ppermute | solution.py:32
  91.6 0.6 copy-done.2
  92.3 17.2 %collective-permute-start.11 = (f32[8,192,192]{2,1,0:T(8,128)S(1)}, f32[8,192,192]{2,1,0:T(8,128)}, u32[]{:S(2)}, u32[]{:S(2)}) collective-permute-start(f32[8,192,192]{2,1,0:T(8,128)S(1)} %get-tuple-element.6.refs_3_), channel_id=1, source_target_pairs={{0,1},{1,2},{2,3},{3,4},{4,5},{5,6},{6,7},{8,9},{9,10},{10,11},{11... | collective-permute-start | bytes 3538952 | tf_op jit(solution)/shard_map/ppermute | solution.py:18
  109.5 1.9 collective-permute-start.12
  111.4 1.9 collective-permute-start.13
  113.3 3.8 %collective-permute-start.6 = (f32[8,192,192]{2,1,0:T(8,128)S(1)}, f32[8,192,192]{2,1,0:T(8,128)}, u32[]{:S(2)}, u32[]{:S(2)}) collective-permute-start(f32[8,192,192]{2,1,0:T(8,128)S(1)} %get-tuple-element.7.refs_2_), channel_id=1, source_target_pairs={{0,1},{1,2},{2,3},{3,4},{4,5},{5,6},{6,7},{8,9},{9,10},{10,11},{11... | collective-permute-start | bytes 3538952 | tf_op jit(solution)/shard_map/ppermute | solution.py:18
  117.2 0.6 broadcast_in_dim.26.refs_9_
  117.9 0.6 reshape.20.nb_ref
  118.5 1.7 copy.14.refs_8_
  120.3 0.7 reshape.21.fock_ref
  121.0 5.2 %pad_maximum_fusion = (f32[16,192,192]{2,1,0:T(8,128)}, f32[16,192,192]{2,1,0:T(8,128)}) fusion(f32[8,192,192]{2,1,0:T(8,128)} %copy-done.2, f32[8,192,192]{2,1,0:T(8,128)} %copy-done.3, f32[8,192,192]{2,1,0:T(8,128)S(1)} %get-tuple-element.6.refs_3_, f32[8,192,192]{2,1,0:T(8,128)S(1)} %get-tuple-element.7.refs_2_), kind=kLoop, calls=%fused_computation | loop fusion | flops 1179648 | bytes 9437184 | tf_op jit(solution)/shard_map/concatenate | solution.py:288
  126.1 0.7 collective-permute-done.11.refs_1_
  126.8 4.5 %collective-permute-done.12.refs_4_ = f32[8,192,192]{2,1,0:T(8,128)} collective-permute-done((f32[8,192,192]{2,1,0:T(8,128)S(1)}, f32[8,192,192]{2,1,0:T(8,128)}, u32[]{:S(2)}, u32[]{:S(2)}) %collective-permute-start.12) | collective-permute-done | bytes 1179680 | tf_op jit(solution)/shard_map/ppermute | solution.py:19
  131.3 16.9 %collective-permute-done.13.refs_5_ = f32[8,192,192]{2,1,0:T(8,128)} collective-permute-done((f32[8,192,192]{2,1,0:T(8,128)S(1)}, f32[8,192,192]{2,1,0:T(8,128)}, u32[]{:S(2)}, u32[]{:S(2)}) %collective-permute-start.13) | collective-permute-done | bytes 1179680 | tf_op jit(solution)/shard_map/ppermute | solution.py:19
  148.2 9.1 %shard_map.97.refs_2_ = f32[8,192,192]{2,1,0:T(8,128)} custom-call(s32[32]{0:T(128)} %reshape.20.nb_ref, s32[16]{0:T(128)} %compare_select_fusion.2.size_ref, f32[32]{0:T(128)} %reshape.21.fock_ref, f32[8,192,192]{2,1,0:T(8,128)} %collective-permute-done.6.refs_0_, f32[8,192,192]{2,1,0:T(8,128)} %collective-permute-done.11.refs_1_, ...), custom_call_target="tpu_custom_call" | custom-call | flops 905969664 | bytes 7077888 | tf_op jit(solution)/shard_map/pallas_call | solution.py:241
  157.3 2.1 collective-permute-start.14
  159.3 2.5 %collective-permute-start.16 = (f32[8,192,192]{2,1,0:T(8,128)}, f32[8,192,192]{2,1,0:T(8,128)}, u32[]{:S(2)}, u32[]{:S(2)}) collective-permute-start(f32[8,192,192]{2,1,0:T(8,128)} %shard_map.97.refs_2_), channel_id=1, source_target_pairs={{1,0},{2,1},{3,2},{4,3},{5,4},{6,5},{7,6},{9,8},{10,9},{11,10},{12... | collective-permute-start | bytes 3538952 | tf_op jit(solution)/shard_map/ppermute | solution.py:19
  161.8 8.8 %shard_map.98.refs_3_ = f32[8,192,192]{2,1,0:T(8,128)} custom-call(s32[32]{0:T(128)} %reshape.20.nb_ref, s32[16]{0:T(128)} %compare_select_fusion.2.size_ref, f32[32]{0:T(128)} %reshape.21.fock_ref, f32[8,192,192]{2,1,0:T(8,128)} %collective-permute-done.6.refs_0_, f32[8,192,192]{2,1,0:T(8,128)} %collective-permute-done.11.refs_1_, ...), custom_call_target="tpu_custom_call" | custom-call | flops 905969664 | bytes 7077888 | tf_op jit(solution)/shard_map/pallas_call | solution.py:241
  170.7 3.0 %collective-permute-start.15 = (f32[8,192,192]{2,1,0:T(8,128)}, f32[8,192,192]{2,1,0:T(8,128)}, u32[]{:S(2)}, u32[]{:S(2)}) collective-permute-start(f32[8,192,192]{2,1,0:T(8,128)} %shard_map.98.refs_3_), channel_id=1, source_target_pairs={{0,1},{1,2},{2,3},{3,4},{4,5},{5,6},{6,7},{8,9},{9,10},{10,11},{11... | collective-permute-start | bytes 3538952 | tf_op jit(solution)/shard_map/ppermute | solution.py:18
  173.7 2.7 %collective-permute-start.17 = (f32[8,192,192]{2,1,0:T(8,128)}, f32[8,192,192]{2,1,0:T(8,128)}, u32[]{:S(2)}, u32[]{:S(2)}) collective-permute-start(f32[8,192,192]{2,1,0:T(8,128)} %shard_map.98.refs_3_), channel_id=1, source_target_pairs={{1,0},{2,1},{3,2},{4,3},{5,4},{6,5},{7,6},{9,8},{10,9},{11,10},{12... | collective-permute-start | bytes 3538952 | tf_op jit(solution)/shard_map/ppermute | solution.py:19
  176.4 3.4 %pad_maximum_fusion.2.refs_10_ = f32[16,192,192]{2,1,0:T(8,128)} fusion(f32[8,192,192]{2,1,0:T(8,128)} %shard_map.98.refs_3_, f32[8,192,192]{2,1,0:T(8,128)S(1)} %copy-done.4), kind=kLoop, calls=%fused_computation.2 | loop fusion | flops 589824 | bytes 4718592 | tf_op jit(solution)/shard_map/concatenate | solution.py:308
  179.8 1.5 collective-permute-done.16.refs_4_
  181.4 12.5 %collective-permute-done.15.refs_1_ = f32[8,192,192]{2,1,0:T(8,128)} collective-permute-done((f32[8,192,192]{2,1,0:T(8,128)}, f32[8,192,192]{2,1,0:T(8,128)}, u32[]{:S(2)}, u32[]{:S(2)}) %collective-permute-start.15) | collective-permute-done | bytes 1179680 | tf_op jit(solution)/shard_map/ppermute | solution.py:18
  193.8 4.4 %collective-permute-done.17.refs_5_ = f32[8,192,192]{2,1,0:T(8,128)} collective-permute-done((f32[8,192,192]{2,1,0:T(8,128)}, f32[8,192,192]{2,1,0:T(8,128)}, u32[]{:S(2)}, u32[]{:S(2)}) %collective-permute-start.17) | collective-permute-done | bytes 1179680 | tf_op jit(solution)/shard_map/ppermute | solution.py:19
  198.2 13.4 %shard_map.99 = f32[16,192,192]{2,1,0:T(8,128)} custom-call(s32[32]{0:T(128)} %reshape.20.nb_ref, s32[16]{0:T(128)} %compare_select_fusion.2.size_ref, f32[32]{0:T(128)} %reshape.21.fock_ref, f32[8,192,192]{2,1,0:T(8,128)} %copy-done.9, f32[8,192,192]{2,1,0:T(8,128)} %collective-permute-done.15.refs_1_, f32[8,192,192]{2,1,0:T(8,128)} %shard_map.97.refs_2_, ...), custom_call_target="tpu_custom_call" | custom-call | flops 1811939328 | bytes 14155776 | tf_op jit(solution)/shard_map/pallas_call | solution.py:241
  (51 shorter events, 3.4 us)
Async XLA Ops:
  0.6 16.6 %collective-permute-start = (bf16[4,512,256]{2,1,0:T(8,128)(2,1)}, bf16[4,512,256]{2,1,0:T(8,128)(2,1)S(1)}, u32[]{:S(2)}, u32[]{:S(2)}) collective-permute-start(bf16[4,512,256]{2,1,0:T(8,128)(2,1)} %t_own.3), channel_id=1, source_target_pairs={{0,1},{1,2},{2,3},{3,4},{4,5},{5,6},{6,7},{8,9},{9,10},{10,11},{11... | collective-permute-start | bytes 3145736 | tf_op jit(solution)/shard_map/ppermute | solution.py:18
  5.2 16.3 %collective-permute-start.1 = (bf16[4,512,256]{2,1,0:T(8,128)(2,1)}, bf16[4,512,256]{2,1,0:T(8,128)(2,1)S(1)}, u32[]{:S(2)}, u32[]{:S(2)}) collective-permute-start(bf16[4,512,256]{2,1,0:T(8,128)(2,1)} %t_own.3), channel_id=1, source_target_pairs={{1,0},{2,1},{3,2},{4,3},{5,4},{6,5},{7,6},{9,8},{10,9},{11,10},{12... | collective-permute-start | bytes 3145736 | tf_op jit(solution)/shard_map/ppermute | solution.py:19
  17.3 4.3 %copy-start.7 = (bf16[4,512,256]{2,1,0:T(8,128)(2,1)}, bf16[4,512,256]{2,1,0:T(8,128)(2,1)S(1)}, u32[]{:S(2)}) copy-start(bf16[4,512,256]{2,1,0:T(8,128)(2,1)S(1)} %collective-permute-done.t_left) | copy-start | bytes 3145732
  21.6 1.0 copy-start.8
  31.7 12.9 %collective-permute-start.2 = (f32[4,192,192]{2,1,0:T(8,128)S(1)}, f32[4,192,192]{2,1,0:T(8,128)S(1)}, u32[]{:S(2)}, u32[]{:S(2)}) collective-permute-start(f32[4,192,192]{2,1,0:T(8,128)S(1)} %constant_dynamic-slice_fusion.3), channel_id=1, source_target_pairs={{0,8},{8,0},{16,24},{24,16},{1,9},{9,1},{17,25},{25,17},{2,10},{10... | collective-permute-start | bytes 1769480 | tf_op jit(solution)/shard_map/ppermute | solution.py:29
  41.2 3.5 %copy-start.5 = (f32[8,192,192]{2,1,0:T(8,128)S(1)}, f32[8,192,192]{2,1,0:T(8,128)}, u32[]{:S(2)}) copy-start(f32[8,192,192]{2,1,0:T(8,128)} %shard_map.95) | copy-start | bytes 3538948
  43.4 16.0 %collective-permute-start.7 = (f32[4,192,192]{2,1,0:T(8,128)}, f32[4,192,192]{2,1,0:T(8,128)}, u32[]{:S(2)}, u32[]{:S(2)}) collective-permute-start(f32[4,192,192]{2,1,0:T(8,128)} %constant_dynamic-slice_fusion.1), channel_id=1, source_target_pairs={{0,16},{8,24},{16,0},{24,8},{1,17},{9,25},{17,1},{25,9},{2,18},{10... | collective-permute-start | bytes 1769480 | tf_op jit(solution)/shard_map/ppermute | solution.py:29
  44.6 14.8 %copy-start.6 = (f32[8,192,192]{2,1,0:T(8,128)S(1)}, f32[8,192,192]{2,1,0:T(8,128)}, u32[]{:S(2)}) copy-start(f32[8,192,192]{2,1,0:T(8,128)} %shard_map.96) | copy-start | bytes 3538948
  44.8 19.4 %collective-permute-start.3 = (f32[2,192,192]{2,1,0:T(8,128)S(1)}, f32[2,192,192]{2,1,0:T(8,128)S(1)}, u32[]{:S(2)}, u32[]{:S(2)}) collective-permute-start(f32[2,192,192]{2,1,0:T(8,128)S(1)} %constant_dynamic-slice_fusion.2), channel_id=1, source_target_pairs={{0,16},{8,24},{16,0},{24,8},{1,17},{9,25},{17,1},{25,9},{2,18},{10... | collective-permute-start | bytes 884744 | tf_op jit(solution)/shard_map/ppermute | solution.py:29
  60.7 9.8 %collective-permute-start.8 = (f32[2,192,192]{2,1,0:T(8,128)S(1)}, f32[2,192,192]{2,1,0:T(8,128)S(1)}, u32[]{:S(2)}, u32[]{:S(2)}) collective-permute-start(f32[2,192,192]{2,1,0:T(8,128)S(1)} %constant_dynamic-slice_fusion), channel_id=1, source_target_pairs={{0,8},{8,0},{16,24},{24,16},{1,9},{9,1},{17,25},{25,17},{2,10},{10... | collective-permute-start | bytes 884744 | tf_op jit(solution)/shard_map/ppermute | solution.py:29
  64.3 11.3 %collective-permute-start.4 = (f32[2,192,192]{2,1,0:T(8,128)S(1)}, f32[2,192,192]{2,1,0:T(8,128)S(1)}, u32[]{:S(2)}, u32[]{:S(2)}) collective-permute-start(f32[2,192,192]{2,1,0:T(8,128)S(1)} %get-tuple-element.5), channel_id=1, source_target_pairs={{0,16},{8,24},{16,0},{24,8},{1,17},{9,25},{17,1},{25,9},{2,18},{10... | collective-permute-start | bytes 884744 | tf_op jit(solution)/shard_map/ppermute | solution.py:32
  70.5 10.8 %copy-start.10 = (f32[16,192]{1,0:T(8,128)S(1)}, f32[16,192]{1,0:T(8,128)}, u32[]{:S(2)}) copy-start(f32[16,192]{1,0:T(8,128)} %param.12) | copy-start | bytes 36868
  70.6 9.4 %collective-permute-start.9 = (f32[2,192,192]{2,1,0:T(8,128)S(1)}, f32[2,192,192]{2,1,0:T(8,128)S(1)}, u32[]{:S(2)}, u32[]{:S(2)}) collective-permute-start(f32[2,192,192]{2,1,0:T(8,128)S(1)} %get-tuple-element.3), channel_id=1, source_target_pairs={{0,8},{8,0},{16,24},{24,16},{1,9},{9,1},{17,25},{25,17},{2,10},{10... | collective-permute-start | bytes 884744 | tf_op jit(solution)/shard_map/ppermute | solution.py:32
  75.6 12.8 %collective-permute-start.5 = (f32[4,192,192]{2,1,0:T(8,128)S(1)}, f32[4,192,192]{2,1,0:T(8,128)S(1)}, u32[]{:S(2)}, u32[]{:S(2)}) collective-permute-start(f32[4,192,192]{2,1,0:T(8,128)S(1)} %constant_dynamic-update-slice_fusion.6), channel_id=1, source_target_pairs={{0,8},{8,0},{16,24},{24,16},{1,9},{9,1},{17,25},{25,17},{2,10},{10... | collective-permute-start | bytes 1769480 | tf_op jit(solution)/shard_map/ppermute | solution.py:32
  80.0 10.9 %collective-permute-start.10 = (f32[4,192,192]{2,1,0:T(8,128)S(1)}, f32[4,192,192]{2,1,0:T(8,128)S(1)}, u32[]{:S(2)}, u32[]{:S(2)}) collective-permute-start(f32[4,192,192]{2,1,0:T(8,128)S(1)} %constant_dynamic-update-slice_fusion.2), channel_id=1, source_target_pairs={{0,16},{8,24},{16,0},{24,8},{1,17},{9,25},{17,1},{25,9},{2,18},{10... | collective-permute-start | bytes 1769480 | tf_op jit(solution)/shard_map/ppermute | solution.py:32
  88.5 3.1 %copy-start.3 = (f32[8,192,192]{2,1,0:T(8,128)}, f32[8,192,192]{2,1,0:T(8,128)S(1)}, u32[]{:S(2)}) copy-start(f32[8,192,192]{2,1,0:T(8,128)S(1)} %constant_dynamic-update-slice_fusion.4) | copy-start | bytes 3538948
  91.0 1.3 copy-start.2
  91.0 26.8 %copy-start.12 = (s32[16,2]{0,1:T(2,128)S(1)}, s32[16,2]{0,1:T(2,128)}, u32[]{:S(2)}) copy-start(s32[16,2]{0,1:T(2,128)} %param.14) | copy-start | bytes 388
  92.3 33.9 %copy-start = (f32[8,192,192]{2,1,0:T(8,128)}, f32[8,192,192]{2,1,0:T(8,128)S(1)}, u32[]{:S(2)}) copy-start(f32[8,192,192]{2,1,0:T(8,128)S(1)} %get-tuple-element.6.refs_3_) | copy-start | bytes 3538948
  92.3 33.9 %copy-start.1 = (f32[8,192,192]{2,1,0:T(8,128)}, f32[8,192,192]{2,1,0:T(8,128)S(1)}, u32[]{:S(2)}) copy-start(f32[8,192,192]{2,1,0:T(8,128)S(1)} %get-tuple-element.7.refs_2_) | copy-start | bytes 3538948
  92.3 27.9 %copy-start.11 = (f32[16,2]{0,1:T(2,128)S(1)}, f32[16,2]{0,1:T(2,128)}, u32[]{:S(2)}) copy-start(f32[16,2]{0,1:T(2,128)} %param.15) | copy-start | bytes 388
  92.3 34.6 %collective-permute-start.11 = (f32[8,192,192]{2,1,0:T(8,128)S(1)}, f32[8,192,192]{2,1,0:T(8,128)}, u32[]{:S(2)}, u32[]{:S(2)}) collective-permute-start(f32[8,192,192]{2,1,0:T(8,128)S(1)} %get-tuple-element.6.refs_3_), channel_id=1, source_target_pairs={{0,1},{1,2},{2,3},{3,4},{4,5},{5,6},{6,7},{8,9},{9,10},{10,11},{11... | collective-permute-start | bytes 3538952 | tf_op jit(solution)/shard_map/ppermute | solution.py:18
  109.5 21.8 %collective-permute-start.12 = (f32[8,192,192]{2,1,0:T(8,128)S(1)}, f32[8,192,192]{2,1,0:T(8,128)}, u32[]{:S(2)}, u32[]{:S(2)}) collective-permute-start(f32[8,192,192]{2,1,0:T(8,128)S(1)} %get-tuple-element.7.refs_2_), channel_id=1, source_target_pairs={{1,0},{2,1},{3,2},{4,3},{5,4},{6,5},{7,6},{9,8},{10,9},{11,10},{12... | collective-permute-start | bytes 3538952 | tf_op jit(solution)/shard_map/ppermute | solution.py:19
  111.4 36.8 %collective-permute-start.13 = (f32[8,192,192]{2,1,0:T(8,128)S(1)}, f32[8,192,192]{2,1,0:T(8,128)}, u32[]{:S(2)}, u32[]{:S(2)}) collective-permute-start(f32[8,192,192]{2,1,0:T(8,128)S(1)} %get-tuple-element.6.refs_3_), channel_id=1, source_target_pairs={{1,0},{2,1},{3,2},{4,3},{5,4},{6,5},{7,6},{9,8},{10,9},{11,10},{12... | collective-permute-start | bytes 3538952 | tf_op jit(solution)/shard_map/ppermute | solution.py:19
  113.3 34.8 %collective-permute-start.6 = (f32[8,192,192]{2,1,0:T(8,128)S(1)}, f32[8,192,192]{2,1,0:T(8,128)}, u32[]{:S(2)}, u32[]{:S(2)}) collective-permute-start(f32[8,192,192]{2,1,0:T(8,128)S(1)} %get-tuple-element.7.refs_2_), channel_id=1, source_target_pairs={{0,1},{1,2},{2,3},{3,4},{4,5},{5,6},{6,7},{8,9},{9,10},{10,11},{11... | collective-permute-start | bytes 3538952 | tf_op jit(solution)/shard_map/ppermute | solution.py:18
  157.2 19.2 %copy-start.4 = (f32[8,192,192]{2,1,0:T(8,128)S(1)}, f32[8,192,192]{2,1,0:T(8,128)}, u32[]{:S(2)}) copy-start(f32[8,192,192]{2,1,0:T(8,128)} %shard_map.97.refs_2_) | copy-start | bytes 3538948
  157.3 22.6 %collective-permute-start.14 = (f32[8,192,192]{2,1,0:T(8,128)}, f32[8,192,192]{2,1,0:T(8,128)S(1)}, u32[]{:S(2)}, u32[]{:S(2)}) collective-permute-start(f32[8,192,192]{2,1,0:T(8,128)} %shard_map.97.refs_2_), channel_id=1, source_target_pairs={{0,1},{1,2},{2,3},{3,4},{4,5},{5,6},{6,7},{8,9},{9,10},{10,11},{11... | collective-permute-start | bytes 3538952 | tf_op jit(solution)/shard_map/ppermute | solution.py:18
  159.3 22.1 %collective-permute-start.16 = (f32[8,192,192]{2,1,0:T(8,128)}, f32[8,192,192]{2,1,0:T(8,128)}, u32[]{:S(2)}, u32[]{:S(2)}) collective-permute-start(f32[8,192,192]{2,1,0:T(8,128)} %shard_map.97.refs_2_), channel_id=1, source_target_pairs={{1,0},{2,1},{3,2},{4,3},{5,4},{6,5},{7,6},{9,8},{10,9},{11,10},{12... | collective-permute-start | bytes 3538952 | tf_op jit(solution)/shard_map/ppermute | solution.py:19
  170.7 23.2 %collective-permute-start.15 = (f32[8,192,192]{2,1,0:T(8,128)}, f32[8,192,192]{2,1,0:T(8,128)}, u32[]{:S(2)}, u32[]{:S(2)}) collective-permute-start(f32[8,192,192]{2,1,0:T(8,128)} %shard_map.98.refs_3_), channel_id=1, source_target_pairs={{0,1},{1,2},{2,3},{3,4},{4,5},{5,6},{6,7},{8,9},{9,10},{10,11},{11... | collective-permute-start | bytes 3538952 | tf_op jit(solution)/shard_map/ppermute | solution.py:18
  173.7 24.5 %collective-permute-start.17 = (f32[8,192,192]{2,1,0:T(8,128)}, f32[8,192,192]{2,1,0:T(8,128)}, u32[]{:S(2)}, u32[]{:S(2)}) collective-permute-start(f32[8,192,192]{2,1,0:T(8,128)} %shard_map.98.refs_3_), channel_id=1, source_target_pairs={{1,0},{2,1},{3,2},{4,3},{5,4},{6,5},{7,6},{9,8},{10,9},{11,10},{12... | collective-permute-start | bytes 3538952 | tf_op jit(solution)/shard_map/ppermute | solution.py:19
  179.8 18.4 %copy-start.9 = (f32[8,192,192]{2,1,0:T(8,128)}, f32[8,192,192]{2,1,0:T(8,128)S(1)}, u32[]{:S(2)}) copy-start(f32[8,192,192]{2,1,0:T(8,128)S(1)} %collective-permute-done.14.refs_0_) | copy-start | bytes 3538948

commit v15 on v13

--- a/solution.py
+++ b/solution.py
@@ -20,12 +20,15 @@
     return (from_left, cells, from_right)
 
 
-def halving_stream(piece, index, count, bits):
-    for bit in bits:
+def halving_stream(piece, index, count, bits, presplit=False):
+    for step, bit in enumerate(bits):
         side = (index // bit) % 2
         half = piece.shape[0] // 2
-        keep = lax.dynamic_slice_in_dim(piece, side * half, half, axis=0)
-        send = lax.dynamic_slice_in_dim(piece, (1 - side) * half, half, axis=0)
+        if presplit and step == 0:
+            keep, send = piece[half:], piece[:half]
+        else:
+            keep = lax.dynamic_slice_in_dim(piece, side * half, half, axis=0)
+            send = lax.dynamic_slice_in_dim(piece, (1 - side) * half, half, axis=0)
         piece = keep + lax.ppermute(send, "aux", [(i, i ^ bit) for i in range(count)])
     for bit in reversed(bits):
         side = (index // bit) % 2
@@ -37,13 +40,22 @@
     return piece
 
 
-def sum_over_aux(halves):
+def halving_ready(halves):
+    return lax.axis_size("aux") == 4 and halves % 8 == 0
+
+
+def send_first(half_index):
+    index = lax.axis_index("aux")
+    return (1 - (index // (1, 2)[half_index]) % 2).astype(jnp.int32).reshape(1)
+
+
+def sum_over_aux(halves, presplit):
     count = lax.axis_size("aux")
-    if count != 4 or halves[0].shape[0] % 4:
+    if not halving_ready(halves[0].shape[0]):
         return lax.psum(jnp.concatenate(halves, axis=0), "aux")
     index = lax.axis_index("aux")
-    first = halving_stream(halves[0], index, count, (1, 2))
-    second = halving_stream(halves[1], index, count, (2, 1))
+    first = halving_stream(halves[0], index, count, (1, 2), presplit)
+    second = halving_stream(halves[1], index, count, (2, 1), presplit)
     return jnp.concatenate([first, second], axis=0)
 
 
@@ -70,7 +82,7 @@
 
 
 def exchange_kernel(
-    lead_ref, trail_ref, size_ref, t_left, t_own, t_right, coef_ref, out_ref, lbuf, tbuf, sems, *, occ, group, start
+    lead_ref, trail_ref, size_ref, flip_ref, t_left, t_own, t_right, coef_ref, out_ref, lbuf, tbuf, sems, *, occ, group, start
 ):
     i = pl.program_id(0)
     steps = pl.num_programs(0)
@@ -111,23 +123,26 @@
                 )
 
 
-def partial_exchange(lead, trail, sizes, sources, coef_t, start=0, count=None):
+def partial_exchange(lead, trail, sizes, sources, coef_t, start=0, count=None, flip=None):
     pairs = coef_t.shape[0]
     count = pairs if count is None else count
     group = next(g for g in (4, 2, 1) if count % g == 0 and start % g == 0)
     base = start // group
+    steps = count // group
+    if flip is None or steps != 2:
+        flip = jnp.zeros((1,), jnp.int32)
     occ, nfit, npao = sources[1].shape
     hbm = pl.BlockSpec(memory_space=pl.ANY)
     grid_spec = pltpu.PrefetchScalarGridSpec(
-        num_scalar_prefetch=3,
-        grid=(count // group,),
+        num_scalar_prefetch=4,
+        grid=(steps,),
         in_specs=[
             hbm,
             hbm,
             hbm,
-            pl.BlockSpec((group, 2, NPNO, npao), lambda i, a, b, s: (i + base, 0, 0, 0)),
+            pl.BlockSpec((group, 2, NPNO, npao), lambda i, a, b, s, f: (i + base, 0, 0, 0)),
         ],
-        out_specs=pl.BlockSpec((group, NPNO, NPNO), lambda i, a, b, s: (i, 0, 0)),
+        out_specs=pl.BlockSpec((group, NPNO, NPNO), lambda i, a, b, s, f: ((i + f[0]) % steps, 0, 0)),
         scratch_shapes=[
             pltpu.VMEM((2, group, nfit, npao), sources[1].dtype),
             pltpu.VMEM((2, group, nfit, npao), sources[1].dtype),
@@ -144,7 +159,7 @@
             bytes_accessed=count * (2 * nfit * npao * 2 + 2 * npao * NPNO * 2 + NPNO * NPNO * 4),
             transcendentals=0,
         ),
-    )(lead, trail, sizes, *sources, coef_t)
+    )(lead, trail, sizes, flip, *sources, coef_t)
 
 
 def split_bf16(value):
@@ -271,6 +286,7 @@
     blocks = halo_sources(three_index, "pair")
     local_orbitals = (pair_orbitals - (position - 1) * occ_dev).astype(jnp.int32)
     half = pair_dev // 2
+    presplit = halving_ready(half) and half % 8 == 0
     halves = [
         partial_exchange(
             local_orbitals[:, 0] - occ_dev,
@@ -278,12 +294,13 @@
             sizes,
             blocks,
             jnp.swapaxes(pno_coef, 2, 3),
-            start,
+            c * half,
             half,
+            send_first(c) if presplit else None,
         )
-        for start in (0, half)
+        for c in range(2)
     ]
-    exchange_ints = sum_over_aux(halves)
+    exchange_ints = sum_over_aux(halves, presplit)
     denominator = pno_energy[:, :, None] + pno_energy[:, None, :]
     local_rows = (neighbour_pairs - (position - 1) * pair_dev).astype(jnp.int32).reshape(-1)
     fock = fock_coupling.reshape(-1)

time: 204 us -> 204 us (level)
    dynamic_slice x4 -> x2, local copies, waits for them, and re-layouts: 3.46 us -> 0.07 us  [halving_stream(): send = lax.dynamic_slice_in_dim(piece, (1 - side) * half, half, axis=0)]
    slice x0 -> x2, local copies, waits for them, and re-layouts: none -> 3.38 us  [halving_stream(): keep, send = (piece[half:], piece[:half])]
  transfers between devices with their start and end apart: 16 -> 16, of which waited for: 11 -> 12; matrix products, arithmetic and copies ran while one was open for 7% -> 8% of each run, Pallas kernels for 8% -> 8%
where the time goes in v15:
time: 204 us; the launch traced here: 201 us
  waiting for transfers between devices  95.6 us (47%)
  Pallas kernels  45.9 us (22%)
  starting transfers between devices  39.3 us (19%)
  other arithmetic  10.6 us (5%)
  local copies, waits for them, and re-layouts  8.83 us (4%)
    ppermute x4, waiting for transfers between devices, halo_sources(): from_right = lax.ppermute(cells, axis, [(i + 1, i) for i in range(ends)])  53.2 us
    pallas_call x3, Pallas kernels, coupling_step(): pl.pallas_call(kernel, grid_spec=grid_spec, out_shape=jax.ShapeDtypeStruc...  30.3 us
    ppermute x4, starting transfers between devices, halo_sources(): from_left = lax.ppermute(cells, axis, [(i, i + 1) for i in range(ends)])  26 us
    ppermute x4, waiting for transfers between devices, halving_stream(): other = lax.ppermute(piece, 'aux', [(i, i ^ bit) for i in range(count)])  20.3 us
    ppermute x4, waiting for transfers between devices, halving_stream(): lax.ppermute(send, 'aux', [(i, i ^ bit) for i in range(count)])  18.6 us
    pallas_call x2, Pallas kernels, partial_exchange(): pl.pallas_call(functools.partial(exchange_kernel, occ=occ, group=group, s...  15.6 us
    ppermute x4, starting transfers between devices, halo_sources(): from_right = lax.ppermute(cells, axis, [(i + 1, i) for i in range(ends)])  7.85 us
  transfers between devices with their start and end apart: 16, of which 12 were waited for; matrix products, arithmetic and copies ran while one was open for 8% of the time, Pallas kernels for 8%

profile of v15, /device:TPU:1, one launch (start us, length us, event | category | flops | bytes accessed | tf_op | source)
XLA Modules:
  0.0 201.5 jit_solution(1704538569374829692)
XLA Ops:
  0.6 2.0 collective-permute-start.1
  2.6 4.6 %collective-permute-start = (bf16[4,512,256]{2,1,0:T(8,128)(2,1)}, bf16[4,512,256]{2,1,0:T(8,128)(2,1)S(1)}, u32[]{:S(2)}, u32[]{:S(2)}) collective-permute-start(bf16[4,512,256]{2,1,0:T(8,128)(2,1)} %t_own.3), channel_id=1, source_target_pairs={{0,1},{1,2},{2,3},{3,4},{4,5},{5,6},{6,7},{8,9},{9,10},{10,11},{11... | collective-permute-start | bytes 3145736 | tf_op jit(solution)/shard_map/ppermute | solution.py:18
  7.2 1.2 compare_select_fusion.2.size_ref
  8.4 0.7 broadcast_subtract_fusion
  9.1 0.6 slice_bitcast_fusion
  9.6 8.3 %collective-permute-done.1.t_right = bf16[4,512,256]{2,1,0:T(8,128)(2,1)S(1)} collective-permute-done((bf16[4,512,256]{2,1,0:T(8,128)(2,1)}, bf16[4,512,256]{2,1,0:T(8,128)(2,1)S(1)}, u32[]{:S(2)}, u32[]{:S(2)}) %collective-permute-start.1) | collective-permute-done | bytes 1048608 | tf_op jit(solution)/shard_map/ppermute | solution.py:19
  17.9 1.3 collective-permute-done.t_left
  19.2 1.0 copy-done.5
  20.2 7.7 %shard_map.96 = f32[8,192,192]{2,1,0:T(8,128)} custom-call(s32[16]{0:T(128)} %get-tuple-element.9.lead_ref, s32[16]{0:T(128)} %get-tuple-element.8.trail_ref, s32[16]{0:T(128)} %compare_select_fusion.2.size_ref, s32[1]{0:T(128)} %bitcast.4.flip_ref, bf16[4,512,256]{2,1,0:T(8,128)(2,1)} %copy-done.5, bf16[4,512,256]{2,1,0:T(8,128)(2,1)} %t_own.3, ...), custom_call_target="tpu_custom_call" | custom-call | flops 1107296256 | bytes 6946816 | tf_op jit(solution)/shard_map/pallas_call | solution.py:153
  27.9 1.2 slice.29
  29.1 1.3 collective-permute-start.6
  30.4 7.9 %shard_map.95 = f32[8,192,192]{2,1,0:T(8,128)} custom-call(s32[16]{0:T(128)} %get-tuple-element.9.lead_ref, s32[16]{0:T(128)} %get-tuple-element.8.trail_ref, s32[16]{0:T(128)} %compare_select_fusion.2.size_ref, s32[1]{0:T(128)} %bitcast.2.flip_ref, bf16[4,512,256]{2,1,0:T(8,128)(2,1)} %copy-done.5, bf16[4,512,256]{2,1,0:T(8,128)(2,1)} %t_own.3, ...), custom_call_target="tpu_custom_call" | custom-call | flops 1107296256 | bytes 6946816 | tf_op jit(solution)/shard_map/pallas_call | solution.py:153
  38.3 2.2 %slice.27 = f32[4,192,192]{2,1,0:T(8,128)} slice(f32[8,192,192]{2,1,0:T(8,128)} %shard_map.95), slice={[0:4], [0:192], [0:192]} | slice | bytes 1179648 | tf_op jit(solution)/shard_map/slice | solution.py:28
  40.5 1.2 collective-permute-start.2
  41.7 1.4 slice_add_fusion
  43.1 0.3 collective-permute-start.7
  43.4 13.1 %collective-permute-done.2 = f32[4,192,192]{2,1,0:T(8,128)} collective-permute-done((f32[4,192,192]{2,1,0:T(8,128)}, f32[4,192,192]{2,1,0:T(8,128)}, u32[]{:S(2)}, u32[]{:S(2)}) %collective-permute-start.2) | collective-permute-done | bytes 589856 | tf_op jit(solution)/shard_map/ppermute | solution.py:32
  56.5 1.2 slice_add_fusion.1
  57.9 5.5 %collective-permute-done.7 = f32[2,192,192]{2,1,0:T(8,128)S(1)} collective-permute-done((f32[2,192,192]{2,1,0:T(8,128)S(1)}, f32[2,192,192]{2,1,0:T(8,128)S(1)}, u32[]{:S(2)}, u32[]{:S(2)}) %collective-permute-start.7) | collective-permute-done | bytes 294944 | tf_op jit(solution)/shard_map/ppermute | solution.py:32
  63.5 1.3 collective-permute-start.8
  65.0 0.3 collective-permute-start.4
  65.2 9.5 %collective-permute-done.8 = f32[2,192,192]{2,1,0:T(8,128)S(1)} collective-permute-done((f32[2,192,192]{2,1,0:T(8,128)S(1)}, f32[2,192,192]{2,1,0:T(8,128)S(1)}, u32[]{:S(2)}, u32[]{:S(2)}) %collective-permute-start.8) | collective-permute-done | bytes 294944 | tf_op jit(solution)/shard_map/ppermute | solution.py:35
  74.8 1.4 collective-permute-done.4
  76.3 0.9 collective-permute-start.5
  77.2 0.1 broadcast.30.clone
  77.4 0.1 broadcast.30.clone.1
  77.6 9.2 %collective-permute-done.9 = f32[4,192,192]{2,1,0:T(8,128)S(1)} collective-permute-done((f32[4,192,192]{2,1,0:T(8,128)S(1)}, f32[4,192,192]{2,1,0:T(8,128)S(1)}, u32[]{:S(2)}, u32[]{:S(2)}) %collective-permute-start.9) | collective-permute-done | bytes 589856 | tf_op jit(solution)/shard_map/ppermute | solution.py:35
  86.9 0.2 collective-permute-done.5
  87.3 2.0 %pad_maximum_fusion = (f32[16,192,192]{2,1,0:T(8,128)}, f32[16,192,192]{2,1,0:T(8,128)S(1)}) fusion(f32[8,192,192]{2,1,0:T(8,128)S(1)} %constant_dynamic-update-slice_fusion, f32[8,192,192]{2,1,0:T(8,128)S(1)} %constant_dynamic-update-slice_fusion.4, f32[16,192]{1,0:T(8,128)S(1)} %copy-done.7), kind=kLoop, calls=%fused_computation | loop fusion | flops 2359296 | bytes 7090176 | tf_op jit(solution)/shard_map/concatenate | solution.py:59
  89.3 1.9 collective-permute-start.11
  91.2 13.5 %collective-permute-start.10 = (f32[16,192,192]{2,1,0:T(8,128)S(1)}, f32[16,192,192]{2,1,0:T(8,128)}, u32[]{:S(2)}, u32[]{:S(2)}) collective-permute-start(f32[16,192,192]{2,1,0:T(8,128)S(1)} %get-tuple-element.7.refs_1_.refs_7_), channel_id=1, source_target_pairs={{0,1},{1,2},{2,3},{3,4},{4,5},{5,6},{6,7},{8,9},{9,10},{10,11},{11... | collective-permute-start | bytes 7077896 | tf_op jit(solution)/shard_map/ppermute | solution.py:18
  104.7 0.6 broadcast_in_dim.26.refs_6_.refs_9_
  105.3 0.1 copy.12
  105.4 0.6 reshape.26.nb_ref
  106.1 0.6 reshape.27.fock_ref
  106.7 1.7 copy.14.refs_5_.refs_8_
  108.4 29.3 %collective-permute-done.11.refs_2_ = f32[16,192,192]{2,1,0:T(8,128)} collective-permute-done((f32[16,192,192]{2,1,0:T(8,128)S(1)}, f32[16,192,192]{2,1,0:T(8,128)}, u32[]{:S(2)}, u32[]{:S(2)}) %collective-permute-start.11) | collective-permute-done | bytes 2359328 | tf_op jit(solution)/shard_map/ppermute | solution.py:19
  137.6 1.1 collective-permute-done.10.refs_0_
  138.7 8.9 %shard_map.97.refs_2_ = f32[8,192,192]{2,1,0:T(8,128)} custom-call(s32[32]{0:T(128)} %reshape.26.nb_ref, s32[16]{0:T(128)} %compare_select_fusion.2.size_ref, f32[32]{0:T(128)} %reshape.27.fock_ref, f32[16,192,192]{2,1,0:T(8,128)} %collective-permute-done.10.refs_0_, f32[16,192,192]{2,1,0:T(8,128)} %copy-done, ...), custom_call_target="tpu_custom_call" | custom-call | flops 905969664 | bytes 7077888 | tf_op jit(solution)/shard_map/pallas_call | solution.py:255
  147.7 2.1 %collective-permute-start.14 = (f32[8,192,192]{2,1,0:T(8,128)}, f32[8,192,192]{2,1,0:T(8,128)S(1)}, u32[]{:S(2)}, u32[]{:S(2)}) collective-permute-start(f32[8,192,192]{2,1,0:T(8,128)} %shard_map.97.refs_2_), channel_id=1, source_target_pairs={{1,0},{2,1},{3,2},{4,3},{5,4},{6,5},{7,6},{9,8},{10,9},{11,10},{12... | collective-permute-start | bytes 3538952 | tf_op jit(solution)/shard_map/ppermute | solution.py:19
  149.7 4.1 %collective-permute-start.12 = (f32[8,192,192]{2,1,0:T(8,128)}, f32[8,192,192]{2,1,0:T(8,128)}, u32[]{:S(2)}, u32[]{:S(2)}) collective-permute-start(f32[8,192,192]{2,1,0:T(8,128)} %shard_map.97.refs_2_), channel_id=1, source_target_pairs={{0,1},{1,2},{2,3},{3,4},{4,5},{5,6},{6,7},{8,9},{9,10},{10,11},{11... | collective-permute-start | bytes 3538952 | tf_op jit(solution)/shard_map/ppermute | solution.py:18
  153.8 8.4 %shard_map.98.refs_3_ = f32[8,192,192]{2,1,0:T(8,128)} custom-call(s32[32]{0:T(128)} %reshape.26.nb_ref, s32[16]{0:T(128)} %compare_select_fusion.2.size_ref, f32[32]{0:T(128)} %reshape.27.fock_ref, f32[16,192,192]{2,1,0:T(8,128)} %collective-permute-done.10.refs_0_, f32[16,192,192]{2,1,0:T(8,128)} %copy-done, ...), custom_call_target="tpu_custom_call" | custom-call | flops 905969664 | bytes 7077888 | tf_op jit(solution)/shard_map/pallas_call | solution.py:255
  162.2 1.9 collective-permute-start.15
  164.2 3.9 %collective-permute-start.13 = (f32[8,192,192]{2,1,0:T(8,128)}, f32[8,192,192]{2,1,0:T(8,128)}, u32[]{:S(2)}, u32[]{:S(2)}) collective-permute-start(f32[8,192,192]{2,1,0:T(8,128)} %shard_map.98.refs_3_), channel_id=1, source_target_pairs={{0,1},{1,2},{2,3},{3,4},{4,5},{5,6},{6,7},{8,9},{9,10},{10,11},{11... | collective-permute-start | bytes 3538952 | tf_op jit(solution)/shard_map/ppermute | solution.py:18
  168.1 3.4 %pad_maximum_fusion.1.refs_10_ = f32[16,192,192]{2,1,0:T(8,128)} fusion(f32[8,192,192]{2,1,0:T(8,128)} %shard_map.98.refs_3_, f32[8,192,192]{2,1,0:T(8,128)S(1)} %copy-done.1), kind=kLoop, calls=%fused_computation.1 | loop fusion | flops 589824 | bytes 4718592 | tf_op jit(solution)/shard_map/concatenate | solution.py:321
  171.5 15.6 %collective-permute-done.15.refs_5_ = f32[8,192,192]{2,1,0:T(8,128)} collective-permute-done((f32[8,192,192]{2,1,0:T(8,128)}, f32[8,192,192]{2,1,0:T(8,128)}, u32[]{:S(2)}, u32[]{:S(2)}) %collective-permute-start.15) | collective-permute-done | bytes 1179680 | tf_op jit(solution)/shard_map/ppermute | solution.py:19
  187.1 1.2 collective-permute-done.13.refs_1_
  188.3 13.0 %shard_map.99 = f32[16,192,192]{2,1,0:T(8,128)} custom-call(s32[32]{0:T(128)} %reshape.26.nb_ref, s32[16]{0:T(128)} %compare_select_fusion.2.size_ref, f32[32]{0:T(128)} %reshape.27.fock_ref, f32[8,192,192]{2,1,0:T(8,128)} %collective-permute-done.12.refs_0_, f32[8,192,192]{2,1,0:T(8,128)} %collective-permute-done.13.refs_1_, ...), custom_call_target="tpu_custom_call" | custom-call | flops 1811939328 | bytes 14155776 | tf_op jit(solution)/shard_map/pallas_call | solution.py:255
  (39 shorter events, 0.9 us)
Async XLA Ops:
  0.6 17.3 %collective-permute-start.1 = (bf16[4,512,256]{2,1,0:T(8,128)(2,1)}, bf16[4,512,256]{2,1,0:T(8,128)(2,1)S(1)}, u32[]{:S(2)}, u32[]{:S(2)}) collective-permute-start(bf16[4,512,256]{2,1,0:T(8,128)(2,1)} %t_own.3), channel_id=1, source_target_pairs={{1,0},{2,1},{3,2},{4,3},{5,4},{6,5},{7,6},{9,8},{10,9},{11,10},{12... | collective-permute-start | bytes 3145736 | tf_op jit(solution)/shard_map/ppermute | solution.py:19
  2.6 16.6 %collective-permute-start = (bf16[4,512,256]{2,1,0:T(8,128)(2,1)}, bf16[4,512,256]{2,1,0:T(8,128)(2,1)S(1)}, u32[]{:S(2)}, u32[]{:S(2)}) collective-permute-start(bf16[4,512,256]{2,1,0:T(8,128)(2,1)} %t_own.3), channel_id=1, source_target_pairs={{0,1},{1,2},{2,3},{3,4},{4,5},{5,6},{6,7},{8,9},{9,10},{10,11},{11... | collective-permute-start | bytes 3145736 | tf_op jit(solution)/shard_map/ppermute | solution.py:18
  17.9 1.3 copy-start.4
  19.2 1.0 copy-start.5
  29.1 12.7 %collective-permute-start.6 = (f32[4,192,192]{2,1,0:T(8,128)S(1)}, f32[4,192,192]{2,1,0:T(8,128)}, u32[]{:S(2)}, u32[]{:S(2)}) collective-permute-start(f32[4,192,192]{2,1,0:T(8,128)S(1)} %slice.29), channel_id=1, source_target_pairs={{0,16},{8,24},{16,0},{24,8},{1,17},{9,25},{17,1},{25,9},{2,18},{10... | collective-permute-start | bytes 1769480 | tf_op jit(solution)/shard_map/ppermute | solution.py:32
  38.3 3.4 %copy-start.2 = (f32[8,192,192]{2,1,0:T(8,128)S(1)}, f32[8,192,192]{2,1,0:T(8,128)}, u32[]{:S(2)}) copy-start(f32[8,192,192]{2,1,0:T(8,128)} %shard_map.96) | copy-start | bytes 3538948
  40.5 16.0 %collective-permute-start.2 = (f32[4,192,192]{2,1,0:T(8,128)}, f32[4,192,192]{2,1,0:T(8,128)}, u32[]{:S(2)}, u32[]{:S(2)}) collective-permute-start(f32[4,192,192]{2,1,0:T(8,128)} %slice.27), channel_id=1, source_target_pairs={{0,8},{8,0},{16,24},{24,16},{1,9},{9,1},{17,25},{25,17},{2,10},{10... | collective-permute-start | bytes 1769480 | tf_op jit(solution)/shard_map/ppermute | solution.py:32
  41.7 14.8 %copy-start.3 = (f32[8,192,192]{2,1,0:T(8,128)S(1)}, f32[8,192,192]{2,1,0:T(8,128)}, u32[]{:S(2)}) copy-start(f32[8,192,192]{2,1,0:T(8,128)} %shard_map.95) | copy-start | bytes 3538948
  43.1 20.3 %collective-permute-start.7 = (f32[2,192,192]{2,1,0:T(8,128)S(1)}, f32[2,192,192]{2,1,0:T(8,128)S(1)}, u32[]{:S(2)}, u32[]{:S(2)}) collective-permute-start(f32[2,192,192]{2,1,0:T(8,128)S(1)} %constant_dynamic-slice_fusion), channel_id=1, source_target_pairs={{0,8},{8,0},{16,24},{24,16},{1,9},{9,1},{17,25},{25,17},{2,10},{10... | collective-permute-start | bytes 884744 | tf_op jit(solution)/shard_map/ppermute | solution.py:32
  57.8 7.0 %collective-permute-start.3 = (f32[2,192,192]{2,1,0:T(8,128)S(1)}, f32[2,192,192]{2,1,0:T(8,128)S(1)}, u32[]{:S(2)}, u32[]{:S(2)}) collective-permute-start(f32[2,192,192]{2,1,0:T(8,128)S(1)} %constant_dynamic-slice_fusion.1), channel_id=1, source_target_pairs={{0,16},{8,24},{16,0},{24,8},{1,17},{9,25},{17,1},{25,9},{2,18},{10... | collective-permute-start | bytes 884744 | tf_op jit(solution)/shard_map/ppermute | solution.py:32
  63.5 11.2 %collective-permute-start.8 = (f32[2,192,192]{2,1,0:T(8,128)S(1)}, f32[2,192,192]{2,1,0:T(8,128)S(1)}, u32[]{:S(2)}, u32[]{:S(2)}) collective-permute-start(f32[2,192,192]{2,1,0:T(8,128)S(1)} %get-tuple-element.5), channel_id=1, source_target_pairs={{0,8},{8,0},{16,24},{24,16},{1,9},{9,1},{17,25},{25,17},{2,10},{10... | collective-permute-start | bytes 884744 | tf_op jit(solution)/shard_map/ppermute | solution.py:35
  65.0 11.3 %collective-permute-start.4 = (f32[2,192,192]{2,1,0:T(8,128)S(1)}, f32[2,192,192]{2,1,0:T(8,128)S(1)}, u32[]{:S(2)}, u32[]{:S(2)}) collective-permute-start(f32[2,192,192]{2,1,0:T(8,128)S(1)} %get-tuple-element.3), channel_id=1, source_target_pairs={{0,16},{8,24},{16,0},{24,8},{1,17},{9,25},{17,1},{25,9},{2,18},{10... | collective-permute-start | bytes 884744 | tf_op jit(solution)/shard_map/ppermute | solution.py:35
  74.8 12.1 %collective-permute-start.9 = (f32[4,192,192]{2,1,0:T(8,128)S(1)}, f32[4,192,192]{2,1,0:T(8,128)S(1)}, u32[]{:S(2)}, u32[]{:S(2)}) collective-permute-start(f32[4,192,192]{2,1,0:T(8,128)S(1)} %constant_dynamic-update-slice_fusion.2), channel_id=1, source_target_pairs={{0,16},{8,24},{16,0},{24,8},{1,17},{9,25},{17,1},{25,9},{2,18},{10... | collective-permute-start | bytes 1769480 | tf_op jit(solution)/shard_map/ppermute | solution.py:35
  76.3 10.9 %collective-permute-start.5 = (f32[4,192,192]{2,1,0:T(8,128)S(1)}, f32[4,192,192]{2,1,0:T(8,128)S(1)}, u32[]{:S(2)}, u32[]{:S(2)}) collective-permute-start(f32[4,192,192]{2,1,0:T(8,128)S(1)} %constant_dynamic-update-slice_fusion.6), channel_id=1, source_target_pairs={{0,8},{8,0},{16,24},{24,16},{1,9},{9,1},{17,25},{25,17},{2,10},{10... | collective-permute-start | bytes 1769480 | tf_op jit(solution)/shard_map/ppermute | solution.py:35
  77.6 9.6 %copy-start.7 = (f32[16,192]{1,0:T(8,128)S(1)}, f32[16,192]{1,0:T(8,128)}, u32[]{:S(2)}) copy-start(f32[16,192]{1,0:T(8,128)} %param.12) | copy-start | bytes 36868
  87.2 18.1 %copy-start.9 = (s32[16,2]{0,1:T(2,128)S(1)}, s32[16,2]{0,1:T(2,128)}, u32[]{:S(2)}) copy-start(s32[16,2]{0,1:T(2,128)} %param.14) | copy-start | bytes 388
  87.3 18.8 %copy-start.8 = (f32[16,2]{0,1:T(2,128)S(1)}, f32[16,2]{0,1:T(2,128)}, u32[]{:S(2)}) copy-start(f32[16,2]{0,1:T(2,128)} %param.15) | copy-start | bytes 388
  89.3 49.4 %copy-start = (f32[16,192,192]{2,1,0:T(8,128)}, f32[16,192,192]{2,1,0:T(8,128)S(1)}, u32[]{:S(2)}) copy-start(f32[16,192,192]{2,1,0:T(8,128)S(1)} %get-tuple-element.7.refs_1_.refs_7_) | copy-start | bytes 7077892
  89.3 48.3 %collective-permute-start.11 = (f32[16,192,192]{2,1,0:T(8,128)S(1)}, f32[16,192,192]{2,1,0:T(8,128)}, u32[]{:S(2)}, u32[]{:S(2)}) collective-permute-start(f32[16,192,192]{2,1,0:T(8,128)S(1)} %get-tuple-element.7.refs_1_.refs_7_), channel_id=1, source_target_pairs={{1,0},{2,1},{3,2},{4,3},{5,4},{6,5},{7,6},{9,8},{10,9},{11,10},{12... | collective-permute-start | bytes 7077896 | tf_op jit(solution)/shard_map/ppermute | solution.py:19
  91.2 47.5 %collective-permute-start.10 = (f32[16,192,192]{2,1,0:T(8,128)S(1)}, f32[16,192,192]{2,1,0:T(8,128)}, u32[]{:S(2)}, u32[]{:S(2)}) collective-permute-start(f32[16,192,192]{2,1,0:T(8,128)S(1)} %get-tuple-element.7.refs_1_.refs_7_), channel_id=1, source_target_pairs={{0,1},{1,2},{2,3},{3,4},{4,5},{5,6},{6,7},{8,9},{9,10},{10,11},{11... | collective-permute-start | bytes 7077896 | tf_op jit(solution)/shard_map/ppermute | solution.py:18
  147.7 20.4 %copy-start.1 = (f32[8,192,192]{2,1,0:T(8,128)S(1)}, f32[8,192,192]{2,1,0:T(8,128)}, u32[]{:S(2)}) copy-start(f32[8,192,192]{2,1,0:T(8,128)} %shard_map.97.refs_2_) | copy-start | bytes 3538948
  147.7 23.8 %collective-permute-start.14 = (f32[8,192,192]{2,1,0:T(8,128)}, f32[8,192,192]{2,1,0:T(8,128)S(1)}, u32[]{:S(2)}, u32[]{:S(2)}) collective-permute-start(f32[8,192,192]{2,1,0:T(8,128)} %shard_map.97.refs_2_), channel_id=1, source_target_pairs={{1,0},{2,1},{3,2},{4,3},{5,4},{6,5},{7,6},{9,8},{10,9},{11,10},{12... | collective-permute-start | bytes 3538952 | tf_op jit(solution)/shard_map/ppermute | solution.py:19
  149.7 21.8 %collective-permute-start.12 = (f32[8,192,192]{2,1,0:T(8,128)}, f32[8,192,192]{2,1,0:T(8,128)}, u32[]{:S(2)}, u32[]{:S(2)}) collective-permute-start(f32[8,192,192]{2,1,0:T(8,128)} %shard_map.97.refs_2_), channel_id=1, source_target_pairs={{0,1},{1,2},{2,3},{3,4},{4,5},{5,6},{6,7},{8,9},{9,10},{10,11},{11... | collective-permute-start | bytes 3538952 | tf_op jit(solution)/shard_map/ppermute | solution.py:18
  162.2 24.9 %collective-permute-start.15 = (f32[8,192,192]{2,1,0:T(8,128)}, f32[8,192,192]{2,1,0:T(8,128)}, u32[]{:S(2)}, u32[]{:S(2)}) collective-permute-start(f32[8,192,192]{2,1,0:T(8,128)} %shard_map.98.refs_3_), channel_id=1, source_target_pairs={{1,0},{2,1},{3,2},{4,3},{5,4},{6,5},{7,6},{9,8},{10,9},{11,10},{12... | collective-permute-start | bytes 3538952 | tf_op jit(solution)/shard_map/ppermute | solution.py:19
  164.2 24.1 %collective-permute-start.13 = (f32[8,192,192]{2,1,0:T(8,128)}, f32[8,192,192]{2,1,0:T(8,128)}, u32[]{:S(2)}, u32[]{:S(2)}) collective-permute-start(f32[8,192,192]{2,1,0:T(8,128)} %shard_map.98.refs_3_), channel_id=1, source_target_pairs={{0,1},{1,2},{2,3},{3,4},{4,5},{5,6},{6,7},{8,9},{9,10},{10,11},{11... | collective-permute-start | bytes 3538952 | tf_op jit(solution)/shard_map/ppermute | solution.py:18
  171.5 16.8 %copy-start.6 = (f32[8,192,192]{2,1,0:T(8,128)}, f32[8,192,192]{2,1,0:T(8,128)S(1)}, u32[]{:S(2)}) copy-start(f32[8,192,192]{2,1,0:T(8,128)S(1)} %collective-permute-done.14.refs_4_) | copy-start | bytes 3538948

commit v16 on v15

--- a/solution.py
+++ b/solution.py
@@ -20,8 +20,20 @@
     return (from_left, cells, from_right)
 
 
-def halving_stream(piece, index, count, bits, presplit=False):
-    for step, bit in enumerate(bits):
+def swap_over_aux(value, bit_even, bit_odd):
+    pairs = lax.axis_size("pair")
+    count = lax.axis_size("aux")
+    perm = []
+    for p in range(pairs):
+        bit = bit_even if p % 2 == 0 else bit_odd
+        perm += [(a * pairs + p, (a ^ bit) * pairs + p) for a in range(count)]
+    return lax.ppermute(value, ("aux", "pair"), perm)
+
+
+def halving_stream(piece, index, parity, bits, presplit=False):
+    steps = [(b, o) for b, o in zip(bits, reversed(bits))]
+    for step, (bit_even, bit_odd) in enumerate(steps):
+        bit = jnp.where(parity == 0, bit_even, bit_odd)
         side = (index // bit) % 2
         half = piece.shape[0] // 2
         if presplit and step == 0:
@@ -29,10 +41,11 @@
         else:
             keep = lax.dynamic_slice_in_dim(piece, side * half, half, axis=0)
             send = lax.dynamic_slice_in_dim(piece, (1 - side) * half, half, axis=0)
-        piece = keep + lax.ppermute(send, "aux", [(i, i ^ bit) for i in range(count)])
-    for bit in reversed(bits):
+        piece = keep + swap_over_aux(send, bit_even, bit_odd)
+    for bit_even, bit_odd in reversed(steps):
+        bit = jnp.where(parity == 0, bit_even, bit_odd)
         side = (index // bit) % 2
-        other = lax.ppermute(piece, "aux", [(i, i ^ bit) for i in range(count)])
+        other = swap_over_aux(piece, bit_even, bit_odd)
         length = piece.shape[0]
         full = jnp.zeros((2 * length,) + piece.shape[1:], piece.dtype)
         full = lax.dynamic_update_slice_in_dim(full, piece, side * length, axis=0)
@@ -44,18 +57,23 @@
     return lax.axis_size("aux") == 4 and halves % 8 == 0
 
 
+STREAM_ORDERS = ((1, 2), (2, 1))
+
+
 def send_first(half_index):
     index = lax.axis_index("aux")
-    return (1 - (index // (1, 2)[half_index]) % 2).astype(jnp.int32).reshape(1)
+    even, odd = STREAM_ORDERS[half_index][0], STREAM_ORDERS[half_index][1]
+    bit = jnp.where(lax.axis_index("pair") % 2 == 0, even, odd)
+    return (1 - (index // bit) % 2).astype(jnp.int32).reshape(1)
 
 
 def sum_over_aux(halves, presplit):
-    count = lax.axis_size("aux")
     if not halving_ready(halves[0].shape[0]):
         return lax.psum(jnp.concatenate(halves, axis=0), "aux")
     index = lax.axis_index("aux")
-    first = halving_stream(halves[0], index, count, (1, 2), presplit)
-    second = halving_stream(halves[1], index, count, (2, 1), presplit)
+    parity = lax.axis_index("pair") % 2
+    first = halving_stream(halves[0], index, parity, STREAM_ORDERS[0], presplit)
+    second = halving_stream(halves[1], index, parity, STREAM_ORDERS[1], presplit)
     return jnp.concatenate([first, second], axis=0)
 
 

time: 204 us -> 199 us (0.975)
  waiting for transfers between devices: 95.6 us -> 91.1 us
    ppermute x4, starting transfers between devices: 26 us -> 21.1 us  [halo_sources(): from_left = lax.ppermute(cells, axis, [(i, i + 1) for i in range(ends)])]
    ppermute x8, waiting for transfers between devices: 38.9 us -> 35.2 us  [swap_over_aux(): return lax.ppermute(value, ('aux', 'pair'), perm)]
    ppermute x8, starting transfers between devices: 5.5 us -> 8.59 us  [swap_over_aux(): return lax.ppermute(value, ('aux', 'pair'), perm)]
  transfers between devices with their start and end apart: 16 -> 16, of which waited for: 12 -> 14; matrix products, arithmetic and copies ran while one was open for 8% -> 8% of each run, Pallas kernels for 8% -> 9%
where the time goes in v16:
time: 199 us; the launch traced here: 197 us
  waiting for transfers between devices  91.1 us (46%)
  Pallas kernels  46.9 us (24%)
  starting transfers between devices  38.9 us (20%)
  other arithmetic  10.5 us (5%)
  local copies, waits for them, and re-layouts  8.83 us (4%)
    ppermute x4, waiting for transfers between devices, halo_sources(): from_right = lax.ppermute(cells, axis, [(i + 1, i) for i in range(ends)])  52.4 us
    ppermute x8, waiting for transfers between devices, swap_over_aux(): return lax.ppermute(value, ('aux', 'pair'), perm)  35.2 us
    pallas_call x3, Pallas kernels, coupling_step(): pl.pallas_call(kernel, grid_spec=grid_spec, out_shape=jax.ShapeDtypeStruc...  30.8 us
    ppermute x4, starting transfers between devices, halo_sources(): from_left = lax.ppermute(cells, axis, [(i, i + 1) for i in range(ends)])  21.1 us
    pallas_call x2, Pallas kernels, partial_exchange(): pl.pallas_call(functools.partial(exchange_kernel, occ=occ, group=group, s...  16 us
    ppermute x4, starting transfers between devices, halo_sources(): from_right = lax.ppermute(cells, axis, [(i + 1, i) for i in range(ends)])  9.27 us
    ppermute x8, starting transfers between devices, swap_over_aux(): return lax.ppermute(value, ('aux', 'pair'), perm)  8.59 us
  transfers between devices with their start and end apart: 16, of which 14 were waited for; matrix products, arithmetic and copies ran while one was open for 8% of the time, Pallas kernels for 9%

profile of v16, /device:TPU:1, one launch (start us, length us, event | category | flops | bytes accessed | tf_op | source)
XLA Modules:
  0.0 197.4 jit_solution(799919352172755456)
XLA Ops:
  0.6 2.0 collective-permute-start.1
  2.6 4.6 %collective-permute-start = (bf16[4,512,256]{2,1,0:T(8,128)(2,1)}, bf16[4,512,256]{2,1,0:T(8,128)(2,1)S(1)}, u32[]{:S(2)}, u32[]{:S(2)}) collective-permute-start(bf16[4,512,256]{2,1,0:T(8,128)(2,1)} %t_own.3), channel_id=1, source_target_pairs={{0,1},{1,2},{2,3},{3,4},{4,5},{5,6},{6,7},{8,9},{9,10},{10,11},{11... | collective-permute-start | bytes 3145736 | tf_op jit(solution)/shard_map/ppermute | solution.py:18
  7.2 1.2 compare_select_fusion.2.size_ref
  8.4 0.7 broadcast_subtract_fusion
  9.1 0.6 slice_bitcast_fusion
  9.7 8.2 %collective-permute-done.1.t_right = bf16[4,512,256]{2,1,0:T(8,128)(2,1)S(1)} collective-permute-done((bf16[4,512,256]{2,1,0:T(8,128)(2,1)}, bf16[4,512,256]{2,1,0:T(8,128)(2,1)S(1)}, u32[]{:S(2)}, u32[]{:S(2)}) %collective-permute-start.1) | collective-permute-done | bytes 1048608 | tf_op jit(solution)/shard_map/ppermute | solution.py:19
  17.9 1.3 collective-permute-done.t_left
  19.2 1.0 copy-done.5
  20.2 8.2 %shard_map.96 = f32[8,192,192]{2,1,0:T(8,128)} custom-call(s32[16]{0:T(128)} %get-tuple-element.9.lead_ref, s32[16]{0:T(128)} %get-tuple-element.8.trail_ref, s32[16]{0:T(128)} %compare_select_fusion.2.size_ref, s32[1]{0:T(128)} %bitcast.4.flip_ref, bf16[4,512,256]{2,1,0:T(8,128)(2,1)} %copy-done.5, bf16[4,512,256]{2,1,0:T(8,128)(2,1)} %t_own.3, ...), custom_call_target="tpu_custom_call" | custom-call | flops 1107296256 | bytes 6946816 | tf_op jit(solution)/shard_map/pallas_call | solution.py:171
  28.4 1.2 slice.29
  29.6 1.3 collective-permute-start.6
  30.8 7.8 %shard_map.95 = f32[8,192,192]{2,1,0:T(8,128)} custom-call(s32[16]{0:T(128)} %get-tuple-element.9.lead_ref, s32[16]{0:T(128)} %get-tuple-element.8.trail_ref, s32[16]{0:T(128)} %compare_select_fusion.2.size_ref, s32[1]{0:T(128)} %bitcast.2.flip_ref, bf16[4,512,256]{2,1,0:T(8,128)(2,1)} %copy-done.5, bf16[4,512,256]{2,1,0:T(8,128)(2,1)} %t_own.3, ...), custom_call_target="tpu_custom_call" | custom-call | flops 1107296256 | bytes 6946816 | tf_op jit(solution)/shard_map/pallas_call | solution.py:171
  38.7 2.2 %slice.27 = f32[4,192,192]{2,1,0:T(8,128)} slice(f32[8,192,192]{2,1,0:T(8,128)} %shard_map.95), slice={[0:4], [0:192], [0:192]} | slice | bytes 1179648 | tf_op jit(solution)/shard_map/slice | solution.py:40
  40.9 1.2 collective-permute-start.2
  42.1 4.6 %collective-permute-done.6 = f32[4,192,192]{2,1,0:T(8,128)} collective-permute-done((f32[4,192,192]{2,1,0:T(8,128)S(1)}, f32[4,192,192]{2,1,0:T(8,128)}, u32[]{:S(2)}, u32[]{:S(2)}) %collective-permute-start.6) | collective-permute-done | bytes 589856 | tf_op jit(solution)/shard_map/ppermute | solution.py:30
  46.7 1.2 slice_add_fusion
  48.0 2.8 %collective-permute-start.7 = (f32[2,192,192]{2,1,0:T(8,128)S(1)}, f32[2,192,192]{2,1,0:T(8,128)S(1)}, u32[]{:S(2)}, u32[]{:S(2)}) collective-permute-start(f32[2,192,192]{2,1,0:T(8,128)S(1)} %constant_dynamic-slice_fusion), channel_id=1, source_target_pairs={{0,8},{8,0},{16,24},{24,16},{1,17},{9,25},{17,1},{25,9},{2,10},{10... | collective-permute-start | bytes 884744 | tf_op jit(solution)/shard_map/ppermute | solution.py:30
  50.8 1.4 collective-permute-done.2
  52.2 1.2 slice_add_fusion.1
  53.5 0.3 collective-permute-start.3
  53.8 4.8 %collective-permute-done.7 = f32[2,192,192]{2,1,0:T(8,128)S(1)} collective-permute-done((f32[2,192,192]{2,1,0:T(8,128)S(1)}, f32[2,192,192]{2,1,0:T(8,128)S(1)}, u32[]{:S(2)}, u32[]{:S(2)}) %collective-permute-start.7) | collective-permute-done | bytes 294944 | tf_op jit(solution)/shard_map/ppermute | solution.py:30
  58.8 1.5 collective-permute-start.8
  60.2 3.7 %collective-permute-done.3 = f32[2,192,192]{2,1,0:T(8,128)S(1)} collective-permute-done((f32[2,192,192]{2,1,0:T(8,128)S(1)}, f32[2,192,192]{2,1,0:T(8,128)S(1)}, u32[]{:S(2)}, u32[]{:S(2)}) %collective-permute-start.3) | collective-permute-done | bytes 294944 | tf_op jit(solution)/shard_map/ppermute | solution.py:30
  64.1 2.9 %collective-permute-done.8 = f32[2,192,192]{2,1,0:T(8,128)S(1)} collective-permute-done((f32[2,192,192]{2,1,0:T(8,128)S(1)}, f32[2,192,192]{2,1,0:T(8,128)S(1)}, u32[]{:S(2)}, u32[]{:S(2)}) %collective-permute-start.8) | collective-permute-done | bytes 294944 | tf_op jit(solution)/shard_map/ppermute | solution.py:30
  67.1 3.9 %collective-permute-done.4 = f32[2,192,192]{2,1,0:T(8,128)S(1)} collective-permute-done((f32[2,192,192]{2,1,0:T(8,128)S(1)}, f32[2,192,192]{2,1,0:T(8,128)S(1)}, u32[]{:S(2)}, u32[]{:S(2)}) %collective-permute-start.4) | collective-permute-done | bytes 294944 | tf_op jit(solution)/shard_map/ppermute | solution.py:30
  71.0 1.3 collective-permute-start.5
  72.6 0.1 broadcast.29.clone.1
  72.8 12.4 %collective-permute-done.9 = f32[4,192,192]{2,1,0:T(8,128)S(1)} collective-permute-done((f32[4,192,192]{2,1,0:T(8,128)S(1)}, f32[4,192,192]{2,1,0:T(8,128)S(1)}, u32[]{:S(2)}, u32[]{:S(2)}) %collective-permute-start.9) | collective-permute-done | bytes 589856 | tf_op jit(solution)/shard_map/ppermute | solution.py:30
  85.2 1.6 collective-permute-done.5
  86.9 2.0 %pad_maximum_fusion = (f32[16,192,192]{2,1,0:T(8,128)}, f32[16,192,192]{2,1,0:T(8,128)S(1)}) fusion(f32[8,192,192]{2,1,0:T(8,128)S(1)} %constant_dynamic-update-slice_fusion, f32[8,192,192]{2,1,0:T(8,128)S(1)} %constant_dynamic-update-slice_fusion.4, f32[16,192]{1,0:T(8,128)S(1)} %copy-done.7), kind=kLoop, calls=%fused_computation | loop fusion | flops 2359296 | bytes 7090176 | tf_op jit(solution)/shard_map/concatenate | solution.py:77
  89.0 3.3 %collective-permute-start.11 = (f32[16,192,192]{2,1,0:T(8,128)S(1)}, f32[16,192,192]{2,1,0:T(8,128)}, u32[]{:S(2)}, u32[]{:S(2)}) collective-permute-start(f32[16,192,192]{2,1,0:T(8,128)S(1)} %get-tuple-element.7.refs_1_.refs_7_), channel_id=1, source_target_pairs={{1,0},{2,1},{3,2},{4,3},{5,4},{6,5},{7,6},{9,8},{10,9},{11,10},{12... | collective-permute-start | bytes 7077896 | tf_op jit(solution)/shard_map/ppermute | solution.py:19
  92.3 8.0 %collective-permute-start.10 = (f32[16,192,192]{2,1,0:T(8,128)S(1)}, f32[16,192,192]{2,1,0:T(8,128)}, u32[]{:S(2)}, u32[]{:S(2)}) collective-permute-start(f32[16,192,192]{2,1,0:T(8,128)S(1)} %get-tuple-element.7.refs_1_.refs_7_), channel_id=1, source_target_pairs={{0,1},{1,2},{2,3},{3,4},{4,5},{5,6},{6,7},{8,9},{9,10},{10,11},{11... | collective-permute-start | bytes 7077896 | tf_op jit(solution)/shard_map/ppermute | solution.py:18
  100.3 0.6 broadcast_in_dim.26.refs_6_.refs_9_
  101.0 0.6 reshape.26.nb_ref
  101.7 0.6 reshape.27.fock_ref
  102.3 1.7 copy.14.refs_5_.refs_8_
  103.9 29.3 %collective-permute-done.11.refs_2_ = f32[16,192,192]{2,1,0:T(8,128)} collective-permute-done((f32[16,192,192]{2,1,0:T(8,128)S(1)}, f32[16,192,192]{2,1,0:T(8,128)}, u32[]{:S(2)}, u32[]{:S(2)}) %collective-permute-start.11) | collective-permute-done | bytes 2359328 | tf_op jit(solution)/shard_map/ppermute | solution.py:19
  133.2 1.1 collective-permute-done.10.refs_0_
  134.3 8.4 %shard_map.97.refs_2_ = f32[8,192,192]{2,1,0:T(8,128)} custom-call(s32[32]{0:T(128)} %reshape.26.nb_ref, s32[16]{0:T(128)} %compare_select_fusion.2.size_ref, f32[32]{0:T(128)} %reshape.27.fock_ref, f32[16,192,192]{2,1,0:T(8,128)} %collective-permute-done.10.refs_0_, f32[16,192,192]{2,1,0:T(8,128)} %copy-done, ...), custom_call_target="tpu_custom_call" | custom-call | flops 905969664 | bytes 7077888 | tf_op jit(solution)/shard_map/pallas_call | solution.py:273
  142.7 2.1 %collective-permute-start.14 = (f32[8,192,192]{2,1,0:T(8,128)}, f32[8,192,192]{2,1,0:T(8,128)S(1)}, u32[]{:S(2)}, u32[]{:S(2)}) collective-permute-start(f32[8,192,192]{2,1,0:T(8,128)} %shard_map.97.refs_2_), channel_id=1, source_target_pairs={{1,0},{2,1},{3,2},{4,3},{5,4},{6,5},{7,6},{9,8},{10,9},{11,10},{12... | collective-permute-start | bytes 3538952 | tf_op jit(solution)/shard_map/ppermute | solution.py:19
  144.8 4.7 %collective-permute-start.12 = (f32[8,192,192]{2,1,0:T(8,128)}, f32[8,192,192]{2,1,0:T(8,128)}, u32[]{:S(2)}, u32[]{:S(2)}) collective-permute-start(f32[8,192,192]{2,1,0:T(8,128)} %shard_map.97.refs_2_), channel_id=1, source_target_pairs={{0,1},{1,2},{2,3},{3,4},{4,5},{5,6},{6,7},{8,9},{9,10},{10,11},{11... | collective-permute-start | bytes 3538952 | tf_op jit(solution)/shard_map/ppermute | solution.py:18
  149.5 9.2 %shard_map.98.refs_3_ = f32[8,192,192]{2,1,0:T(8,128)} custom-call(s32[32]{0:T(128)} %reshape.26.nb_ref, s32[16]{0:T(128)} %compare_select_fusion.2.size_ref, f32[32]{0:T(128)} %reshape.27.fock_ref, f32[16,192,192]{2,1,0:T(8,128)} %collective-permute-done.10.refs_0_, f32[16,192,192]{2,1,0:T(8,128)} %copy-done, ...), custom_call_target="tpu_custom_call" | custom-call | flops 905969664 | bytes 7077888 | tf_op jit(solution)/shard_map/pallas_call | solution.py:273
  158.7 1.9 collective-permute-start.15
  160.6 3.9 %collective-permute-start.13 = (f32[8,192,192]{2,1,0:T(8,128)}, f32[8,192,192]{2,1,0:T(8,128)}, u32[]{:S(2)}, u32[]{:S(2)}) collective-permute-start(f32[8,192,192]{2,1,0:T(8,128)} %shard_map.98.refs_3_), channel_id=1, source_target_pairs={{0,1},{1,2},{2,3},{3,4},{4,5},{5,6},{6,7},{8,9},{9,10},{10,11},{11... | collective-permute-start | bytes 3538952 | tf_op jit(solution)/shard_map/ppermute | solution.py:18
  164.5 3.4 %pad_maximum_fusion.1.refs_10_ = f32[16,192,192]{2,1,0:T(8,128)} fusion(f32[8,192,192]{2,1,0:T(8,128)} %shard_map.98.refs_3_, f32[8,192,192]{2,1,0:T(8,128)S(1)} %copy-done.1), kind=kLoop, calls=%fused_computation.1 | loop fusion | flops 589824 | bytes 4718592 | tf_op jit(solution)/shard_map/concatenate | solution.py:339
  167.9 14.9 %collective-permute-done.15.refs_5_ = f32[8,192,192]{2,1,0:T(8,128)} collective-permute-done((f32[8,192,192]{2,1,0:T(8,128)}, f32[8,192,192]{2,1,0:T(8,128)}, u32[]{:S(2)}, u32[]{:S(2)}) %collective-permute-start.15) | collective-permute-done | bytes 1179680 | tf_op jit(solution)/shard_map/ppermute | solution.py:19
  182.8 1.2 collective-permute-done.13.refs_1_
  184.0 13.2 %shard_map.99 = f32[16,192,192]{2,1,0:T(8,128)} custom-call(s32[32]{0:T(128)} %reshape.26.nb_ref, s32[16]{0:T(128)} %compare_select_fusion.2.size_ref, f32[32]{0:T(128)} %reshape.27.fock_ref, f32[8,192,192]{2,1,0:T(8,128)} %collective-permute-done.12.refs_0_, f32[8,192,192]{2,1,0:T(8,128)} %collective-permute-done.13.refs_1_, ...), custom_call_target="tpu_custom_call" | custom-call | flops 1811939328 | bytes 14155776 | tf_op jit(solution)/shard_map/pallas_call | solution.py:273
  (39 shorter events, 1.1 us)
Async XLA Ops:
  0.6 17.3 %collective-permute-start.1 = (bf16[4,512,256]{2,1,0:T(8,128)(2,1)}, bf16[4,512,256]{2,1,0:T(8,128)(2,1)S(1)}, u32[]{:S(2)}, u32[]{:S(2)}) collective-permute-start(bf16[4,512,256]{2,1,0:T(8,128)(2,1)} %t_own.3), channel_id=1, source_target_pairs={{1,0},{2,1},{3,2},{4,3},{5,4},{6,5},{7,6},{9,8},{10,9},{11,10},{12... | collective-permute-start | bytes 3145736 | tf_op jit(solution)/shard_map/ppermute | solution.py:19
  2.6 16.6 %collective-permute-start = (bf16[4,512,256]{2,1,0:T(8,128)(2,1)}, bf16[4,512,256]{2,1,0:T(8,128)(2,1)S(1)}, u32[]{:S(2)}, u32[]{:S(2)}) collective-permute-start(bf16[4,512,256]{2,1,0:T(8,128)(2,1)} %t_own.3), channel_id=1, source_target_pairs={{0,1},{1,2},{2,3},{3,4},{4,5},{5,6},{6,7},{8,9},{9,10},{10,11},{11... | collective-permute-start | bytes 3145736 | tf_op jit(solution)/shard_map/ppermute | solution.py:18
  17.9 1.3 copy-start.4
  19.2 1.0 copy-start.5
  29.6 17.2 %collective-permute-start.6 = (f32[4,192,192]{2,1,0:T(8,128)S(1)}, f32[4,192,192]{2,1,0:T(8,128)}, u32[]{:S(2)}, u32[]{:S(2)}) collective-permute-start(f32[4,192,192]{2,1,0:T(8,128)S(1)} %slice.29), channel_id=1, source_target_pairs={{0,16},{8,24},{16,0},{24,8},{1,9},{9,1},{17,25},{25,17},{2,18},{10... | collective-permute-start | bytes 1769480 | tf_op jit(solution)/shard_map/ppermute | solution.py:30
  38.7 8.1 %copy-start.2 = (f32[8,192,192]{2,1,0:T(8,128)S(1)}, f32[8,192,192]{2,1,0:T(8,128)}, u32[]{:S(2)}) copy-start(f32[8,192,192]{2,1,0:T(8,128)} %shard_map.96) | copy-start | bytes 3538948
  40.9 11.3 %collective-permute-start.2 = (f32[4,192,192]{2,1,0:T(8,128)}, f32[4,192,192]{2,1,0:T(8,128)}, u32[]{:S(2)}, u32[]{:S(2)}) collective-permute-start(f32[4,192,192]{2,1,0:T(8,128)} %slice.27), channel_id=1, source_target_pairs={{0,8},{8,0},{16,24},{24,16},{1,17},{9,25},{17,1},{25,9},{2,10},{10... | collective-permute-start | bytes 1769480 | tf_op jit(solution)/shard_map/ppermute | solution.py:30
  42.1 10.1 %copy-start.3 = (f32[8,192,192]{2,1,0:T(8,128)S(1)}, f32[8,192,192]{2,1,0:T(8,128)}, u32[]{:S(2)}) copy-start(f32[8,192,192]{2,1,0:T(8,128)} %shard_map.95) | copy-start | bytes 3538948
  48.0 10.6 %collective-permute-start.7 = (f32[2,192,192]{2,1,0:T(8,128)S(1)}, f32[2,192,192]{2,1,0:T(8,128)S(1)}, u32[]{:S(2)}, u32[]{:S(2)}) collective-permute-start(f32[2,192,192]{2,1,0:T(8,128)S(1)} %constant_dynamic-slice_fusion), channel_id=1, source_target_pairs={{0,8},{8,0},{16,24},{24,16},{1,17},{9,25},{17,1},{25,9},{2,10},{10... | collective-permute-start | bytes 884744 | tf_op jit(solution)/shard_map/ppermute | solution.py:30
  53.5 10.4 %collective-permute-start.3 = (f32[2,192,192]{2,1,0:T(8,128)S(1)}, f32[2,192,192]{2,1,0:T(8,128)S(1)}, u32[]{:S(2)}, u32[]{:S(2)}) collective-permute-start(f32[2,192,192]{2,1,0:T(8,128)S(1)} %constant_dynamic-slice_fusion.1), channel_id=1, source_target_pairs={{0,16},{8,24},{16,0},{24,8},{1,9},{9,1},{17,25},{25,17},{2,18},{10... | collective-permute-start | bytes 884744 | tf_op jit(solution)/shard_map/ppermute | solution.py:30
  58.8 8.2 %collective-permute-start.8 = (f32[2,192,192]{2,1,0:T(8,128)S(1)}, f32[2,192,192]{2,1,0:T(8,128)S(1)}, u32[]{:S(2)}, u32[]{:S(2)}) collective-permute-start(f32[2,192,192]{2,1,0:T(8,128)S(1)} %get-tuple-element.5), channel_id=1, source_target_pairs={{0,8},{8,0},{16,24},{24,16},{1,17},{9,25},{17,1},{25,9},{2,10},{10... | collective-permute-start | bytes 884744 | tf_op jit(solution)/shard_map/ppermute | solution.py:30
  64.0 7.0 %collective-permute-start.4 = (f32[2,192,192]{2,1,0:T(8,128)S(1)}, f32[2,192,192]{2,1,0:T(8,128)S(1)}, u32[]{:S(2)}, u32[]{:S(2)}) collective-permute-start(f32[2,192,192]{2,1,0:T(8,128)S(1)} %get-tuple-element.3), channel_id=1, source_target_pairs={{0,16},{8,24},{16,0},{24,8},{1,9},{9,1},{17,25},{25,17},{2,18},{10... | collective-permute-start | bytes 884744 | tf_op jit(solution)/shard_map/ppermute | solution.py:30
  67.0 18.1 %collective-permute-start.9 = (f32[4,192,192]{2,1,0:T(8,128)S(1)}, f32[4,192,192]{2,1,0:T(8,128)S(1)}, u32[]{:S(2)}, u32[]{:S(2)}) collective-permute-start(f32[4,192,192]{2,1,0:T(8,128)S(1)} %constant_dynamic-update-slice_fusion.2), channel_id=1, source_target_pairs={{0,16},{8,24},{16,0},{24,8},{1,9},{9,1},{17,25},{25,17},{2,18},{10... | collective-permute-start | bytes 1769480 | tf_op jit(solution)/shard_map/ppermute | solution.py:30
  71.0 15.8 %collective-permute-start.5 = (f32[4,192,192]{2,1,0:T(8,128)S(1)}, f32[4,192,192]{2,1,0:T(8,128)S(1)}, u32[]{:S(2)}, u32[]{:S(2)}) collective-permute-start(f32[4,192,192]{2,1,0:T(8,128)S(1)} %constant_dynamic-update-slice_fusion.6), channel_id=1, source_target_pairs={{0,8},{8,0},{16,24},{24,16},{1,17},{9,25},{17,1},{25,9},{2,10},{10... | collective-permute-start | bytes 1769480 | tf_op jit(solution)/shard_map/ppermute | solution.py:30
  72.8 14.1 %copy-start.7 = (f32[16,192]{1,0:T(8,128)S(1)}, f32[16,192]{1,0:T(8,128)}, u32[]{:S(2)}) copy-start(f32[16,192]{1,0:T(8,128)} %param.12) | copy-start | bytes 36868
  86.9 14.0 %copy-start.9 = (s32[16,2]{0,1:T(2,128)S(1)}, s32[16,2]{0,1:T(2,128)}, u32[]{:S(2)}) copy-start(s32[16,2]{0,1:T(2,128)} %param.14) | copy-start | bytes 388
  86.9 14.7 %copy-start.8 = (f32[16,2]{0,1:T(2,128)S(1)}, f32[16,2]{0,1:T(2,128)}, u32[]{:S(2)}) copy-start(f32[16,2]{0,1:T(2,128)} %param.15) | copy-start | bytes 388
  89.0 45.3 %copy-start = (f32[16,192,192]{2,1,0:T(8,128)}, f32[16,192,192]{2,1,0:T(8,128)S(1)}, u32[]{:S(2)}) copy-start(f32[16,192,192]{2,1,0:T(8,128)S(1)} %get-tuple-element.7.refs_1_.refs_7_) | copy-start | bytes 7077892
  89.0 44.2 %collective-permute-start.11 = (f32[16,192,192]{2,1,0:T(8,128)S(1)}, f32[16,192,192]{2,1,0:T(8,128)}, u32[]{:S(2)}, u32[]{:S(2)}) collective-permute-start(f32[16,192,192]{2,1,0:T(8,128)S(1)} %get-tuple-element.7.refs_1_.refs_7_), channel_id=1, source_target_pairs={{1,0},{2,1},{3,2},{4,3},{5,4},{6,5},{7,6},{9,8},{10,9},{11,10},{12... | collective-permute-start | bytes 7077896 | tf_op jit(solution)/shard_map/ppermute | solution.py:19
  92.3 42.0 %collective-permute-start.10 = (f32[16,192,192]{2,1,0:T(8,128)S(1)}, f32[16,192,192]{2,1,0:T(8,128)}, u32[]{:S(2)}, u32[]{:S(2)}) collective-permute-start(f32[16,192,192]{2,1,0:T(8,128)S(1)} %get-tuple-element.7.refs_1_.refs_7_), channel_id=1, source_target_pairs={{0,1},{1,2},{2,3},{3,4},{4,5},{5,6},{6,7},{8,9},{9,10},{10,11},{11... | collective-permute-start | bytes 7077896 | tf_op jit(solution)/shard_map/ppermute | solution.py:18
  142.7 21.8 %copy-start.1 = (f32[8,192,192]{2,1,0:T(8,128)S(1)}, f32[8,192,192]{2,1,0:T(8,128)}, u32[]{:S(2)}) copy-start(f32[8,192,192]{2,1,0:T(8,128)} %shard_map.97.refs_2_) | copy-start | bytes 3538948
  142.7 25.2 %collective-permute-start.14 = (f32[8,192,192]{2,1,0:T(8,128)}, f32[8,192,192]{2,1,0:T(8,128)S(1)}, u32[]{:S(2)}, u32[]{:S(2)}) collective-permute-start(f32[8,192,192]{2,1,0:T(8,128)} %shard_map.97.refs_2_), channel_id=1, source_target_pairs={{1,0},{2,1},{3,2},{4,3},{5,4},{6,5},{7,6},{9,8},{10,9},{11,10},{12... | collective-permute-start | bytes 3538952 | tf_op jit(solution)/shard_map/ppermute | solution.py:19
  144.8 23.2 %collective-permute-start.12 = (f32[8,192,192]{2,1,0:T(8,128)}, f32[8,192,192]{2,1,0:T(8,128)}, u32[]{:S(2)}, u32[]{:S(2)}) collective-permute-start(f32[8,192,192]{2,1,0:T(8,128)} %shard_map.97.refs_2_), channel_id=1, source_target_pairs={{0,1},{1,2},{2,3},{3,4},{4,5},{5,6},{6,7},{8,9},{9,10},{10,11},{11... | collective-permute-start | bytes 3538952 | tf_op jit(solution)/shard_map/ppermute | solution.py:18
  158.7 24.1 %collective-permute-start.15 = (f32[8,192,192]{2,1,0:T(8,128)}, f32[8,192,192]{2,1,0:T(8,128)}, u32[]{:S(2)}, u32[]{:S(2)}) collective-permute-start(f32[8,192,192]{2,1,0:T(8,128)} %shard_map.98.refs_3_), channel_id=1, source_target_pairs={{1,0},{2,1},{3,2},{4,3},{5,4},{6,5},{7,6},{9,8},{10,9},{11,10},{12... | collective-permute-start | bytes 3538952 | tf_op jit(solution)/shard_map/ppermute | solution.py:19
  160.6 23.4 %collective-permute-start.13 = (f32[8,192,192]{2,1,0:T(8,128)}, f32[8,192,192]{2,1,0:T(8,128)}, u32[]{:S(2)}, u32[]{:S(2)}) collective-permute-start(f32[8,192,192]{2,1,0:T(8,128)} %shard_map.98.refs_3_), channel_id=1, source_target_pairs={{0,1},{1,2},{2,3},{3,4},{4,5},{5,6},{6,7},{8,9},{9,10},{10,11},{11... | collective-permute-start | bytes 3538952 | tf_op jit(solution)/shard_map/ppermute | solution.py:18
  167.9 16.1 %copy-start.6 = (f32[8,192,192]{2,1,0:T(8,128)}, f32[8,192,192]{2,1,0:T(8,128)S(1)}, u32[]{:S(2)}) copy-start(f32[8,192,192]{2,1,0:T(8,128)S(1)} %collective-permute-done.14.refs_4_) | copy-start | bytes 3538948

commit v17 on v16

--- a/solution.py
+++ b/solution.py
@@ -35,9 +35,9 @@
     for step, (bit_even, bit_odd) in enumerate(steps):
         bit = jnp.where(parity == 0, bit_even, bit_odd)
         side = (index // bit) % 2
-        half = piece.shape[0] // 2
+        half = piece[0].shape[0] if presplit and step == 0 else piece.shape[0] // 2
         if presplit and step == 0:
-            keep, send = piece[half:], piece[:half]
+            send, keep = piece
         else:
             keep = lax.dynamic_slice_in_dim(piece, side * half, half, axis=0)
             send = lax.dynamic_slice_in_dim(piece, (1 - side) * half, half, axis=0)
@@ -68,8 +68,9 @@
 
 
 def sum_over_aux(halves, presplit):
-    if not halving_ready(halves[0].shape[0]):
-        return lax.psum(jnp.concatenate(halves, axis=0), "aux")
+    if not presplit:
+        if not halving_ready(halves[0].shape[0]):
+            return lax.psum(jnp.concatenate(halves, axis=0), "aux")
     index = lax.axis_index("aux")
     parity = lax.axis_index("pair") % 2
     first = halving_stream(halves[0], index, parity, STREAM_ORDERS[0], presplit)
@@ -99,9 +100,12 @@
             pltpu.make_async_copy(src.at[row], dst, sem).start()
 
 
-def exchange_kernel(
-    lead_ref, trail_ref, size_ref, flip_ref, t_left, t_own, t_right, coef_ref, out_ref, lbuf, tbuf, sems, *, occ, group, start
-):
+def exchange_kernel(lead_ref, trail_ref, size_ref, flip_ref, *refs, occ, group, start, split):
+    if split:
+        t_left, t_own, t_right, coef_ref, send_ref, keep_ref, lbuf, tbuf, sems, res_ref = refs
+    else:
+        t_left, t_own, t_right, coef_ref, res_ref, lbuf, tbuf, sems = refs
+    out_ref = res_ref
     i = pl.program_id(0)
     steps = pl.num_programs(0)
     sources = (t_left, t_own, t_right)
@@ -140,6 +144,15 @@
                     left_t.astype(jnp.bfloat16), right.astype(jnp.bfloat16), preferred_element_type=jnp.float32
                 )
 
+    if split:
+        @pl.when((i + flip_ref[0]) % 2 == 0)
+        def _():
+            send_ref[...] = res_ref[...]
+
+        @pl.when((i + flip_ref[0]) % 2 == 1)
+        def _():
+            keep_ref[...] = res_ref[...]
+
 
 def partial_exchange(lead, trail, sizes, sources, coef_t, start=0, count=None, flip=None):
     pairs = coef_t.shape[0]
@@ -147,10 +160,25 @@
     group = next(g for g in (4, 2, 1) if count % g == 0 and start % g == 0)
     base = start // group
     steps = count // group
-    if flip is None or steps != 2:
+    split = flip is not None and steps == 2
+    if not split:
         flip = jnp.zeros((1,), jnp.int32)
     occ, nfit, npao = sources[1].shape
     hbm = pl.BlockSpec(memory_space=pl.ANY)
+    scratch = [
+        pltpu.VMEM((2, group, nfit, npao), sources[1].dtype),
+        pltpu.VMEM((2, group, nfit, npao), sources[1].dtype),
+        pltpu.SemaphoreType.DMA((2, 2, group)),
+    ]
+    block = (group, NPNO, NPNO)
+    if split:
+        fixed = pl.BlockSpec(block, lambda i, a, b, s, f: (0, 0, 0))
+        out_specs = [fixed, fixed]
+        out_shape = [jax.ShapeDtypeStruct(block, jnp.float32)] * 2
+        scratch.append(pltpu.VMEM(block, jnp.float32))
+    else:
+        out_specs = pl.BlockSpec(block, lambda i, a, b, s, f: (i, 0, 0))
+        out_shape = jax.ShapeDtypeStruct((count, NPNO, NPNO), jnp.float32)
     grid_spec = pltpu.PrefetchScalarGridSpec(
         num_scalar_prefetch=4,
         grid=(steps,),
@@ -160,18 +188,14 @@
             hbm,
             pl.BlockSpec((group, 2, NPNO, npao), lambda i, a, b, s, f: (i + base, 0, 0, 0)),
         ],
-        out_specs=pl.BlockSpec((group, NPNO, NPNO), lambda i, a, b, s, f: ((i + f[0]) % steps, 0, 0)),
-        scratch_shapes=[
-            pltpu.VMEM((2, group, nfit, npao), sources[1].dtype),
-            pltpu.VMEM((2, group, nfit, npao), sources[1].dtype),
-            pltpu.SemaphoreType.DMA((2, 2, group)),
-        ],
+        out_specs=out_specs,
+        scratch_shapes=scratch,
     )
     flops = count * (2 * 2 * nfit * npao * NPNO + 2 * nfit * NPNO * NPNO)
     return pl.pallas_call(
-        functools.partial(exchange_kernel, occ=occ, group=group, start=start),
+        functools.partial(exchange_kernel, occ=occ, group=group, start=start, split=split),
         grid_spec=grid_spec,
-        out_shape=jax.ShapeDtypeStruct((count, NPNO, NPNO), jnp.float32),
+        out_shape=out_shape,
         cost_estimate=pl.CostEstimate(
             flops=flops,
             bytes_accessed=count * (2 * nfit * npao * 2 + 2 * npao * NPNO * 2 + NPNO * NPNO * 4),

time: 199 us -> 195 us (0.980)
  local copies, waits for them, and re-layouts: 8.83 us -> 5.43 us
    slice x2 -> x0, local copies, waits for them, and re-layouts: 3.38 us -> none  [halving_stream(): keep, send = (piece[half:], piece[:half])]
    ppermute x8, starting transfers between devices: 8.59 us -> 11.8 us  [swap_over_aux(): return lax.ppermute(value, ('aux', 'pair'), perm)]
    ppermute x4, starting transfers between devices: 21.1 us -> 18.7 us  [halo_sources(): from_left = lax.ppermute(cells, axis, [(i, i + 1) for i in range(ends)])]
  transfers between devices with their start and end apart: 16 -> 16, of which waited for: 14 -> 11; matrix products, arithmetic and copies ran while one was open for 8% -> 6% of each run, Pallas kernels for 9% -> 9%
where the time goes in v17:
time: 195 us; the launch traced here: 193 us
  waiting for transfers between devices  91.5 us (47%)
  Pallas kernels  46.7 us (24%)
  starting transfers between devices  39.2 us (20%)
  other arithmetic  9.37 us (5%)
  local copies, waits for them, and re-layouts  5.43 us (3%)
    ppermute x4, waiting for transfers between devices, halo_sources(): from_right = lax.ppermute(cells, axis, [(i + 1, i) for i in range(ends)])  52.9 us
    ppermute x8, waiting for transfers between devices, swap_over_aux(): return lax.ppermute(value, ('aux', 'pair'), perm)  35.1 us
    pallas_call x3, Pallas kernels, coupling_step(): pl.pallas_call(kernel, grid_spec=grid_spec, out_shape=jax.ShapeDtypeStruc...  30.1 us
    ppermute x4, starting transfers between devices, halo_sources(): from_left = lax.ppermute(cells, axis, [(i, i + 1) for i in range(ends)])  18.7 us
    pallas_call x2, Pallas kernels, partial_exchange(): pl.pallas_call(functools.partial(exchange_kernel, occ=occ, group=group, s...  16.6 us
    ppermute x8, starting transfers between devices, swap_over_aux(): return lax.ppermute(value, ('aux', 'pair'), perm)  11.8 us
    ppermute x4, starting transfers between devices, halo_sources(): from_right = lax.ppermute(cells, axis, [(i + 1, i) for i in range(ends)])  8.68 us
  transfers between devices with their start and end apart: 16, of which 11 were waited for; matrix products, arithmetic and copies ran while one was open for 6% of the time, Pallas kernels for 9%

profile of v17, /device:TPU:1, one launch (start us, length us, event | category | flops | bytes accessed | tf_op | source)
XLA Modules:
  0.0 193.4 jit_solution(11734453434314781457)
XLA Ops:
  0.6 2.0 %collective-permute-start.1 = (bf16[4,512,256]{2,1,0:T(8,128)(2,1)}, bf16[4,512,256]{2,1,0:T(8,128)(2,1)S(1)}, u32[]{:S(2)}, u32[]{:S(2)}) collective-permute-start(bf16[4,512,256]{2,1,0:T(8,128)(2,1)} %refs_1_.3), channel_id=1, source_target_pairs={{1,0},{2,1},{3,2},{4,3},{5,4},{6,5},{7,6},{9,8},{10,9},{11,10},{12... | collective-permute-start | bytes 3145736 | tf_op jit(solution)/shard_map/ppermute | solution.py:19
  2.6 4.6 %collective-permute-start = (bf16[4,512,256]{2,1,0:T(8,128)(2,1)}, bf16[4,512,256]{2,1,0:T(8,128)(2,1)S(1)}, u32[]{:S(2)}, u32[]{:S(2)}) collective-permute-start(bf16[4,512,256]{2,1,0:T(8,128)(2,1)} %refs_1_.3), channel_id=1, source_target_pairs={{0,1},{1,2},{2,3},{3,4},{4,5},{5,6},{6,7},{8,9},{9,10},{10,11},{11... | collective-permute-start | bytes 3145736 | tf_op jit(solution)/shard_map/ppermute | solution.py:18
  7.2 1.2 compare_select_fusion.2.size_ref
  8.4 0.7 broadcast_subtract_fusion
  9.1 0.6 slice_bitcast_fusion
  9.7 8.2 %collective-permute-done.1.refs_2_ = bf16[4,512,256]{2,1,0:T(8,128)(2,1)S(1)} collective-permute-done((bf16[4,512,256]{2,1,0:T(8,128)(2,1)}, bf16[4,512,256]{2,1,0:T(8,128)(2,1)S(1)}, u32[]{:S(2)}, u32[]{:S(2)}) %collective-permute-start.1) | collective-permute-done | bytes 1048608 | tf_op jit(solution)/shard_map/ppermute | solution.py:19
  17.9 1.3 collective-permute-done.refs_0_
  19.2 1.0 copy-done.3
  20.2 8.2 %shard_map.96 = (f32[4,192,192]{2,1,0:T(8,128)}, f32[4,192,192]{2,1,0:T(8,128)}) custom-call(s32[16]{0:T(128)} %get-tuple-element.17.lead_ref, s32[16]{0:T(128)} %get-tuple-element.16.trail_ref, s32[16]{0:T(128)} %compare_select_fusion.2.size_ref, s32[1]{0:T(128)} %bitcast.4.flip_ref, bf16[4,512,256]{2,1,0:T(8,128)(2,1)} %copy-done.3, ...), custom_call_target="tpu_custom_call" | custom-call | flops 1107296256 | bytes 6946816 | tf_op jit(solution)/shard_map/pallas_call | solution.py:195
  28.4 1.3 collective-permute-start.6
  29.7 8.4 %shard_map.95 = (f32[4,192,192]{2,1,0:T(8,128)}, f32[4,192,192]{2,1,0:T(8,128)}) custom-call(s32[16]{0:T(128)} %get-tuple-element.17.lead_ref, s32[16]{0:T(128)} %get-tuple-element.16.trail_ref, s32[16]{0:T(128)} %compare_select_fusion.2.size_ref, s32[1]{0:T(128)} %bitcast.2.flip_ref, bf16[4,512,256]{2,1,0:T(8,128)(2,1)} %copy-done.3, ...), custom_call_target="tpu_custom_call" | custom-call | flops 1107296256 | bytes 6946816 | tf_op jit(solution)/shard_map/pallas_call | solution.py:195
  38.1 1.3 collective-permute-start.2
  39.4 7.9 %collective-permute-done.6 = f32[4,192,192]{2,1,0:T(8,128)S(1)} collective-permute-done((f32[4,192,192]{2,1,0:T(8,128)}, f32[4,192,192]{2,1,0:T(8,128)S(1)}, u32[]{:S(2)}, u32[]{:S(2)}) %collective-permute-start.6) | collective-permute-done | bytes 589856 | tf_op jit(solution)/shard_map/ppermute | solution.py:30
  47.3 0.1 add.85
  47.5 2.1 %collective-permute-start.7 = (f32[2,192,192]{2,1,0:T(8,128)S(1)}, f32[2,192,192]{2,1,0:T(8,128)S(1)}, u32[]{:S(2)}, u32[]{:S(2)}) collective-permute-start(f32[2,192,192]{2,1,0:T(8,128)S(1)} %constant_dynamic-slice_fusion), channel_id=1, source_target_pairs={{0,8},{8,0},{16,24},{24,16},{1,17},{9,25},{17,1},{25,9},{2,10},{10... | collective-permute-start | bytes 884744 | tf_op jit(solution)/shard_map/ppermute | solution.py:30
  49.6 1.2 add.78
  50.9 1.5 collective-permute-start.3
  52.4 4.7 %collective-permute-done.7 = f32[2,192,192]{2,1,0:T(8,128)S(1)} collective-permute-done((f32[2,192,192]{2,1,0:T(8,128)S(1)}, f32[2,192,192]{2,1,0:T(8,128)S(1)}, u32[]{:S(2)}, u32[]{:S(2)}) %collective-permute-start.7) | collective-permute-done | bytes 294944 | tf_op jit(solution)/shard_map/ppermute | solution.py:30
  57.2 2.3 %collective-permute-start.8 = (f32[2,192,192]{2,1,0:T(8,128)S(1)}, f32[2,192,192]{2,1,0:T(8,128)S(1)}, u32[]{:S(2)}, u32[]{:S(2)}) collective-permute-start(f32[2,192,192]{2,1,0:T(8,128)S(1)} %get-tuple-element.13), channel_id=1, source_target_pairs={{0,8},{8,0},{16,24},{24,16},{1,17},{9,25},{17,1},{25,9},{2,10},{10... | collective-permute-start | bytes 884744 | tf_op jit(solution)/shard_map/ppermute | solution.py:30
  59.7 1.6 collective-permute-start.4
  61.3 5.6 %collective-permute-done.8 = f32[2,192,192]{2,1,0:T(8,128)S(1)} collective-permute-done((f32[2,192,192]{2,1,0:T(8,128)S(1)}, f32[2,192,192]{2,1,0:T(8,128)S(1)}, u32[]{:S(2)}, u32[]{:S(2)}) %collective-permute-start.8) | collective-permute-done | bytes 294944 | tf_op jit(solution)/shard_map/ppermute | solution.py:30
  66.9 0.2 collective-permute-start.9
  67.1 1.5 collective-permute-start.5
  68.7 0.1 broadcast.29.clone
  68.9 0.1 broadcast.29.clone.1
  69.1 14.1 %collective-permute-done.9 = f32[4,192,192]{2,1,0:T(8,128)S(1)} collective-permute-done((f32[4,192,192]{2,1,0:T(8,128)S(1)}, f32[4,192,192]{2,1,0:T(8,128)S(1)}, u32[]{:S(2)}, u32[]{:S(2)}) %collective-permute-start.9) | collective-permute-done | bytes 589856 | tf_op jit(solution)/shard_map/ppermute | solution.py:30
  83.3 2.8 %collective-permute-done.5 = f32[4,192,192]{2,1,0:T(8,128)S(1)} collective-permute-done((f32[4,192,192]{2,1,0:T(8,128)S(1)}, f32[4,192,192]{2,1,0:T(8,128)S(1)}, u32[]{:S(2)}, u32[]{:S(2)}) %collective-permute-start.5) | collective-permute-done | bytes 589856 | tf_op jit(solution)/shard_map/ppermute | solution.py:30
  86.2 2.0 %pad_maximum_fusion = (f32[16,192,192]{2,1,0:T(8,128)}, f32[16,192,192]{2,1,0:T(8,128)S(1)}) fusion(f32[8,192,192]{2,1,0:T(8,128)S(1)} %constant_dynamic-update-slice_fusion, f32[8,192,192]{2,1,0:T(8,128)S(1)} %constant_dynamic-update-slice_fusion.4, f32[16,192]{1,0:T(8,128)S(1)} %copy-done.7), kind=kLoop, calls=%fused_computation | loop fusion | flops 2359296 | bytes 7090176 | tf_op jit(solution)/shard_map/concatenate | solution.py:78
  88.2 2.7 %collective-permute-start.11 = (f32[16,192,192]{2,1,0:T(8,128)S(1)}, f32[16,192,192]{2,1,0:T(8,128)}, u32[]{:S(2)}, u32[]{:S(2)}) collective-permute-start(f32[16,192,192]{2,1,0:T(8,128)S(1)} %get-tuple-element.15.refs_1_.refs_7_), channel_id=1, source_target_pairs={{1,0},{2,1},{3,2},{4,3},{5,4},{6,5},{7,6},{9,8},{10,9},{11,10},{12... | collective-permute-start | bytes 7077896 | tf_op jit(solution)/shard_map/ppermute | solution.py:19
  90.9 5.8 %collective-permute-start.10 = (f32[16,192,192]{2,1,0:T(8,128)S(1)}, f32[16,192,192]{2,1,0:T(8,128)}, u32[]{:S(2)}, u32[]{:S(2)}) collective-permute-start(f32[16,192,192]{2,1,0:T(8,128)S(1)} %get-tuple-element.15.refs_1_.refs_7_), channel_id=1, source_target_pairs={{0,1},{1,2},{2,3},{3,4},{4,5},{5,6},{6,7},{8,9},{9,10},{10,11},{11... | collective-permute-start | bytes 7077896 | tf_op jit(solution)/shard_map/ppermute | solution.py:18
  96.8 0.6 broadcast_in_dim.26.refs_6_.refs_9_
  97.4 0.1 copy.12
  97.5 0.6 reshape.26.nb_ref
  98.1 0.1 copy.13
  98.2 0.6 reshape.27.fock_ref
  98.8 1.7 copy.14.refs_5_.refs_8_
  100.4 29.3 %collective-permute-done.11.refs_2_ = f32[16,192,192]{2,1,0:T(8,128)} collective-permute-done((f32[16,192,192]{2,1,0:T(8,128)S(1)}, f32[16,192,192]{2,1,0:T(8,128)}, u32[]{:S(2)}, u32[]{:S(2)}) %collective-permute-start.11) | collective-permute-done | bytes 2359328 | tf_op jit(solution)/shard_map/ppermute | solution.py:19
  129.7 1.1 collective-permute-done.10.refs_0_
  130.8 8.5 %shard_map.97.refs_2_ = f32[8,192,192]{2,1,0:T(8,128)} custom-call(s32[32]{0:T(128)} %reshape.26.nb_ref, s32[16]{0:T(128)} %compare_select_fusion.2.size_ref, f32[32]{0:T(128)} %reshape.27.fock_ref, f32[16,192,192]{2,1,0:T(8,128)} %collective-permute-done.10.refs_0_, f32[16,192,192]{2,1,0:T(8,128)} %copy-done, ...), custom_call_target="tpu_custom_call" | custom-call | flops 905969664 | bytes 7077888 | tf_op jit(solution)/shard_map/pallas_call | solution.py:297
  139.3 2.1 %collective-permute-start.14 = (f32[8,192,192]{2,1,0:T(8,128)}, f32[8,192,192]{2,1,0:T(8,128)S(1)}, u32[]{:S(2)}, u32[]{:S(2)}) collective-permute-start(f32[8,192,192]{2,1,0:T(8,128)} %shard_map.97.refs_2_), channel_id=1, source_target_pairs={{1,0},{2,1},{3,2},{4,3},{5,4},{6,5},{7,6},{9,8},{10,9},{11,10},{12... | collective-permute-start | bytes 3538952 | tf_op jit(solution)/shard_map/ppermute | solution.py:19
  141.4 4.5 %collective-permute-start.12 = (f32[8,192,192]{2,1,0:T(8,128)}, f32[8,192,192]{2,1,0:T(8,128)}, u32[]{:S(2)}, u32[]{:S(2)}) collective-permute-start(f32[8,192,192]{2,1,0:T(8,128)} %shard_map.97.refs_2_), channel_id=1, source_target_pairs={{0,1},{1,2},{2,3},{3,4},{4,5},{5,6},{6,7},{8,9},{9,10},{10,11},{11... | collective-permute-start | bytes 3538952 | tf_op jit(solution)/shard_map/ppermute | solution.py:18
  145.9 8.7 %shard_map.98.refs_3_ = f32[8,192,192]{2,1,0:T(8,128)} custom-call(s32[32]{0:T(128)} %reshape.26.nb_ref, s32[16]{0:T(128)} %compare_select_fusion.2.size_ref, f32[32]{0:T(128)} %reshape.27.fock_ref, f32[16,192,192]{2,1,0:T(8,128)} %collective-permute-done.10.refs_0_, f32[16,192,192]{2,1,0:T(8,128)} %copy-done, ...), custom_call_target="tpu_custom_call" | custom-call | flops 905969664 | bytes 7077888 | tf_op jit(solution)/shard_map/pallas_call | solution.py:297
  154.6 1.9 collective-permute-start.15
  156.5 3.9 %collective-permute-start.13 = (f32[8,192,192]{2,1,0:T(8,128)}, f32[8,192,192]{2,1,0:T(8,128)}, u32[]{:S(2)}, u32[]{:S(2)}) collective-permute-start(f32[8,192,192]{2,1,0:T(8,128)} %shard_map.98.refs_3_), channel_id=1, source_target_pairs={{0,1},{1,2},{2,3},{3,4},{4,5},{5,6},{6,7},{8,9},{9,10},{10,11},{11... | collective-permute-start | bytes 3538952 | tf_op jit(solution)/shard_map/ppermute | solution.py:18
  160.4 3.4 %pad_maximum_fusion.1.refs_10_ = f32[16,192,192]{2,1,0:T(8,128)} fusion(f32[8,192,192]{2,1,0:T(8,128)} %shard_map.98.refs_3_, f32[8,192,192]{2,1,0:T(8,128)S(1)} %copy-done.1), kind=kLoop, calls=%fused_computation.1 | loop fusion | flops 589824 | bytes 4718592 | tf_op jit(solution)/shard_map/concatenate | solution.py:363
  163.8 15.4 %collective-permute-done.15.refs_5_ = f32[8,192,192]{2,1,0:T(8,128)} collective-permute-done((f32[8,192,192]{2,1,0:T(8,128)}, f32[8,192,192]{2,1,0:T(8,128)}, u32[]{:S(2)}, u32[]{:S(2)}) %collective-permute-start.15) | collective-permute-done | bytes 1179680 | tf_op jit(solution)/shard_map/ppermute | solution.py:19
  179.2 1.2 collective-permute-done.13.refs_1_
  180.4 12.9 %shard_map.99 = f32[16,192,192]{2,1,0:T(8,128)} custom-call(s32[32]{0:T(128)} %reshape.26.nb_ref, s32[16]{0:T(128)} %compare_select_fusion.2.size_ref, f32[32]{0:T(128)} %reshape.27.fock_ref, f32[8,192,192]{2,1,0:T(8,128)} %collective-permute-done.12.refs_0_, f32[8,192,192]{2,1,0:T(8,128)} %collective-permute-done.13.refs_1_, ...), custom_call_target="tpu_custom_call" | custom-call | flops 1811939328 | bytes 14155776 | tf_op jit(solution)/shard_map/pallas_call | solution.py:297
  (37 shorter events, 0.7 us)
Async XLA Ops:
  0.6 17.3 %collective-permute-start.1 = (bf16[4,512,256]{2,1,0:T(8,128)(2,1)}, bf16[4,512,256]{2,1,0:T(8,128)(2,1)S(1)}, u32[]{:S(2)}, u32[]{:S(2)}) collective-permute-start(bf16[4,512,256]{2,1,0:T(8,128)(2,1)} %refs_1_.3), channel_id=1, source_target_pairs={{1,0},{2,1},{3,2},{4,3},{5,4},{6,5},{7,6},{9,8},{10,9},{11,10},{12... | collective-permute-start | bytes 3145736 | tf_op jit(solution)/shard_map/ppermute | solution.py:19
  2.6 16.6 %collective-permute-start = (bf16[4,512,256]{2,1,0:T(8,128)(2,1)}, bf16[4,512,256]{2,1,0:T(8,128)(2,1)S(1)}, u32[]{:S(2)}, u32[]{:S(2)}) collective-permute-start(bf16[4,512,256]{2,1,0:T(8,128)(2,1)} %refs_1_.3), channel_id=1, source_target_pairs={{0,1},{1,2},{2,3},{3,4},{4,5},{5,6},{6,7},{8,9},{9,10},{10,11},{11... | collective-permute-start | bytes 3145736 | tf_op jit(solution)/shard_map/ppermute | solution.py:18
  17.9 1.3 copy-start.2
  19.2 1.0 copy-start.3
  28.4 18.9 %collective-permute-start.6 = (f32[4,192,192]{2,1,0:T(8,128)}, f32[4,192,192]{2,1,0:T(8,128)S(1)}, u32[]{:S(2)}, u32[]{:S(2)}) collective-permute-start(f32[4,192,192]{2,1,0:T(8,128)} %get-tuple-element.9), channel_id=1, source_target_pairs={{0,16},{8,24},{16,0},{24,8},{1,9},{9,1},{17,25},{25,17},{2,18},{10... | collective-permute-start | bytes 1769480 | tf_op jit(solution)/shard_map/ppermute | solution.py:30
  29.7 17.6 %copy-start.5 = (f32[4,192,192]{2,1,0:T(8,128)S(1)}, f32[4,192,192]{2,1,0:T(8,128)}, u32[]{:S(2)}) copy-start(f32[4,192,192]{2,1,0:T(8,128)} %get-tuple-element.8) | copy-start | bytes 1769476
  38.1 11.5 %collective-permute-start.2 = (f32[4,192,192]{2,1,0:T(8,128)}, f32[4,192,192]{2,1,0:T(8,128)}, u32[]{:S(2)}, u32[]{:S(2)}) collective-permute-start(f32[4,192,192]{2,1,0:T(8,128)} %get-tuple-element.7), channel_id=1, source_target_pairs={{0,8},{8,0},{16,24},{24,16},{1,17},{9,25},{17,1},{25,9},{2,10},{10... | collective-permute-start | bytes 1769480 | tf_op jit(solution)/shard_map/ppermute | solution.py:30
  47.3 2.3 %copy-start.6 = (f32[4,192,192]{2,1,0:T(8,128)S(1)}, f32[4,192,192]{2,1,0:T(8,128)}, u32[]{:S(2)}) copy-start(f32[4,192,192]{2,1,0:T(8,128)} %get-tuple-element.6) | copy-start | bytes 1769476
  47.5 9.6 %collective-permute-start.7 = (f32[2,192,192]{2,1,0:T(8,128)S(1)}, f32[2,192,192]{2,1,0:T(8,128)S(1)}, u32[]{:S(2)}, u32[]{:S(2)}) collective-permute-start(f32[2,192,192]{2,1,0:T(8,128)S(1)} %constant_dynamic-slice_fusion), channel_id=1, source_target_pairs={{0,8},{8,0},{16,24},{24,16},{1,17},{9,25},{17,1},{25,9},{2,10},{10... | collective-permute-start | bytes 884744 | tf_op jit(solution)/shard_map/ppermute | solution.py:30
  50.9 8.6 %collective-permute-start.3 = (f32[2,192,192]{2,1,0:T(8,128)S(1)}, f32[2,192,192]{2,1,0:T(8,128)S(1)}, u32[]{:S(2)}, u32[]{:S(2)}) collective-permute-start(f32[2,192,192]{2,1,0:T(8,128)S(1)} %constant_dynamic-slice_fusion.1), channel_id=1, source_target_pairs={{0,16},{8,24},{16,0},{24,8},{1,9},{9,1},{17,25},{25,17},{2,18},{10... | collective-permute-start | bytes 884744 | tf_op jit(solution)/shard_map/ppermute | solution.py:30
  57.2 9.6 %collective-permute-start.8 = (f32[2,192,192]{2,1,0:T(8,128)S(1)}, f32[2,192,192]{2,1,0:T(8,128)S(1)}, u32[]{:S(2)}, u32[]{:S(2)}) collective-permute-start(f32[2,192,192]{2,1,0:T(8,128)S(1)} %get-tuple-element.13), channel_id=1, source_target_pairs={{0,8},{8,0},{16,24},{24,16},{1,17},{9,25},{17,1},{25,9},{2,10},{10... | collective-permute-start | bytes 884744 | tf_op jit(solution)/shard_map/ppermute | solution.py:30
  59.7 7.5 %collective-permute-start.4 = (f32[2,192,192]{2,1,0:T(8,128)S(1)}, f32[2,192,192]{2,1,0:T(8,128)S(1)}, u32[]{:S(2)}, u32[]{:S(2)}) collective-permute-start(f32[2,192,192]{2,1,0:T(8,128)S(1)} %get-tuple-element.11), channel_id=1, source_target_pairs={{0,16},{8,24},{16,0},{24,8},{1,9},{9,1},{17,25},{25,17},{2,18},{10... | collective-permute-start | bytes 884744 | tf_op jit(solution)/shard_map/ppermute | solution.py:30
  66.9 16.3 %collective-permute-start.9 = (f32[4,192,192]{2,1,0:T(8,128)S(1)}, f32[4,192,192]{2,1,0:T(8,128)S(1)}, u32[]{:S(2)}, u32[]{:S(2)}) collective-permute-start(f32[4,192,192]{2,1,0:T(8,128)S(1)} %constant_dynamic-update-slice_fusion.2), channel_id=1, source_target_pairs={{0,16},{8,24},{16,0},{24,8},{1,9},{9,1},{17,25},{25,17},{2,18},{10... | collective-permute-start | bytes 1769480 | tf_op jit(solution)/shard_map/ppermute | solution.py:30
  67.1 18.9 %collective-permute-start.5 = (f32[4,192,192]{2,1,0:T(8,128)S(1)}, f32[4,192,192]{2,1,0:T(8,128)S(1)}, u32[]{:S(2)}, u32[]{:S(2)}) collective-permute-start(f32[4,192,192]{2,1,0:T(8,128)S(1)} %constant_dynamic-update-slice_fusion.6), channel_id=1, source_target_pairs={{0,8},{8,0},{16,24},{24,16},{1,17},{9,25},{17,1},{25,9},{2,10},{10... | collective-permute-start | bytes 1769480 | tf_op jit(solution)/shard_map/ppermute | solution.py:30
  69.1 17.0 %copy-start.7 = (f32[16,192]{1,0:T(8,128)S(1)}, f32[16,192]{1,0:T(8,128)}, u32[]{:S(2)}) copy-start(f32[16,192]{1,0:T(8,128)} %param.12) | copy-start | bytes 36868
  86.1 11.3 %copy-start.9 = (s32[16,2]{0,1:T(2,128)S(1)}, s32[16,2]{0,1:T(2,128)}, u32[]{:S(2)}) copy-start(s32[16,2]{0,1:T(2,128)} %param.14) | copy-start | bytes 388
  86.1 12.0 %copy-start.8 = (f32[16,2]{0,1:T(2,128)S(1)}, f32[16,2]{0,1:T(2,128)}, u32[]{:S(2)}) copy-start(f32[16,2]{0,1:T(2,128)} %param.15) | copy-start | bytes 388
  88.2 42.6 %copy-start = (f32[16,192,192]{2,1,0:T(8,128)}, f32[16,192,192]{2,1,0:T(8,128)S(1)}, u32[]{:S(2)}) copy-start(f32[16,192,192]{2,1,0:T(8,128)S(1)} %get-tuple-element.15.refs_1_.refs_7_) | copy-start | bytes 7077892
  88.2 41.5 %collective-permute-start.11 = (f32[16,192,192]{2,1,0:T(8,128)S(1)}, f32[16,192,192]{2,1,0:T(8,128)}, u32[]{:S(2)}, u32[]{:S(2)}) collective-permute-start(f32[16,192,192]{2,1,0:T(8,128)S(1)} %get-tuple-element.15.refs_1_.refs_7_), channel_id=1, source_target_pairs={{1,0},{2,1},{3,2},{4,3},{5,4},{6,5},{7,6},{9,8},{10,9},{11,10},{12... | collective-permute-start | bytes 7077896 | tf_op jit(solution)/shard_map/ppermute | solution.py:19
  90.9 39.8 %collective-permute-start.10 = (f32[16,192,192]{2,1,0:T(8,128)S(1)}, f32[16,192,192]{2,1,0:T(8,128)}, u32[]{:S(2)}, u32[]{:S(2)}) collective-permute-start(f32[16,192,192]{2,1,0:T(8,128)S(1)} %get-tuple-element.15.refs_1_.refs_7_), channel_id=1, source_target_pairs={{0,1},{1,2},{2,3},{3,4},{4,5},{5,6},{6,7},{8,9},{9,10},{10,11},{11... | collective-permute-start | bytes 7077896 | tf_op jit(solution)/shard_map/ppermute | solution.py:18
  139.3 21.1 %copy-start.1 = (f32[8,192,192]{2,1,0:T(8,128)S(1)}, f32[8,192,192]{2,1,0:T(8,128)}, u32[]{:S(2)}) copy-start(f32[8,192,192]{2,1,0:T(8,128)} %shard_map.97.refs_2_) | copy-start | bytes 3538948
  139.3 24.5 %collective-permute-start.14 = (f32[8,192,192]{2,1,0:T(8,128)}, f32[8,192,192]{2,1,0:T(8,128)S(1)}, u32[]{:S(2)}, u32[]{:S(2)}) collective-permute-start(f32[8,192,192]{2,1,0:T(8,128)} %shard_map.97.refs_2_), channel_id=1, source_target_pairs={{1,0},{2,1},{3,2},{4,3},{5,4},{6,5},{7,6},{9,8},{10,9},{11,10},{12... | collective-permute-start | bytes 3538952 | tf_op jit(solution)/shard_map/ppermute | solution.py:19
  141.4 22.4 %collective-permute-start.12 = (f32[8,192,192]{2,1,0:T(8,128)}, f32[8,192,192]{2,1,0:T(8,128)}, u32[]{:S(2)}, u32[]{:S(2)}) collective-permute-start(f32[8,192,192]{2,1,0:T(8,128)} %shard_map.97.refs_2_), channel_id=1, source_target_pairs={{0,1},{1,2},{2,3},{3,4},{4,5},{5,6},{6,7},{8,9},{9,10},{10,11},{11... | collective-permute-start | bytes 3538952 | tf_op jit(solution)/shard_map/ppermute | solution.py:18
  154.6 24.6 %collective-permute-start.15 = (f32[8,192,192]{2,1,0:T(8,128)}, f32[8,192,192]{2,1,0:T(8,128)}, u32[]{:S(2)}, u32[]{:S(2)}) collective-permute-start(f32[8,192,192]{2,1,0:T(8,128)} %shard_map.98.refs_3_), channel_id=1, source_target_pairs={{1,0},{2,1},{3,2},{4,3},{5,4},{6,5},{7,6},{9,8},{10,9},{11,10},{12... | collective-permute-start | bytes 3538952 | tf_op jit(solution)/shard_map/ppermute | solution.py:19
  156.5 23.9 %collective-permute-start.13 = (f32[8,192,192]{2,1,0:T(8,128)}, f32[8,192,192]{2,1,0:T(8,128)}, u32[]{:S(2)}, u32[]{:S(2)}) collective-permute-start(f32[8,192,192]{2,1,0:T(8,128)} %shard_map.98.refs_3_), channel_id=1, source_target_pairs={{0,1},{1,2},{2,3},{3,4},{4,5},{5,6},{6,7},{8,9},{9,10},{10,11},{11... | collective-permute-start | bytes 3538952 | tf_op jit(solution)/shard_map/ppermute | solution.py:18
  163.8 16.6 %copy-start.4 = (f32[8,192,192]{2,1,0:T(8,128)}, f32[8,192,192]{2,1,0:T(8,128)S(1)}, u32[]{:S(2)}) copy-start(f32[8,192,192]{2,1,0:T(8,128)S(1)} %collective-permute-done.14.refs_4_) | copy-start | bytes 3538948

commit v18 on v17

--- a/solution.py
+++ b/solution.py
@@ -100,11 +100,73 @@
             pltpu.make_async_copy(src.at[row], dst, sem).start()
 
 
+def left_kernel(lead_ref, size_ref, t_own, coef_ref, out_ref, lbuf, sems, *, occ, group):
+    i = pl.program_id(0)
+    steps = pl.num_programs(0)
+
+    def fetch(step, slot):
+        for g in range(group):
+            p = step * group + g
+            pltpu.make_async_copy(t_own.at[lead_ref[p] % occ], lbuf.at[slot, g], sems.at[slot, g]).start()
+
+    @pl.when(i == 0)
+    def _():
+        fetch(0, 0)
+
+    @pl.when(i + 1 < steps)
+    def _():
+        fetch(i + 1, (i + 1) % 2)
+
+    slot = i % 2
+    transposed = (((1,), (1,)), ((), ()))
+    for g in range(group):
+        p = i * group + g
+        pltpu.make_async_copy(t_own.at[0], lbuf.at[slot, g], sems.at[slot, g]).wait()
+        size = size_ref[p]
+        out_ref[g] = jnp.zeros(out_ref.shape[1:], out_ref.dtype)
+        for m in CLASS_SIZES:
+
+            @pl.when(size == m)
+            def _():
+                first = coef_ref[g, 0, :m, :]
+                left_t = lax.dot_general(first, lbuf[slot, g], transposed, preferred_element_type=jnp.float32)
+                out_ref[g, :m, :] = left_t.astype(jnp.bfloat16)
+
+
+def left_halves(lead, sizes, t_own, coef_t):
+    pairs = coef_t.shape[0]
+    group = next(g for g in (4, 2, 1) if pairs % g == 0)
+    occ, nfit, npao = t_own.shape
+    grid_spec = pltpu.PrefetchScalarGridSpec(
+        num_scalar_prefetch=2,
+        grid=(pairs // group,),
+        in_specs=[
+            pl.BlockSpec(memory_space=pl.ANY),
+            pl.BlockSpec((group, 2, NPNO, npao), lambda i, a, s: (i, 0, 0, 0)),
+        ],
+        out_specs=pl.BlockSpec((group, NPNO, nfit), lambda i, a, s: (i, 0, 0)),
+        scratch_shapes=[
+            pltpu.VMEM((2, group, nfit, npao), t_own.dtype),
+            pltpu.SemaphoreType.DMA((2, group)),
+        ],
+    )
+    return pl.pallas_call(
+        functools.partial(left_kernel, occ=occ, group=group),
+        grid_spec=grid_spec,
+        out_shape=jax.ShapeDtypeStruct((pairs, NPNO, nfit), jnp.bfloat16),
+        cost_estimate=pl.CostEstimate(
+            flops=pairs * 2 * nfit * npao * NPNO,
+            bytes_accessed=pairs * (nfit * npao * 2 + 2 * npao * NPNO * 2 + NPNO * nfit * 2),
+            transcendentals=0,
+        ),
+    )(lead, sizes, t_own, coef_t)
+
+
 def exchange_kernel(lead_ref, trail_ref, size_ref, flip_ref, *refs, occ, group, start, split):
     if split:
-        t_left, t_own, t_right, coef_ref, send_ref, keep_ref, lbuf, tbuf, sems, res_ref = refs
+        t_left, t_own, t_right, left_ref, coef_ref, send_ref, keep_ref, tbuf, sems, res_ref = refs
     else:
-        t_left, t_own, t_right, coef_ref, res_ref, lbuf, tbuf, sems = refs
+        t_left, t_own, t_right, left_ref, coef_ref, res_ref, tbuf, sems = refs
     out_ref = res_ref
     i = pl.program_id(0)
     steps = pl.num_programs(0)
@@ -113,8 +175,7 @@
     def fetch(step, slot):
         for g in range(group):
             p = start + step * group + g
-            pltpu.make_async_copy(t_own.at[lead_ref[p] % occ], lbuf.at[slot, g], sems.at[slot, 0, g]).start()
-            fetch_block(sources, occ, trail_ref[p], tbuf.at[slot, g], sems.at[slot, 1, g])
+            fetch_block(sources, occ, trail_ref[p], tbuf.at[slot, g], sems.at[slot, g])
 
     @pl.when(i == 0)
     def _():
@@ -128,20 +189,17 @@
     transposed = (((1,), (1,)), ((), ()))
     for g in range(group):
         p = start + i * group + g
-        pltpu.make_async_copy(t_own.at[0], lbuf.at[slot, g], sems.at[slot, 0, g]).wait()
-        pltpu.make_async_copy(t_own.at[0], tbuf.at[slot, g], sems.at[slot, 1, g]).wait()
+        pltpu.make_async_copy(t_own.at[0], tbuf.at[slot, g], sems.at[slot, g]).wait()
         size = size_ref[p]
         out_ref[g] = jnp.zeros((NPNO, NPNO), jnp.float32)
         for m in CLASS_SIZES:
 
             @pl.when(size == m)
             def _():
-                first = coef_ref[g, 0, :m, :]
                 second = coef_ref[g, 1, :m, :]
-                left_t = lax.dot_general(first, lbuf[slot, g], transposed, preferred_element_type=jnp.float32)
                 right = lax.dot_general(tbuf[slot, g], second, transposed, preferred_element_type=jnp.float32)
                 out_ref[g, :m, :m] = jnp.dot(
-                    left_t.astype(jnp.bfloat16), right.astype(jnp.bfloat16), preferred_element_type=jnp.float32
+                    left_ref[g, :m, :], right.astype(jnp.bfloat16), preferred_element_type=jnp.float32
                 )
 
     if split:
@@ -154,7 +212,7 @@
             keep_ref[...] = res_ref[...]
 
 
-def partial_exchange(lead, trail, sizes, sources, coef_t, start=0, count=None, flip=None):
+def partial_exchange(lead, trail, sizes, sources, left_t, coef_t, start=0, count=None, flip=None):
     pairs = coef_t.shape[0]
     count = pairs if count is None else count
     group = next(g for g in (4, 2, 1) if count % g == 0 and start % g == 0)
@@ -167,8 +225,7 @@
     hbm = pl.BlockSpec(memory_space=pl.ANY)
     scratch = [
         pltpu.VMEM((2, group, nfit, npao), sources[1].dtype),
-        pltpu.VMEM((2, group, nfit, npao), sources[1].dtype),
-        pltpu.SemaphoreType.DMA((2, 2, group)),
+        pltpu.SemaphoreType.DMA((2, group)),
     ]
     block = (group, NPNO, NPNO)
     if split:
@@ -186,6 +243,7 @@
             hbm,
             hbm,
             hbm,
+            pl.BlockSpec((group, NPNO, nfit), lambda i, a, b, s, f: (i + base, 0, 0)),
             pl.BlockSpec((group, 2, NPNO, npao), lambda i, a, b, s, f: (i + base, 0, 0, 0)),
         ],
         out_specs=out_specs,
@@ -201,7 +259,7 @@
             bytes_accessed=count * (2 * nfit * npao * 2 + 2 * npao * NPNO * 2 + NPNO * NPNO * 4),
             transcendentals=0,
         ),
-    )(lead, trail, sizes, flip, *sources, coef_t)
+    )(lead, trail, sizes, flip, *sources, left_t, coef_t)
 
 
 def split_bf16(value):
@@ -329,13 +387,16 @@
     local_orbitals = (pair_orbitals - (position - 1) * occ_dev).astype(jnp.int32)
     half = pair_dev // 2
     presplit = halving_ready(half) and half % 8 == 0
+    coef_t = jnp.swapaxes(pno_coef, 2, 3)
+    left_t = left_halves(local_orbitals[:, 0] - occ_dev, sizes, three_index, coef_t)
     halves = [
         partial_exchange(
             local_orbitals[:, 0] - occ_dev,
             local_orbitals[:, 1],
             sizes,
             blocks,
-            jnp.swapaxes(pno_coef, 2, 3),
+            left_t,
+            coef_t,
             c * half,
             half,
             send_first(c) if presplit else None,

time: 195 us -> 194 us (level)
  waiting for transfers between devices: 91.5 us -> 83.3 us
  Pallas kernels: 46.7 us -> 53.8 us
    pallas_call x0 -> x1, Pallas kernels: none -> 8.1 us  [left_halves(): pl.pallas_call(functools.partial(left_kernel, occ=occ, group=group), grid...]
    ppermute x4, waiting for transfers between devices: 52.9 us -> 44.9 us  [halo_sources(): from_right = lax.ppermute(cells, axis, [(i + 1, i) for i in range(ends)])]
    ppermute x4, starting transfers between devices: 18.7 us -> 21.5 us  [halo_sources(): from_left = lax.ppermute(cells, axis, [(i, i + 1) for i in range(ends)])]
  transfers between devices with their start and end apart: 16 -> 16, of which waited for: 11 -> 14; matrix products, arithmetic and copies ran while one was open for 6% -> 6% of each run, Pallas kernels for 9% -> 13%
where the time goes in v18:
time: 194 us; the launch traced here: 193 us
  waiting for transfers between devices  83.3 us (43%)
  Pallas kernels  53.8 us (28%)
  starting transfers between devices  39.4 us (20%)
  other arithmetic  9.35 us (5%)
  local copies, waits for them, and re-layouts  5.43 us (3%)
    ppermute x4, waiting for transfers between devices, halo_sources(): from_right = lax.ppermute(cells, axis, [(i + 1, i) for i in range(ends)])  44.9 us
    ppermute x8, waiting for transfers between devices, swap_over_aux(): return lax.ppermute(value, ('aux', 'pair'), perm)  34.9 us
    pallas_call x3, Pallas kernels, coupling_step(): pl.pallas_call(kernel, grid_spec=grid_spec, out_shape=jax.ShapeDtypeStruc...  30.1 us
    ppermute x4, starting transfers between devices, halo_sources(): from_left = lax.ppermute(cells, axis, [(i, i + 1) for i in range(ends)])  21.5 us
    pallas_call x2, Pallas kernels, partial_exchange(): pl.pallas_call(functools.partial(exchange_kernel, occ=occ, group=group, s...  15.6 us
    ppermute x8, starting transfers between devices, swap_over_aux(): return lax.ppermute(value, ('aux', 'pair'), perm)  10.1 us
    pallas_call x1, Pallas kernels, left_halves(): pl.pallas_call(functools.partial(left_kernel, occ=occ, group=group), grid...  8.1 us
    ppermute x4, starting transfers between devices, halo_sources(): from_right = lax.ppermute(cells, axis, [(i + 1, i) for i in range(ends)])  7.85 us
  transfers between devices with their start and end apart: 16, of which 14 were waited for; matrix products, arithmetic and copies ran while one was open for 6% of the time, Pallas kernels for 13%

profile of v18, /device:TPU:1, one launch (start us, length us, event | category | flops | bytes accessed | tf_op | source)
XLA Modules:
  0.0 192.6 jit_solution(1716436702008148358)
XLA Ops:
  0.6 2.0 %collective-permute-start.1 = (bf16[4,512,256]{2,1,0:T(8,128)(2,1)}, bf16[4,512,256]{2,1,0:T(8,128)(2,1)S(1)}, u32[]{:S(2)}, u32[]{:S(2)}) collective-permute-start(bf16[4,512,256]{2,1,0:T(8,128)(2,1)} %refs_1_.3), channel_id=1, source_target_pairs={{1,0},{2,1},{3,2},{4,3},{5,4},{6,5},{7,6},{9,8},{10,9},{11,10},{12... | collective-permute-start | bytes 3145736 | tf_op jit(solution)/shard_map/ppermute | solution.py:19
  2.6 4.6 %collective-permute-start = (bf16[4,512,256]{2,1,0:T(8,128)(2,1)}, bf16[4,512,256]{2,1,0:T(8,128)(2,1)S(1)}, u32[]{:S(2)}, u32[]{:S(2)}) collective-permute-start(bf16[4,512,256]{2,1,0:T(8,128)(2,1)} %refs_1_.3), channel_id=1, source_target_pairs={{0,1},{1,2},{2,3},{3,4},{4,5},{5,6},{6,7},{8,9},{9,10},{10,11},{11... | collective-permute-start | bytes 3145736 | tf_op jit(solution)/shard_map/ppermute | solution.py:18
  7.2 1.2 compare_select_fusion.2.size_ref
  8.4 0.7 broadcast_subtract_fusion
  9.1 0.6 slice_bitcast_fusion
  9.7 8.1 %shard_map.95.refs_3_ = bf16[16,192,512]{2,1,0:T(8,128)(2,1)} custom-call(s32[16]{0:T(128)} %get-tuple-element.17.lead_ref, s32[16]{0:T(128)} %compare_select_fusion.2.size_ref, bf16[4,512,256]{2,1,0:T(8,128)(2,1)} %refs_1_.3, bf16[16,2,192,256]{3,2,1,0:T(8,128)(2,1)} %bitcast.8), custom_call_target="tpu_custom_call" | custom-call | flops 805306368 | bytes 10485760 | tf_op jit(solution)/shard_map/pallas_call | solution.py:153
  17.8 0.2 collective-permute-done.1.refs_2_
  17.9 1.3 collective-permute-done.refs_0_
  19.2 1.0 copy-done.3
  20.2 7.8 %shard_map.97 = (f32[4,192,192]{2,1,0:T(8,128)}, f32[4,192,192]{2,1,0:T(8,128)}) custom-call(s32[16]{0:T(128)} %get-tuple-element.17.lead_ref, s32[16]{0:T(128)} %get-tuple-element.16.trail_ref, s32[16]{0:T(128)} %compare_select_fusion.2.size_ref, s32[1]{0:T(128)} %bitcast.4.flip_ref, bf16[4,512,256]{2,1,0:T(8,128)(2,1)} %copy-done.3, ...), custom_call_target="tpu_custom_call" | custom-call | flops 1107296256 | bytes 6946816 | tf_op jit(solution)/shard_map/pallas_call | solution.py:253
  27.9 1.3 collective-permute-start.6
  29.2 7.9 %shard_map.96 = (f32[4,192,192]{2,1,0:T(8,128)}, f32[4,192,192]{2,1,0:T(8,128)}) custom-call(s32[16]{0:T(128)} %get-tuple-element.17.lead_ref, s32[16]{0:T(128)} %get-tuple-element.16.trail_ref, s32[16]{0:T(128)} %compare_select_fusion.2.size_ref, s32[1]{0:T(128)} %bitcast.2.flip_ref, bf16[4,512,256]{2,1,0:T(8,128)(2,1)} %copy-done.3, ...), custom_call_target="tpu_custom_call" | custom-call | flops 1107296256 | bytes 6946816 | tf_op jit(solution)/shard_map/pallas_call | solution.py:253
  37.1 1.3 collective-permute-start.2
  38.4 0.6 collective-permute-done.6
  39.2 3.1 %collective-permute-start.7 = (f32[2,192,192]{2,1,0:T(8,128)S(1)}, f32[2,192,192]{2,1,0:T(8,128)S(1)}, u32[]{:S(2)}, u32[]{:S(2)}) collective-permute-start(f32[2,192,192]{2,1,0:T(8,128)S(1)} %constant_dynamic-slice_fusion), channel_id=1, source_target_pairs={{0,8},{8,0},{16,24},{24,16},{1,17},{9,25},{17,1},{25,9},{2,10},{10... | collective-permute-start | bytes 884744 | tf_op jit(solution)/shard_map/ppermute | solution.py:30
  42.3 6.2 %collective-permute-done.2 = f32[4,192,192]{2,1,0:T(8,128)} collective-permute-done((f32[4,192,192]{2,1,0:T(8,128)}, f32[4,192,192]{2,1,0:T(8,128)}, u32[]{:S(2)}, u32[]{:S(2)}) %collective-permute-start.2) | collective-permute-done | bytes 589856 | tf_op jit(solution)/shard_map/ppermute | solution.py:30
  48.5 1.2 add.78
  49.8 0.4 collective-permute-start.3
  50.2 2.2 %collective-permute-done.7 = f32[2,192,192]{2,1,0:T(8,128)S(1)} collective-permute-done((f32[2,192,192]{2,1,0:T(8,128)S(1)}, f32[2,192,192]{2,1,0:T(8,128)S(1)}, u32[]{:S(2)}, u32[]{:S(2)}) %collective-permute-start.7) | collective-permute-done | bytes 294944 | tf_op jit(solution)/shard_map/ppermute | solution.py:30
  52.6 1.3 collective-permute-start.8
  53.9 3.9 %collective-permute-done.3 = f32[2,192,192]{2,1,0:T(8,128)S(1)} collective-permute-done((f32[2,192,192]{2,1,0:T(8,128)S(1)}, f32[2,192,192]{2,1,0:T(8,128)S(1)}, u32[]{:S(2)}, u32[]{:S(2)}) %collective-permute-start.3) | collective-permute-done | bytes 294944 | tf_op jit(solution)/shard_map/ppermute | solution.py:30
  58.0 3.2 %collective-permute-done.8 = f32[2,192,192]{2,1,0:T(8,128)S(1)} collective-permute-done((f32[2,192,192]{2,1,0:T(8,128)S(1)}, f32[2,192,192]{2,1,0:T(8,128)S(1)}, u32[]{:S(2)}, u32[]{:S(2)}) %collective-permute-start.8) | collective-permute-done | bytes 294944 | tf_op jit(solution)/shard_map/ppermute | solution.py:30
  61.3 1.3 collective-permute-start.9
  62.5 2.7 %collective-permute-done.4 = f32[2,192,192]{2,1,0:T(8,128)S(1)} collective-permute-done((f32[2,192,192]{2,1,0:T(8,128)S(1)}, f32[2,192,192]{2,1,0:T(8,128)S(1)}, u32[]{:S(2)}, u32[]{:S(2)}) %collective-permute-start.4) | collective-permute-done | bytes 294944 | tf_op jit(solution)/shard_map/ppermute | solution.py:30
  65.3 1.3 collective-permute-start.5
  66.6 0.1 broadcast.29.clone
  66.8 0.1 broadcast.29.clone.1
  67.0 9.9 %collective-permute-done.9 = f32[4,192,192]{2,1,0:T(8,128)S(1)} collective-permute-done((f32[4,192,192]{2,1,0:T(8,128)S(1)}, f32[4,192,192]{2,1,0:T(8,128)S(1)}, u32[]{:S(2)}, u32[]{:S(2)}) %collective-permute-start.9) | collective-permute-done | bytes 589856 | tf_op jit(solution)/shard_map/ppermute | solution.py:30
  76.9 6.2 %collective-permute-done.5 = f32[4,192,192]{2,1,0:T(8,128)S(1)} collective-permute-done((f32[4,192,192]{2,1,0:T(8,128)S(1)}, f32[4,192,192]{2,1,0:T(8,128)S(1)}, u32[]{:S(2)}, u32[]{:S(2)}) %collective-permute-start.5) | collective-permute-done | bytes 589856 | tf_op jit(solution)/shard_map/ppermute | solution.py:30
  83.2 2.0 %pad_maximum_fusion = (f32[16,192,192]{2,1,0:T(8,128)}, f32[16,192,192]{2,1,0:T(8,128)S(1)}) fusion(f32[8,192,192]{2,1,0:T(8,128)S(1)} %constant_dynamic-update-slice_fusion, f32[8,192,192]{2,1,0:T(8,128)S(1)} %constant_dynamic-update-slice_fusion.4, f32[16,192]{1,0:T(8,128)S(1)} %copy-done.7), kind=kLoop, calls=%fused_computation | loop fusion | flops 2359296 | bytes 7090176 | tf_op jit(solution)/shard_map/concatenate | solution.py:78
  85.3 1.9 collective-permute-start.11
  87.2 8.4 %collective-permute-start.10 = (f32[16,192,192]{2,1,0:T(8,128)S(1)}, f32[16,192,192]{2,1,0:T(8,128)}, u32[]{:S(2)}, u32[]{:S(2)}) collective-permute-start(f32[16,192,192]{2,1,0:T(8,128)S(1)} %get-tuple-element.15.refs_1_.refs_7_), channel_id=1, source_target_pairs={{0,1},{1,2},{2,3},{3,4},{4,5},{5,6},{6,7},{8,9},{9,10},{10,11},{11... | collective-permute-start | bytes 7077896 | tf_op jit(solution)/shard_map/ppermute | solution.py:18
  95.6 0.6 broadcast_in_dim.26.refs_6_.refs_9_
  96.3 0.6 reshape.26.nb_ref
  97.0 0.6 reshape.27.fock_ref
  97.6 1.7 copy.14.refs_5_.refs_8_
  99.2 29.3 %collective-permute-done.11.refs_2_ = f32[16,192,192]{2,1,0:T(8,128)} collective-permute-done((f32[16,192,192]{2,1,0:T(8,128)S(1)}, f32[16,192,192]{2,1,0:T(8,128)}, u32[]{:S(2)}, u32[]{:S(2)}) %collective-permute-start.11) | collective-permute-done | bytes 2359328 | tf_op jit(solution)/shard_map/ppermute | solution.py:19
  128.5 1.1 collective-permute-done.10.refs_0_
  129.6 8.6 %shard_map.98.refs_2_ = f32[8,192,192]{2,1,0:T(8,128)} custom-call(s32[32]{0:T(128)} %reshape.26.nb_ref, s32[16]{0:T(128)} %compare_select_fusion.2.size_ref, f32[32]{0:T(128)} %reshape.27.fock_ref, f32[16,192,192]{2,1,0:T(8,128)} %collective-permute-done.10.refs_0_, f32[16,192,192]{2,1,0:T(8,128)} %copy-done, ...), custom_call_target="tpu_custom_call" | custom-call | flops 905969664 | bytes 7077888 | tf_op jit(solution)/shard_map/pallas_call | solution.py:355
  138.2 2.1 %collective-permute-start.14 = (f32[8,192,192]{2,1,0:T(8,128)}, f32[8,192,192]{2,1,0:T(8,128)S(1)}, u32[]{:S(2)}, u32[]{:S(2)}) collective-permute-start(f32[8,192,192]{2,1,0:T(8,128)} %shard_map.98.refs_2_), channel_id=1, source_target_pairs={{1,0},{2,1},{3,2},{4,3},{5,4},{6,5},{7,6},{9,8},{10,9},{11,10},{12... | collective-permute-start | bytes 3538952 | tf_op jit(solution)/shard_map/ppermute | solution.py:19
  140.3 4.7 %collective-permute-start.12 = (f32[8,192,192]{2,1,0:T(8,128)}, f32[8,192,192]{2,1,0:T(8,128)}, u32[]{:S(2)}, u32[]{:S(2)}) collective-permute-start(f32[8,192,192]{2,1,0:T(8,128)} %shard_map.98.refs_2_), channel_id=1, source_target_pairs={{0,1},{1,2},{2,3},{3,4},{4,5},{5,6},{6,7},{8,9},{9,10},{10,11},{11... | collective-permute-start | bytes 3538952 | tf_op jit(solution)/shard_map/ppermute | solution.py:18
  145.0 8.6 %shard_map.99.refs_3_ = f32[8,192,192]{2,1,0:T(8,128)} custom-call(s32[32]{0:T(128)} %reshape.26.nb_ref, s32[16]{0:T(128)} %compare_select_fusion.2.size_ref, f32[32]{0:T(128)} %reshape.27.fock_ref, f32[16,192,192]{2,1,0:T(8,128)} %collective-permute-done.10.refs_0_, f32[16,192,192]{2,1,0:T(8,128)} %copy-done, ...), custom_call_target="tpu_custom_call" | custom-call | flops 905969664 | bytes 7077888 | tf_op jit(solution)/shard_map/pallas_call | solution.py:355
  153.6 1.9 collective-permute-start.15
  155.6 3.9 %collective-permute-start.13 = (f32[8,192,192]{2,1,0:T(8,128)}, f32[8,192,192]{2,1,0:T(8,128)}, u32[]{:S(2)}, u32[]{:S(2)}) collective-permute-start(f32[8,192,192]{2,1,0:T(8,128)} %shard_map.99.refs_3_), channel_id=1, source_target_pairs={{0,1},{1,2},{2,3},{3,4},{4,5},{5,6},{6,7},{8,9},{9,10},{10,11},{11... | collective-permute-start | bytes 3538952 | tf_op jit(solution)/shard_map/ppermute | solution.py:18
  159.5 3.4 %pad_maximum_fusion.1.refs_10_ = f32[16,192,192]{2,1,0:T(8,128)} fusion(f32[8,192,192]{2,1,0:T(8,128)} %shard_map.99.refs_3_, f32[8,192,192]{2,1,0:T(8,128)S(1)} %copy-done.1), kind=kLoop, calls=%fused_computation.1 | loop fusion | flops 589824 | bytes 4718592 | tf_op jit(solution)/shard_map/concatenate | solution.py:424
  162.9 15.4 %collective-permute-done.15.refs_5_ = f32[8,192,192]{2,1,0:T(8,128)} collective-permute-done((f32[8,192,192]{2,1,0:T(8,128)}, f32[8,192,192]{2,1,0:T(8,128)}, u32[]{:S(2)}, u32[]{:S(2)}) %collective-permute-start.15) | collective-permute-done | bytes 1179680 | tf_op jit(solution)/shard_map/ppermute | solution.py:19
  178.3 1.2 collective-permute-done.13.refs_1_
  179.5 12.9 %shard_map.100 = f32[16,192,192]{2,1,0:T(8,128)} custom-call(s32[32]{0:T(128)} %reshape.26.nb_ref, s32[16]{0:T(128)} %compare_select_fusion.2.size_ref, f32[32]{0:T(128)} %reshape.27.fock_ref, f32[8,192,192]{2,1,0:T(8,128)} %collective-permute-done.12.refs_0_, f32[8,192,192]{2,1,0:T(8,128)} %collective-permute-done.13.refs_1_, ...), custom_call_target="tpu_custom_call" | custom-call | flops 1811939328 | bytes 14155776 | tf_op jit(solution)/shard_map/pallas_call | solution.py:355
  (38 shorter events, 1.0 us)
Async XLA Ops:
  0.6 17.3 %collective-permute-start.1 = (bf16[4,512,256]{2,1,0:T(8,128)(2,1)}, bf16[4,512,256]{2,1,0:T(8,128)(2,1)S(1)}, u32[]{:S(2)}, u32[]{:S(2)}) collective-permute-start(bf16[4,512,256]{2,1,0:T(8,128)(2,1)} %refs_1_.3), channel_id=1, source_target_pairs={{1,0},{2,1},{3,2},{4,3},{5,4},{6,5},{7,6},{9,8},{10,9},{11,10},{12... | collective-permute-start | bytes 3145736 | tf_op jit(solution)/shard_map/ppermute | solution.py:19
  2.6 16.6 %collective-permute-start = (bf16[4,512,256]{2,1,0:T(8,128)(2,1)}, bf16[4,512,256]{2,1,0:T(8,128)(2,1)S(1)}, u32[]{:S(2)}, u32[]{:S(2)}) collective-permute-start(bf16[4,512,256]{2,1,0:T(8,128)(2,1)} %refs_1_.3), channel_id=1, source_target_pairs={{0,1},{1,2},{2,3},{3,4},{4,5},{5,6},{6,7},{8,9},{9,10},{10,11},{11... | collective-permute-start | bytes 3145736 | tf_op jit(solution)/shard_map/ppermute | solution.py:18
  17.9 1.3 copy-start.2
  19.2 1.0 copy-start.3
  27.9 11.1 %collective-permute-start.6 = (f32[4,192,192]{2,1,0:T(8,128)}, f32[4,192,192]{2,1,0:T(8,128)S(1)}, u32[]{:S(2)}, u32[]{:S(2)}) collective-permute-start(f32[4,192,192]{2,1,0:T(8,128)} %get-tuple-element.9), channel_id=1, source_target_pairs={{0,16},{8,24},{16,0},{24,8},{1,9},{9,1},{17,25},{25,17},{2,18},{10... | collective-permute-start | bytes 1769480 | tf_op jit(solution)/shard_map/ppermute | solution.py:30
  29.2 9.8 %copy-start.5 = (f32[4,192,192]{2,1,0:T(8,128)S(1)}, f32[4,192,192]{2,1,0:T(8,128)}, u32[]{:S(2)}) copy-start(f32[4,192,192]{2,1,0:T(8,128)} %get-tuple-element.8) | copy-start | bytes 1769476
  37.1 11.4 %collective-permute-start.2 = (f32[4,192,192]{2,1,0:T(8,128)}, f32[4,192,192]{2,1,0:T(8,128)}, u32[]{:S(2)}, u32[]{:S(2)}) collective-permute-start(f32[4,192,192]{2,1,0:T(8,128)} %get-tuple-element.7), channel_id=1, source_target_pairs={{0,8},{8,0},{16,24},{24,16},{1,17},{9,25},{17,1},{25,9},{2,10},{10... | collective-permute-start | bytes 1769480 | tf_op jit(solution)/shard_map/ppermute | solution.py:30
  39.1 9.5 %copy-start.6 = (f32[4,192,192]{2,1,0:T(8,128)S(1)}, f32[4,192,192]{2,1,0:T(8,128)}, u32[]{:S(2)}) copy-start(f32[4,192,192]{2,1,0:T(8,128)} %get-tuple-element.6) | copy-start | bytes 1769476
  39.2 13.2 %collective-permute-start.7 = (f32[2,192,192]{2,1,0:T(8,128)S(1)}, f32[2,192,192]{2,1,0:T(8,128)S(1)}, u32[]{:S(2)}, u32[]{:S(2)}) collective-permute-start(f32[2,192,192]{2,1,0:T(8,128)S(1)} %constant_dynamic-slice_fusion), channel_id=1, source_target_pairs={{0,8},{8,0},{16,24},{24,16},{1,17},{9,25},{17,1},{25,9},{2,10},{10... | collective-permute-start | bytes 884744 | tf_op jit(solution)/shard_map/ppermute | solution.py:30
  49.8 8.0 %collective-permute-start.3 = (f32[2,192,192]{2,1,0:T(8,128)S(1)}, f32[2,192,192]{2,1,0:T(8,128)S(1)}, u32[]{:S(2)}, u32[]{:S(2)}) collective-permute-start(f32[2,192,192]{2,1,0:T(8,128)S(1)} %constant_dynamic-slice_fusion.1), channel_id=1, source_target_pairs={{0,16},{8,24},{16,0},{24,8},{1,9},{9,1},{17,25},{25,17},{2,18},{10... | collective-permute-start | bytes 884744 | tf_op jit(solution)/shard_map/ppermute | solution.py:30
  52.6 8.6 %collective-permute-start.8 = (f32[2,192,192]{2,1,0:T(8,128)S(1)}, f32[2,192,192]{2,1,0:T(8,128)S(1)}, u32[]{:S(2)}, u32[]{:S(2)}) collective-permute-start(f32[2,192,192]{2,1,0:T(8,128)S(1)} %get-tuple-element.13), channel_id=1, source_target_pairs={{0,8},{8,0},{16,24},{24,16},{1,17},{9,25},{17,1},{25,9},{2,10},{10... | collective-permute-start | bytes 884744 | tf_op jit(solution)/shard_map/ppermute | solution.py:30
  57.9 7.3 %collective-permute-start.4 = (f32[2,192,192]{2,1,0:T(8,128)S(1)}, f32[2,192,192]{2,1,0:T(8,128)S(1)}, u32[]{:S(2)}, u32[]{:S(2)}) collective-permute-start(f32[2,192,192]{2,1,0:T(8,128)S(1)} %get-tuple-element.11), channel_id=1, source_target_pairs={{0,16},{8,24},{16,0},{24,8},{1,9},{9,1},{17,25},{25,17},{2,18},{10... | collective-permute-start | bytes 884744 | tf_op jit(solution)/shard_map/ppermute | solution.py:30
  61.3 15.6 %collective-permute-start.9 = (f32[4,192,192]{2,1,0:T(8,128)S(1)}, f32[4,192,192]{2,1,0:T(8,128)S(1)}, u32[]{:S(2)}, u32[]{:S(2)}) collective-permute-start(f32[4,192,192]{2,1,0:T(8,128)S(1)} %constant_dynamic-update-slice_fusion.2), channel_id=1, source_target_pairs={{0,16},{8,24},{16,0},{24,8},{1,9},{9,1},{17,25},{25,17},{2,18},{10... | collective-permute-start | bytes 1769480 | tf_op jit(solution)/shard_map/ppermute | solution.py:30
  65.3 17.9 %collective-permute-start.5 = (f32[4,192,192]{2,1,0:T(8,128)S(1)}, f32[4,192,192]{2,1,0:T(8,128)S(1)}, u32[]{:S(2)}, u32[]{:S(2)}) collective-permute-start(f32[4,192,192]{2,1,0:T(8,128)S(1)} %constant_dynamic-update-slice_fusion.6), channel_id=1, source_target_pairs={{0,8},{8,0},{16,24},{24,16},{1,17},{9,25},{17,1},{25,9},{2,10},{10... | collective-permute-start | bytes 1769480 | tf_op jit(solution)/shard_map/ppermute | solution.py:30
  67.0 16.2 %copy-start.7 = (f32[16,192]{1,0:T(8,128)S(1)}, f32[16,192]{1,0:T(8,128)}, u32[]{:S(2)}) copy-start(f32[16,192]{1,0:T(8,128)} %param.12) | copy-start | bytes 36868
  83.2 13.0 %copy-start.9 = (s32[16,2]{0,1:T(2,128)S(1)}, s32[16,2]{0,1:T(2,128)}, u32[]{:S(2)}) copy-start(s32[16,2]{0,1:T(2,128)} %param.14) | copy-start | bytes 388
  83.2 13.7 %copy-start.8 = (f32[16,2]{0,1:T(2,128)S(1)}, f32[16,2]{0,1:T(2,128)}, u32[]{:S(2)}) copy-start(f32[16,2]{0,1:T(2,128)} %param.15) | copy-start | bytes 388
  85.3 44.3 %copy-start = (f32[16,192,192]{2,1,0:T(8,128)}, f32[16,192,192]{2,1,0:T(8,128)S(1)}, u32[]{:S(2)}) copy-start(f32[16,192,192]{2,1,0:T(8,128)S(1)} %get-tuple-element.15.refs_1_.refs_7_) | copy-start | bytes 7077892
  85.3 43.2 %collective-permute-start.11 = (f32[16,192,192]{2,1,0:T(8,128)S(1)}, f32[16,192,192]{2,1,0:T(8,128)}, u32[]{:S(2)}, u32[]{:S(2)}) collective-permute-start(f32[16,192,192]{2,1,0:T(8,128)S(1)} %get-tuple-element.15.refs_1_.refs_7_), channel_id=1, source_target_pairs={{1,0},{2,1},{3,2},{4,3},{5,4},{6,5},{7,6},{9,8},{10,9},{11,10},{12... | collective-permute-start | bytes 7077896 | tf_op jit(solution)/shard_map/ppermute | solution.py:19
  87.2 42.4 %collective-permute-start.10 = (f32[16,192,192]{2,1,0:T(8,128)S(1)}, f32[16,192,192]{2,1,0:T(8,128)}, u32[]{:S(2)}, u32[]{:S(2)}) collective-permute-start(f32[16,192,192]{2,1,0:T(8,128)S(1)} %get-tuple-element.15.refs_1_.refs_7_), channel_id=1, source_target_pairs={{0,1},{1,2},{2,3},{3,4},{4,5},{5,6},{6,7},{8,9},{9,10},{10,11},{11... | collective-permute-start | bytes 7077896 | tf_op jit(solution)/shard_map/ppermute | solution.py:18
  138.2 21.3 %copy-start.1 = (f32[8,192,192]{2,1,0:T(8,128)S(1)}, f32[8,192,192]{2,1,0:T(8,128)}, u32[]{:S(2)}) copy-start(f32[8,192,192]{2,1,0:T(8,128)} %shard_map.98.refs_2_) | copy-start | bytes 3538948
  138.2 24.7 %collective-permute-start.14 = (f32[8,192,192]{2,1,0:T(8,128)}, f32[8,192,192]{2,1,0:T(8,128)S(1)}, u32[]{:S(2)}, u32[]{:S(2)}) collective-permute-start(f32[8,192,192]{2,1,0:T(8,128)} %shard_map.98.refs_2_), channel_id=1, source_target_pairs={{1,0},{2,1},{3,2},{4,3},{5,4},{6,5},{7,6},{9,8},{10,9},{11,10},{12... | collective-permute-start | bytes 3538952 | tf_op jit(solution)/shard_map/ppermute | solution.py:19
  140.3 22.6 %collective-permute-start.12 = (f32[8,192,192]{2,1,0:T(8,128)}, f32[8,192,192]{2,1,0:T(8,128)}, u32[]{:S(2)}, u32[]{:S(2)}) collective-permute-start(f32[8,192,192]{2,1,0:T(8,128)} %shard_map.98.refs_2_), channel_id=1, source_target_pairs={{0,1},{1,2},{2,3},{3,4},{4,5},{5,6},{6,7},{8,9},{9,10},{10,11},{11... | collective-permute-start | bytes 3538952 | tf_op jit(solution)/shard_map/ppermute | solution.py:18
  153.6 24.7 %collective-permute-start.15 = (f32[8,192,192]{2,1,0:T(8,128)}, f32[8,192,192]{2,1,0:T(8,128)}, u32[]{:S(2)}, u32[]{:S(2)}) collective-permute-start(f32[8,192,192]{2,1,0:T(8,128)} %shard_map.99.refs_3_), channel_id=1, source_target_pairs={{1,0},{2,1},{3,2},{4,3},{5,4},{6,5},{7,6},{9,8},{10,9},{11,10},{12... | collective-permute-start | bytes 3538952 | tf_op jit(solution)/shard_map/ppermute | solution.py:19
  155.6 23.9 %collective-permute-start.13 = (f32[8,192,192]{2,1,0:T(8,128)}, f32[8,192,192]{2,1,0:T(8,128)}, u32[]{:S(2)}, u32[]{:S(2)}) collective-permute-start(f32[8,192,192]{2,1,0:T(8,128)} %shard_map.99.refs_3_), channel_id=1, source_target_pairs={{0,1},{1,2},{2,3},{3,4},{4,5},{5,6},{6,7},{8,9},{9,10},{10,11},{11... | collective-permute-start | bytes 3538952 | tf_op jit(solution)/shard_map/ppermute | solution.py:18
  162.9 16.6 %copy-start.4 = (f32[8,192,192]{2,1,0:T(8,128)}, f32[8,192,192]{2,1,0:T(8,128)S(1)}, u32[]{:S(2)}) copy-start(f32[8,192,192]{2,1,0:T(8,128)S(1)} %collective-permute-done.14.refs_4_) | copy-start | bytes 3538948

commit v19 on v18

--- a/solution.py
+++ b/solution.py
@@ -135,7 +135,7 @@
 
 def left_halves(lead, sizes, t_own, coef_t):
     pairs = coef_t.shape[0]
-    group = next(g for g in (4, 2, 1) if pairs % g == 0)
+    group = next(g for g in (8, 4, 2, 1) if pairs % g == 0 and pairs // g >= 2)
     occ, nfit, npao = t_own.shape
     grid_spec = pltpu.PrefetchScalarGridSpec(
         num_scalar_prefetch=2,
@@ -325,7 +325,7 @@
 def coupling_step(nb, sizes, fock, sources, margin, exchange, energy, own, final, start=0, count=None):
     pairs = own.shape[0]
     count = pairs if count is None else count
-    group = next(g for g in (4, 2, 1) if count % g == 0 and start % g == 0)
+    group = next(g for g in (8, 4, 2, 1) if count % g == 0 and start % g == 0 and count // g >= 2)
     base = start // group
     column = energy.reshape(pairs, NPNO, 1)
     row = energy.reshape(pairs, 1, NPNO)

time: 194 us -> 195 us (level)
  no operation moved by 1% of the time
where the time goes in v19:
time: 195 us; the launch traced here: 194 us
  waiting for transfers between devices  83.8 us (43%)
  Pallas kernels  55.6 us (29%)
  starting transfers between devices  38.9 us (20%)
  other arithmetic  9.35 us (5%)
  local copies, waits for them, and re-layouts  5.43 us (3%)
    ppermute x4, waiting for transfers between devices, halo_sources(): from_right = lax.ppermute(cells, axis, [(i + 1, i) for i in range(ends)])  44.8 us
    ppermute x8, waiting for transfers between devices, swap_over_aux(): return lax.ppermute(value, ('aux', 'pair'), perm)  35.4 us
    pallas_call x3, Pallas kernels, coupling_step(): pl.pallas_call(kernel, grid_spec=grid_spec, out_shape=jax.ShapeDtypeStruc...  31.9 us
    ppermute x4, starting transfers between devices, halo_sources(): from_left = lax.ppermute(cells, axis, [(i, i + 1) for i in range(ends)])  21.3 us
    pallas_call x2, Pallas kernels, partial_exchange(): pl.pallas_call(functools.partial(exchange_kernel, occ=occ, group=group, s...  15.6 us
    ppermute x8, starting transfers between devices, swap_over_aux(): return lax.ppermute(value, ('aux', 'pair'), perm)  9.68 us
    pallas_call x1, Pallas kernels, left_halves(): pl.pallas_call(functools.partial(left_kernel, occ=occ, group=group), grid...  8.1 us
    ppermute x4, starting transfers between devices, halo_sources(): from_right = lax.ppermute(cells, axis, [(i + 1, i) for i in range(ends)])  7.85 us
  transfers between devices with their start and end apart: 16, of which 14 were waited for; matrix products, arithmetic and copies ran while one was open for 6% of the time, Pallas kernels for 13%

profile of v19, /device:TPU:1, one launch (start us, length us, event | category | flops | bytes accessed | tf_op | source)
XLA Modules:
  0.0 194.2 jit_solution(11998671930408122474)
XLA Ops:
  0.6 2.0 %collective-permute-start.1 = (bf16[4,512,256]{2,1,0:T(8,128)(2,1)}, bf16[4,512,256]{2,1,0:T(8,128)(2,1)S(1)}, u32[]{:S(2)}, u32[]{:S(2)}) collective-permute-start(bf16[4,512,256]{2,1,0:T(8,128)(2,1)} %refs_1_.3), channel_id=1, source_target_pairs={{1,0},{2,1},{3,2},{4,3},{5,4},{6,5},{7,6},{9,8},{10,9},{11,10},{12... | collective-permute-start | bytes 3145736 | tf_op jit(solution)/shard_map/ppermute | solution.py:19
  2.6 4.6 %collective-permute-start = (bf16[4,512,256]{2,1,0:T(8,128)(2,1)}, bf16[4,512,256]{2,1,0:T(8,128)(2,1)S(1)}, u32[]{:S(2)}, u32[]{:S(2)}) collective-permute-start(bf16[4,512,256]{2,1,0:T(8,128)(2,1)} %refs_1_.3), channel_id=1, source_target_pairs={{0,1},{1,2},{2,3},{3,4},{4,5},{5,6},{6,7},{8,9},{9,10},{10,11},{11... | collective-permute-start | bytes 3145736 | tf_op jit(solution)/shard_map/ppermute | solution.py:18
  7.2 1.2 compare_select_fusion.2.size_ref
  8.4 0.7 broadcast_subtract_fusion
  9.1 0.6 slice_bitcast_fusion
  9.7 8.1 %shard_map.95.refs_3_ = bf16[16,192,512]{2,1,0:T(8,128)(2,1)} custom-call(s32[16]{0:T(128)} %get-tuple-element.17.lead_ref, s32[16]{0:T(128)} %compare_select_fusion.2.size_ref, bf16[4,512,256]{2,1,0:T(8,128)(2,1)} %refs_1_.3, bf16[16,2,192,256]{3,2,1,0:T(8,128)(2,1)} %bitcast.8), custom_call_target="tpu_custom_call" | custom-call | flops 805306368 | bytes 10485760 | tf_op jit(solution)/shard_map/pallas_call | solution.py:153
  17.8 0.2 collective-permute-done.1.refs_2_
  17.9 1.3 collective-permute-done.refs_0_
  19.2 1.0 copy-done.3
  20.2 7.7 %shard_map.97 = (f32[4,192,192]{2,1,0:T(8,128)}, f32[4,192,192]{2,1,0:T(8,128)}) custom-call(s32[16]{0:T(128)} %get-tuple-element.17.lead_ref, s32[16]{0:T(128)} %get-tuple-element.16.trail_ref, s32[16]{0:T(128)} %compare_select_fusion.2.size_ref, s32[1]{0:T(128)} %bitcast.4.flip_ref, bf16[4,512,256]{2,1,0:T(8,128)(2,1)} %copy-done.3, ...), custom_call_target="tpu_custom_call" | custom-call | flops 1107296256 | bytes 6946816 | tf_op jit(solution)/shard_map/pallas_call | solution.py:253
  27.9 1.2 collective-permute-start.6
  29.2 7.9 %shard_map.96 = (f32[4,192,192]{2,1,0:T(8,128)}, f32[4,192,192]{2,1,0:T(8,128)}) custom-call(s32[16]{0:T(128)} %get-tuple-element.17.lead_ref, s32[16]{0:T(128)} %get-tuple-element.16.trail_ref, s32[16]{0:T(128)} %compare_select_fusion.2.size_ref, s32[1]{0:T(128)} %bitcast.2.flip_ref, bf16[4,512,256]{2,1,0:T(8,128)(2,1)} %copy-done.3, ...), custom_call_target="tpu_custom_call" | custom-call | flops 1107296256 | bytes 6946816 | tf_op jit(solution)/shard_map/pallas_call | solution.py:253
  37.0 1.3 collective-permute-start.2
  38.3 1.4 collective-permute-done.6
  39.9 2.7 %collective-permute-start.7 = (f32[2,192,192]{2,1,0:T(8,128)S(1)}, f32[2,192,192]{2,1,0:T(8,128)S(1)}, u32[]{:S(2)}, u32[]{:S(2)}) collective-permute-start(f32[2,192,192]{2,1,0:T(8,128)S(1)} %constant_dynamic-slice_fusion), channel_id=1, source_target_pairs={{0,8},{8,0},{16,24},{24,16},{1,17},{9,25},{17,1},{25,9},{2,10},{10... | collective-permute-start | bytes 884744 | tf_op jit(solution)/shard_map/ppermute | solution.py:30
  42.6 5.8 %collective-permute-done.2 = f32[4,192,192]{2,1,0:T(8,128)} collective-permute-done((f32[4,192,192]{2,1,0:T(8,128)}, f32[4,192,192]{2,1,0:T(8,128)}, u32[]{:S(2)}, u32[]{:S(2)}) %collective-permute-start.2) | collective-permute-done | bytes 589856 | tf_op jit(solution)/shard_map/ppermute | solution.py:30
  48.5 1.2 add.78
  49.7 0.5 collective-permute-start.3
  50.2 2.2 %collective-permute-done.7 = f32[2,192,192]{2,1,0:T(8,128)S(1)} collective-permute-done((f32[2,192,192]{2,1,0:T(8,128)S(1)}, f32[2,192,192]{2,1,0:T(8,128)S(1)}, u32[]{:S(2)}, u32[]{:S(2)}) %collective-permute-start.7) | collective-permute-done | bytes 294944 | tf_op jit(solution)/shard_map/ppermute | solution.py:30
  52.5 1.3 collective-permute-start.8
  53.8 3.8 %collective-permute-done.3 = f32[2,192,192]{2,1,0:T(8,128)S(1)} collective-permute-done((f32[2,192,192]{2,1,0:T(8,128)S(1)}, f32[2,192,192]{2,1,0:T(8,128)S(1)}, u32[]{:S(2)}, u32[]{:S(2)}) %collective-permute-start.3) | collective-permute-done | bytes 294944 | tf_op jit(solution)/shard_map/ppermute | solution.py:30
  57.9 3.3 %collective-permute-done.8 = f32[2,192,192]{2,1,0:T(8,128)S(1)} collective-permute-done((f32[2,192,192]{2,1,0:T(8,128)S(1)}, f32[2,192,192]{2,1,0:T(8,128)S(1)}, u32[]{:S(2)}, u32[]{:S(2)}) %collective-permute-start.8) | collective-permute-done | bytes 294944 | tf_op jit(solution)/shard_map/ppermute | solution.py:30
  61.2 1.2 collective-permute-start.9
  62.5 2.7 %collective-permute-done.4 = f32[2,192,192]{2,1,0:T(8,128)S(1)} collective-permute-done((f32[2,192,192]{2,1,0:T(8,128)S(1)}, f32[2,192,192]{2,1,0:T(8,128)S(1)}, u32[]{:S(2)}, u32[]{:S(2)}) %collective-permute-start.4) | collective-permute-done | bytes 294944 | tf_op jit(solution)/shard_map/ppermute | solution.py:30
  65.2 1.3 collective-permute-start.5
  66.5 0.1 broadcast.29.clone
  66.7 0.1 broadcast.29.clone.1
  66.9 9.8 %collective-permute-done.9 = f32[4,192,192]{2,1,0:T(8,128)S(1)} collective-permute-done((f32[4,192,192]{2,1,0:T(8,128)S(1)}, f32[4,192,192]{2,1,0:T(8,128)S(1)}, u32[]{:S(2)}, u32[]{:S(2)}) %collective-permute-start.9) | collective-permute-done | bytes 589856 | tf_op jit(solution)/shard_map/ppermute | solution.py:30
  76.8 6.3 %collective-permute-done.5 = f32[4,192,192]{2,1,0:T(8,128)S(1)} collective-permute-done((f32[4,192,192]{2,1,0:T(8,128)S(1)}, f32[4,192,192]{2,1,0:T(8,128)S(1)}, u32[]{:S(2)}, u32[]{:S(2)}) %collective-permute-start.5) | collective-permute-done | bytes 589856 | tf_op jit(solution)/shard_map/ppermute | solution.py:30
  83.3 2.0 %pad_maximum_fusion = (f32[16,192,192]{2,1,0:T(8,128)}, f32[16,192,192]{2,1,0:T(8,128)S(1)}) fusion(f32[8,192,192]{2,1,0:T(8,128)S(1)} %constant_dynamic-update-slice_fusion, f32[8,192,192]{2,1,0:T(8,128)S(1)} %constant_dynamic-update-slice_fusion.4, f32[16,192]{1,0:T(8,128)S(1)} %copy-done.7), kind=kLoop, calls=%fused_computation | loop fusion | flops 2359296 | bytes 7090176 | tf_op jit(solution)/shard_map/concatenate | solution.py:78
  85.3 1.9 collective-permute-start.11
  87.2 8.4 %collective-permute-start.10 = (f32[16,192,192]{2,1,0:T(8,128)S(1)}, f32[16,192,192]{2,1,0:T(8,128)}, u32[]{:S(2)}, u32[]{:S(2)}) collective-permute-start(f32[16,192,192]{2,1,0:T(8,128)S(1)} %get-tuple-element.15.refs_1_.refs_7_), channel_id=1, source_target_pairs={{0,1},{1,2},{2,3},{3,4},{4,5},{5,6},{6,7},{8,9},{9,10},{10,11},{11... | collective-permute-start | bytes 7077896 | tf_op jit(solution)/shard_map/ppermute | solution.py:18
  95.7 0.6 broadcast_in_dim.26.refs_6_.refs_9_
  96.4 0.6 reshape.26.nb_ref
  97.1 0.6 reshape.27.fock_ref
  97.6 1.7 copy.14.refs_5_.refs_8_
  99.3 29.3 %collective-permute-done.11.refs_2_ = f32[16,192,192]{2,1,0:T(8,128)} collective-permute-done((f32[16,192,192]{2,1,0:T(8,128)S(1)}, f32[16,192,192]{2,1,0:T(8,128)}, u32[]{:S(2)}, u32[]{:S(2)}) %collective-permute-start.11) | collective-permute-done | bytes 2359328 | tf_op jit(solution)/shard_map/ppermute | solution.py:19
  128.6 1.1 collective-permute-done.10.refs_0_
  129.7 8.6 %shard_map.98.refs_2_ = f32[8,192,192]{2,1,0:T(8,128)} custom-call(s32[32]{0:T(128)} %reshape.26.nb_ref, s32[16]{0:T(128)} %compare_select_fusion.2.size_ref, f32[32]{0:T(128)} %reshape.27.fock_ref, f32[16,192,192]{2,1,0:T(8,128)} %collective-permute-done.10.refs_0_, f32[16,192,192]{2,1,0:T(8,128)} %copy-done, ...), custom_call_target="tpu_custom_call" | custom-call | flops 905969664 | bytes 7077888 | tf_op jit(solution)/shard_map/pallas_call | solution.py:355
  138.3 2.1 %collective-permute-start.14 = (f32[8,192,192]{2,1,0:T(8,128)}, f32[8,192,192]{2,1,0:T(8,128)S(1)}, u32[]{:S(2)}, u32[]{:S(2)}) collective-permute-start(f32[8,192,192]{2,1,0:T(8,128)} %shard_map.98.refs_2_), channel_id=1, source_target_pairs={{1,0},{2,1},{3,2},{4,3},{5,4},{6,5},{7,6},{9,8},{10,9},{11,10},{12... | collective-permute-start | bytes 3538952 | tf_op jit(solution)/shard_map/ppermute | solution.py:19
  140.4 4.5 %collective-permute-start.12 = (f32[8,192,192]{2,1,0:T(8,128)}, f32[8,192,192]{2,1,0:T(8,128)}, u32[]{:S(2)}, u32[]{:S(2)}) collective-permute-start(f32[8,192,192]{2,1,0:T(8,128)} %shard_map.98.refs_2_), channel_id=1, source_target_pairs={{0,1},{1,2},{2,3},{3,4},{4,5},{5,6},{6,7},{8,9},{9,10},{10,11},{11... | collective-permute-start | bytes 3538952 | tf_op jit(solution)/shard_map/ppermute | solution.py:18
  144.9 8.7 %shard_map.99.refs_3_ = f32[8,192,192]{2,1,0:T(8,128)} custom-call(s32[32]{0:T(128)} %reshape.26.nb_ref, s32[16]{0:T(128)} %compare_select_fusion.2.size_ref, f32[32]{0:T(128)} %reshape.27.fock_ref, f32[16,192,192]{2,1,0:T(8,128)} %collective-permute-done.10.refs_0_, f32[16,192,192]{2,1,0:T(8,128)} %copy-done, ...), custom_call_target="tpu_custom_call" | custom-call | flops 905969664 | bytes 7077888 | tf_op jit(solution)/shard_map/pallas_call | solution.py:355
  153.6 1.9 collective-permute-start.15
  155.5 3.9 %collective-permute-start.13 = (f32[8,192,192]{2,1,0:T(8,128)}, f32[8,192,192]{2,1,0:T(8,128)}, u32[]{:S(2)}, u32[]{:S(2)}) collective-permute-start(f32[8,192,192]{2,1,0:T(8,128)} %shard_map.99.refs_3_), channel_id=1, source_target_pairs={{0,1},{1,2},{2,3},{3,4},{4,5},{5,6},{6,7},{8,9},{9,10},{10,11},{11... | collective-permute-start | bytes 3538952 | tf_op jit(solution)/shard_map/ppermute | solution.py:18
  159.4 3.4 %pad_maximum_fusion.1.refs_10_ = f32[16,192,192]{2,1,0:T(8,128)} fusion(f32[8,192,192]{2,1,0:T(8,128)} %shard_map.99.refs_3_, f32[8,192,192]{2,1,0:T(8,128)S(1)} %copy-done.1), kind=kLoop, calls=%fused_computation.1 | loop fusion | flops 589824 | bytes 4718592 | tf_op jit(solution)/shard_map/concatenate | solution.py:424
  162.8 15.4 %collective-permute-done.15.refs_5_ = f32[8,192,192]{2,1,0:T(8,128)} collective-permute-done((f32[8,192,192]{2,1,0:T(8,128)}, f32[8,192,192]{2,1,0:T(8,128)}, u32[]{:S(2)}, u32[]{:S(2)}) %collective-permute-start.15) | collective-permute-done | bytes 1179680 | tf_op jit(solution)/shard_map/ppermute | solution.py:19
  178.2 1.2 collective-permute-done.13.refs_1_
  179.4 14.6 %shard_map.100 = f32[16,192,192]{2,1,0:T(8,128)} custom-call(s32[32]{0:T(128)} %reshape.26.nb_ref, s32[16]{0:T(128)} %compare_select_fusion.2.size_ref, f32[32]{0:T(128)} %reshape.27.fock_ref, f32[8,192,192]{2,1,0:T(8,128)} %collective-permute-done.12.refs_0_, f32[8,192,192]{2,1,0:T(8,128)} %collective-permute-done.13.refs_1_, ...), custom_call_target="tpu_custom_call" | custom-call | flops 1811939328 | bytes 14155776 | tf_op jit(solution)/shard_map/pallas_call | solution.py:355
  (38 shorter events, 1.0 us)
Async XLA Ops:
  0.6 17.3 %collective-permute-start.1 = (bf16[4,512,256]{2,1,0:T(8,128)(2,1)}, bf16[4,512,256]{2,1,0:T(8,128)(2,1)S(1)}, u32[]{:S(2)}, u32[]{:S(2)}) collective-permute-start(bf16[4,512,256]{2,1,0:T(8,128)(2,1)} %refs_1_.3), channel_id=1, source_target_pairs={{1,0},{2,1},{3,2},{4,3},{5,4},{6,5},{7,6},{9,8},{10,9},{11,10},{12... | collective-permute-start | bytes 3145736 | tf_op jit(solution)/shard_map/ppermute | solution.py:19
  2.6 16.6 %collective-permute-start = (bf16[4,512,256]{2,1,0:T(8,128)(2,1)}, bf16[4,512,256]{2,1,0:T(8,128)(2,1)S(1)}, u32[]{:S(2)}, u32[]{:S(2)}) collective-permute-start(bf16[4,512,256]{2,1,0:T(8,128)(2,1)} %refs_1_.3), channel_id=1, source_target_pairs={{0,1},{1,2},{2,3},{3,4},{4,5},{5,6},{6,7},{8,9},{9,10},{10,11},{11... | collective-permute-start | bytes 3145736 | tf_op jit(solution)/shard_map/ppermute | solution.py:18
  17.9 1.3 copy-start.2
  19.2 1.0 copy-start.3
  27.9 11.8 %collective-permute-start.6 = (f32[4,192,192]{2,1,0:T(8,128)}, f32[4,192,192]{2,1,0:T(8,128)S(1)}, u32[]{:S(2)}, u32[]{:S(2)}) collective-permute-start(f32[4,192,192]{2,1,0:T(8,128)} %get-tuple-element.9), channel_id=1, source_target_pairs={{0,16},{8,24},{16,0},{24,8},{1,9},{9,1},{17,25},{25,17},{2,18},{10... | collective-permute-start | bytes 1769480 | tf_op jit(solution)/shard_map/ppermute | solution.py:30
  29.2 10.5 %copy-start.5 = (f32[4,192,192]{2,1,0:T(8,128)S(1)}, f32[4,192,192]{2,1,0:T(8,128)}, u32[]{:S(2)}) copy-start(f32[4,192,192]{2,1,0:T(8,128)} %get-tuple-element.8) | copy-start | bytes 1769476
  37.0 11.4 %collective-permute-start.2 = (f32[4,192,192]{2,1,0:T(8,128)}, f32[4,192,192]{2,1,0:T(8,128)}, u32[]{:S(2)}, u32[]{:S(2)}) collective-permute-start(f32[4,192,192]{2,1,0:T(8,128)} %get-tuple-element.7), channel_id=1, source_target_pairs={{0,8},{8,0},{16,24},{24,16},{1,17},{9,25},{17,1},{25,9},{2,10},{10... | collective-permute-start | bytes 1769480 | tf_op jit(solution)/shard_map/ppermute | solution.py:30
  39.7 8.7 %copy-start.6 = (f32[4,192,192]{2,1,0:T(8,128)S(1)}, f32[4,192,192]{2,1,0:T(8,128)}, u32[]{:S(2)}) copy-start(f32[4,192,192]{2,1,0:T(8,128)} %get-tuple-element.6) | copy-start | bytes 1769476
  39.9 12.5 %collective-permute-start.7 = (f32[2,192,192]{2,1,0:T(8,128)S(1)}, f32[2,192,192]{2,1,0:T(8,128)S(1)}, u32[]{:S(2)}, u32[]{:S(2)}) collective-permute-start(f32[2,192,192]{2,1,0:T(8,128)S(1)} %constant_dynamic-slice_fusion), channel_id=1, source_target_pairs={{0,8},{8,0},{16,24},{24,16},{1,17},{9,25},{17,1},{25,9},{2,10},{10... | collective-permute-start | bytes 884744 | tf_op jit(solution)/shard_map/ppermute | solution.py:30
  49.7 7.9 %collective-permute-start.3 = (f32[2,192,192]{2,1,0:T(8,128)S(1)}, f32[2,192,192]{2,1,0:T(8,128)S(1)}, u32[]{:S(2)}, u32[]{:S(2)}) collective-permute-start(f32[2,192,192]{2,1,0:T(8,128)S(1)} %constant_dynamic-slice_fusion.1), channel_id=1, source_target_pairs={{0,16},{8,24},{16,0},{24,8},{1,9},{9,1},{17,25},{25,17},{2,18},{10... | collective-permute-start | bytes 884744 | tf_op jit(solution)/shard_map/ppermute | solution.py:30
  52.5 8.7 %collective-permute-start.8 = (f32[2,192,192]{2,1,0:T(8,128)S(1)}, f32[2,192,192]{2,1,0:T(8,128)S(1)}, u32[]{:S(2)}, u32[]{:S(2)}) collective-permute-start(f32[2,192,192]{2,1,0:T(8,128)S(1)} %get-tuple-element.13), channel_id=1, source_target_pairs={{0,8},{8,0},{16,24},{24,16},{1,17},{9,25},{17,1},{25,9},{2,10},{10... | collective-permute-start | bytes 884744 | tf_op jit(solution)/shard_map/ppermute | solution.py:30
  57.8 7.4 %collective-permute-start.4 = (f32[2,192,192]{2,1,0:T(8,128)S(1)}, f32[2,192,192]{2,1,0:T(8,128)S(1)}, u32[]{:S(2)}, u32[]{:S(2)}) collective-permute-start(f32[2,192,192]{2,1,0:T(8,128)S(1)} %get-tuple-element.11), channel_id=1, source_target_pairs={{0,16},{8,24},{16,0},{24,8},{1,9},{9,1},{17,25},{25,17},{2,18},{10... | collective-permute-start | bytes 884744 | tf_op jit(solution)/shard_map/ppermute | solution.py:30
  61.2 15.5 %collective-permute-start.9 = (f32[4,192,192]{2,1,0:T(8,128)S(1)}, f32[4,192,192]{2,1,0:T(8,128)S(1)}, u32[]{:S(2)}, u32[]{:S(2)}) collective-permute-start(f32[4,192,192]{2,1,0:T(8,128)S(1)} %constant_dynamic-update-slice_fusion.2), channel_id=1, source_target_pairs={{0,16},{8,24},{16,0},{24,8},{1,9},{9,1},{17,25},{25,17},{2,18},{10... | collective-permute-start | bytes 1769480 | tf_op jit(solution)/shard_map/ppermute | solution.py:30
  65.2 18.0 %collective-permute-start.5 = (f32[4,192,192]{2,1,0:T(8,128)S(1)}, f32[4,192,192]{2,1,0:T(8,128)S(1)}, u32[]{:S(2)}, u32[]{:S(2)}) collective-permute-start(f32[4,192,192]{2,1,0:T(8,128)S(1)} %constant_dynamic-update-slice_fusion.6), channel_id=1, source_target_pairs={{0,8},{8,0},{16,24},{24,16},{1,17},{9,25},{17,1},{25,9},{2,10},{10... | collective-permute-start | bytes 1769480 | tf_op jit(solution)/shard_map/ppermute | solution.py:30
  66.9 16.3 %copy-start.7 = (f32[16,192]{1,0:T(8,128)S(1)}, f32[16,192]{1,0:T(8,128)}, u32[]{:S(2)}) copy-start(f32[16,192]{1,0:T(8,128)} %param.12) | copy-start | bytes 36868
  83.3 13.0 %copy-start.9 = (s32[16,2]{0,1:T(2,128)S(1)}, s32[16,2]{0,1:T(2,128)}, u32[]{:S(2)}) copy-start(s32[16,2]{0,1:T(2,128)} %param.14) | copy-start | bytes 388
  83.3 13.7 %copy-start.8 = (f32[16,2]{0,1:T(2,128)S(1)}, f32[16,2]{0,1:T(2,128)}, u32[]{:S(2)}) copy-start(f32[16,2]{0,1:T(2,128)} %param.15) | copy-start | bytes 388
  85.3 44.3 %copy-start = (f32[16,192,192]{2,1,0:T(8,128)}, f32[16,192,192]{2,1,0:T(8,128)S(1)}, u32[]{:S(2)}) copy-start(f32[16,192,192]{2,1,0:T(8,128)S(1)} %get-tuple-element.15.refs_1_.refs_7_) | copy-start | bytes 7077892
  85.3 43.3 %collective-permute-start.11 = (f32[16,192,192]{2,1,0:T(8,128)S(1)}, f32[16,192,192]{2,1,0:T(8,128)}, u32[]{:S(2)}, u32[]{:S(2)}) collective-permute-start(f32[16,192,192]{2,1,0:T(8,128)S(1)} %get-tuple-element.15.refs_1_.refs_7_), channel_id=1, source_target_pairs={{1,0},{2,1},{3,2},{4,3},{5,4},{6,5},{7,6},{9,8},{10,9},{11,10},{12... | collective-permute-start | bytes 7077896 | tf_op jit(solution)/shard_map/ppermute | solution.py:19
  87.2 42.4 %collective-permute-start.10 = (f32[16,192,192]{2,1,0:T(8,128)S(1)}, f32[16,192,192]{2,1,0:T(8,128)}, u32[]{:S(2)}, u32[]{:S(2)}) collective-permute-start(f32[16,192,192]{2,1,0:T(8,128)S(1)} %get-tuple-element.15.refs_1_.refs_7_), channel_id=1, source_target_pairs={{0,1},{1,2},{2,3},{3,4},{4,5},{5,6},{6,7},{8,9},{9,10},{10,11},{11... | collective-permute-start | bytes 7077896 | tf_op jit(solution)/shard_map/ppermute | solution.py:18
  138.3 21.1 %copy-start.1 = (f32[8,192,192]{2,1,0:T(8,128)S(1)}, f32[8,192,192]{2,1,0:T(8,128)}, u32[]{:S(2)}) copy-start(f32[8,192,192]{2,1,0:T(8,128)} %shard_map.98.refs_2_) | copy-start | bytes 3538948
  138.3 24.5 %collective-permute-start.14 = (f32[8,192,192]{2,1,0:T(8,128)}, f32[8,192,192]{2,1,0:T(8,128)S(1)}, u32[]{:S(2)}, u32[]{:S(2)}) collective-permute-start(f32[8,192,192]{2,1,0:T(8,128)} %shard_map.98.refs_2_), channel_id=1, source_target_pairs={{1,0},{2,1},{3,2},{4,3},{5,4},{6,5},{7,6},{9,8},{10,9},{11,10},{12... | collective-permute-start | bytes 3538952 | tf_op jit(solution)/shard_map/ppermute | solution.py:19
  140.4 22.4 %collective-permute-start.12 = (f32[8,192,192]{2,1,0:T(8,128)}, f32[8,192,192]{2,1,0:T(8,128)}, u32[]{:S(2)}, u32[]{:S(2)}) collective-permute-start(f32[8,192,192]{2,1,0:T(8,128)} %shard_map.98.refs_2_), channel_id=1, source_target_pairs={{0,1},{1,2},{2,3},{3,4},{4,5},{5,6},{6,7},{8,9},{9,10},{10,11},{11... | collective-permute-start | bytes 3538952 | tf_op jit(solution)/shard_map/ppermute | solution.py:18
  153.6 24.7 %collective-permute-start.15 = (f32[8,192,192]{2,1,0:T(8,128)}, f32[8,192,192]{2,1,0:T(8,128)}, u32[]{:S(2)}, u32[]{:S(2)}) collective-permute-start(f32[8,192,192]{2,1,0:T(8,128)} %shard_map.99.refs_3_), channel_id=1, source_target_pairs={{1,0},{2,1},{3,2},{4,3},{5,4},{6,5},{7,6},{9,8},{10,9},{11,10},{12... | collective-permute-start | bytes 3538952 | tf_op jit(solution)/shard_map/ppermute | solution.py:19
  155.5 23.9 %collective-permute-start.13 = (f32[8,192,192]{2,1,0:T(8,128)}, f32[8,192,192]{2,1,0:T(8,128)}, u32[]{:S(2)}, u32[]{:S(2)}) collective-permute-start(f32[8,192,192]{2,1,0:T(8,128)} %shard_map.99.refs_3_), channel_id=1, source_target_pairs={{0,1},{1,2},{2,3},{3,4},{4,5},{5,6},{6,7},{8,9},{9,10},{10,11},{11... | collective-permute-start | bytes 3538952 | tf_op jit(solution)/shard_map/ppermute | solution.py:18
  162.8 16.6 %copy-start.4 = (f32[8,192,192]{2,1,0:T(8,128)}, f32[8,192,192]{2,1,0:T(8,128)S(1)}, u32[]{:S(2)}) copy-start(f32[8,192,192]{2,1,0:T(8,128)S(1)} %collective-permute-done.14.refs_4_) | copy-start | bytes 3538948

commit v20 on v18

--- a/solution.py
+++ b/solution.py
@@ -30,18 +30,30 @@
     return lax.ppermute(value, ("aux", "pair"), perm)
 
 
+def sum_pair(kept, received):
+    return kept + received
+
+
 def halving_stream(piece, index, parity, bits, presplit=False):
     steps = [(b, o) for b, o in zip(bits, reversed(bits))]
     for step, (bit_even, bit_odd) in enumerate(steps):
         bit = jnp.where(parity == 0, bit_even, bit_odd)
         side = (index // bit) % 2
-        half = piece[0].shape[0] if presplit and step == 0 else piece.shape[0] // 2
+        half = piece[0].shape[0] if presplit and step == 0 else None
         if presplit and step == 0:
             send, keep = piece
+        elif isinstance(piece, tuple):
+            def cut(offset):
+                return sum_pair(*(lax.dynamic_slice_in_dim(v, offset, half, axis=0) for v in piece))
+
+            half = piece[0].shape[0] // 2
+            keep, send = cut(side * half), cut((1 - side) * half)
         else:
+            half = piece.shape[0] // 2
             keep = lax.dynamic_slice_in_dim(piece, side * half, half, axis=0)
             send = lax.dynamic_slice_in_dim(piece, (1 - side) * half, half, axis=0)
-        piece = keep + swap_over_aux(send, bit_even, bit_odd)
+        piece = (keep, swap_over_aux(send, bit_even, bit_odd))
+    piece = sum_pair(*piece)
     for bit_even, bit_odd in reversed(steps):
         bit = jnp.where(parity == 0, bit_even, bit_odd)
         side = (index // bit) % 2

time: 194 us -> 196 us (1.010)
  transfers between devices with their start and end apart: 16 -> 16, of which waited for: 14 -> 13; matrix products, arithmetic and copies ran while one was open for 6% -> 7% of each run, Pallas kernels for 13% -> 13%
where the time goes in v20:
time: 196 us; the launch traced here: 195 us
  waiting for transfers between devices  84.3 us (43%)
  Pallas kernels  54.1 us (28%)
  starting transfers between devices  38.7 us (20%)
  other arithmetic  10.9 us (6%)
  local copies, waits for them, and re-layouts  5.36 us (3%)
    ppermute x4, waiting for transfers between devices, halo_sources(): from_right = lax.ppermute(cells, axis, [(i + 1, i) for i in range(ends)])  44.7 us
    ppermute x8, waiting for transfers between devices, swap_over_aux(): return lax.ppermute(value, ('aux', 'pair'), perm)  36 us
    pallas_call x3, Pallas kernels, coupling_step(): pl.pallas_call(kernel, grid_spec=grid_spec, out_shape=jax.ShapeDtypeStruc...  30.1 us
    ppermute x4, starting transfers between devices, halo_sources(): from_left = lax.ppermute(cells, axis, [(i, i + 1) for i in range(ends)])  21.4 us
    pallas_call x2, Pallas kernels, partial_exchange(): pl.pallas_call(functools.partial(exchange_kernel, occ=occ, group=group, s...  15.8 us
    ppermute x8, starting transfers between devices, swap_over_aux(): return lax.ppermute(value, ('aux', 'pair'), perm)  9.48 us
    pallas_call x1, Pallas kernels, left_halves(): pl.pallas_call(functools.partial(left_kernel, occ=occ, group=group), grid...  8.26 us
    ppermute x4, starting transfers between devices, halo_sources(): from_right = lax.ppermute(cells, axis, [(i + 1, i) for i in range(ends)])  7.85 us
  transfers between devices with their start and end apart: 16, of which 13 were waited for; matrix products, arithmetic and copies ran while one was open for 7% of the time, Pallas kernels for 13%

profile of v20, /device:TPU:1, one launch (start us, length us, event | category | flops | bytes accessed | tf_op | source)
XLA Modules:
  0.0 194.5 jit_solution(4858354401872622793)
XLA Ops:
  0.6 2.0 %collective-permute-start.1 = (bf16[4,512,256]{2,1,0:T(8,128)(2,1)}, bf16[4,512,256]{2,1,0:T(8,128)(2,1)S(1)}, u32[]{:S(2)}, u32[]{:S(2)}) collective-permute-start(bf16[4,512,256]{2,1,0:T(8,128)(2,1)} %refs_1_.3), channel_id=1, source_target_pairs={{1,0},{2,1},{3,2},{4,3},{5,4},{6,5},{7,6},{9,8},{10,9},{11,10},{12... | collective-permute-start | bytes 3145736 | tf_op jit(solution)/shard_map/ppermute | solution.py:19
  2.6 4.6 %collective-permute-start = (bf16[4,512,256]{2,1,0:T(8,128)(2,1)}, bf16[4,512,256]{2,1,0:T(8,128)(2,1)S(1)}, u32[]{:S(2)}, u32[]{:S(2)}) collective-permute-start(bf16[4,512,256]{2,1,0:T(8,128)(2,1)} %refs_1_.3), channel_id=1, source_target_pairs={{0,1},{1,2},{2,3},{3,4},{4,5},{5,6},{6,7},{8,9},{9,10},{10,11},{11... | collective-permute-start | bytes 3145736 | tf_op jit(solution)/shard_map/ppermute | solution.py:18
  7.2 1.2 compare_select_fusion.2.size_ref
  8.4 0.7 broadcast_subtract_fusion
  9.1 0.6 slice_bitcast_fusion
  9.7 8.3 %shard_map.95.refs_3_ = bf16[16,192,512]{2,1,0:T(8,128)(2,1)} custom-call(s32[16]{0:T(128)} %get-tuple-element.17.lead_ref, s32[16]{0:T(128)} %compare_select_fusion.2.size_ref, bf16[4,512,256]{2,1,0:T(8,128)(2,1)} %refs_1_.3, bf16[16,2,192,256]{3,2,1,0:T(8,128)(2,1)} %bitcast.8), custom_call_target="tpu_custom_call" | custom-call | flops 805306368 | bytes 10485760 | tf_op jit(solution)/shard_map/pallas_call | solution.py:165
  17.9 1.3 collective-permute-done.refs_0_
  19.2 1.0 copy-done.3
  20.2 7.8 %shard_map.97 = (f32[4,192,192]{2,1,0:T(8,128)}, f32[4,192,192]{2,1,0:T(8,128)}) custom-call(s32[16]{0:T(128)} %get-tuple-element.17.lead_ref, s32[16]{0:T(128)} %get-tuple-element.16.trail_ref, s32[16]{0:T(128)} %compare_select_fusion.2.size_ref, s32[1]{0:T(128)} %bitcast.4.flip_ref, bf16[4,512,256]{2,1,0:T(8,128)(2,1)} %copy-done.3, ...), custom_call_target="tpu_custom_call" | custom-call | flops 1107296256 | bytes 6946816 | tf_op jit(solution)/shard_map/pallas_call | solution.py:265
  27.9 1.3 collective-permute-start.6
  29.2 8.0 %shard_map.96 = (f32[4,192,192]{2,1,0:T(8,128)}, f32[4,192,192]{2,1,0:T(8,128)}) custom-call(s32[16]{0:T(128)} %get-tuple-element.17.lead_ref, s32[16]{0:T(128)} %get-tuple-element.16.trail_ref, s32[16]{0:T(128)} %compare_select_fusion.2.size_ref, s32[1]{0:T(128)} %bitcast.2.flip_ref, bf16[4,512,256]{2,1,0:T(8,128)(2,1)} %copy-done.3, ...), custom_call_target="tpu_custom_call" | custom-call | flops 1107296256 | bytes 6946816 | tf_op jit(solution)/shard_map/pallas_call | solution.py:265
  37.2 1.3 collective-permute-start.2
  38.5 0.5 collective-permute-done.6
  39.1 2.9 %collective-permute-start.7 = (f32[2,192,192]{2,1,0:T(8,128)S(1)}, f32[2,192,192]{2,1,0:T(8,128)S(1)}, u32[]{:S(2)}, u32[]{:S(2)}) collective-permute-start(f32[2,192,192]{2,1,0:T(8,128)S(1)} %dynamic-slice_add_fusion), channel_id=1, source_target_pairs={{0,8},{8,0},{16,24},{24,16},{1,17},{9,25},{17,1},{25,9},{2,10},{10... | collective-permute-start | bytes 884744 | tf_op jit(solution)/shard_map/ppermute | solution.py:30
  42.0 6.6 %collective-permute-done.2 = f32[4,192,192]{2,1,0:T(8,128)S(1)} collective-permute-done((f32[4,192,192]{2,1,0:T(8,128)}, f32[4,192,192]{2,1,0:T(8,128)S(1)}, u32[]{:S(2)}, u32[]{:S(2)}) %collective-permute-start.2) | collective-permute-done | bytes 589856 | tf_op jit(solution)/shard_map/ppermute | solution.py:30
  48.6 1.8 dynamic-slice_add_fusion.1
  50.4 0.3 collective-permute-start.3
  50.7 1.9 collective-permute-done.7
  52.7 1.3 collective-permute-start.8
  54.0 5.3 %collective-permute-done.3 = f32[2,192,192]{2,1,0:T(8,128)} collective-permute-done((f32[2,192,192]{2,1,0:T(8,128)}, f32[2,192,192]{2,1,0:T(8,128)}, u32[]{:S(2)}, u32[]{:S(2)}) %collective-permute-start.3) | collective-permute-done | bytes 294944 | tf_op jit(solution)/shard_map/ppermute | solution.py:30
  59.4 1.1 constant_dynamic-update-slice_fusion.6
  60.6 1.2 collective-permute-done.8
  61.8 1.0 collective-permute-start.9
  62.8 4.7 %collective-permute-done.4 = f32[2,192,192]{2,1,0:T(8,128)S(1)} collective-permute-done((f32[2,192,192]{2,1,0:T(8,128)S(1)}, f32[2,192,192]{2,1,0:T(8,128)S(1)}, u32[]{:S(2)}, u32[]{:S(2)}) %collective-permute-start.4) | collective-permute-done | bytes 294944 | tf_op jit(solution)/shard_map/ppermute | solution.py:30
  67.5 1.3 collective-permute-start.5
  68.9 0.1 broadcast.29.clone
  69.1 0.1 broadcast.29.clone.1
  69.3 9.9 %collective-permute-done.9 = f32[4,192,192]{2,1,0:T(8,128)S(1)} collective-permute-done((f32[4,192,192]{2,1,0:T(8,128)S(1)}, f32[4,192,192]{2,1,0:T(8,128)S(1)}, u32[]{:S(2)}, u32[]{:S(2)}) %collective-permute-start.9) | collective-permute-done | bytes 589856 | tf_op jit(solution)/shard_map/ppermute | solution.py:30
  79.2 6.0 %collective-permute-done.5 = f32[4,192,192]{2,1,0:T(8,128)S(1)} collective-permute-done((f32[4,192,192]{2,1,0:T(8,128)S(1)}, f32[4,192,192]{2,1,0:T(8,128)S(1)}, u32[]{:S(2)}, u32[]{:S(2)}) %collective-permute-start.5) | collective-permute-done | bytes 589856 | tf_op jit(solution)/shard_map/ppermute | solution.py:30
  85.3 2.0 %pad_maximum_fusion = (f32[16,192,192]{2,1,0:T(8,128)}, f32[16,192,192]{2,1,0:T(8,128)S(1)}) fusion(f32[8,192,192]{2,1,0:T(8,128)S(1)} %constant_dynamic-update-slice_fusion.2, f32[8,192,192]{2,1,0:T(8,128)S(1)} %constant_dynamic-update-slice_fusion.3, f32[16,192]{1,0:T(8,128)S(1)} %copy-done.7), kind=kLoop, calls=%fused_computation | loop fusion | flops 2359296 | bytes 7090176 | tf_op jit(solution)/shard_map/concatenate | solution.py:90
  87.4 1.9 collective-permute-start.11
  89.3 8.4 %collective-permute-start.10 = (f32[16,192,192]{2,1,0:T(8,128)S(1)}, f32[16,192,192]{2,1,0:T(8,128)}, u32[]{:S(2)}, u32[]{:S(2)}) collective-permute-start(f32[16,192,192]{2,1,0:T(8,128)S(1)} %get-tuple-element.15.refs_1_.refs_7_), channel_id=1, source_target_pairs={{0,1},{1,2},{2,3},{3,4},{4,5},{5,6},{6,7},{8,9},{9,10},{10,11},{11... | collective-permute-start | bytes 7077896 | tf_op jit(solution)/shard_map/ppermute | solution.py:18
  97.7 0.6 broadcast_in_dim.26.refs_6_.refs_9_
  98.4 0.6 reshape.26.nb_ref
  99.1 0.6 reshape.27.fock_ref
  99.7 1.7 copy.14.refs_5_.refs_8_
  101.4 29.3 %collective-permute-done.11.refs_2_ = f32[16,192,192]{2,1,0:T(8,128)} collective-permute-done((f32[16,192,192]{2,1,0:T(8,128)S(1)}, f32[16,192,192]{2,1,0:T(8,128)}, u32[]{:S(2)}, u32[]{:S(2)}) %collective-permute-start.11) | collective-permute-done | bytes 2359328 | tf_op jit(solution)/shard_map/ppermute | solution.py:19
  130.7 1.1 collective-permute-done.10.refs_0_
  131.7 8.5 %shard_map.98.refs_2_ = f32[8,192,192]{2,1,0:T(8,128)} custom-call(s32[32]{0:T(128)} %reshape.26.nb_ref, s32[16]{0:T(128)} %compare_select_fusion.2.size_ref, f32[32]{0:T(128)} %reshape.27.fock_ref, f32[16,192,192]{2,1,0:T(8,128)} %collective-permute-done.10.refs_0_, f32[16,192,192]{2,1,0:T(8,128)} %copy-done, ...), custom_call_target="tpu_custom_call" | custom-call | flops 905969664 | bytes 7077888 | tf_op jit(solution)/shard_map/pallas_call | solution.py:367
  140.3 2.1 %collective-permute-start.14 = (f32[8,192,192]{2,1,0:T(8,128)}, f32[8,192,192]{2,1,0:T(8,128)S(1)}, u32[]{:S(2)}, u32[]{:S(2)}) collective-permute-start(f32[8,192,192]{2,1,0:T(8,128)} %shard_map.98.refs_2_), channel_id=1, source_target_pairs={{1,0},{2,1},{3,2},{4,3},{5,4},{6,5},{7,6},{9,8},{10,9},{11,10},{12... | collective-permute-start | bytes 3538952 | tf_op jit(solution)/shard_map/ppermute | solution.py:19
  142.4 4.6 %collective-permute-start.12 = (f32[8,192,192]{2,1,0:T(8,128)}, f32[8,192,192]{2,1,0:T(8,128)}, u32[]{:S(2)}, u32[]{:S(2)}) collective-permute-start(f32[8,192,192]{2,1,0:T(8,128)} %shard_map.98.refs_2_), channel_id=1, source_target_pairs={{0,1},{1,2},{2,3},{3,4},{4,5},{5,6},{6,7},{8,9},{9,10},{10,11},{11... | collective-permute-start | bytes 3538952 | tf_op jit(solution)/shard_map/ppermute | solution.py:18
  146.9 8.6 %shard_map.99.refs_3_ = f32[8,192,192]{2,1,0:T(8,128)} custom-call(s32[32]{0:T(128)} %reshape.26.nb_ref, s32[16]{0:T(128)} %compare_select_fusion.2.size_ref, f32[32]{0:T(128)} %reshape.27.fock_ref, f32[16,192,192]{2,1,0:T(8,128)} %collective-permute-done.10.refs_0_, f32[16,192,192]{2,1,0:T(8,128)} %copy-done, ...), custom_call_target="tpu_custom_call" | custom-call | flops 905969664 | bytes 7077888 | tf_op jit(solution)/shard_map/pallas_call | solution.py:367
  155.6 1.9 collective-permute-start.15
  157.5 3.9 %collective-permute-start.13 = (f32[8,192,192]{2,1,0:T(8,128)}, f32[8,192,192]{2,1,0:T(8,128)}, u32[]{:S(2)}, u32[]{:S(2)}) collective-permute-start(f32[8,192,192]{2,1,0:T(8,128)} %shard_map.99.refs_3_), channel_id=1, source_target_pairs={{0,1},{1,2},{2,3},{3,4},{4,5},{5,6},{6,7},{8,9},{9,10},{10,11},{11... | collective-permute-start | bytes 3538952 | tf_op jit(solution)/shard_map/ppermute | solution.py:18
  161.4 3.4 %pad_maximum_fusion.1.refs_10_ = f32[16,192,192]{2,1,0:T(8,128)} fusion(f32[8,192,192]{2,1,0:T(8,128)} %shard_map.99.refs_3_, f32[8,192,192]{2,1,0:T(8,128)S(1)} %copy-done.1), kind=kLoop, calls=%fused_computation.1 | loop fusion | flops 589824 | bytes 4718592 | tf_op jit(solution)/shard_map/concatenate | solution.py:436
  164.8 15.4 %collective-permute-done.15.refs_5_ = f32[8,192,192]{2,1,0:T(8,128)} collective-permute-done((f32[8,192,192]{2,1,0:T(8,128)}, f32[8,192,192]{2,1,0:T(8,128)}, u32[]{:S(2)}, u32[]{:S(2)}) %collective-permute-start.15) | collective-permute-done | bytes 1179680 | tf_op jit(solution)/shard_map/ppermute | solution.py:19
  180.3 1.2 collective-permute-done.13.refs_1_
  181.5 12.9 %shard_map.100 = f32[16,192,192]{2,1,0:T(8,128)} custom-call(s32[32]{0:T(128)} %reshape.26.nb_ref, s32[16]{0:T(128)} %compare_select_fusion.2.size_ref, f32[32]{0:T(128)} %reshape.27.fock_ref, f32[8,192,192]{2,1,0:T(8,128)} %collective-permute-done.12.refs_0_, f32[8,192,192]{2,1,0:T(8,128)} %collective-permute-done.13.refs_1_, ...), custom_call_target="tpu_custom_call" | custom-call | flops 1811939328 | bytes 14155776 | tf_op jit(solution)/shard_map/pallas_call | solution.py:367
  (36 shorter events, 0.9 us)
Async XLA Ops:
  0.6 17.3 %collective-permute-start.1 = (bf16[4,512,256]{2,1,0:T(8,128)(2,1)}, bf16[4,512,256]{2,1,0:T(8,128)(2,1)S(1)}, u32[]{:S(2)}, u32[]{:S(2)}) collective-permute-start(bf16[4,512,256]{2,1,0:T(8,128)(2,1)} %refs_1_.3), channel_id=1, source_target_pairs={{1,0},{2,1},{3,2},{4,3},{5,4},{6,5},{7,6},{9,8},{10,9},{11,10},{12... | collective-permute-start | bytes 3145736 | tf_op jit(solution)/shard_map/ppermute | solution.py:19
  2.6 16.6 %collective-permute-start = (bf16[4,512,256]{2,1,0:T(8,128)(2,1)}, bf16[4,512,256]{2,1,0:T(8,128)(2,1)S(1)}, u32[]{:S(2)}, u32[]{:S(2)}) collective-permute-start(bf16[4,512,256]{2,1,0:T(8,128)(2,1)} %refs_1_.3), channel_id=1, source_target_pairs={{0,1},{1,2},{2,3},{3,4},{4,5},{5,6},{6,7},{8,9},{9,10},{10,11},{11... | collective-permute-start | bytes 3145736 | tf_op jit(solution)/shard_map/ppermute | solution.py:18
  17.9 1.3 copy-start.2
  19.2 1.0 copy-start.3
  27.9 11.1 %collective-permute-start.6 = (f32[4,192,192]{2,1,0:T(8,128)}, f32[4,192,192]{2,1,0:T(8,128)S(1)}, u32[]{:S(2)}, u32[]{:S(2)}) collective-permute-start(f32[4,192,192]{2,1,0:T(8,128)} %get-tuple-element.9), channel_id=1, source_target_pairs={{0,16},{8,24},{16,0},{24,8},{1,9},{9,1},{17,25},{25,17},{2,18},{10... | collective-permute-start | bytes 1769480 | tf_op jit(solution)/shard_map/ppermute | solution.py:30
  29.2 9.8 %copy-start.5 = (f32[4,192,192]{2,1,0:T(8,128)S(1)}, f32[4,192,192]{2,1,0:T(8,128)}, u32[]{:S(2)}) copy-start(f32[4,192,192]{2,1,0:T(8,128)} %get-tuple-element.8) | copy-start | bytes 1769476
  37.2 11.4 %collective-permute-start.2 = (f32[4,192,192]{2,1,0:T(8,128)}, f32[4,192,192]{2,1,0:T(8,128)S(1)}, u32[]{:S(2)}, u32[]{:S(2)}) collective-permute-start(f32[4,192,192]{2,1,0:T(8,128)} %get-tuple-element.7), channel_id=1, source_target_pairs={{0,8},{8,0},{16,24},{24,16},{1,17},{9,25},{17,1},{25,9},{2,10},{10... | collective-permute-start | bytes 1769480 | tf_op jit(solution)/shard_map/ppermute | solution.py:30
  39.1 13.5 %collective-permute-start.7 = (f32[2,192,192]{2,1,0:T(8,128)S(1)}, f32[2,192,192]{2,1,0:T(8,128)S(1)}, u32[]{:S(2)}, u32[]{:S(2)}) collective-permute-start(f32[2,192,192]{2,1,0:T(8,128)S(1)} %dynamic-slice_add_fusion), channel_id=1, source_target_pairs={{0,8},{8,0},{16,24},{24,16},{1,17},{9,25},{17,1},{25,9},{2,10},{10... | collective-permute-start | bytes 884744 | tf_op jit(solution)/shard_map/ppermute | solution.py:30
  50.4 8.9 %collective-permute-start.3 = (f32[2,192,192]{2,1,0:T(8,128)}, f32[2,192,192]{2,1,0:T(8,128)}, u32[]{:S(2)}, u32[]{:S(2)}) collective-permute-start(f32[2,192,192]{2,1,0:T(8,128)} %dynamic-slice_add_fusion.1), channel_id=1, source_target_pairs={{0,16},{8,24},{16,0},{24,8},{1,9},{9,1},{17,25},{25,17},{2,18},{10... | collective-permute-start | bytes 884744 | tf_op jit(solution)/shard_map/ppermute | solution.py:30
  52.6 6.8 %copy-start.6 = (f32[4,192,192]{2,1,0:T(8,128)S(1)}, f32[4,192,192]{2,1,0:T(8,128)}, u32[]{:S(2)}) copy-start(f32[4,192,192]{2,1,0:T(8,128)} %get-tuple-element.6) | copy-start | bytes 1769476
  52.7 9.0 %collective-permute-start.8 = (f32[2,192,192]{2,1,0:T(8,128)S(1)}, f32[2,192,192]{2,1,0:T(8,128)S(1)}, u32[]{:S(2)}, u32[]{:S(2)}) collective-permute-start(f32[2,192,192]{2,1,0:T(8,128)S(1)} %get-tuple-element.13), channel_id=1, source_target_pairs={{0,8},{8,0},{16,24},{24,16},{1,17},{9,25},{17,1},{25,9},{2,10},{10... | collective-permute-start | bytes 884744 | tf_op jit(solution)/shard_map/ppermute | solution.py:30
  60.5 7.0 %collective-permute-start.4 = (f32[2,192,192]{2,1,0:T(8,128)S(1)}, f32[2,192,192]{2,1,0:T(8,128)S(1)}, u32[]{:S(2)}, u32[]{:S(2)}) collective-permute-start(f32[2,192,192]{2,1,0:T(8,128)S(1)} %get-tuple-element.11), channel_id=1, source_target_pairs={{0,16},{8,24},{16,0},{24,8},{1,9},{9,1},{17,25},{25,17},{2,18},{10... | collective-permute-start | bytes 884744 | tf_op jit(solution)/shard_map/ppermute | solution.py:30
  61.8 17.4 %collective-permute-start.9 = (f32[4,192,192]{2,1,0:T(8,128)S(1)}, f32[4,192,192]{2,1,0:T(8,128)S(1)}, u32[]{:S(2)}, u32[]{:S(2)}) collective-permute-start(f32[4,192,192]{2,1,0:T(8,128)S(1)} %constant_dynamic-update-slice_fusion), channel_id=1, source_target_pairs={{0,16},{8,24},{16,0},{24,8},{1,9},{9,1},{17,25},{25,17},{2,18},{10... | collective-permute-start | bytes 1769480 | tf_op jit(solution)/shard_map/ppermute | solution.py:30
  67.5 17.7 %collective-permute-start.5 = (f32[4,192,192]{2,1,0:T(8,128)S(1)}, f32[4,192,192]{2,1,0:T(8,128)S(1)}, u32[]{:S(2)}, u32[]{:S(2)}) collective-permute-start(f32[4,192,192]{2,1,0:T(8,128)S(1)} %constant_dynamic-update-slice_fusion.5), channel_id=1, source_target_pairs={{0,8},{8,0},{16,24},{24,16},{1,17},{9,25},{17,1},{25,9},{2,10},{10... | collective-permute-start | bytes 1769480 | tf_op jit(solution)/shard_map/ppermute | solution.py:30
  69.3 16.0 %copy-start.7 = (f32[16,192]{1,0:T(8,128)S(1)}, f32[16,192]{1,0:T(8,128)}, u32[]{:S(2)}) copy-start(f32[16,192]{1,0:T(8,128)} %param.12) | copy-start | bytes 36868
  85.3 13.0 %copy-start.9 = (s32[16,2]{0,1:T(2,128)S(1)}, s32[16,2]{0,1:T(2,128)}, u32[]{:S(2)}) copy-start(s32[16,2]{0,1:T(2,128)} %param.14) | copy-start | bytes 388
  85.3 13.7 %copy-start.8 = (f32[16,2]{0,1:T(2,128)S(1)}, f32[16,2]{0,1:T(2,128)}, u32[]{:S(2)}) copy-start(f32[16,2]{0,1:T(2,128)} %param.15) | copy-start | bytes 388
  87.4 44.4 %copy-start = (f32[16,192,192]{2,1,0:T(8,128)}, f32[16,192,192]{2,1,0:T(8,128)S(1)}, u32[]{:S(2)}) copy-start(f32[16,192,192]{2,1,0:T(8,128)S(1)} %get-tuple-element.15.refs_1_.refs_7_) | copy-start | bytes 7077892
  87.4 43.3 %collective-permute-start.11 = (f32[16,192,192]{2,1,0:T(8,128)S(1)}, f32[16,192,192]{2,1,0:T(8,128)}, u32[]{:S(2)}, u32[]{:S(2)}) collective-permute-start(f32[16,192,192]{2,1,0:T(8,128)S(1)} %get-tuple-element.15.refs_1_.refs_7_), channel_id=1, source_target_pairs={{1,0},{2,1},{3,2},{4,3},{5,4},{6,5},{7,6},{9,8},{10,9},{11,10},{12... | collective-permute-start | bytes 7077896 | tf_op jit(solution)/shard_map/ppermute | solution.py:19
  89.3 42.4 %collective-permute-start.10 = (f32[16,192,192]{2,1,0:T(8,128)S(1)}, f32[16,192,192]{2,1,0:T(8,128)}, u32[]{:S(2)}, u32[]{:S(2)}) collective-permute-start(f32[16,192,192]{2,1,0:T(8,128)S(1)} %get-tuple-element.15.refs_1_.refs_7_), channel_id=1, source_target_pairs={{0,1},{1,2},{2,3},{3,4},{4,5},{5,6},{6,7},{8,9},{9,10},{10,11},{11... | collective-permute-start | bytes 7077896 | tf_op jit(solution)/shard_map/ppermute | solution.py:18
  140.3 21.1 %copy-start.1 = (f32[8,192,192]{2,1,0:T(8,128)S(1)}, f32[8,192,192]{2,1,0:T(8,128)}, u32[]{:S(2)}) copy-start(f32[8,192,192]{2,1,0:T(8,128)} %shard_map.98.refs_2_) | copy-start | bytes 3538948
  140.3 24.5 %collective-permute-start.14 = (f32[8,192,192]{2,1,0:T(8,128)}, f32[8,192,192]{2,1,0:T(8,128)S(1)}, u32[]{:S(2)}, u32[]{:S(2)}) collective-permute-start(f32[8,192,192]{2,1,0:T(8,128)} %shard_map.98.refs_2_), channel_id=1, source_target_pairs={{1,0},{2,1},{3,2},{4,3},{5,4},{6,5},{7,6},{9,8},{10,9},{11,10},{12... | collective-permute-start | bytes 3538952 | tf_op jit(solution)/shard_map/ppermute | solution.py:19
  142.4 22.5 %collective-permute-start.12 = (f32[8,192,192]{2,1,0:T(8,128)}, f32[8,192,192]{2,1,0:T(8,128)}, u32[]{:S(2)}, u32[]{:S(2)}) collective-permute-start(f32[8,192,192]{2,1,0:T(8,128)} %shard_map.98.refs_2_), channel_id=1, source_target_pairs={{0,1},{1,2},{2,3},{3,4},{4,5},{5,6},{6,7},{8,9},{9,10},{10,11},{11... | collective-permute-start | bytes 3538952 | tf_op jit(solution)/shard_map/ppermute | solution.py:18
  155.6 24.7 %collective-permute-start.15 = (f32[8,192,192]{2,1,0:T(8,128)}, f32[8,192,192]{2,1,0:T(8,128)}, u32[]{:S(2)}, u32[]{:S(2)}) collective-permute-start(f32[8,192,192]{2,1,0:T(8,128)} %shard_map.99.refs_3_), channel_id=1, source_target_pairs={{1,0},{2,1},{3,2},{4,3},{5,4},{6,5},{7,6},{9,8},{10,9},{11,10},{12... | collective-permute-start | bytes 3538952 | tf_op jit(solution)/shard_map/ppermute | solution.py:19
  157.5 23.9 %collective-permute-start.13 = (f32[8,192,192]{2,1,0:T(8,128)}, f32[8,192,192]{2,1,0:T(8,128)}, u32[]{:S(2)}, u32[]{:S(2)}) collective-permute-start(f32[8,192,192]{2,1,0:T(8,128)} %shard_map.99.refs_3_), channel_id=1, source_target_pairs={{0,1},{1,2},{2,3},{3,4},{4,5},{5,6},{6,7},{8,9},{9,10},{10,11},{11... | collective-permute-start | bytes 3538952 | tf_op jit(solution)/shard_map/ppermute | solution.py:18
  164.8 16.6 %copy-start.4 = (f32[8,192,192]{2,1,0:T(8,128)}, f32[8,192,192]{2,1,0:T(8,128)S(1)}, u32[]{:S(2)}) copy-start(f32[8,192,192]{2,1,0:T(8,128)S(1)} %collective-permute-done.14.refs_4_) | copy-start | bytes 3538948

commit v21 on v18

--- a/solution.py
+++ b/solution.py
@@ -46,10 +46,9 @@
         bit = jnp.where(parity == 0, bit_even, bit_odd)
         side = (index // bit) % 2
         other = swap_over_aux(piece, bit_even, bit_odd)
-        length = piece.shape[0]
-        full = jnp.zeros((2 * length,) + piece.shape[1:], piece.dtype)
-        full = lax.dynamic_update_slice_in_dim(full, piece, side * length, axis=0)
-        piece = lax.dynamic_update_slice_in_dim(full, other, (1 - side) * length, axis=0)
+        piece = jnp.where(
+            side == 0, jnp.concatenate([piece, other], axis=0), jnp.concatenate([other, piece], axis=0)
+        )
     return piece
 
 

time: 194 us -> 195 us (level)
  no operation moved by 1% of the time
where the time goes in v21:
time: 195 us; the launch traced here: 194 us
  waiting for transfers between devices  84.1 us (43%)
  Pallas kernels  54.4 us (28%)
  starting transfers between devices  40.2 us (21%)
  other arithmetic  9.7 us (5%)
  local copies, waits for them, and re-layouts  4.74 us (2%)
    ppermute x4, waiting for transfers between devices, halo_sources(): from_right = lax.ppermute(cells, axis, [(i + 1, i) for i in range(ends)])  44.8 us
    ppermute x8, waiting for transfers between devices, swap_over_aux(): return lax.ppermute(value, ('aux', 'pair'), perm)  35.7 us
    pallas_call x3, Pallas kernels, coupling_step(): pl.pallas_call(kernel, grid_spec=grid_spec, out_shape=jax.ShapeDtypeStruc...  30.6 us
    ppermute x4, starting transfers between devices, halo_sources(): from_left = lax.ppermute(cells, axis, [(i, i + 1) for i in range(ends)])  22.8 us
    pallas_call x2, Pallas kernels, partial_exchange(): pl.pallas_call(functools.partial(exchange_kernel, occ=occ, group=group, s...  15.6 us
    ppermute x8, starting transfers between devices, swap_over_aux(): return lax.ppermute(value, ('aux', 'pair'), perm)  9.58 us
    pallas_call x1, Pallas kernels, left_halves(): pl.pallas_call(functools.partial(left_kernel, occ=occ, group=group), grid...  8.2 us
    ppermute x4, starting transfers between devices, halo_sources(): from_right = lax.ppermute(cells, axis, [(i + 1, i) for i in range(ends)])  7.85 us
  transfers between devices with their start and end apart: 16, of which 14 were waited for; matrix products, arithmetic and copies ran while one was open for 6% of the time, Pallas kernels for 13%

profile of v21, /device:TPU:1, one launch (start us, length us, event | category | flops | bytes accessed | tf_op | source)
XLA Modules:
  0.0 194.3 jit_solution(13689741728285399089)
XLA Ops:
  0.6 2.0 %collective-permute-start.1 = (bf16[4,512,256]{2,1,0:T(8,128)(2,1)}, bf16[4,512,256]{2,1,0:T(8,128)(2,1)S(1)}, u32[]{:S(2)}, u32[]{:S(2)}) collective-permute-start(bf16[4,512,256]{2,1,0:T(8,128)(2,1)} %refs_1_.3), channel_id=1, source_target_pairs={{1,0},{2,1},{3,2},{4,3},{5,4},{6,5},{7,6},{9,8},{10,9},{11,10},{12... | collective-permute-start | bytes 3145736 | tf_op jit(solution)/shard_map/ppermute | solution.py:19
  2.6 4.6 %collective-permute-start = (bf16[4,512,256]{2,1,0:T(8,128)(2,1)}, bf16[4,512,256]{2,1,0:T(8,128)(2,1)S(1)}, u32[]{:S(2)}, u32[]{:S(2)}) collective-permute-start(bf16[4,512,256]{2,1,0:T(8,128)(2,1)} %refs_1_.3), channel_id=1, source_target_pairs={{0,1},{1,2},{2,3},{3,4},{4,5},{5,6},{6,7},{8,9},{9,10},{10,11},{11... | collective-permute-start | bytes 3145736 | tf_op jit(solution)/shard_map/ppermute | solution.py:18
  7.2 1.2 compare_select_fusion.2.size_ref
  8.4 0.7 broadcast_subtract_fusion
  9.1 0.5 slice_bitcast_fusion
  9.6 8.2 %shard_map.95.refs_3_ = bf16[16,192,512]{2,1,0:T(8,128)(2,1)} custom-call(s32[16]{0:T(128)} %get-tuple-element.13.lead_ref, s32[16]{0:T(128)} %compare_select_fusion.2.size_ref, bf16[4,512,256]{2,1,0:T(8,128)(2,1)} %refs_1_.3, bf16[16,2,192,256]{3,2,1,0:T(8,128)(2,1)} %bitcast.8), custom_call_target="tpu_custom_call" | custom-call | flops 805306368 | bytes 10485760 | tf_op jit(solution)/shard_map/pallas_call | solution.py:152
  17.9 1.3 collective-permute-done.refs_0_
  19.2 1.0 copy-done.3
  20.2 7.7 %shard_map.97 = (f32[4,192,192]{2,1,0:T(8,128)}, f32[4,192,192]{2,1,0:T(8,128)}) custom-call(s32[16]{0:T(128)} %get-tuple-element.13.lead_ref, s32[16]{0:T(128)} %get-tuple-element.12.trail_ref, s32[16]{0:T(128)} %compare_select_fusion.2.size_ref, s32[1]{0:T(128)} %bitcast.4.flip_ref, bf16[4,512,256]{2,1,0:T(8,128)(2,1)} %copy-done.3, ...), custom_call_target="tpu_custom_call" | custom-call | flops 1107296256 | bytes 6946816 | tf_op jit(solution)/shard_map/pallas_call | solution.py:252
  27.8 1.3 collective-permute-start.6
  29.1 8.0 %shard_map.96 = (f32[4,192,192]{2,1,0:T(8,128)}, f32[4,192,192]{2,1,0:T(8,128)}) custom-call(s32[16]{0:T(128)} %get-tuple-element.13.lead_ref, s32[16]{0:T(128)} %get-tuple-element.12.trail_ref, s32[16]{0:T(128)} %compare_select_fusion.2.size_ref, s32[1]{0:T(128)} %bitcast.2.flip_ref, bf16[4,512,256]{2,1,0:T(8,128)(2,1)} %copy-done.3, ...), custom_call_target="tpu_custom_call" | custom-call | flops 1107296256 | bytes 6946816 | tf_op jit(solution)/shard_map/pallas_call | solution.py:252
  37.1 1.3 collective-permute-start.2
  38.4 1.1 collective-permute-done.6
  39.5 0.1 add.67
  39.6 2.7 %collective-permute-start.7 = (f32[2,192,192]{2,1,0:T(8,128)S(1)}, f32[2,192,192]{2,1,0:T(8,128)S(1)}, u32[]{:S(2)}, u32[]{:S(2)}) collective-permute-start(f32[2,192,192]{2,1,0:T(8,128)S(1)} %constant_dynamic-slice_fusion), channel_id=1, source_target_pairs={{0,8},{8,0},{16,24},{24,16},{1,17},{9,25},{17,1},{25,9},{2,10},{10... | collective-permute-start | bytes 884744 | tf_op jit(solution)/shard_map/ppermute | solution.py:30
  42.4 6.1 %collective-permute-done.2 = f32[4,192,192]{2,1,0:T(8,128)} collective-permute-done((f32[4,192,192]{2,1,0:T(8,128)}, f32[4,192,192]{2,1,0:T(8,128)}, u32[]{:S(2)}, u32[]{:S(2)}) %collective-permute-start.2) | collective-permute-done | bytes 589856 | tf_op jit(solution)/shard_map/ppermute | solution.py:30
  48.5 1.2 add.63
  49.8 0.4 collective-permute-start.3
  50.2 2.2 %collective-permute-done.7 = f32[2,192,192]{2,1,0:T(8,128)S(1)} collective-permute-done((f32[2,192,192]{2,1,0:T(8,128)S(1)}, f32[2,192,192]{2,1,0:T(8,128)S(1)}, u32[]{:S(2)}, u32[]{:S(2)}) %collective-permute-start.7) | collective-permute-done | bytes 294944 | tf_op jit(solution)/shard_map/ppermute | solution.py:30
  52.5 1.3 collective-permute-start.8
  53.8 4.1 %collective-permute-done.3 = f32[2,192,192]{2,1,0:T(8,128)S(1)} collective-permute-done((f32[2,192,192]{2,1,0:T(8,128)S(1)}, f32[2,192,192]{2,1,0:T(8,128)S(1)}, u32[]{:S(2)}, u32[]{:S(2)}) %collective-permute-start.3) | collective-permute-done | bytes 294944 | tf_op jit(solution)/shard_map/ppermute | solution.py:30
  58.1 3.1 %collective-permute-done.8 = f32[2,192,192]{2,1,0:T(8,128)S(1)} collective-permute-done((f32[2,192,192]{2,1,0:T(8,128)S(1)}, f32[2,192,192]{2,1,0:T(8,128)S(1)}, u32[]{:S(2)}, u32[]{:S(2)}) %collective-permute-start.8) | collective-permute-done | bytes 294944 | tf_op jit(solution)/shard_map/ppermute | solution.py:30
  61.2 1.1 collective-permute-start.9
  62.4 2.8 %collective-permute-done.4 = f32[2,192,192]{2,1,0:T(8,128)S(1)} collective-permute-done((f32[2,192,192]{2,1,0:T(8,128)S(1)}, f32[2,192,192]{2,1,0:T(8,128)S(1)}, u32[]{:S(2)}, u32[]{:S(2)}) %collective-permute-start.4) | collective-permute-done | bytes 294944 | tf_op jit(solution)/shard_map/ppermute | solution.py:30
  65.3 1.3 collective-permute-start.5
  66.6 10.4 %collective-permute-done.9 = f32[4,192,192]{2,1,0:T(8,128)S(1)} collective-permute-done((f32[4,192,192]{2,1,0:T(8,128)S(1)}, f32[4,192,192]{2,1,0:T(8,128)S(1)}, u32[]{:S(2)}, u32[]{:S(2)}) %collective-permute-start.9) | collective-permute-done | bytes 589856 | tf_op jit(solution)/shard_map/ppermute | solution.py:30
  77.0 0.2 maximum_select_fusion.1
  77.2 5.8 %collective-permute-done.5 = f32[4,192,192]{2,1,0:T(8,128)S(1)} collective-permute-done((f32[4,192,192]{2,1,0:T(8,128)S(1)}, f32[4,192,192]{2,1,0:T(8,128)S(1)}, u32[]{:S(2)}, u32[]{:S(2)}) %collective-permute-start.5) | collective-permute-done | bytes 589856 | tf_op jit(solution)/shard_map/ppermute | solution.py:30
  83.0 0.2 maximum_select_fusion
  83.2 2.0 %pad_maximum_fusion = (f32[16,192,192]{2,1,0:T(8,128)}, f32[16,192,192]{2,1,0:T(8,128)S(1)}) fusion(f32[8,192,192]{2,1,0:T(8,128)S(1)} %maximum_select_fusion.1, f32[8,192,192]{2,1,0:T(8,128)S(1)} %maximum_select_fusion, f32[16,192]{1,0:T(8,128)S(1)} %copy-done.7), kind=kLoop, calls=%fused_computation | loop fusion | flops 2359296 | bytes 7090176 | tf_op jit(solution)/shard_map/concatenate | solution.py:77
  85.2 1.9 collective-permute-start.11
  87.2 9.6 %collective-permute-start.10 = (f32[16,192,192]{2,1,0:T(8,128)S(1)}, f32[16,192,192]{2,1,0:T(8,128)}, u32[]{:S(2)}, u32[]{:S(2)}) collective-permute-start(f32[16,192,192]{2,1,0:T(8,128)S(1)} %get-tuple-element.11.refs_1_.refs_7_), channel_id=1, source_target_pairs={{0,1},{1,2},{2,3},{3,4},{4,5},{5,6},{6,7},{8,9},{9,10},{10,11},{11... | collective-permute-start | bytes 7077896 | tf_op jit(solution)/shard_map/ppermute | solution.py:18
  96.7 0.6 broadcast_in_dim.26.refs_6_.refs_9_
  97.4 0.6 reshape.26.nb_ref
  98.1 0.6 reshape.27.fock_ref
  98.7 1.7 copy.14.refs_5_.refs_8_
  100.4 29.3 %collective-permute-done.11.refs_2_ = f32[16,192,192]{2,1,0:T(8,128)} collective-permute-done((f32[16,192,192]{2,1,0:T(8,128)S(1)}, f32[16,192,192]{2,1,0:T(8,128)}, u32[]{:S(2)}, u32[]{:S(2)}) %collective-permute-start.11) | collective-permute-done | bytes 2359328 | tf_op jit(solution)/shard_map/ppermute | solution.py:19
  129.7 1.1 collective-permute-done.10.refs_0_
  130.7 8.9 %shard_map.98.refs_2_ = f32[8,192,192]{2,1,0:T(8,128)} custom-call(s32[32]{0:T(128)} %reshape.26.nb_ref, s32[16]{0:T(128)} %compare_select_fusion.2.size_ref, f32[32]{0:T(128)} %reshape.27.fock_ref, f32[16,192,192]{2,1,0:T(8,128)} %collective-permute-done.10.refs_0_, f32[16,192,192]{2,1,0:T(8,128)} %copy-done, ...), custom_call_target="tpu_custom_call" | custom-call | flops 905969664 | bytes 7077888 | tf_op jit(solution)/shard_map/pallas_call | solution.py:354
  139.6 2.1 %collective-permute-start.14 = (f32[8,192,192]{2,1,0:T(8,128)}, f32[8,192,192]{2,1,0:T(8,128)S(1)}, u32[]{:S(2)}, u32[]{:S(2)}) collective-permute-start(f32[8,192,192]{2,1,0:T(8,128)} %shard_map.98.refs_2_), channel_id=1, source_target_pairs={{1,0},{2,1},{3,2},{4,3},{5,4},{6,5},{7,6},{9,8},{10,9},{11,10},{12... | collective-permute-start | bytes 3538952 | tf_op jit(solution)/shard_map/ppermute | solution.py:19
  141.7 4.8 %collective-permute-start.12 = (f32[8,192,192]{2,1,0:T(8,128)}, f32[8,192,192]{2,1,0:T(8,128)}, u32[]{:S(2)}, u32[]{:S(2)}) collective-permute-start(f32[8,192,192]{2,1,0:T(8,128)} %shard_map.98.refs_2_), channel_id=1, source_target_pairs={{0,1},{1,2},{2,3},{3,4},{4,5},{5,6},{6,7},{8,9},{9,10},{10,11},{11... | collective-permute-start | bytes 3538952 | tf_op jit(solution)/shard_map/ppermute | solution.py:18
  146.5 8.6 %shard_map.99.refs_3_ = f32[8,192,192]{2,1,0:T(8,128)} custom-call(s32[32]{0:T(128)} %reshape.26.nb_ref, s32[16]{0:T(128)} %compare_select_fusion.2.size_ref, f32[32]{0:T(128)} %reshape.27.fock_ref, f32[16,192,192]{2,1,0:T(8,128)} %collective-permute-done.10.refs_0_, f32[16,192,192]{2,1,0:T(8,128)} %copy-done, ...), custom_call_target="tpu_custom_call" | custom-call | flops 905969664 | bytes 7077888 | tf_op jit(solution)/shard_map/pallas_call | solution.py:354
  155.1 1.9 collective-permute-start.15
  157.0 3.9 %collective-permute-start.13 = (f32[8,192,192]{2,1,0:T(8,128)}, f32[8,192,192]{2,1,0:T(8,128)}, u32[]{:S(2)}, u32[]{:S(2)}) collective-permute-start(f32[8,192,192]{2,1,0:T(8,128)} %shard_map.99.refs_3_), channel_id=1, source_target_pairs={{0,1},{1,2},{2,3},{3,4},{4,5},{5,6},{6,7},{8,9},{9,10},{10,11},{11... | collective-permute-start | bytes 3538952 | tf_op jit(solution)/shard_map/ppermute | solution.py:18
  160.9 3.4 %pad_maximum_fusion.1.refs_10_ = f32[16,192,192]{2,1,0:T(8,128)} fusion(f32[8,192,192]{2,1,0:T(8,128)} %shard_map.99.refs_3_, f32[8,192,192]{2,1,0:T(8,128)S(1)} %copy-done.1), kind=kLoop, calls=%fused_computation.1 | loop fusion | flops 589824 | bytes 4718592 | tf_op jit(solution)/shard_map/concatenate | solution.py:423
  164.3 15.5 %collective-permute-done.15.refs_5_ = f32[8,192,192]{2,1,0:T(8,128)} collective-permute-done((f32[8,192,192]{2,1,0:T(8,128)}, f32[8,192,192]{2,1,0:T(8,128)}, u32[]{:S(2)}, u32[]{:S(2)}) %collective-permute-start.15) | collective-permute-done | bytes 1179680 | tf_op jit(solution)/shard_map/ppermute | solution.py:19
  179.8 1.2 collective-permute-done.13.refs_1_
  181.0 13.1 %shard_map.100 = f32[16,192,192]{2,1,0:T(8,128)} custom-call(s32[32]{0:T(128)} %reshape.26.nb_ref, s32[16]{0:T(128)} %compare_select_fusion.2.size_ref, f32[32]{0:T(128)} %reshape.27.fock_ref, f32[8,192,192]{2,1,0:T(8,128)} %collective-permute-done.12.refs_0_, f32[8,192,192]{2,1,0:T(8,128)} %collective-permute-done.13.refs_1_, ...), custom_call_target="tpu_custom_call" | custom-call | flops 1811939328 | bytes 14155776 | tf_op jit(solution)/shard_map/pallas_call | solution.py:354
  (32 shorter events, 0.7 us)
Async XLA Ops:
  0.6 17.3 %collective-permute-start.1 = (bf16[4,512,256]{2,1,0:T(8,128)(2,1)}, bf16[4,512,256]{2,1,0:T(8,128)(2,1)S(1)}, u32[]{:S(2)}, u32[]{:S(2)}) collective-permute-start(bf16[4,512,256]{2,1,0:T(8,128)(2,1)} %refs_1_.3), channel_id=1, source_target_pairs={{1,0},{2,1},{3,2},{4,3},{5,4},{6,5},{7,6},{9,8},{10,9},{11,10},{12... | collective-permute-start | bytes 3145736 | tf_op jit(solution)/shard_map/ppermute | solution.py:19
  2.6 16.6 %collective-permute-start = (bf16[4,512,256]{2,1,0:T(8,128)(2,1)}, bf16[4,512,256]{2,1,0:T(8,128)(2,1)S(1)}, u32[]{:S(2)}, u32[]{:S(2)}) collective-permute-start(bf16[4,512,256]{2,1,0:T(8,128)(2,1)} %refs_1_.3), channel_id=1, source_target_pairs={{0,1},{1,2},{2,3},{3,4},{4,5},{5,6},{6,7},{8,9},{9,10},{10,11},{11... | collective-permute-start | bytes 3145736 | tf_op jit(solution)/shard_map/ppermute | solution.py:18
  17.9 1.3 copy-start.2
  19.2 1.0 copy-start.3
  27.8 11.6 %collective-permute-start.6 = (f32[4,192,192]{2,1,0:T(8,128)}, f32[4,192,192]{2,1,0:T(8,128)S(1)}, u32[]{:S(2)}, u32[]{:S(2)}) collective-permute-start(f32[4,192,192]{2,1,0:T(8,128)} %get-tuple-element.9), channel_id=1, source_target_pairs={{0,16},{8,24},{16,0},{24,8},{1,9},{9,1},{17,25},{25,17},{2,18},{10... | collective-permute-start | bytes 1769480 | tf_op jit(solution)/shard_map/ppermute | solution.py:30
  29.1 10.4 %copy-start.5 = (f32[4,192,192]{2,1,0:T(8,128)S(1)}, f32[4,192,192]{2,1,0:T(8,128)}, u32[]{:S(2)}) copy-start(f32[4,192,192]{2,1,0:T(8,128)} %get-tuple-element.8) | copy-start | bytes 1769476
  37.1 11.4 %collective-permute-start.2 = (f32[4,192,192]{2,1,0:T(8,128)}, f32[4,192,192]{2,1,0:T(8,128)}, u32[]{:S(2)}, u32[]{:S(2)}) collective-permute-start(f32[4,192,192]{2,1,0:T(8,128)} %get-tuple-element.7), channel_id=1, source_target_pairs={{0,8},{8,0},{16,24},{24,16},{1,17},{9,25},{17,1},{25,9},{2,10},{10... | collective-permute-start | bytes 1769480 | tf_op jit(solution)/shard_map/ppermute | solution.py:30
  39.5 9.0 %copy-start.6 = (f32[4,192,192]{2,1,0:T(8,128)S(1)}, f32[4,192,192]{2,1,0:T(8,128)}, u32[]{:S(2)}) copy-start(f32[4,192,192]{2,1,0:T(8,128)} %get-tuple-element.6) | copy-start | bytes 1769476
  39.6 12.8 %collective-permute-start.7 = (f32[2,192,192]{2,1,0:T(8,128)S(1)}, f32[2,192,192]{2,1,0:T(8,128)S(1)}, u32[]{:S(2)}, u32[]{:S(2)}) collective-permute-start(f32[2,192,192]{2,1,0:T(8,128)S(1)} %constant_dynamic-slice_fusion), channel_id=1, source_target_pairs={{0,8},{8,0},{16,24},{24,16},{1,17},{9,25},{17,1},{25,9},{2,10},{10... | collective-permute-start | bytes 884744 | tf_op jit(solution)/shard_map/ppermute | solution.py:30
  49.8 8.1 %collective-permute-start.3 = (f32[2,192,192]{2,1,0:T(8,128)S(1)}, f32[2,192,192]{2,1,0:T(8,128)S(1)}, u32[]{:S(2)}, u32[]{:S(2)}) collective-permute-start(f32[2,192,192]{2,1,0:T(8,128)S(1)} %constant_dynamic-slice_fusion.1), channel_id=1, source_target_pairs={{0,16},{8,24},{16,0},{24,8},{1,9},{9,1},{17,25},{25,17},{2,18},{10... | collective-permute-start | bytes 884744 | tf_op jit(solution)/shard_map/ppermute | solution.py:30
  52.5 8.7 %collective-permute-start.8 = (f32[2,192,192]{2,1,0:T(8,128)S(1)}, f32[2,192,192]{2,1,0:T(8,128)S(1)}, u32[]{:S(2)}, u32[]{:S(2)}) collective-permute-start(f32[2,192,192]{2,1,0:T(8,128)S(1)} %dynamic-slice_add_fusion), channel_id=1, source_target_pairs={{0,8},{8,0},{16,24},{24,16},{1,17},{9,25},{17,1},{25,9},{2,10},{10... | collective-permute-start | bytes 884744 | tf_op jit(solution)/shard_map/ppermute | solution.py:30
  58.0 7.2 %collective-permute-start.4 = (f32[2,192,192]{2,1,0:T(8,128)S(1)}, f32[2,192,192]{2,1,0:T(8,128)S(1)}, u32[]{:S(2)}, u32[]{:S(2)}) collective-permute-start(f32[2,192,192]{2,1,0:T(8,128)S(1)} %dynamic-slice_add_fusion.1), channel_id=1, source_target_pairs={{0,16},{8,24},{16,0},{24,8},{1,9},{9,1},{17,25},{25,17},{2,18},{10... | collective-permute-start | bytes 884744 | tf_op jit(solution)/shard_map/ppermute | solution.py:30
  61.2 15.8 %collective-permute-start.9 = (f32[4,192,192]{2,1,0:T(8,128)S(1)}, f32[4,192,192]{2,1,0:T(8,128)S(1)}, u32[]{:S(2)}, u32[]{:S(2)}) collective-permute-start(f32[4,192,192]{2,1,0:T(8,128)S(1)} %maximum_select_fusion.3), channel_id=1, source_target_pairs={{0,16},{8,24},{16,0},{24,8},{1,9},{9,1},{17,25},{25,17},{2,18},{10... | collective-permute-start | bytes 1769480 | tf_op jit(solution)/shard_map/ppermute | solution.py:30
  65.3 17.7 %collective-permute-start.5 = (f32[4,192,192]{2,1,0:T(8,128)S(1)}, f32[4,192,192]{2,1,0:T(8,128)S(1)}, u32[]{:S(2)}, u32[]{:S(2)}) collective-permute-start(f32[4,192,192]{2,1,0:T(8,128)S(1)} %maximum_select_fusion.2), channel_id=1, source_target_pairs={{0,8},{8,0},{16,24},{24,16},{1,17},{9,25},{17,1},{25,9},{2,10},{10... | collective-permute-start | bytes 1769480 | tf_op jit(solution)/shard_map/ppermute | solution.py:30
  77.2 6.0 %copy-start.7 = (f32[16,192]{1,0:T(8,128)S(1)}, f32[16,192]{1,0:T(8,128)}, u32[]{:S(2)}) copy-start(f32[16,192]{1,0:T(8,128)} %param.12) | copy-start | bytes 36868
  83.2 14.2 %copy-start.9 = (s32[16,2]{0,1:T(2,128)S(1)}, s32[16,2]{0,1:T(2,128)}, u32[]{:S(2)}) copy-start(s32[16,2]{0,1:T(2,128)} %param.14) | copy-start | bytes 388
  83.2 14.9 %copy-start.8 = (f32[16,2]{0,1:T(2,128)S(1)}, f32[16,2]{0,1:T(2,128)}, u32[]{:S(2)}) copy-start(f32[16,2]{0,1:T(2,128)} %param.15) | copy-start | bytes 388
  85.2 45.5 %copy-start = (f32[16,192,192]{2,1,0:T(8,128)}, f32[16,192,192]{2,1,0:T(8,128)S(1)}, u32[]{:S(2)}) copy-start(f32[16,192,192]{2,1,0:T(8,128)S(1)} %get-tuple-element.11.refs_1_.refs_7_) | copy-start | bytes 7077892
  85.2 44.4 %collective-permute-start.11 = (f32[16,192,192]{2,1,0:T(8,128)S(1)}, f32[16,192,192]{2,1,0:T(8,128)}, u32[]{:S(2)}, u32[]{:S(2)}) collective-permute-start(f32[16,192,192]{2,1,0:T(8,128)S(1)} %get-tuple-element.11.refs_1_.refs_7_), channel_id=1, source_target_pairs={{1,0},{2,1},{3,2},{4,3},{5,4},{6,5},{7,6},{9,8},{10,9},{11,10},{12... | collective-permute-start | bytes 7077896 | tf_op jit(solution)/shard_map/ppermute | solution.py:19
  87.2 43.6 %collective-permute-start.10 = (f32[16,192,192]{2,1,0:T(8,128)S(1)}, f32[16,192,192]{2,1,0:T(8,128)}, u32[]{:S(2)}, u32[]{:S(2)}) collective-permute-start(f32[16,192,192]{2,1,0:T(8,128)S(1)} %get-tuple-element.11.refs_1_.refs_7_), channel_id=1, source_target_pairs={{0,1},{1,2},{2,3},{3,4},{4,5},{5,6},{6,7},{8,9},{9,10},{10,11},{11... | collective-permute-start | bytes 7077896 | tf_op jit(solution)/shard_map/ppermute | solution.py:18
  139.6 21.3 %copy-start.1 = (f32[8,192,192]{2,1,0:T(8,128)S(1)}, f32[8,192,192]{2,1,0:T(8,128)}, u32[]{:S(2)}) copy-start(f32[8,192,192]{2,1,0:T(8,128)} %shard_map.98.refs_2_) | copy-start | bytes 3538948
  139.6 24.7 %collective-permute-start.14 = (f32[8,192,192]{2,1,0:T(8,128)}, f32[8,192,192]{2,1,0:T(8,128)S(1)}, u32[]{:S(2)}, u32[]{:S(2)}) collective-permute-start(f32[8,192,192]{2,1,0:T(8,128)} %shard_map.98.refs_2_), channel_id=1, source_target_pairs={{1,0},{2,1},{3,2},{4,3},{5,4},{6,5},{7,6},{9,8},{10,9},{11,10},{12... | collective-permute-start | bytes 3538952 | tf_op jit(solution)/shard_map/ppermute | solution.py:19
  141.7 22.6 %collective-permute-start.12 = (f32[8,192,192]{2,1,0:T(8,128)}, f32[8,192,192]{2,1,0:T(8,128)}, u32[]{:S(2)}, u32[]{:S(2)}) collective-permute-start(f32[8,192,192]{2,1,0:T(8,128)} %shard_map.98.refs_2_), channel_id=1, source_target_pairs={{0,1},{1,2},{2,3},{3,4},{4,5},{5,6},{6,7},{8,9},{9,10},{10,11},{11... | collective-permute-start | bytes 3538952 | tf_op jit(solution)/shard_map/ppermute | solution.py:18
  155.1 24.7 %collective-permute-start.15 = (f32[8,192,192]{2,1,0:T(8,128)}, f32[8,192,192]{2,1,0:T(8,128)}, u32[]{:S(2)}, u32[]{:S(2)}) collective-permute-start(f32[8,192,192]{2,1,0:T(8,128)} %shard_map.99.refs_3_), channel_id=1, source_target_pairs={{1,0},{2,1},{3,2},{4,3},{5,4},{6,5},{7,6},{9,8},{10,9},{11,10},{12... | collective-permute-start | bytes 3538952 | tf_op jit(solution)/shard_map/ppermute | solution.py:19
  157.0 24.0 %collective-permute-start.13 = (f32[8,192,192]{2,1,0:T(8,128)}, f32[8,192,192]{2,1,0:T(8,128)}, u32[]{:S(2)}, u32[]{:S(2)}) collective-permute-start(f32[8,192,192]{2,1,0:T(8,128)} %shard_map.99.refs_3_), channel_id=1, source_target_pairs={{0,1},{1,2},{2,3},{3,4},{4,5},{5,6},{6,7},{8,9},{9,10},{10,11},{11... | collective-permute-start | bytes 3538952 | tf_op jit(solution)/shard_map/ppermute | solution.py:18
  164.3 16.7 %copy-start.4 = (f32[8,192,192]{2,1,0:T(8,128)}, f32[8,192,192]{2,1,0:T(8,128)S(1)}, u32[]{:S(2)}) copy-start(f32[8,192,192]{2,1,0:T(8,128)S(1)} %collective-permute-done.14.refs_4_) | copy-start | bytes 3538948
